TPU v7x, 32 devices: a whole 2x2x4 slice. The times are simulated.
32 devices in a mesh: dp: 2 (over y), vocab: 16 (over z, x, core).
Axes of the slice: x: 2, y: 2, z: 4, core: 2. Of those that a mesh axis runs over, the one named last changes fastest.
Arguments:
- hidden: bfloat16 [256, 8192], P('dp', 'vocab')
- weight: bfloat16 [16384, 8192], P('vocab', 'dp')
- teacher_ids: int32 [256, 64], P('dp'), may hold values from 0 to 16383, as said below
- teacher_logp: float32 [256, 64], P('dp'), may hold values from -12 to 0
- union_blocks: int32 [2, 16], replicated, may hold values from 0 to 127, as said below
Outputs:
- loss: float32 [256], P('dp')
- grad_hidden: bfloat16 [256, 8192], P('dp', 'vocab')
- grad_weight: bfloat16 [16384, 8192], P('vocab', 'dp')
Inputs may be any that keep to these rules, and one draw needn't show every extreme that they name: `union_blocks`: each row lists distinct blocks; at most 2 blocks of a row lie among the 8 blocks of one index of vocab (blocks b with b // 8 equal), and every row reaches 2 for some index. `teacher_ids`: the entries of a row are distinct and lie in blocks listed in union_blocks for the token's tile.
All inputs are finite; a program needn't handle non-finite values.
Results may differ from a plain program's by a relative error of at most 0.0053.
Values may be sent and summed in bfloat16 or wider, within the bound.
No kernel may reach another device: no remote copies, remote signals or barrier semaphores. Data moves between devices by JAX's collectives and lax.ppermute only.
A program may use at most 128 MiB of HBM per device.

v0:
```python
import jax
import jax.numpy as jnp
from jax import lax
from jax.sharding import PartitionSpec as P

BLOCK = 128
SLOTS = 2


negative = -1e30


def slot_table(union_blocks, column, per_dev):
    inside = union_blocks // per_dev == column
    rank = jnp.cumsum(inside.astype(jnp.int32), axis=1) - 1
    slot_ids = jnp.arange(SLOTS, dtype=jnp.int32)
    picks = inside[:, :, None] & (rank[:, :, None] == slot_ids[None, None, :])
    return jnp.sum(jnp.where(picks, union_blocks[:, :, None] + 1, 0), axis=1) - 1


def shards(hidden, weight, teacher_ids, teacher_logp, union_blocks):
    tokens_here = hidden.shape[0]
    n_groups = lax.axis_size("dp")
    per_dev = weight.shape[0] // BLOCK
    piece = weight.shape[1]
    width = SLOTS * BLOCK
    dp_row = lax.axis_index("dp")
    column = lax.axis_index("vocab")
    table = slot_table(union_blocks, column, per_dev)
    filled = table >= 0
    local = jnp.where(filled, table - column * per_dev, -1)
    blocks = weight.reshape(per_dev, BLOCK, piece)
    chosen = jnp.take(blocks, jnp.maximum(local, 0).reshape(-1), axis=0).reshape(
        n_groups, width, piece
    )
    full_rows = lax.all_gather(hidden, "vocab", axis=1, tiled=True)
    wide = full_rows.reshape(tokens_here, n_groups, piece)
    own_slots = lax.dynamic_index_in_dim(table, dp_row, 0, keepdims=False)
    col_mask = jnp.repeat(own_slots >= 0, BLOCK)
    rows_w = lax.all_to_all(chosen, "dp", split_axis=0, concat_axis=0, tiled=True)
    logits = jnp.einsum("tkd,krd->tr", wide, rows_w, preferred_element_type=jnp.float32)
    offsets = teacher_ids % BLOCK
    match = (teacher_ids // BLOCK)[:, :, None] == own_slots[None, None, :]
    starts = jnp.arange(SLOTS, dtype=jnp.int32) * BLOCK
    position = jnp.sum(jnp.where(match, starts[None, None, :] + offsets[:, :, None], 0), axis=-1)
    hit = jnp.any(match, axis=-1)
    teacher_q = jax.nn.softmax(teacher_logp, axis=-1) * hit.astype(jnp.float32)
    onehot = (position[:, :, None] == jnp.arange(width, dtype=jnp.int32)[None, None, :]).astype(
        jnp.float32
    )
    target = jnp.einsum("tk,tkr->tr", teacher_q, onehot)
    masked = jnp.where(col_mask[None, :], logits, negative)
    local_top = jnp.max(masked, axis=1)
    aimed = jnp.sum(target * logits, axis=1)
    top = lax.pmax(local_top, "vocab")
    local_total = jnp.sum(jnp.where(col_mask[None, :], jnp.exp(masked - top[:, None]), 0.0), axis=1)
    total, picked = lax.psum((local_total, aimed), "vocab")
    lse = top + jnp.log(total)
    loss = lse - picked
    probs = jnp.where(col_mask[None, :], jnp.exp(logits - lse[:, None]), 0.0)
    dlog = (probs - target).astype(jnp.bfloat16)
    hidden_terms = jnp.einsum("tr,krd->tkd", dlog, rows_w, preferred_element_type=jnp.float32)
    pieces_w = jnp.einsum("tr,tkd->krd", dlog, wide, preferred_element_type=jnp.float32).astype(
        jnp.bfloat16
    )
    received = lax.all_to_all(pieces_w, "dp", split_axis=0, concat_axis=0, tiled=True)
    hidden_terms = hidden_terms.reshape(tokens_here, n_groups * piece)
    grad_hidden = lax.psum_scatter(hidden_terms, "vocab", scatter_dimension=1, tiled=True).astype(
        jnp.bfloat16
    )
    owner_hot = (
        local.reshape(-1)[None, :] == jnp.arange(per_dev, dtype=jnp.int32)[:, None]
    ).astype(jnp.bfloat16)
    spread = received.reshape(n_groups * SLOTS, BLOCK * piece)
    grad_weight = jnp.einsum("vs,sx->vx", owner_hot, spread, preferred_element_type=jnp.float32)
    grad_weight = grad_weight.astype(jnp.bfloat16).reshape(per_dev * BLOCK, piece)
    return (loss, grad_hidden, grad_weight)


def solution(mesh):
    return jax.shard_map(
        shards,
        mesh=mesh,
        in_specs=(P("dp", "vocab"), P("vocab", "dp"), P("dp", None), P("dp", None), P()),
        out_specs=(P("dp"), P("dp", "vocab"), P("vocab", "dp")),
        check_vma=False,
    )
```

profile of v0, /device:TPU:0, one launch (start us, length us, event | category | flops | bytes accessed | tf_op | source)
XLA Modules:
  0.0 242.1 jit_solution(3332901610750979458)
XLA Ops:
  7.2 1.7 copy.19
  8.9 0.7 fusion.10
  9.6 0.2 reduce_window_sum.11
  9.8 0.7 broadcast_add_fusion.1
  10.5 0.1 fusion.6
  10.7 0.1 reshape.113
  10.8 6.2 %gather_fusion = bf16[4,128,4096]{2,1,0:T(8,128)(2,1)} fusion(bf16[8,128,4096]{2,1,0:T(8,128)(2,1)} %bitcast.36, s32[1024]{0:T(1024)S(1)} %pad_clamp_fusion), kind=kCustom, calls=%fused_computation | custom fusion | bytes 8388624 | tf_op jit(solution)/shard_map/jit(_take)/gather | solution.py:33
  17.0 4.6 %bitcast_select_fusion = bf16[2,256,4096]{2,1,0:T(8,128)(2,1)} fusion(pred[2,256]{1,0:T(4,128)(4,1)S(1)} %bitcast.37, bf16[2,256,4096]{2,1,0:T(8,128)(2,1)} %bitcast.33), kind=kLoop, calls=%fused_computation.6 | loop fusion | flops 2097152 | bytes 8389120 | tf_op jit(solution)/shard_map/jit(_take)/select_n | solution.py:33
  21.7 5.8 %all-to-all-start = ((bf16[2,256,4096]{2,1,0:T(8,128)(2,1)}), bf16[2,256,4096]{2,1,0:T(8,128)(2,1)}, u32[]{:S(2)}, u32[]{:S(2)}) async-start(bf16[2,256,4096]{2,1,0:T(8,128)(2,1)} %bitcast_select_fusion), calls=%async_computation | async-start | bytes 8388608 | tf_op jit(solution)/shard_map/all_to_all | solution.py:40
  27.7 0.1 copy.35
  27.8 0.1 fusion.1
  27.9 0.1 copy.21
  28.0 2.8 %select_reduce_fusion = f32[128,256]{1,0:T(8,128)S(1)} fusion(f32[128,64]{1,0:T(8,128)S(1)} %copy.35, s32[128,64]{1,0:T(8,128)S(1)} %copy.21), kind=kLoop, calls=%fused_computation.2 | loop fusion | flops 6258688 | bytes 196608
  30.9 0.1 copy.30
  31.0 45.3 %all-to-all-done = bf16[2,256,4096]{2,1,0:T(8,128)(2,1)} async-done(((bf16[2,256,4096]{2,1,0:T(8,128)(2,1)}), bf16[2,256,4096]{2,1,0:T(8,128)(2,1)}, u32[]{:S(2)}, u32[]{:S(2)}) %all-to-all-start) | async-done | bytes 4194336 | tf_op jit(solution)/shard_map/all_to_all | solution.py:40
  76.3 4.1 %select_reduce_fusion.2 = (f32[128]{0:T(128)S(1)}, f32[128,256]{0,1:T(8,128)S(1)}) fusion(pred[256]{0:T(512)(128)(4,1)S(1)} %broadcast_bitcast_fusion.1, bf16[2,256,4096]{2,1,0:T(8,128)(2,1)} %all-to-all-done, bf16[128,2,4096]{0,2,1:T(8,128)(2,1)} %bitcast.34), kind=kOutput, calls=%fused_computation.11 | convolution fusion | flops 536936320 | bytes 6423296 | tf_op jit(solution)/shard_map/tkd,krd->tr/dot_general | solution.py:41
  80.4 32.8 %pmax.7 = f32[128]{0:T(128)S(1)} all-reduce(f32[128]{0:T(128)S(1)} %get-tuple-element.23), channel_id=1, replica_groups=mesh['dp'=2,'vocab'=16] {'vocab'}, use_global_device_ids=true, to_apply=%region_3.4 | all-reduce | flops 128 | bytes 1024 | tf_op jit(solution)/shard_map/pmax | solution.py:55
  113.3 0.1 multiply_reduce_fusion
  113.4 29.5 %all-reduce = (f32[128]{0:T(128)S(1)}, f32[128]{0:T(128)S(1)}) all-reduce(f32[128]{0:T(128)S(1)} %get-tuple-element.10, f32[128]{0:T(128)S(1)} %get-tuple-element.9), channel_id=1, replica_groups=mesh['dp'=2,'vocab'=16] {'vocab'}, use_global_device_ids=true, to_apply=%region_5.6 | all-reduce | flops 256 | bytes 2048 | tf_op jit(solution)/shard_map/psum | solution.py:57
  142.9 0.5 fusion.9
  143.4 0.1 fusion.2
  143.5 5.9 %fusion.12 = f32[128,2,4096]{0,2,1:T(8,128)} fusion(bf16[128,256,1]{0,1,2:T(8,128)(2,1)S(1)} %fusion.2, bf16[2,256,4096]{2,1,0:T(8,128)(2,1)} %all-to-all-done), kind=kOutput, calls=%fused_computation.52 | convolution fusion | flops 536870912 | bytes 8454144 | tf_op jit(solution)/shard_map/tr,krd->tkd/dot_general | solution.py:62
  149.5 1.6 copy-done
  151.1 3.3 %fusion = bf16[2,256,4096]{2,1,0:T(8,128)(2,1)} fusion(bf16[128,256,1]{0,1,2:T(8,128)(2,1)S(1)} %fusion.2, bf16[128,2,4096]{0,2,1:T(8,128)(2,1)S(1)} %bitcast.35), kind=kOutput, calls=%fused_computation.5 | convolution fusion | flops 538968064 | bytes 6356992 | tf_op jit(solution)/shard_map/tr,tkd->krd/dot_general | solution.py:63
  154.3 5.9 %all-to-all-start.1 = ((bf16[2,256,4096]{2,1,0:T(8,128)(2,1)}), bf16[2,256,4096]{2,1,0:T(8,128)(2,1)}, u32[]{:S(2)}, u32[]{:S(2)}) async-start(bf16[2,256,4096]{2,1,0:T(8,128)(2,1)} %fusion), calls=%async_computation.2 | async-start | bytes 8388608 | tf_op jit(solution)/shard_map/all_to_all | solution.py:66
  160.2 0.1 select_n.84
  160.3 47.4 %all-to-all-done.1 = bf16[2,256,4096]{2,1,0:T(8,128)(2,1)} async-done(((bf16[2,256,4096]{2,1,0:T(8,128)(2,1)}), bf16[2,256,4096]{2,1,0:T(8,128)(2,1)}, u32[]{:S(2)}, u32[]{:S(2)}) %all-to-all-start.1) | async-done | bytes 4194336 | tf_op jit(solution)/shard_map/all_to_all | solution.py:66
  207.7 7.5 %reshape.109 = bf16[4,524288]{1,0:T(4,128)(2,1)} reshape(bf16[2,256,4096]{2,1,0:T(8,128)(2,1)} %all-to-all-done.1) | data formatting | bytes 8388608 | tf_op jit(solution)/shard_map/reshape | solution.py:74
  215.2 7.7 %convolution_convert_fusion = bf16[8,524288]{1,0:T(8,128)(2,1)} fusion(bf16[4,524288]{1,0:T(4,128)(2,1)} %reshape.109, s32[4]{0:T(128)S(1)} %select_n.84), kind=kOutput, calls=%fused_computation.1 | convolution fusion | flops 37748768 | bytes 12582928 | tf_op jit(solution)/shard_map/vs,sx->vx/dot_general | solution.py:75
  222.9 10.6 %reshape.110 = bf16[1024,4096]{1,0:T(8,128)(2,1)} reshape(bf16[8,524288]{1,0:T(8,128)(2,1)} %convolution_convert_fusion) | data formatting | bytes 16777216 | tf_op jit(solution)/shard_map/reshape | solution.py:76
  233.5 1.0 convert_element_type.23
  234.5 0.8 copy.25
  (25 shorter events, 0.5 us)
Async XLA Ops:
  7.2 69.2 %all-gather.2.cloned.1.call-start = ((), (), s32[]{:S(2)}) async-start(), calls=%async_computation.3 | async-start | bytes 2228224 | tf_op jit(solution)/shard_map/all_gather | solution.py:36
  21.7 5.8 %copy-start.1 = (f32[128,64]{0,1:T(8,128)S(1)}, f32[128,64]{0,1:T(8,128)}, u32[]{:S(2)}) copy-start(f32[128,64]{0,1:T(8,128)} %param.8) | copy-start | bytes 98308
  21.7 5.9 %copy-start.2 = (s32[128,64]{0,1:T(8,128)S(1)}, s32[128,64]{0,1:T(8,128)}, u32[]{:S(2)}) copy-start(s32[128,64]{0,1:T(8,128)} %param.7) | copy-start | bytes 98308
  21.7 54.6 %all-to-all-start = ((bf16[2,256,4096]{2,1,0:T(8,128)(2,1)}), bf16[2,256,4096]{2,1,0:T(8,128)(2,1)}, u32[]{:S(2)}, u32[]{:S(2)}) async-start(bf16[2,256,4096]{2,1,0:T(8,128)(2,1)} %bitcast_select_fusion), calls=%async_computation | async-start | bytes 8388608 | tf_op jit(solution)/shard_map/all_to_all | solution.py:40
  27.4 206.1 %reduce-scatter.2.cloned.1.call-start = ((), (), s32[]{:S(2)}) async-start(), calls=%async_computation.4 | async-start | bytes 4456448 | tf_op jit(solution)/shard_map/reduce_scatter | solution.py:68
  149.5 1.6 copy-start
  154.3 53.4 %all-to-all-start.1 = ((bf16[2,256,4096]{2,1,0:T(8,128)(2,1)}), bf16[2,256,4096]{2,1,0:T(8,128)(2,1)}, u32[]{:S(2)}, u32[]{:S(2)}) async-start(bf16[2,256,4096]{2,1,0:T(8,128)(2,1)} %fusion), calls=%async_computation.2 | async-start | bytes 8388608 | tf_op jit(solution)/shard_map/all_to_all | solution.py:66
Sparse Core Ops, SparseCore 0:
  10.7 44.1 all-gather.1
  149.6 69.0 reduce-scatter.1
where the time goes:
time: 243 us; the launch traced here: 242 us
  waiting for transfers between devices  92.8 us (38%)
  blocking collectives  62.3 us (26%)
  local copies, waits for them, and re-layouts  28.8 us (12%)
  matrix products  21.1 us (9%)
  between operations  14.2 us (6%)
  starting transfers between devices  11.7 us (5%)
  other arithmetic  11.2 us (5%)
    all_to_all x1, waiting for transfers between devices, shards(): lax.all_to_all(pieces_w, 'dp', split_axis=0, concat_axis=0, tiled=True)  47.4 us
    all_to_all x1, waiting for transfers between devices, shards(): lax.all_to_all(chosen, 'dp', split_axis=0, concat_axis=0, tiled=True)  45.3 us
    pmax x1, blocking collectives, shards(): top = lax.pmax(local_top, 'vocab')  32.8 us
    psum x1, blocking collectives, shards(): total, picked = lax.psum((local_total, aimed), 'vocab')  29.5 us
    reshape x1, local copies, waits for them, and re-layouts, shards(): grad_weight.astype(jnp.bfloat16).reshape(per_dev * BLOCK, piece)  10.6 us
    dot_general x1, matrix products, shards(): jnp.einsum('vs,sx->vx', owner_hot, spread, preferred_element_type=jnp.flo...  7.74 us
    reshape x1, local copies, waits for them, and re-layouts, shards(): spread = received.reshape(n_groups * SLOTS, BLOCK * piece)  7.46 us
    gather x1, local copies, waits for them, and re-layouts, shards(): jnp.take(blocks, jnp.maximum(local, 0).reshape(-1), axis=0)  6.21 us
  transfers between devices with their start and end apart: 4, of which 2 were waited for; matrix products, arithmetic and copies ran while one was open for 19% of the time, Pallas kernels for 0%

commit v1 on v0

--- a/solution.py
+++ b/solution.py
@@ -52,9 +52,11 @@
     masked = jnp.where(col_mask[None, :], logits, negative)
     local_top = jnp.max(masked, axis=1)
     aimed = jnp.sum(target * logits, axis=1)
-    top = lax.pmax(local_top, "vocab")
-    local_total = jnp.sum(jnp.where(col_mask[None, :], jnp.exp(masked - top[:, None]), 0.0), axis=1)
-    total, picked = lax.psum((local_total, aimed), "vocab")
+    local_total = jnp.sum(jnp.where(col_mask[None, :], jnp.exp(masked - local_top[:, None]), 0.0), axis=1)
+    stats = lax.all_gather(jnp.stack([local_top, local_total, aimed]), "vocab")
+    top = jnp.max(stats[:, 0], axis=0)
+    total = jnp.sum(stats[:, 1] * jnp.exp(stats[:, 0] - top[None, :]), axis=0)
+    picked = jnp.sum(stats[:, 2], axis=0)
     lse = top + jnp.log(total)
     loss = lse - picked
     probs = jnp.where(col_mask[None, :], jnp.exp(logits - lse[:, None]), 0.0)
@@ -68,11 +70,14 @@
     grad_hidden = lax.psum_scatter(hidden_terms, "vocab", scatter_dimension=1, tiled=True).astype(
         jnp.bfloat16
     )
-    owner_hot = (
-        local.reshape(-1)[None, :] == jnp.arange(per_dev, dtype=jnp.int32)[:, None]
-    ).astype(jnp.bfloat16)
-    spread = received.reshape(n_groups * SLOTS, BLOCK * piece)
-    grad_weight = jnp.einsum("vs,sx->vx", owner_hot, spread, preferred_element_type=jnp.float32)
+    spread = received.reshape(n_groups * SLOTS, BLOCK, piece)
+    owners = local.reshape(-1)
+    block_ids = jnp.arange(per_dev, dtype=jnp.int32)[:, None, None]
+    grad_weight = jnp.zeros((per_dev, BLOCK, piece), jnp.float32)
+    for q in range(n_groups * SLOTS):
+        grad_weight = grad_weight + jnp.where(
+            block_ids == owners[q], spread[q][None].astype(jnp.float32), 0.0
+        )
     grad_weight = grad_weight.astype(jnp.bfloat16).reshape(per_dev * BLOCK, piece)
     return (loss, grad_hidden, grad_weight)
 

time: 243 us -> 193 us (0.79)
  blocking collectives: 62.3 us -> 21.9 us
  other arithmetic: 11.2 us -> 30 us
  local copies, waits for them, and re-layouts: 28.8 us -> 11.7 us
  matrix products: 21.1 us -> 13.3 us
  waiting for transfers between devices: 92.8 us -> 90.1 us
    pmax x1 -> x0, blocking collectives: 32.8 us -> none  [shards(): top = lax.pmax(local_top, 'vocab')]
    psum x1 -> x0, blocking collectives: 29.5 us -> none  [shards(): total, picked = lax.psum((local_total, aimed), 'vocab')]
    all_gather x0 -> x1, blocking collectives: none -> 21.9 us  [shards(): stats = lax.all_gather(jnp.stack([local_top, local_total, aimed]), 'vocab')]
    reshape x2 -> x0, local copies, waits for them, and re-layouts: 18 us -> none  [the longest x1 10.6 us: shards(): grad_weight.astype(jnp.bfloat16).reshape(per_dev * BLOCK, piece)]
    convert_element_type x0 -> x1, other arithmetic: none -> 13 us  [shards(): grad_weight.astype(jnp.bfloat16).reshape(per_dev * BLOCK, piece)]
    dot_general x1 -> x0, matrix products: 7.74 us -> none  [shards(): jnp.einsum('vs,sx->vx', owner_hot, spread, preferred_element_type=jnp.flo...]
    broadcast_in_dim x0 -> x1, other arithmetic: none -> 3.27 us  [shards(): jnp.where(block_ids == owners[q], spread[q][None].astype(jnp.float32), 0.0)]
    all_to_all x1, waiting for transfers between devices: 47.4 us -> 44.7 us  [shards(): lax.all_to_all(pieces_w, 'dp', split_axis=0, concat_axis=0, tiled=True)]
  transfers between devices with their start and end apart: 4 -> 4, of which waited for: 2 -> 2; matrix products, arithmetic and copies ran while one was open for 19% -> 20% of each run, Pallas kernels for 0% -> 0%
where the time goes in v1:
time: 193 us
  waiting for transfers between devices  90.1 us (47%)
  other arithmetic  30 us (16%)
  blocking collectives  21.9 us (11%)
  between operations  14.2 us (7%)
  matrix products  13.3 us (7%)
  local copies, waits for them, and re-layouts  11.7 us (6%)
  starting transfers between devices  11.5 us (6%)
    all_to_all x1, waiting for transfers between devices, shards(): lax.all_to_all(chosen, 'dp', split_axis=0, concat_axis=0, tiled=True)  45.4 us
    all_to_all x1, waiting for transfers between devices, shards(): lax.all_to_all(pieces_w, 'dp', split_axis=0, concat_axis=0, tiled=True)  44.7 us
    all_gather x1, blocking collectives, shards(): stats = lax.all_gather(jnp.stack([local_top, local_total, aimed]), 'vocab')  21.9 us
    convert_element_type x1, other arithmetic, shards(): grad_weight.astype(jnp.bfloat16).reshape(per_dev * BLOCK, piece)  13 us
    gather x1, local copies, waits for them, and re-layouts, shards(): jnp.take(blocks, jnp.maximum(local, 0).reshape(-1), axis=0)  6.21 us
    dot_general x1, matrix products, shards(): jnp.einsum('tr,krd->tkd', dlog, rows_w, preferred_element_type=jnp.float32)  5.89 us
    all_to_all x1, starting transfers between devices, shards(): lax.all_to_all(chosen, 'dp', split_axis=0, concat_axis=0, tiled=True)  5.73 us
    all_to_all x1, starting transfers between devices, shards(): lax.all_to_all(pieces_w, 'dp', split_axis=0, concat_axis=0, tiled=True)  5.7 us
  transfers between devices with their start and end apart: 4, of which 2 were waited for; matrix products, arithmetic and copies ran while one was open for 20% of the time, Pallas kernels for 0%

profile of v1, /device:TPU:0, one launch (start us, length us, event | category | flops | bytes accessed | tf_op | source)
XLA Modules:
  0.0 192.8 jit_solution(9365572206780852521)
XLA Ops:
  7.2 1.7 copy.30
  8.9 0.7 fusion.17
  9.6 0.2 reduce_window_sum.11
  9.8 0.7 broadcast_add_fusion.1
  10.5 0.1 fusion.14
  10.8 6.2 %gather_fusion = bf16[4,128,4096]{2,1,0:T(8,128)(2,1)} fusion(bf16[8,128,4096]{2,1,0:T(8,128)(2,1)} %bitcast.99, s32[1024]{0:T(1024)S(1)} %pad_clamp_fusion), kind=kCustom, calls=%fused_computation | custom fusion | bytes 8388624 | tf_op jit(solution)/shard_map/jit(_take)/gather | solution.py:33
  17.0 4.6 %bitcast_select_fusion.4 = bf16[2,256,4096]{2,1,0:T(8,128)(2,1)} fusion(pred[2,256]{1,0:T(4,128)(4,1)S(1)} %bitcast.104, bf16[2,256,4096]{2,1,0:T(8,128)(2,1)} %bitcast.96), kind=kLoop, calls=%fused_computation.13 | loop fusion | flops 2097152 | bytes 8389120 | tf_op jit(solution)/shard_map/jit(_take)/select_n | solution.py:33
  21.7 5.7 %all-to-all-start = ((bf16[2,256,4096]{2,1,0:T(8,128)(2,1)}), bf16[2,256,4096]{2,1,0:T(8,128)(2,1)}, u32[]{:S(2)}, u32[]{:S(2)}) async-start(bf16[2,256,4096]{2,1,0:T(8,128)(2,1)} %bitcast_select_fusion.4), calls=%async_computation | async-start | bytes 8388608 | tf_op jit(solution)/shard_map/all_to_all | solution.py:40
  27.7 0.1 copy.48
  27.9 0.1 copy.32
  28.0 2.8 %select_reduce_fusion = f32[128,256]{1,0:T(8,128)S(1)} fusion(f32[128,64]{1,0:T(8,128)S(1)} %copy.48, s32[128,64]{1,0:T(8,128)S(1)} %copy.32), kind=kLoop, calls=%fused_computation.9 | loop fusion | flops 6258688 | bytes 196608
  30.8 0.1 copy.42
  31.0 45.4 %all-to-all-done = bf16[2,256,4096]{2,1,0:T(8,128)(2,1)} async-done(((bf16[2,256,4096]{2,1,0:T(8,128)(2,1)}), bf16[2,256,4096]{2,1,0:T(8,128)(2,1)}, u32[]{:S(2)}, u32[]{:S(2)}) %all-to-all-start) | async-done | bytes 4194336 | tf_op jit(solution)/shard_map/all_to_all | solution.py:40
  76.4 4.1 %select_reduce_fusion.2 = (f32[128]{0:T(128)S(1)}, f32[128,256]{0,1:T(8,128)S(1)}) fusion(pred[256]{0:T(512)(128)(4,1)S(1)} %broadcast_bitcast_fusion.5, bf16[2,256,4096]{2,1,0:T(8,128)(2,1)} %all-to-all-done, bf16[128,2,4096]{0,2,1:T(8,128)(2,1)} %bitcast.97), kind=kOutput, calls=%fused_computation.26 | convolution fusion | flops 536936320 | bytes 6423296 | tf_op jit(solution)/shard_map/tkd,krd->tr/dot_general | solution.py:41
  80.5 0.1 select_reduce_fusion.1
  80.6 21.9 %all-gather.1 = f32[16,3,128]{2,1,0:T(4,128)S(1)} all-gather(f32[1,3,128]{2,1,0:T(4,128)S(1)} %maximum_bitcast_fusion), channel_id=2, replica_groups=mesh['dp'=2,'vocab'=16] {'vocab'}, dimensions={0}, use_global_device_ids=true | all-gather | bytes 26112 | tf_op jit(solution)/shard_map/all_gather | solution.py:56
  102.6 0.5 fusion.16
  103.1 0.1 fusion.10
  103.2 5.9 %fusion.21 = f32[128,2,4096]{0,2,1:T(8,128)} fusion(bf16[128,256,1]{0,1,2:T(8,128)(2,1)S(1)} %fusion.10, bf16[2,256,4096]{2,1,0:T(8,128)(2,1)} %all-to-all-done), kind=kOutput, calls=%fused_computation.78 | convolution fusion | flops 536870912 | bytes 8454144 | tf_op jit(solution)/shard_map/tr,krd->tkd/dot_general | solution.py:64
  109.2 1.6 copy-done
  110.7 3.3 %fusion.4 = bf16[2,256,4096]{2,1,0:T(8,128)(2,1)} fusion(bf16[128,256,1]{0,1,2:T(8,128)(2,1)S(1)} %fusion.10, bf16[128,2,4096]{0,2,1:T(8,128)(2,1)S(1)} %bitcast.98), kind=kOutput, calls=%fused_computation.12 | convolution fusion | flops 538968064 | bytes 6356992 | tf_op jit(solution)/shard_map/tr,tkd->krd/dot_general | solution.py:65
  114.0 5.7 %all-to-all-start.1 = ((bf16[2,256,4096]{2,1,0:T(8,128)(2,1)}), bf16[2,256,4096]{2,1,0:T(8,128)(2,1)}, u32[]{:S(2)}, u32[]{:S(2)}) async-start(bf16[2,256,4096]{2,1,0:T(8,128)(2,1)} %fusion.4), calls=%async_computation.2 | async-start | bytes 8388608 | tf_op jit(solution)/shard_map/all_to_all | solution.py:68
  119.8 0.6 fusion.20
  120.4 0.7 iota_compare_fusion.4
  121.0 0.6 iota_compare_fusion.1
  121.6 0.6 iota_compare_fusion.2
  122.3 0.6 iota_compare_fusion.3
  123.1 44.7 %all-to-all-done.1 = bf16[2,256,4096]{2,1,0:T(8,128)(2,1)} async-done(((bf16[2,256,4096]{2,1,0:T(8,128)(2,1)}), bf16[2,256,4096]{2,1,0:T(8,128)(2,1)}, u32[]{:S(2)}, u32[]{:S(2)}) %all-to-all-start.1) | async-done | bytes 4194336 | tf_op jit(solution)/shard_map/all_to_all | solution.py:68
  167.9 3.3 %fusion.8 = (f32[128,4096]{1,0:T(8,128)S(1)}, f32[128,4096]{1,0:T(8,128)S(1)}, f32[128,4096]{1,0:T(8,128)S(1)}, f32[128,4096]{1,0:T(8,128)S(1)}) fusion(bf16[4,128,4096]{2,1,0:T(8,128)(2,1)} %bitcast.20), kind=kLoop, calls=%fused_computation.22 | loop fusion | flops 2097152 | bytes 12582912 | tf_op jit(solution)/shard_map/jit(_where)/broadcast_in_dim | solution.py:78
  171.2 13.0 %fusion.1 = bf16[1024,4096]{1,0:T(8,128)(2,1)} fusion(f32[128,4096]{1,0:T(8,128)S(1)} %get-tuple-element.23, f32[128,4096]{1,0:T(8,128)S(1)} %get-tuple-element.24, f32[128,4096]{1,0:T(8,128)S(1)} %get-tuple-element.25, f32[128,4096]{1,0:T(8,128)S(1)} %get-tuple-element.22, pred[1024]{0:T(1024)(128)(4,1)S(1)} %broadcast_bitcast_fusion.1, ...), kind=kLoop, calls=%fused_computation.3 | loop fusion | flops 33554432 | bytes 16781312 | tf_op jit(solution)/shard_map/convert_element_type | solution.py:81
  184.2 1.0 convert_element_type.27
  185.2 0.8 copy.37
  (36 shorter events, 1.1 us)
Async XLA Ops:
  7.2 69.2 %all-gather.4.cloned.1.call-start = ((), (), s32[]{:S(2)}) async-start(), calls=%async_computation.3 | async-start | bytes 2228224 | tf_op jit(solution)/shard_map/all_gather | solution.py:36
  21.7 5.8 %copy-start.1 = (f32[128,64]{0,1:T(8,128)S(1)}, f32[128,64]{0,1:T(8,128)}, u32[]{:S(2)}) copy-start(f32[128,64]{0,1:T(8,128)} %param.8) | copy-start | bytes 98308
  21.7 5.9 %copy-start.2 = (s32[128,64]{0,1:T(8,128)S(1)}, s32[128,64]{0,1:T(8,128)}, u32[]{:S(2)}) copy-start(s32[128,64]{0,1:T(8,128)} %param.7) | copy-start | bytes 98308
  21.7 54.7 %all-to-all-start = ((bf16[2,256,4096]{2,1,0:T(8,128)(2,1)}), bf16[2,256,4096]{2,1,0:T(8,128)(2,1)}, u32[]{:S(2)}, u32[]{:S(2)}) async-start(bf16[2,256,4096]{2,1,0:T(8,128)(2,1)} %bitcast_select_fusion.4), calls=%async_computation | async-start | bytes 8388608 | tf_op jit(solution)/shard_map/all_to_all | solution.py:40
  27.4 156.8 %reduce-scatter.2.cloned.1.call-start = ((), (), s32[]{:S(2)}) async-start(), calls=%async_computation.4 | async-start | bytes 4456448 | tf_op jit(solution)/shard_map/reduce_scatter | solution.py:70
  109.1 1.6 copy-start
  114.0 53.9 %all-to-all-start.1 = ((bf16[2,256,4096]{2,1,0:T(8,128)(2,1)}), bf16[2,256,4096]{2,1,0:T(8,128)(2,1)}, u32[]{:S(2)}, u32[]{:S(2)}) async-start(bf16[2,256,4096]{2,1,0:T(8,128)(2,1)} %fusion.4), calls=%async_computation.2 | async-start | bytes 8388608 | tf_op jit(solution)/shard_map/all_to_all | solution.py:68
Sparse Core Ops, SparseCore 0:
  10.7 44.1 all-gather.3
  109.3 68.8 reduce-scatter.1

commit v2 on v1

--- a/solution.py
+++ b/solution.py
@@ -35,6 +35,7 @@
     )
     full_rows = lax.all_gather(hidden, "vocab", axis=1, tiled=True)
     wide = full_rows.reshape(tokens_here, n_groups, piece)
+    halves = lax.all_to_all(wide, "dp", split_axis=1, concat_axis=1, tiled=True)
     own_slots = lax.dynamic_index_in_dim(table, dp_row, 0, keepdims=False)
     col_mask = jnp.repeat(own_slots >= 0, BLOCK)
     rows_w = lax.all_to_all(chosen, "dp", split_axis=0, concat_axis=0, tiled=True)
@@ -62,23 +63,22 @@
     probs = jnp.where(col_mask[None, :], jnp.exp(logits - lse[:, None]), 0.0)
     dlog = (probs - target).astype(jnp.bfloat16)
     hidden_terms = jnp.einsum("tr,krd->tkd", dlog, rows_w, preferred_element_type=jnp.float32)
-    pieces_w = jnp.einsum("tr,tkd->krd", dlog, wide, preferred_element_type=jnp.float32).astype(
-        jnp.bfloat16
-    )
-    received = lax.all_to_all(pieces_w, "dp", split_axis=0, concat_axis=0, tiled=True)
     hidden_terms = hidden_terms.reshape(tokens_here, n_groups * piece)
     grad_hidden = lax.psum_scatter(hidden_terms, "vocab", scatter_dimension=1, tiled=True).astype(
         jnp.bfloat16
     )
-    spread = received.reshape(n_groups * SLOTS, BLOCK, piece)
-    owners = local.reshape(-1)
-    block_ids = jnp.arange(per_dev, dtype=jnp.int32)[:, None, None]
-    grad_weight = jnp.zeros((per_dev, BLOCK, piece), jnp.float32)
-    for q in range(n_groups * SLOTS):
-        grad_weight = grad_weight + jnp.where(
-            block_ids == owners[q], spread[q][None].astype(jnp.float32), 0.0
+    dlog_all = lax.all_gather(dlog, "dp").reshape(n_groups, tokens_here, SLOTS, BLOCK)
+    block_ids = jnp.arange(per_dev, dtype=jnp.int32)
+    placed = jnp.zeros((n_groups, tokens_here, per_dev, BLOCK), jnp.bfloat16)
+    for q in range(SLOTS):
+        hit_q = local[:, q][:, None] == block_ids[None, :]
+        placed = placed + jnp.where(
+            hit_q[:, None, :, None], dlog_all[:, :, q, :][:, :, None, :], jnp.zeros((), jnp.bfloat16)
         )
-    grad_weight = grad_weight.astype(jnp.bfloat16).reshape(per_dev * BLOCK, piece)
+    placed = placed.reshape(n_groups, tokens_here, per_dev * BLOCK)
+    grad_weight = jnp.einsum(
+        "str,tsd->rd", placed, halves, preferred_element_type=jnp.float32
+    ).astype(jnp.bfloat16)
     return (loss, grad_hidden, grad_weight)
 
 

time: 193 us -> 187 us (0.969)
  blocking collectives: 21.9 us -> 48.6 us
  other arithmetic: 30 us -> 12.2 us
  waiting for transfers between devices: 90.1 us -> 73.7 us
  local copies, waits for them, and re-layouts: 11.7 us -> 13.8 us
    all_to_all x1, waiting for transfers between devices: 44.7 us -> 0.01 us  [shards(): halves = lax.all_to_all(wide, 'dp', split_axis=1, concat_axis=1, tiled=True)]
    reduce_scatter x1, waiting for transfers between devices: 0.01 us -> 28.3 us  [shards(): lax.psum_scatter(hidden_terms, 'vocab', scatter_dimension=1, tiled=True)]
    all_gather x0 -> x1, blocking collectives: none -> 26.7 us  [shards(): lax.all_gather(dlog, 'dp').reshape(n_groups, tokens_here, SLOTS, BLOCK)]
    convert_element_type x1 -> x0, other arithmetic: 13 us -> none  [shards(): grad_weight.astype(jnp.bfloat16).reshape(per_dev * BLOCK, piece)]
    broadcast_in_dim x1 -> x0, other arithmetic: 3.27 us -> none  [shards(): jnp.where(block_ids == owners[q], spread[q][None].astype(jnp.float32), 0.0)]
    reshape x0 -> x2, local copies, waits for them, and re-layouts: none -> 2.74 us  [the longest x1 2.71 us: shards(): wide = full_rows.reshape(tokens_here, n_groups, piece)]
    eq x4 -> x2, other arithmetic: 2.43 us -> 0.15 us  [shards(): hit_q = local[:, q][:, None] == block_ids[None, :]]
    unnamed x11 -> x15, local copies, waits for them, and re-layouts: 4.19 us -> 4.18 us
  transfers between devices with their start and end apart: 4 -> 4, of which waited for: 2 -> 2; matrix products, arithmetic and copies ran while one was open for 20% -> 13% of each run, Pallas kernels for 0% -> 0%
where the time goes in v2:
time: 187 us
  waiting for transfers between devices  73.7 us (39%)
  blocking collectives  48.6 us (26%)
  matrix products  14.7 us (8%)
  between operations  14.2 us (8%)
  local copies, waits for them, and re-layouts  13.8 us (7%)
  other arithmetic  12.2 us (7%)
  starting transfers between devices  9.63 us (5%)
    all_to_all x1, waiting for transfers between devices, shards(): lax.all_to_all(chosen, 'dp', split_axis=0, concat_axis=0, tiled=True)  45.4 us
    reduce_scatter x1, waiting for transfers between devices, shards(): lax.psum_scatter(hidden_terms, 'vocab', scatter_dimension=1, tiled=True)  28.3 us
    all_gather x1, blocking collectives, shards(): lax.all_gather(dlog, 'dp').reshape(n_groups, tokens_here, SLOTS, BLOCK)  26.7 us
    all_gather x1, blocking collectives, shards(): stats = lax.all_gather(jnp.stack([local_top, local_total, aimed]), 'vocab')  21.9 us
    gather x1, local copies, waits for them, and re-layouts, shards(): jnp.take(blocks, jnp.maximum(local, 0).reshape(-1), axis=0)  6.21 us
    dot_general x1, matrix products, shards(): jnp.einsum('tr,krd->tkd', dlog, rows_w, preferred_element_type=jnp.float32)  5.89 us
    all_to_all x1, starting transfers between devices, shards(): lax.all_to_all(chosen, 'dp', split_axis=0, concat_axis=0, tiled=True)  5.73 us
    dot_general x1, matrix products, shards(): jnp.einsum('str,tsd->rd', placed, halves, preferred_element_type=jnp.floa...  4.68 us
  transfers between devices with their start and end apart: 4, of which 2 were waited for; matrix products, arithmetic and copies ran while one was open for 13% of the time, Pallas kernels for 0%

profile of v2, /device:TPU:0, one launch (start us, length us, event | category | flops | bytes accessed | tf_op | source)
XLA Modules:
  0.0 186.8 jit_solution(15829139449347344201)
XLA Ops:
  7.2 1.7 copy.52
  8.9 0.7 fusion.10
  9.6 0.2 reduce_window_sum.11
  9.8 0.7 broadcast_add_fusion.1
  10.5 0.1 fusion.7
  10.7 0.1 reshape.146
  10.8 6.2 %gather_fusion = bf16[4,128,4096]{2,1,0:T(8,128)(2,1)} fusion(bf16[8,128,4096]{2,1,0:T(8,128)(2,1)} %bitcast.67, s32[1024]{0:T(1024)S(1)} %pad_clamp_fusion), kind=kCustom, calls=%fused_computation | custom fusion | bytes 8388624 | tf_op jit(solution)/shard_map/jit(_take)/gather | solution.py:33
  17.0 4.6 %bitcast_select_fusion = bf16[2,256,4096]{2,1,0:T(8,128)(2,1)} fusion(pred[2,256]{1,0:T(4,128)(4,1)S(1)} %bitcast.74, bf16[2,256,4096]{2,1,0:T(8,128)(2,1)} %bitcast.64), kind=kLoop, calls=%fused_computation.4 | loop fusion | flops 2097152 | bytes 8389120 | tf_op jit(solution)/shard_map/jit(_take)/select_n | solution.py:33
  21.7 5.7 %all-to-all-start = ((bf16[2,256,4096]{2,1,0:T(8,128)(2,1)}), bf16[2,256,4096]{2,1,0:T(8,128)(2,1)}, u32[]{:S(2)}, u32[]{:S(2)}) async-start(bf16[2,256,4096]{2,1,0:T(8,128)(2,1)} %bitcast_select_fusion), calls=%async_computation | async-start | bytes 8388608 | tf_op jit(solution)/shard_map/all_to_all | solution.py:41
  27.7 0.1 copy.71
  27.8 0.1 fusion.1
  27.9 0.1 copy.54
  28.0 2.8 %select_reduce_fusion = f32[128,256]{1,0:T(8,128)S(1)} fusion(f32[128,64]{1,0:T(8,128)S(1)} %copy.71, s32[128,64]{1,0:T(8,128)S(1)} %copy.54), kind=kLoop, calls=%fused_computation.2 | loop fusion | flops 6258688 | bytes 196608
  30.8 0.1 copy.66
  31.0 45.4 %all-to-all-done = bf16[2,256,4096]{2,1,0:T(8,128)(2,1)} async-done(((bf16[2,256,4096]{2,1,0:T(8,128)(2,1)}), bf16[2,256,4096]{2,1,0:T(8,128)(2,1)}, u32[]{:S(2)}, u32[]{:S(2)}) %all-to-all-start) | async-done | bytes 4194336 | tf_op jit(solution)/shard_map/all_to_all | solution.py:41
  76.4 4.1 %select_reduce_fusion.2 = (f32[128]{0:T(128)S(1)}, f32[128,256]{0,1:T(8,128)S(1)}) fusion(pred[256]{0:T(512)(128)(4,1)S(1)} %broadcast_bitcast_fusion.3, bf16[2,256,4096]{2,1,0:T(8,128)(2,1)} %all-to-all-done, bf16[128,2,4096]{0,2,1:T(8,128)(2,1)} %bitcast.65), kind=kOutput, calls=%fused_computation.12 | convolution fusion | flops 536936320 | bytes 6423296 | tf_op jit(solution)/shard_map/tkd,krd->tr/dot_general | solution.py:42
  80.5 0.1 select_reduce_fusion.1
  80.6 21.9 %all-gather.2 = f32[16,3,128]{2,1,0:T(4,128)S(1)} all-gather(f32[1,3,128]{2,1,0:T(4,128)S(1)} %maximum_bitcast_fusion), channel_id=2, replica_groups=mesh['dp'=2,'vocab'=16] {'vocab'}, dimensions={0}, use_global_device_ids=true | all-gather | bytes 26112 | tf_op jit(solution)/shard_map/all_gather | solution.py:57
  102.6 0.5 fusion.9
  103.1 0.1 subtract_convert_fusion
  103.2 5.9 %fusion.2 = f32[128,2,4096]{0,2,1:T(8,128)} fusion(bf16[2,256,4096]{2,1,0:T(8,128)(2,1)} %all-to-all-done, bf16[128,256]{0,1:T(8,128)(2,1)S(1)} %subtract_convert_fusion), kind=kOutput, calls=%fused_computation.18 | convolution fusion | flops 536870912 | bytes 8454144 | tf_op jit(solution)/shard_map/tr,krd->tkd/dot_general | solution.py:65
  109.2 0.2 slice_reduce_fusion.2
  109.3 1.4 copy-done
  110.7 2.7 %copy.60 = bf16[128,2,4096]{2,0,1:T(8,128)(2,1)} copy(bf16[128,2,4096]{0,2,1:T(8,128)(2,1)S(1)} %bitcast.66) | data formatting | bytes 4194304 | tf_op jit(solution)/shard_map/reshape | solution.py:37
  113.4 3.8 %all-to-all-start.1 = ((bf16[128,2,4096]{2,0,1:T(8,128)(2,1)}), bf16[128,2,4096]{2,0,1:T(8,128)(2,1)S(1)}, u32[]{:S(2)}, u32[]{:S(2)}) async-start(bf16[128,2,4096]{2,0,1:T(8,128)(2,1)} %copy.60), calls=%async_computation.2 | async-start | bytes 4194304 | tf_op jit(solution)/shard_map/all_to_all | solution.py:38
  117.6 26.7 %all-gather.1 = bf16[256,256]{0,1:T(8,128)(2,1)S(1)} all-gather(bf16[128,256]{0,1:T(8,128)(2,1)S(1)} %subtract_convert_fusion), channel_id=3, replica_groups=mesh['dp'=2,'vocab'=16] {'dp'}, dimensions={0}, use_global_device_ids=true | all-gather | bytes 196608 | tf_op jit(solution)/shard_map/all_gather | solution.py:70
  144.3 0.1 slice_bitcast_fusion.1
  144.5 0.7 fusion
  145.2 4.7 %bitcast_convert_fusion = bf16[1024,4096]{1,0:T(8,128)(2,1)} fusion(bf16[2,128,1024]{1,2,0:T(8,128)(2,1)S(1)} %fusion, bf16[128,2,4096]{2,0,1:T(8,128)(2,1)S(1)} %all-to-all-done.1), kind=kOutput, calls=%fused_computation.1 | convolution fusion | flops 2151677952 | bytes 11010048 | tf_op jit(solution)/shard_map/str,tsd->rd/dot_general | solution.py:79
  149.9 28.3 %reduce-scatter.2.cloned.1.call-done = f32[128,512]{0,1:T(8,128)} async-done(((f32[128,8192]{0,1:T(8,128)}), f32[128,512]{0,1:T(8,128)}) %reduce-scatter.2.cloned.1.call-update) | async-done | bytes 262160 | tf_op jit(solution)/shard_map/reduce_scatter | solution.py:67
  178.2 1.0 convert_element_type.16
  179.2 0.8 copy.61
  (38 shorter events, 1.0 us)
Async XLA Ops:
  7.2 69.2 %all-gather.5.cloned.1.call-start = ((), (), s32[]{:S(2)}) async-start(), calls=%async_computation.3 | async-start | bytes 2228224 | tf_op jit(solution)/shard_map/all_gather | solution.py:36
  21.7 5.8 %copy-start.1 = (f32[128,64]{0,1:T(8,128)S(1)}, f32[128,64]{0,1:T(8,128)}, u32[]{:S(2)}) copy-start(f32[128,64]{0,1:T(8,128)} %param.8) | copy-start | bytes 98308
  21.7 5.9 %copy-start.2 = (s32[128,64]{0,1:T(8,128)S(1)}, s32[128,64]{0,1:T(8,128)}, u32[]{:S(2)}) copy-start(s32[128,64]{0,1:T(8,128)} %param.7) | copy-start | bytes 98308
  21.7 54.7 %all-to-all-start = ((bf16[2,256,4096]{2,1,0:T(8,128)(2,1)}), bf16[2,256,4096]{2,1,0:T(8,128)(2,1)}, u32[]{:S(2)}, u32[]{:S(2)}) async-start(bf16[2,256,4096]{2,1,0:T(8,128)(2,1)} %bitcast_select_fusion), calls=%async_computation | async-start | bytes 8388608 | tf_op jit(solution)/shard_map/all_to_all | solution.py:41
  27.4 150.8 %reduce-scatter.2.cloned.1.call-start = ((), (), s32[]{:S(2)}) async-start(), calls=%async_computation.4 | async-start | bytes 4456448 | tf_op jit(solution)/shard_map/reduce_scatter | solution.py:67
  109.1 1.6 copy-start
  113.4 31.8 %all-to-all-start.1 = ((bf16[128,2,4096]{2,0,1:T(8,128)(2,1)}), bf16[128,2,4096]{2,0,1:T(8,128)(2,1)S(1)}, u32[]{:S(2)}, u32[]{:S(2)}) async-start(bf16[128,2,4096]{2,0,1:T(8,128)(2,1)} %copy.60), calls=%async_computation.2 | async-start | bytes 4194304 | tf_op jit(solution)/shard_map/all_to_all | solution.py:38
Sparse Core Ops, SparseCore 0:
  10.7 44.1 all-gather.4
  109.3 68.8 reduce-scatter.1

commit v3 on v2

--- a/solution.py
+++ b/solution.py
@@ -30,7 +30,7 @@
     filled = table >= 0
     local = jnp.where(filled, table - column * per_dev, -1)
     blocks = weight.reshape(per_dev, BLOCK, piece)
-    chosen = jnp.take(blocks, jnp.maximum(local, 0).reshape(-1), axis=0).reshape(
+    chosen = jnp.take(blocks, jnp.maximum(local, 0).reshape(-1), axis=0, mode="clip").reshape(
         n_groups, width, piece
     )
     full_rows = lax.all_gather(hidden, "vocab", axis=1, tiled=True)

time: 187 us -> 183 us (0.979)
  other arithmetic: 12.2 us -> 7.52 us
    select_n x1 -> x0, other arithmetic: 4.64 us -> none  [shards(): jnp.take(blocks, jnp.maximum(local, 0).reshape(-1), axis=0)]
    unnamed x15 -> x13, local copies, waits for them, and re-layouts: 4.18 us -> 4.1 us
  transfers between devices with their start and end apart: 4 -> 4, of which waited for: 2 -> 2; matrix products, arithmetic and copies ran while one was open for 13% -> 11% of each run, Pallas kernels for 0% -> 0%
where the time goes in v3:
time: 183 us; the launch traced here: 182 us
  waiting for transfers between devices  73.8 us (40%)
  blocking collectives  48.6 us (27%)
  matrix products  14.7 us (8%)
  between operations  14.2 us (8%)
  local copies, waits for them, and re-layouts  13.7 us (7%)
  starting transfers between devices  9.65 us (5%)
  other arithmetic  7.52 us (4%)
    all_to_all x1, waiting for transfers between devices, shards(): lax.all_to_all(chosen, 'dp', split_axis=0, concat_axis=0, tiled=True)  45.4 us
    reduce_scatter x1, waiting for transfers between devices, shards(): lax.psum_scatter(hidden_terms, 'vocab', scatter_dimension=1, tiled=True)  28.3 us
    all_gather x1, blocking collectives, shards(): lax.all_gather(dlog, 'dp').reshape(n_groups, tokens_here, SLOTS, BLOCK)  26.7 us
    all_gather x1, blocking collectives, shards(): stats = lax.all_gather(jnp.stack([local_top, local_total, aimed]), 'vocab')  21.9 us
    gather x1, local copies, waits for them, and re-layouts, shards(): jnp.take(blocks, jnp.maximum(local, 0).reshape(-1), axis=0, mode='clip')  6.22 us
    dot_general x1, matrix products, shards(): jnp.einsum('tr,krd->tkd', dlog, rows_w, preferred_element_type=jnp.float32)  5.89 us
    all_to_all x1, starting transfers between devices, shards(): lax.all_to_all(chosen, 'dp', split_axis=0, concat_axis=0, tiled=True)  5.74 us
    dot_general x1, matrix products, shards(): jnp.einsum('str,tsd->rd', placed, halves, preferred_element_type=jnp.floa...  4.68 us
  transfers between devices with their start and end apart: 4, of which 2 were waited for; matrix products, arithmetic and copies ran while one was open for 11% of the time, Pallas kernels for 0%

profile of v3, /device:TPU:0, one launch (start us, length us, event | category | flops | bytes accessed | tf_op | source)
XLA Modules:
  0.0 182.1 jit_solution(12167819207300317795)
XLA Ops:
  7.2 1.7 copy.49
  8.9 0.7 fusion.10
  9.6 0.2 reduce_window_sum.11
  9.8 0.7 broadcast_add_fusion.1
  10.5 0.1 fusion.7
  10.6 0.1 reshape.139
  10.7 6.2 %gather_fusion = bf16[4,128,4096]{2,1,0:T(8,128)(2,1)} fusion(bf16[8,128,4096]{2,1,0:T(8,128)(2,1)} %bitcast.60, s32[1024]{0:T(1024)S(1)} %pad_clamp_fusion), kind=kCustom, calls=%fused_computation | custom fusion | bytes 8388624 | tf_op jit(solution)/shard_map/jit(_take)/gather | solution.py:33
  16.9 5.7 %all-to-all-start = ((bf16[2,256,4096]{2,1,0:T(8,128)(2,1)}), bf16[2,256,4096]{2,1,0:T(8,128)(2,1)}, u32[]{:S(2)}, u32[]{:S(2)}) async-start(bf16[2,256,4096]{2,1,0:T(8,128)(2,1)} %bitcast.57), calls=%async_computation | async-start | bytes 8388608 | tf_op jit(solution)/shard_map/all_to_all | solution.py:41
  22.9 0.1 compare_reduce_fusion
  23.0 0.1 copy.68
  23.1 0.1 fusion.1
  23.2 0.1 copy.51
  23.3 2.8 %select_reduce_fusion = f32[128,256]{1,0:T(8,128)S(1)} fusion(f32[128,64]{1,0:T(8,128)S(1)} %copy.68, s32[128,64]{1,0:T(8,128)S(1)} %copy.51), kind=kLoop, calls=%fused_computation.2 | loop fusion | flops 6258688 | bytes 196608
  26.1 0.1 copy.63
  26.3 45.4 %all-to-all-done = bf16[2,256,4096]{2,1,0:T(8,128)(2,1)} async-done(((bf16[2,256,4096]{2,1,0:T(8,128)(2,1)}), bf16[2,256,4096]{2,1,0:T(8,128)(2,1)}, u32[]{:S(2)}, u32[]{:S(2)}) %all-to-all-start) | async-done | bytes 4194336 | tf_op jit(solution)/shard_map/all_to_all | solution.py:41
  71.7 4.1 %select_reduce_fusion.2 = (f32[128]{0:T(128)S(1)}, f32[128,256]{0,1:T(8,128)S(1)}) fusion(pred[256]{0:T(512)(128)(4,1)S(1)} %broadcast_bitcast_fusion.2, bf16[2,256,4096]{2,1,0:T(8,128)(2,1)} %all-to-all-done, bf16[128,2,4096]{0,2,1:T(8,128)(2,1)} %bitcast.58), kind=kOutput, calls=%fused_computation.11 | convolution fusion | flops 536936320 | bytes 6423296 | tf_op jit(solution)/shard_map/tkd,krd->tr/dot_general | solution.py:42
  75.8 0.1 select_reduce_fusion.1
  75.9 21.9 %all-gather.2 = f32[16,3,128]{2,1,0:T(4,128)S(1)} all-gather(f32[1,3,128]{2,1,0:T(4,128)S(1)} %maximum_bitcast_fusion), channel_id=2, replica_groups=mesh['dp'=2,'vocab'=16] {'vocab'}, dimensions={0}, use_global_device_ids=true | all-gather | bytes 26112 | tf_op jit(solution)/shard_map/all_gather | solution.py:57
  97.9 0.5 fusion.9
  98.4 0.1 subtract_convert_fusion
  98.5 5.9 %fusion.2 = f32[128,2,4096]{0,2,1:T(8,128)} fusion(bf16[2,256,4096]{2,1,0:T(8,128)(2,1)} %all-to-all-done, bf16[128,256]{0,1:T(8,128)(2,1)S(1)} %subtract_convert_fusion), kind=kOutput, calls=%fused_computation.17 | convolution fusion | flops 536870912 | bytes 8454144 | tf_op jit(solution)/shard_map/tr,krd->tkd/dot_general | solution.py:65
  104.5 0.2 slice_reduce_fusion.2
  104.6 1.4 copy-done
  106.0 2.7 %copy.57 = bf16[128,2,4096]{2,0,1:T(8,128)(2,1)} copy(bf16[128,2,4096]{0,2,1:T(8,128)(2,1)S(1)} %bitcast.59) | data formatting | bytes 4194304 | tf_op jit(solution)/shard_map/reshape | solution.py:37
  108.7 3.8 %all-to-all-start.1 = ((bf16[128,2,4096]{2,0,1:T(8,128)(2,1)}), bf16[128,2,4096]{2,0,1:T(8,128)(2,1)S(1)}, u32[]{:S(2)}, u32[]{:S(2)}) async-start(bf16[128,2,4096]{2,0,1:T(8,128)(2,1)} %copy.57), calls=%async_computation.2 | async-start | bytes 4194304 | tf_op jit(solution)/shard_map/all_to_all | solution.py:38
  112.9 26.7 %all-gather.1 = bf16[256,256]{0,1:T(8,128)(2,1)S(1)} all-gather(bf16[128,256]{0,1:T(8,128)(2,1)S(1)} %subtract_convert_fusion), channel_id=3, replica_groups=mesh['dp'=2,'vocab'=16] {'dp'}, dimensions={0}, use_global_device_ids=true | all-gather | bytes 196608 | tf_op jit(solution)/shard_map/all_gather | solution.py:70
  139.6 0.1 slice_bitcast_fusion.1
  139.8 0.7 fusion
  140.5 4.7 %bitcast_convert_fusion = bf16[1024,4096]{1,0:T(8,128)(2,1)} fusion(bf16[2,128,1024]{1,2,0:T(8,128)(2,1)S(1)} %fusion, bf16[128,2,4096]{2,0,1:T(8,128)(2,1)S(1)} %all-to-all-done.1), kind=kOutput, calls=%fused_computation.1 | convolution fusion | flops 2151677952 | bytes 11010048 | tf_op jit(solution)/shard_map/str,tsd->rd/dot_general | solution.py:79
  145.2 28.3 %reduce-scatter.2.cloned.1.call-done = f32[128,512]{0,1:T(8,128)} async-done(((f32[128,8192]{0,1:T(8,128)}), f32[128,512]{0,1:T(8,128)}) %reduce-scatter.2.cloned.1.call-update) | async-done | bytes 262160 | tf_op jit(solution)/shard_map/reduce_scatter | solution.py:67
  173.5 1.0 convert_element_type.16
  174.5 0.8 copy.58
  (33 shorter events, 0.8 us)
Async XLA Ops:
  7.2 64.5 %all-gather.5.cloned.1.call-start = ((), (), s32[]{:S(2)}) async-start(), calls=%async_computation.3 | async-start | bytes 2228224 | tf_op jit(solution)/shard_map/all_gather | solution.py:36
  16.9 5.8 %copy-start.1 = (f32[128,64]{0,1:T(8,128)S(1)}, f32[128,64]{0,1:T(8,128)}, u32[]{:S(2)}) copy-start(f32[128,64]{0,1:T(8,128)} %param.8) | copy-start | bytes 98308
  16.9 5.9 %copy-start.2 = (s32[128,64]{0,1:T(8,128)S(1)}, s32[128,64]{0,1:T(8,128)}, u32[]{:S(2)}) copy-start(s32[128,64]{0,1:T(8,128)} %param.7) | copy-start | bytes 98308
  16.9 54.7 %all-to-all-start = ((bf16[2,256,4096]{2,1,0:T(8,128)(2,1)}), bf16[2,256,4096]{2,1,0:T(8,128)(2,1)}, u32[]{:S(2)}, u32[]{:S(2)}) async-start(bf16[2,256,4096]{2,1,0:T(8,128)(2,1)} %bitcast.57), calls=%async_computation | async-start | bytes 8388608 | tf_op jit(solution)/shard_map/all_to_all | solution.py:41
  22.7 150.9 %reduce-scatter.2.cloned.1.call-start = ((), (), s32[]{:S(2)}) async-start(), calls=%async_computation.4 | async-start | bytes 4456448 | tf_op jit(solution)/shard_map/reduce_scatter | solution.py:67
  104.4 1.6 copy-start
  108.7 31.8 %all-to-all-start.1 = ((bf16[128,2,4096]{2,0,1:T(8,128)(2,1)}), bf16[128,2,4096]{2,0,1:T(8,128)(2,1)S(1)}, u32[]{:S(2)}, u32[]{:S(2)}) async-start(bf16[128,2,4096]{2,0,1:T(8,128)(2,1)} %copy.57), calls=%async_computation.2 | async-start | bytes 4194304 | tf_op jit(solution)/shard_map/all_to_all | solution.py:38
Sparse Core Ops, SparseCore 0:
  10.7 44.1 all-gather.4
  104.6 68.9 reduce-scatter.1

commit v4 on v3

--- a/solution.py
+++ b/solution.py
@@ -16,6 +16,26 @@
     slot_ids = jnp.arange(SLOTS, dtype=jnp.int32)
     picks = inside[:, :, None] & (rank[:, :, None] == slot_ids[None, None, :])
     return jnp.sum(jnp.where(picks, union_blocks[:, :, None] + 1, 0), axis=1) - 1
+
+
+def combine_stats(top, total, picked):
+    n = lax.axis_size("vocab")
+    if n & (n - 1):
+        stats = lax.all_gather(jnp.stack([top, total, picked]), "vocab")
+        best = jnp.max(stats[:, 0], axis=0)
+        total = jnp.sum(stats[:, 1] * jnp.exp(stats[:, 0] - best[None, :]), axis=0)
+        return best, total, jnp.sum(stats[:, 2], axis=0)
+    bit = 1
+    while bit < n:
+        other = lax.ppermute(
+            jnp.stack([top, total, picked]), "vocab", [(k, k ^ bit) for k in range(n)]
+        )
+        best = jnp.maximum(top, other[0])
+        total = total * jnp.exp(top - best) + other[1] * jnp.exp(other[0] - best)
+        picked = picked + other[2]
+        top = best
+        bit *= 2
+    return top, total, picked
 
 
 def shards(hidden, weight, teacher_ids, teacher_logp, union_blocks):
@@ -54,10 +74,7 @@
     local_top = jnp.max(masked, axis=1)
     aimed = jnp.sum(target * logits, axis=1)
     local_total = jnp.sum(jnp.where(col_mask[None, :], jnp.exp(masked - local_top[:, None]), 0.0), axis=1)
-    stats = lax.all_gather(jnp.stack([local_top, local_total, aimed]), "vocab")
-    top = jnp.max(stats[:, 0], axis=0)
-    total = jnp.sum(stats[:, 1] * jnp.exp(stats[:, 0] - top[None, :]), axis=0)
-    picked = jnp.sum(stats[:, 2], axis=0)
+    top, total, picked = combine_stats(local_top, local_total, aimed)
     lse = top + jnp.log(total)
     loss = lse - picked
     probs = jnp.where(col_mask[None, :], jnp.exp(logits - lse[:, None]), 0.0)

time: 183 us -> 178 us (0.973)
  blocking collectives: 48.6 us -> 23.2 us
  waiting for transfers between devices: 73.8 us -> 88.3 us
  starting transfers between devices: 9.65 us -> 16.1 us
    all_gather x1 -> x0, blocking collectives: 21.9 us -> none  [shards(): stats = lax.all_gather(jnp.stack([local_top, local_total, aimed]), 'vocab')]
    reduce_scatter x1, waiting for transfers between devices: 28.3 us -> 36.3 us  [shards(): lax.psum_scatter(hidden_terms, 'vocab', scatter_dimension=1, tiled=True)]
    ppermute x0 -> x4, starting transfers between devices: none -> 6.54 us  [combine_stats(): lax.ppermute(jnp.stack([top, total, picked]), 'vocab', [(k, k ^ bit) for...]
    ppermute x0 -> x4, waiting for transfers between devices: none -> 6.53 us  [combine_stats(): lax.ppermute(jnp.stack([top, total, picked]), 'vocab', [(k, k ^ bit) for...]
    all_gather x1, blocking collectives: 26.7 us -> 23.2 us  [shards(): lax.all_gather(dlog, 'dp').reshape(n_groups, tokens_here, SLOTS, BLOCK)]
  transfers between devices with their start and end apart: 4 -> 8, of which waited for: 2 -> 6; matrix products, arithmetic and copies ran while one was open for 11% -> 11% of each run, Pallas kernels for 0% -> 0%
where the time goes in v4:
time: 178 us
  waiting for transfers between devices  88.3 us (50%)
  blocking collectives  23.2 us (13%)
  starting transfers between devices  16.1 us (9%)
  matrix products  14.7 us (8%)
  between operations  14.2 us (8%)
  local copies, waits for them, and re-layouts  13.7 us (8%)
  other arithmetic  7.51 us (4%)
    all_to_all x1, waiting for transfers between devices, shards(): lax.all_to_all(chosen, 'dp', split_axis=0, concat_axis=0, tiled=True)  45.4 us
    reduce_scatter x1, waiting for transfers between devices, shards(): lax.psum_scatter(hidden_terms, 'vocab', scatter_dimension=1, tiled=True)  36.3 us
    all_gather x1, blocking collectives, shards(): lax.all_gather(dlog, 'dp').reshape(n_groups, tokens_here, SLOTS, BLOCK)  23.2 us
    ppermute x4, starting transfers between devices, combine_stats(): lax.ppermute(jnp.stack([top, total, picked]), 'vocab', [(k, k ^ bit) for...  6.54 us
    ppermute x4, waiting for transfers between devices, combine_stats(): lax.ppermute(jnp.stack([top, total, picked]), 'vocab', [(k, k ^ bit) for...  6.53 us
    gather x1, local copies, waits for them, and re-layouts, shards(): jnp.take(blocks, jnp.maximum(local, 0).reshape(-1), axis=0, mode='clip')  6.22 us
    dot_general x1, matrix products, shards(): jnp.einsum('tr,krd->tkd', dlog, rows_w, preferred_element_type=jnp.float32)  5.89 us
    all_to_all x1, starting transfers between devices, shards(): lax.all_to_all(chosen, 'dp', split_axis=0, concat_axis=0, tiled=True)  5.74 us
  transfers between devices with their start and end apart: 8, of which 6 were waited for; matrix products, arithmetic and copies ran while one was open for 11% of the time, Pallas kernels for 0%

profile of v4, /device:TPU:0, one launch (start us, length us, event | category | flops | bytes accessed | tf_op | source)
XLA Modules:
  0.0 177.8 jit_solution(16002781308688125051)
XLA Ops:
  7.2 1.7 copy.34
  8.9 0.7 fusion.33
  9.6 0.2 reduce_window_sum.11
  9.8 0.7 broadcast_add_fusion.1
  10.5 0.1 fusion.7
  10.7 6.2 %gather_fusion = bf16[4,128,4096]{2,1,0:T(8,128)(2,1)} fusion(bf16[8,128,4096]{2,1,0:T(8,128)(2,1)} %bitcast.177, s32[1024]{0:T(1024)S(1)} %pad_clamp_fusion), kind=kCustom, calls=%fused_computation | custom fusion | bytes 8388624 | tf_op jit(solution)/shard_map/jit(_take)/gather | solution.py:53
  16.9 5.7 %all-to-all-start = ((bf16[2,256,4096]{2,1,0:T(8,128)(2,1)}), bf16[2,256,4096]{2,1,0:T(8,128)(2,1)}, u32[]{:S(2)}, u32[]{:S(2)}) async-start(bf16[2,256,4096]{2,1,0:T(8,128)(2,1)} %bitcast.174), calls=%async_computation | async-start | bytes 8388608 | tf_op jit(solution)/shard_map/all_to_all | solution.py:61
  23.3 2.8 %select_reduce_fusion = f32[128,256]{1,0:T(8,128)S(1)} fusion(f32[128,64]{1,0:T(8,128)S(1)} %copy.51, s32[128,64]{1,0:T(8,128)S(1)} %copy.36), kind=kLoop, calls=%fused_computation.2 | loop fusion | flops 6258688 | bytes 196608
  26.3 45.4 %all-to-all-done = bf16[2,256,4096]{2,1,0:T(8,128)(2,1)} async-done(((bf16[2,256,4096]{2,1,0:T(8,128)(2,1)}), bf16[2,256,4096]{2,1,0:T(8,128)(2,1)}, u32[]{:S(2)}, u32[]{:S(2)}) %all-to-all-start) | async-done | bytes 4194336 | tf_op jit(solution)/shard_map/all_to_all | solution.py:61
  71.7 4.2 %select_reduce_fusion.2 = (f32[128]{0:T(128)S(1)}, f32[128,256]{0,1:T(8,128)S(1)}) fusion(pred[256]{0:T(512)(128)(4,1)S(1)} %broadcast_bitcast_fusion.2, bf16[2,256,4096]{2,1,0:T(8,128)(2,1)} %all-to-all-done, bf16[128,2,4096]{0,2,1:T(8,128)(2,1)} %bitcast.175), kind=kOutput, calls=%fused_computation.11 | convolution fusion | flops 536936320 | bytes 6423296 | tf_op jit(solution)/shard_map/tkd,krd->tr/dot_general | solution.py:62
  75.8 0.1 multiply_reduce_fusion
  76.0 1.1 collective-permute-done
  77.2 1.8 collective-permute-start.1
  79.0 1.9 %collective-permute-done.1 = f32[3,128]{1,0:T(4,128)S(1)} collective-permute-done((f32[3,128]{1,0:T(4,128)S(1)}, f32[3,128]{1,0:T(4,128)S(1)}, u32[]{:S(2)}, u32[]{:S(2)}) %collective-permute-start.1) | collective-permute-done | bytes 1568 | tf_op jit(solution)/shard_map/ppermute | solution.py:30
  80.9 1.8 %collective-permute-start.2 = (f32[3,128]{1,0:T(4,128)S(1)}, f32[3,128]{1,0:T(4,128)S(1)}, u32[]{:S(2)}, u32[]{:S(2)}) collective-permute-start(f32[3,128]{1,0:T(4,128)S(1)} %pad_maximum_fusion.2), channel_id=1, source_target_pairs={{0,4},{1,5},{2,6},{3,7},{4,0},{5,1},{6,2},{7,3},{8,12},{9,13},{10,... | collective-permute-start | bytes 4616 | tf_op jit(solution)/shard_map/ppermute | solution.py:30
  82.8 1.8 %collective-permute-done.2 = f32[3,128]{1,0:T(4,128)S(1)} collective-permute-done((f32[3,128]{1,0:T(4,128)S(1)}, f32[3,128]{1,0:T(4,128)S(1)}, u32[]{:S(2)}, u32[]{:S(2)}) %collective-permute-start.2) | collective-permute-done | bytes 1568 | tf_op jit(solution)/shard_map/ppermute | solution.py:30
  84.6 2.9 %collective-permute-start.3 = (f32[3,128]{1,0:T(4,128)S(1)}, f32[3,128]{1,0:T(4,128)S(1)}, u32[]{:S(2)}, u32[]{:S(2)}) collective-permute-start(f32[3,128]{1,0:T(4,128)S(1)} %pad_maximum_fusion.3), channel_id=1, source_target_pairs={{0,8},{1,9},{2,10},{3,11},{4,12},{5,13},{6,14},{7,15},{8,0},{9,1},... | collective-permute-start | bytes 4616 | tf_op jit(solution)/shard_map/ppermute | solution.py:30
  87.4 1.7 collective-permute-done.3
  89.1 0.5 fusion.9
  89.7 0.1 subtract_convert_fusion
  89.8 5.9 %fusion.2 = f32[128,2,4096]{0,2,1:T(8,128)} fusion(bf16[2,256,4096]{2,1,0:T(8,128)(2,1)} %all-to-all-done, bf16[128,256]{0,1:T(8,128)(2,1)S(1)} %subtract_convert_fusion), kind=kOutput, calls=%fused_computation.17 | convolution fusion | flops 536870912 | bytes 8454144 | tf_op jit(solution)/shard_map/tr,krd->tkd/dot_general | solution.py:82
  95.7 0.2 slice_reduce_fusion.1
  95.9 1.4 copy-done
  97.3 2.7 %copy.41 = bf16[128,2,4096]{2,0,1:T(8,128)(2,1)} copy(bf16[128,2,4096]{0,2,1:T(8,128)(2,1)S(1)} %bitcast.176) | data formatting | bytes 4194304 | tf_op jit(solution)/shard_map/reshape | solution.py:57
  100.0 3.8 %all-to-all-start.1 = ((bf16[128,2,4096]{2,0,1:T(8,128)(2,1)}), bf16[128,2,4096]{2,0,1:T(8,128)(2,1)S(1)}, u32[]{:S(2)}, u32[]{:S(2)}) async-start(bf16[128,2,4096]{2,0,1:T(8,128)(2,1)} %copy.41), calls=%async_computation.2 | async-start | bytes 4194304 | tf_op jit(solution)/shard_map/all_to_all | solution.py:58
  104.1 23.2 %all-gather = bf16[256,256]{0,1:T(8,128)(2,1)S(1)} all-gather(bf16[128,256]{0,1:T(8,128)(2,1)S(1)} %subtract_convert_fusion), channel_id=2, replica_groups=mesh['dp'=2,'vocab'=16] {'dp'}, dimensions={0}, use_global_device_ids=true | all-gather | bytes 196608 | tf_op jit(solution)/shard_map/all_gather | solution.py:87
  127.3 0.1 slice_bitcast_fusion.1
  127.5 0.7 fusion
  128.2 4.7 %bitcast_convert_fusion = bf16[1024,4096]{1,0:T(8,128)(2,1)} fusion(bf16[2,128,1024]{1,2,0:T(8,128)(2,1)S(1)} %fusion, bf16[128,2,4096]{2,0,1:T(8,128)(2,1)S(1)} %all-to-all-done.1), kind=kOutput, calls=%fused_computation.1 | convolution fusion | flops 2151677952 | bytes 11010048 | tf_op jit(solution)/shard_map/str,tsd->rd/dot_general | solution.py:96
  132.9 36.3 %reduce-scatter.2.cloned.1.call-done = f32[128,512]{0,1:T(8,128)} async-done(((f32[128,8192]{0,1:T(8,128)}), f32[128,512]{0,1:T(8,128)}) %reduce-scatter.2.cloned.1.call-update) | async-done | bytes 262160 | tf_op jit(solution)/shard_map/reduce_scatter | solution.py:84
  169.2 1.0 convert_element_type.16
  170.2 0.8 copy.42
  (43 shorter events, 1.4 us)
Async XLA Ops:
  7.2 64.5 %all-gather.3.cloned.1.call-start = ((), (), s32[]{:S(2)}) async-start(), calls=%async_computation.3 | async-start | bytes 2228224 | tf_op jit(solution)/shard_map/all_gather | solution.py:56
  16.9 5.8 %copy-start.1 = (f32[128,64]{0,1:T(8,128)S(1)}, f32[128,64]{0,1:T(8,128)}, u32[]{:S(2)}) copy-start(f32[128,64]{0,1:T(8,128)} %param.8) | copy-start | bytes 98308
  16.9 5.9 %copy-start.2 = (s32[128,64]{0,1:T(8,128)S(1)}, s32[128,64]{0,1:T(8,128)}, u32[]{:S(2)}) copy-start(s32[128,64]{0,1:T(8,128)} %param.7) | copy-start | bytes 98308
  16.9 54.7 %all-to-all-start = ((bf16[2,256,4096]{2,1,0:T(8,128)(2,1)}), bf16[2,256,4096]{2,1,0:T(8,128)(2,1)}, u32[]{:S(2)}, u32[]{:S(2)}) async-start(bf16[2,256,4096]{2,1,0:T(8,128)(2,1)} %bitcast.174), calls=%async_computation | async-start | bytes 8388608 | tf_op jit(solution)/shard_map/all_to_all | solution.py:61
  22.7 146.5 %reduce-scatter.2.cloned.1.call-start = ((), (), s32[]{:S(2)}) async-start(), calls=%async_computation.4 | async-start | bytes 4456448 | tf_op jit(solution)/shard_map/reduce_scatter | solution.py:84
  76.0 1.2 collective-permute-start
  77.2 3.7 %collective-permute-start.1 = (f32[3,128]{1,0:T(4,128)S(1)}, f32[3,128]{1,0:T(4,128)S(1)}, u32[]{:S(2)}, u32[]{:S(2)}) collective-permute-start(f32[3,128]{1,0:T(4,128)S(1)} %pad_maximum_fusion.1), channel_id=1, source_target_pairs={{0,2},{1,3},{2,0},{3,1},{4,6},{5,7},{6,4},{7,5},{8,10},{9,11},{10,... | collective-permute-start | bytes 4616 | tf_op jit(solution)/shard_map/ppermute | solution.py:30
  80.9 3.7 %collective-permute-start.2 = (f32[3,128]{1,0:T(4,128)S(1)}, f32[3,128]{1,0:T(4,128)S(1)}, u32[]{:S(2)}, u32[]{:S(2)}) collective-permute-start(f32[3,128]{1,0:T(4,128)S(1)} %pad_maximum_fusion.2), channel_id=1, source_target_pairs={{0,4},{1,5},{2,6},{3,7},{4,0},{5,1},{6,2},{7,3},{8,12},{9,13},{10,... | collective-permute-start | bytes 4616 | tf_op jit(solution)/shard_map/ppermute | solution.py:30
  84.6 4.5 %collective-permute-start.3 = (f32[3,128]{1,0:T(4,128)S(1)}, f32[3,128]{1,0:T(4,128)S(1)}, u32[]{:S(2)}, u32[]{:S(2)}) collective-permute-start(f32[3,128]{1,0:T(4,128)S(1)} %pad_maximum_fusion.3), channel_id=1, source_target_pairs={{0,8},{1,9},{2,10},{3,11},{4,12},{5,13},{6,14},{7,15},{8,0},{9,1},... | collective-permute-start | bytes 4616 | tf_op jit(solution)/shard_map/ppermute | solution.py:30
  95.7 1.6 copy-start
  100.0 28.3 %all-to-all-start.1 = ((bf16[128,2,4096]{2,0,1:T(8,128)(2,1)}), bf16[128,2,4096]{2,0,1:T(8,128)(2,1)S(1)}, u32[]{:S(2)}, u32[]{:S(2)}) async-start(bf16[128,2,4096]{2,0,1:T(8,128)(2,1)} %copy.41), calls=%async_computation.2 | async-start | bytes 4194304 | tf_op jit(solution)/shard_map/all_to_all | solution.py:58
Sparse Core Ops, SparseCore 0:
  10.7 44.1 all-gather.2
  95.8 73.3 reduce-scatter.1

commit v5 on v4

--- a/solution.py
+++ b/solution.py
@@ -36,6 +36,25 @@
         top = best
         bit *= 2
     return top, total, picked
+
+
+def halving_scatter(terms):
+    n = lax.axis_size("vocab")
+    if n & (n - 1):
+        return lax.psum_scatter(terms, "vocab", scatter_dimension=1, tiled=True)
+    me = lax.axis_index("vocab")
+    rows, width = terms.shape
+    part = terms.reshape(rows, n, width // n)
+    bit = 1
+    while bit < n:
+        halves = part.reshape(rows, part.shape[1] // 2, 2, width // n)
+        mine = (me // bit) % 2
+        keep = lax.dynamic_index_in_dim(halves, mine, 2, keepdims=False)
+        send = lax.dynamic_index_in_dim(halves, 1 - mine, 2, keepdims=False)
+        got = lax.ppermute(send.astype(jnp.bfloat16), "vocab", [(k, k ^ bit) for k in range(n)])
+        part = keep + got.astype(jnp.float32)
+        bit *= 2
+    return part.reshape(rows, width // n)
 
 
 def shards(hidden, weight, teacher_ids, teacher_logp, union_blocks):
@@ -81,9 +100,7 @@
     dlog = (probs - target).astype(jnp.bfloat16)
     hidden_terms = jnp.einsum("tr,krd->tkd", dlog, rows_w, preferred_element_type=jnp.float32)
     hidden_terms = hidden_terms.reshape(tokens_here, n_groups * piece)
-    grad_hidden = lax.psum_scatter(hidden_terms, "vocab", scatter_dimension=1, tiled=True).astype(
-        jnp.bfloat16
-    )
+    grad_hidden = halving_scatter(hidden_terms).astype(jnp.bfloat16)
     dlog_all = lax.all_gather(dlog, "dp").reshape(n_groups, tokens_here, SLOTS, BLOCK)
     block_ids = jnp.arange(per_dev, dtype=jnp.int32)
     placed = jnp.zeros((n_groups, tokens_here, per_dev, BLOCK), jnp.bfloat16)

time: 178 us -> 165 us (0.927)
  waiting for transfers between devices: 88.3 us -> 54.1 us
  local copies, waits for them, and re-layouts: 13.7 us -> 27.1 us
  starting transfers between devices: 16.1 us -> 23.8 us
  blocking collectives: 23.2 us -> 21.1 us
  other arithmetic: 7.51 us -> 9.31 us
    reduce_scatter x1 -> x0, waiting for transfers between devices: 36.3 us -> none  [shards(): lax.psum_scatter(hidden_terms, 'vocab', scatter_dimension=1, tiled=True)]
    dynamic_slice x0 -> x4, local copies, waits for them, and re-layouts: none -> 7.5 us  [the longest x3 6.43 us: halving_scatter(): keep = lax.dynamic_index_in_dim(halves, mine, 2, keepdims=False)]
    ppermute x0 -> x4, starting transfers between devices: none -> 6.38 us  [halving_scatter(): lax.ppermute(send.astype(jnp.bfloat16), 'vocab', [(k, k ^ bit) for k in r...]
    reshape x0 -> x1, local copies, waits for them, and re-layouts: none -> 2.49 us  [halving_scatter(): halves = part.reshape(rows, part.shape[1] // 2, 2, width // n)]
    ppermute x0 -> x4, waiting for transfers between devices: none -> 2.4 us  [halving_scatter(): lax.ppermute(send.astype(jnp.bfloat16), 'vocab', [(k, k ^ bit) for k in r...]
    all_gather x1, blocking collectives: 23.2 us -> 21.1 us  [shards(): lax.all_gather(dlog, 'dp').reshape(n_groups, tokens_here, SLOTS, BLOCK)]
    add x0 -> x3, other arithmetic: none -> 2.08 us  [halving_scatter(): part = keep + got.astype(jnp.float32)]
    convert_element_type x0 -> x4, local copies, waits for them, and re-layouts: none -> 1.94 us  [halving_scatter(): send.astype(jnp.bfloat16)]
  transfers between devices with their start and end apart: 8 -> 11, of which waited for: 6 -> 6; matrix products, arithmetic and copies ran while one was open for 11% -> 18% of each run, Pallas kernels for 0% -> 0%
where the time goes in v5:
time: 165 us; the launch traced here: 164 us
  waiting for transfers between devices  54.1 us (33%)
  local copies, waits for them, and re-layouts  27.1 us (16%)
  starting transfers between devices  23.8 us (14%)
  blocking collectives  21.1 us (13%)
  between operations  14.4 us (9%)
  matrix products  14.3 us (9%)
  other arithmetic  9.31 us (6%)
    all_to_all x1, waiting for transfers between devices, shards(): lax.all_to_all(chosen, 'dp', split_axis=0, concat_axis=0, tiled=True)  45.4 us
    all_gather x1, blocking collectives, shards(): lax.all_gather(dlog, 'dp').reshape(n_groups, tokens_here, SLOTS, BLOCK)  21.1 us
    ppermute x4, starting transfers between devices, combine_stats(): lax.ppermute(jnp.stack([top, total, picked]), 'vocab', [(k, k ^ bit) for...  6.75 us
    dynamic_slice x3, local copies, waits for them, and re-layouts, halving_scatter(): keep = lax.dynamic_index_in_dim(halves, mine, 2, keepdims=False)  6.43 us
    ppermute x4, starting transfers between devices, halving_scatter(): lax.ppermute(send.astype(jnp.bfloat16), 'vocab', [(k, k ^ bit) for k in r...  6.38 us
    ppermute x4, waiting for transfers between devices, combine_stats(): lax.ppermute(jnp.stack([top, total, picked]), 'vocab', [(k, k ^ bit) for...  6.32 us
    dot_general x1, matrix products, shards(): jnp.einsum('str,tsd->rd', placed, halves, preferred_element_type=jnp.floa...  6.25 us
    gather x1, local copies, waits for them, and re-layouts, shards(): jnp.take(blocks, jnp.maximum(local, 0).reshape(-1), axis=0, mode='clip')  6.21 us
  transfers between devices with their start and end apart: 11, of which 6 were waited for; matrix products, arithmetic and copies ran while one was open for 18% of the time, Pallas kernels for 0%

profile of v5, /device:TPU:0, one launch (start us, length us, event | category | flops | bytes accessed | tf_op | source)
XLA Modules:
  0.0 164.1 jit_solution(11334191190633575725)
XLA Ops:
  7.2 1.7 %copy.53 = bf16[128,512]{0,1:T(8,128)(2,1)} copy(bf16[128,512]{1,0:T(8,128)(2,1)} %param.5) | data formatting | bytes 262144 | tf_op args[0]
  8.9 0.7 fusion.38
  10.7 6.2 %gather_fusion = bf16[4,128,4096]{2,1,0:T(8,128)(2,1)} fusion(bf16[8,128,4096]{2,1,0:T(8,128)(2,1)} %bitcast.195, s32[1024]{0:T(1024)S(1)} %pad_clamp_fusion), kind=kCustom, calls=%fused_computation | custom fusion | bytes 8388624 | tf_op jit(solution)/shard_map/jit(_take)/gather | solution.py:72
  16.9 5.8 %all-to-all-start = ((bf16[2,256,4096]{2,1,0:T(8,128)(2,1)}), bf16[2,256,4096]{2,1,0:T(8,128)(2,1)}, u32[]{:S(2)}, u32[]{:S(2)}) async-start(bf16[2,256,4096]{2,1,0:T(8,128)(2,1)} %bitcast.188), calls=%async_computation | async-start | bytes 8388608 | tf_op jit(solution)/shard_map/all_to_all | solution.py:80
  23.2 2.8 %select_reduce_fusion = f32[128,256]{1,0:T(8,128)S(1)} fusion(f32[128,64]{1,0:T(8,128)S(1)} %copy.74, s32[128,64]{1,0:T(8,128)S(1)} %copy.55), kind=kLoop, calls=%fused_computation.2 | loop fusion | flops 6258688 | bytes 196608
  26.2 45.4 %all-to-all-done = bf16[2,256,4096]{2,1,0:T(8,128)(2,1)} async-done(((bf16[2,256,4096]{2,1,0:T(8,128)(2,1)}), bf16[2,256,4096]{2,1,0:T(8,128)(2,1)}, u32[]{:S(2)}, u32[]{:S(2)}) %all-to-all-start) | async-done | bytes 4194336 | tf_op jit(solution)/shard_map/all_to_all | solution.py:80
  71.6 4.1 %select_reduce_fusion.2 = (f32[128]{0:T(128)S(1)}, f32[128,256]{0,1:T(8,128)S(1)}) fusion(pred[256]{0:T(512)(128)(4,1)S(1)} %broadcast_bitcast_fusion.2, bf16[2,256,4096]{2,1,0:T(8,128)(2,1)} %all-to-all-done, bf16[128,2,4096]{0,2,1:T(8,128)(2,1)} %bitcast.191), kind=kOutput, calls=%fused_computation.22 | convolution fusion | flops 536936320 | bytes 6423296 | tf_op jit(solution)/shard_map/tkd,krd->tr/dot_general | solution.py:81
  76.0 1.1 collective-permute-done
  77.1 1.8 %collective-permute-start.1 = (f32[3,128]{1,0:T(4,128)S(1)}, f32[3,128]{1,0:T(4,128)S(1)}, u32[]{:S(2)}, u32[]{:S(2)}) collective-permute-start(f32[3,128]{1,0:T(4,128)S(1)} %pad_maximum_fusion.1), channel_id=1, source_target_pairs={{0,2},{1,3},{2,0},{3,1},{4,6},{5,7},{6,4},{7,5},{8,10},{9,11},{10,... | collective-permute-start | bytes 4616 | tf_op jit(solution)/shard_map/ppermute | solution.py:30
  79.0 1.8 %collective-permute-done.1 = f32[3,128]{1,0:T(4,128)S(1)} collective-permute-done((f32[3,128]{1,0:T(4,128)S(1)}, f32[3,128]{1,0:T(4,128)S(1)}, u32[]{:S(2)}, u32[]{:S(2)}) %collective-permute-start.1) | collective-permute-done | bytes 1568 | tf_op jit(solution)/shard_map/ppermute | solution.py:30
  80.8 1.9 %collective-permute-start.2 = (f32[3,128]{1,0:T(4,128)S(1)}, f32[3,128]{1,0:T(4,128)S(1)}, u32[]{:S(2)}, u32[]{:S(2)}) collective-permute-start(f32[3,128]{1,0:T(4,128)S(1)} %pad_maximum_fusion.2), channel_id=1, source_target_pairs={{0,4},{1,5},{2,6},{3,7},{4,0},{5,1},{6,2},{7,3},{8,12},{9,13},{10,... | collective-permute-start | bytes 4616 | tf_op jit(solution)/shard_map/ppermute | solution.py:30
  82.7 1.7 %collective-permute-done.2 = f32[3,128]{1,0:T(4,128)S(1)} collective-permute-done((f32[3,128]{1,0:T(4,128)S(1)}, f32[3,128]{1,0:T(4,128)S(1)}, u32[]{:S(2)}, u32[]{:S(2)}) %collective-permute-start.2) | collective-permute-done | bytes 1568 | tf_op jit(solution)/shard_map/ppermute | solution.py:30
  84.5 2.9 %collective-permute-start.3 = (f32[3,128]{1,0:T(4,128)S(1)}, f32[3,128]{1,0:T(4,128)S(1)}, u32[]{:S(2)}, u32[]{:S(2)}) collective-permute-start(f32[3,128]{1,0:T(4,128)S(1)} %pad_maximum_fusion.3), channel_id=1, source_target_pairs={{0,8},{1,9},{2,10},{3,11},{4,12},{5,13},{6,14},{7,15},{8,0},{9,1},... | collective-permute-start | bytes 4616 | tf_op jit(solution)/shard_map/ppermute | solution.py:30
  87.4 1.6 collective-permute-done.3
  89.7 4.0 %fusion.5 = f32[128,2,4096]{0,2,1:T(8,128)S(1)} fusion(bf16[2,256,4096]{2,1,0:T(8,128)(2,1)} %all-to-all-done, bf16[128,256]{0,1:T(8,128)(2,1)S(1)} %subtract_convert_fusion), kind=kOutput, calls=%fused_computation.28 | convolution fusion | flops 536870912 | bytes 8454144 | tf_op jit(solution)/shard_map/tr,krd->tkd/dot_general | solution.py:101
  93.7 2.0 %copy-done = f32[128,2,4096]{0,2,1:T(8,128)} copy-done((f32[128,2,4096]{0,2,1:T(8,128)}, f32[128,2,4096]{0,2,1:T(8,128)S(1)}, u32[]{:S(2)}) %copy-start) | copy-done | bytes 4194328
  95.8 1.7 %copy.59 = bf16[128,8,1,512]{3,1,0,2:T(8,128)(2,1)} copy(bf16[128,8,1,512]{0,3,2,1:T(8,128)(2,1)S(1)} %dynamic-slice_convert_fusion) | data formatting | bytes 2097152 | tf_op jit(solution)/shard_map/convert_element_type | solution.py:54
  97.9 3.1 %constant_dynamic-slice_fusion.2 = f32[128,8,1,512]{0,3,2,1:T(8,128)} fusion(f32[128,8,2,512]{0,3,2,1:T(8,128)} %bitcast.190, s32[]{:T(128)S(6)} %select_n.128), kind=kLoop, calls=%fused_computation.49 | loop fusion | bytes 4194308 | tf_op jit(solution)/shard_map/jit(dynamic_index_in_dim)/dynamic_slice | solution.py:52
  101.0 2.2 %copy.58 = f32[128,8,1,512]{3,1,0,2:T(8,128)S(1)} copy(f32[128,8,1,512]{0,3,2,1:T(8,128)} %constant_dynamic-slice_fusion.2) | data formatting | bytes 4194304 | tf_op jit(solution)/shard_map/jit(dynamic_index_in_dim)/dynamic_slice | solution.py:52
  103.3 1.6 %bitcast_add_fusion = f32[128,8,512]{2,1,0:T(8,128)} fusion(f32[128,8,1,512]{3,1,0,2:T(8,128)S(1)} %copy.58, bf16[128,8,512]{2,1,0:T(8,128)(2,1)S(1)} %collective-permute-done.4), kind=kLoop, calls=%fused_computation.4 | loop fusion | flops 1048576 | bytes 5242880 | tf_op jit(solution)/shard_map/add | solution.py:55
  104.9 2.5 %reshape.237 = f32[128,4,2,512]{3,2,1,0:T(2,128)S(1)} reshape(f32[128,8,512]{2,1,0:T(8,128)} %bitcast_add_fusion) | data formatting | bytes 4194304 | tf_op jit(solution)/shard_map/reshape | solution.py:50
  107.4 1.1 constant_dynamic-slice_fusion
  108.8 1.8 %collective-permute-start.5 = (bf16[128,4,512]{2,0,1:T(8,128)(2,1)S(1)}, bf16[128,4,512]{2,0,1:T(8,128)(2,1)S(1)}, u32[]{:S(2)}, u32[]{:S(2)}) collective-permute-start(bf16[128,4,512]{2,0,1:T(8,128)(2,1)S(1)} %bitcast.196), channel_id=1, source_target_pairs={{0,2},{1,3},{2,0},{3,1},{4,6},{5,7},{6,4},{7,5},{8,10},{9,11},{10,... | collective-permute-start | bytes 1572872 | tf_op jit(solution)/shard_map/ppermute | solution.py:54
  110.8 4.1 %copy.64 = bf16[128,2,4096]{2,0,1:T(8,128)(2,1)} copy(bf16[128,2,4096]{0,2,1:T(8,128)(2,1)} %bitcast.192) | data formatting | bytes 4194304 | tf_op jit(solution)/shard_map/reshape | solution.py:76
  114.9 4.8 %all-to-all-start.1 = ((bf16[128,2,4096]{2,0,1:T(8,128)(2,1)}), bf16[128,2,4096]{2,0,1:T(8,128)(2,1)}, u32[]{:S(2)}, u32[]{:S(2)}) async-start(bf16[128,2,4096]{2,0,1:T(8,128)(2,1)} %copy.64), calls=%async_computation.1 | async-start | bytes 4194304 | tf_op jit(solution)/shard_map/all_to_all | solution.py:77
  119.7 1.1 constant_dynamic-slice_fusion.1
  120.8 2.4 %collective-permute-done.5 = bf16[128,4,512]{2,0,1:T(8,128)(2,1)S(1)} collective-permute-done((bf16[128,4,512]{2,0,1:T(8,128)(2,1)S(1)}, bf16[128,4,512]{2,0,1:T(8,128)(2,1)S(1)}, u32[]{:S(2)}, u32[]{:S(2)}) %collective-permute-start.5) | collective-permute-done | bytes 524320 | tf_op jit(solution)/shard_map/ppermute | solution.py:54
  123.6 1.9 %collective-permute-start.6 = (bf16[128,2,512]{2,0,1:T(8,128)(2,1)S(1)}, bf16[128,2,512]{2,0,1:T(8,128)(2,1)S(1)}, u32[]{:S(2)}, u32[]{:S(2)}) collective-permute-start(bf16[128,2,512]{2,0,1:T(8,128)(2,1)S(1)} %fusion.2), channel_id=1, source_target_pairs={{0,4},{1,5},{2,6},{3,7},{4,0},{5,1},{6,2},{7,3},{8,12},{9,13},{10,... | collective-permute-start | bytes 786440 | tf_op jit(solution)/shard_map/ppermute | solution.py:54
  125.5 21.1 %all-gather = bf16[256,256]{0,1:T(8,128)(2,1)S(1)} all-gather(bf16[128,256]{0,1:T(8,128)(2,1)S(1)} %subtract_convert_fusion), channel_id=2, replica_groups=mesh['dp'=2,'vocab'=16] {'dp'}, dimensions={0}, use_global_device_ids=true | all-gather | bytes 196608 | tf_op jit(solution)/shard_map/all_gather | solution.py:104
  146.8 0.7 fusion.1
  147.7 2.7 %collective-permute-start.7 = (bf16[128,1,512]{2,0,1:T(8,128)(2,1)S(1)}, bf16[128,1,512]{2,0,1:T(8,128)(2,1)S(1)}, u32[]{:S(2)}, u32[]{:S(2)}) collective-permute-start(bf16[128,1,512]{2,0,1:T(8,128)(2,1)S(1)} %dynamic-slice_convert_fusion.2), channel_id=1, source_target_pairs={{0,8},{1,9},{2,10},{3,11},{4,12},{5,13},{6,14},{7,15},{8,0},{9,1},... | collective-permute-start | bytes 393224 | tf_op jit(solution)/shard_map/ppermute | solution.py:54
  150.4 6.2 %bitcast_convert_fusion = bf16[1024,4096]{1,0:T(8,128)(2,1)} fusion(bf16[2,128,1024]{1,2,0:T(8,128)(2,1)S(1)} %fusion.1, bf16[128,2,4096]{2,0,1:T(8,128)(2,1)} %all-to-all-done.1), kind=kOutput, calls=%fused_computation.1 | convolution fusion | flops 2151677952 | bytes 11010048 | tf_op jit(solution)/shard_map/str,tsd->rd/dot_general | solution.py:113
  (60 shorter events, 5.0 us)
Async XLA Ops:
  7.2 64.4 %all-gather.3.cloned.1.call-start = ((), (), s32[]{:S(2)}) async-start(), calls=%async_computation.2 | async-start | bytes 2228224 | tf_op jit(solution)/shard_map/all_gather | solution.py:75
  16.9 5.8 %copy-start.1 = (f32[128,64]{0,1:T(8,128)S(1)}, f32[128,64]{0,1:T(8,128)}, u32[]{:S(2)}) copy-start(f32[128,64]{0,1:T(8,128)} %param.8) | copy-start | bytes 98308
  16.9 5.9 %copy-start.2 = (s32[128,64]{0,1:T(8,128)S(1)}, s32[128,64]{0,1:T(8,128)}, u32[]{:S(2)}) copy-start(s32[128,64]{0,1:T(8,128)} %param.7) | copy-start | bytes 98308
  16.9 54.7 %all-to-all-start = ((bf16[2,256,4096]{2,1,0:T(8,128)(2,1)}), bf16[2,256,4096]{2,1,0:T(8,128)(2,1)}, u32[]{:S(2)}, u32[]{:S(2)}) async-start(bf16[2,256,4096]{2,1,0:T(8,128)(2,1)} %bitcast.188), calls=%async_computation | async-start | bytes 8388608 | tf_op jit(solution)/shard_map/all_to_all | solution.py:80
  75.9 1.2 collective-permute-start
  77.1 3.7 %collective-permute-start.1 = (f32[3,128]{1,0:T(4,128)S(1)}, f32[3,128]{1,0:T(4,128)S(1)}, u32[]{:S(2)}, u32[]{:S(2)}) collective-permute-start(f32[3,128]{1,0:T(4,128)S(1)} %pad_maximum_fusion.1), channel_id=1, source_target_pairs={{0,2},{1,3},{2,0},{3,1},{4,6},{5,7},{6,4},{7,5},{8,10},{9,11},{10,... | collective-permute-start | bytes 4616 | tf_op jit(solution)/shard_map/ppermute | solution.py:30
  80.8 3.7 %collective-permute-start.2 = (f32[3,128]{1,0:T(4,128)S(1)}, f32[3,128]{1,0:T(4,128)S(1)}, u32[]{:S(2)}, u32[]{:S(2)}) collective-permute-start(f32[3,128]{1,0:T(4,128)S(1)} %pad_maximum_fusion.2), channel_id=1, source_target_pairs={{0,4},{1,5},{2,6},{3,7},{4,0},{5,1},{6,2},{7,3},{8,12},{9,13},{10,... | collective-permute-start | bytes 4616 | tf_op jit(solution)/shard_map/ppermute | solution.py:30
  84.5 4.5 %collective-permute-start.3 = (f32[3,128]{1,0:T(4,128)S(1)}, f32[3,128]{1,0:T(4,128)S(1)}, u32[]{:S(2)}, u32[]{:S(2)}) collective-permute-start(f32[3,128]{1,0:T(4,128)S(1)} %pad_maximum_fusion.3), channel_id=1, source_target_pairs={{0,8},{1,9},{2,10},{3,11},{4,12},{5,13},{6,14},{7,15},{8,0},{9,1},... | collective-permute-start | bytes 4616 | tf_op jit(solution)/shard_map/ppermute | solution.py:30
  93.7 2.0 %copy-start = (f32[128,2,4096]{0,2,1:T(8,128)}, f32[128,2,4096]{0,2,1:T(8,128)S(1)}, u32[]{:S(2)}) copy-start(f32[128,2,4096]{0,2,1:T(8,128)S(1)} %fusion.5) | copy-start | bytes 12582916
  97.6 5.7 %collective-permute-start.4 = (bf16[128,8,512]{2,1,0:T(8,128)(2,1)}, bf16[128,8,512]{2,1,0:T(8,128)(2,1)S(1)}, u32[]{:S(2)}, u32[]{:S(2)}) collective-permute-start(bf16[128,8,512]{2,1,0:T(8,128)(2,1)} %bitcast.26), channel_id=1, source_target_pairs={{0,1},{1,0},{2,3},{3,2},{4,5},{5,4},{6,7},{7,6},{8,9},{9,8},{10,11... | collective-permute-start | bytes 3145736 | tf_op jit(solution)/shard_map/ppermute | solution.py:54
  108.8 14.4 %collective-permute-start.5 = (bf16[128,4,512]{2,0,1:T(8,128)(2,1)S(1)}, bf16[128,4,512]{2,0,1:T(8,128)(2,1)S(1)}, u32[]{:S(2)}, u32[]{:S(2)}) collective-permute-start(bf16[128,4,512]{2,0,1:T(8,128)(2,1)S(1)} %bitcast.196), channel_id=1, source_target_pairs={{0,2},{1,3},{2,0},{3,1},{4,6},{5,7},{6,4},{7,5},{8,10},{9,11},{10,... | collective-permute-start | bytes 1572872 | tf_op jit(solution)/shard_map/ppermute | solution.py:54
  114.9 35.4 %all-to-all-start.1 = ((bf16[128,2,4096]{2,0,1:T(8,128)(2,1)}), bf16[128,2,4096]{2,0,1:T(8,128)(2,1)}, u32[]{:S(2)}, u32[]{:S(2)}) async-start(bf16[128,2,4096]{2,0,1:T(8,128)(2,1)} %copy.64), calls=%async_computation.1 | async-start | bytes 4194304 | tf_op jit(solution)/shard_map/all_to_all | solution.py:77
  123.6 23.9 %collective-permute-start.6 = (bf16[128,2,512]{2,0,1:T(8,128)(2,1)S(1)}, bf16[128,2,512]{2,0,1:T(8,128)(2,1)S(1)}, u32[]{:S(2)}, u32[]{:S(2)}) collective-permute-start(bf16[128,2,512]{2,0,1:T(8,128)(2,1)S(1)} %fusion.2), channel_id=1, source_target_pairs={{0,4},{1,5},{2,6},{3,7},{4,0},{5,1},{6,2},{7,3},{8,12},{9,13},{10,... | collective-permute-start | bytes 786440 | tf_op jit(solution)/shard_map/ppermute | solution.py:54
  147.7 8.9 %collective-permute-start.7 = (bf16[128,1,512]{2,0,1:T(8,128)(2,1)S(1)}, bf16[128,1,512]{2,0,1:T(8,128)(2,1)S(1)}, u32[]{:S(2)}, u32[]{:S(2)}) collective-permute-start(bf16[128,1,512]{2,0,1:T(8,128)(2,1)S(1)} %dynamic-slice_convert_fusion.2), channel_id=1, source_target_pairs={{0,8},{1,9},{2,10},{3,11},{4,12},{5,13},{6,14},{7,15},{8,0},{9,1},... | collective-permute-start | bytes 393224 | tf_op jit(solution)/shard_map/ppermute | solution.py:54
Sparse Core Ops, SparseCore 0:
  10.7 44.1 all-gather.2

commit v6 on v5

--- a/solution.py
+++ b/solution.py
@@ -57,6 +57,21 @@
     return part.reshape(rows, width // n)
 
 
+def doubling_gather(piece):
+    n = lax.axis_size("dp")
+    if n & (n - 1):
+        return lax.all_gather(piece, "dp")
+    me = lax.axis_index("dp")
+    held = piece[None]
+    bit = 1
+    while bit < n:
+        got = lax.ppermute(held, "dp", [(k, k ^ bit) for k in range(n)])
+        low = (me // bit) % 2 == 0
+        held = jnp.where(low, jnp.concatenate([held, got]), jnp.concatenate([got, held]))
+        bit *= 2
+    return held
+
+
 def shards(hidden, weight, teacher_ids, teacher_logp, union_blocks):
     tokens_here = hidden.shape[0]
     n_groups = lax.axis_size("dp")
@@ -101,7 +116,7 @@
     hidden_terms = jnp.einsum("tr,krd->tkd", dlog, rows_w, preferred_element_type=jnp.float32)
     hidden_terms = hidden_terms.reshape(tokens_here, n_groups * piece)
     grad_hidden = halving_scatter(hidden_terms).astype(jnp.bfloat16)
-    dlog_all = lax.all_gather(dlog, "dp").reshape(n_groups, tokens_here, SLOTS, BLOCK)
+    dlog_all = doubling_gather(dlog).reshape(n_groups, tokens_here, SLOTS, BLOCK)
     block_ids = jnp.arange(per_dev, dtype=jnp.int32)
     placed = jnp.zeros((n_groups, tokens_here, per_dev, BLOCK), jnp.bfloat16)
     for q in range(SLOTS):

time: 165 us -> 165 us (level)
  blocking collectives: 21.1 us -> 0 us
  waiting for transfers between devices: 54.1 us -> 73.2 us
  starting transfers between devices: 23.8 us -> 25.8 us
    all_gather x1 -> x0, blocking collectives: 21.1 us -> none  [shards(): lax.all_gather(dlog, 'dp').reshape(n_groups, tokens_here, SLOTS, BLOCK)]
    ppermute x0 -> x1, waiting for transfers between devices: none -> 21.1 us  [doubling_gather(): got = lax.ppermute(held, 'dp', [(k, k ^ bit) for k in range(n)])]
    ppermute x4, waiting for transfers between devices: 2.4 us -> 0.4 us  [halving_scatter(): lax.ppermute(send.astype(jnp.bfloat16), 'vocab', [(k, k ^ bit) for k in r...]
    ppermute x0 -> x1, starting transfers between devices: none -> 1.82 us  [doubling_gather(): got = lax.ppermute(held, 'dp', [(k, k ^ bit) for k in range(n)])]
  transfers between devices with their start and end apart: 11 -> 12, of which waited for: 6 -> 7; matrix products, arithmetic and copies ran while one was open for 18% -> 18% of each run, Pallas kernels for 0% -> 0%
where the time goes in v6:
time: 165 us; the launch traced here: 164 us
  waiting for transfers between devices  73.2 us (44%)
  local copies, waits for them, and re-layouts  27 us (16%)
  starting transfers between devices  25.8 us (16%)
  between operations  14.4 us (9%)
  matrix products  14.3 us (9%)
  other arithmetic  9.32 us (6%)
    all_to_all x1, waiting for transfers between devices, shards(): lax.all_to_all(chosen, 'dp', split_axis=0, concat_axis=0, tiled=True)  45.4 us
    ppermute x1, waiting for transfers between devices, doubling_gather(): got = lax.ppermute(held, 'dp', [(k, k ^ bit) for k in range(n)])  21.1 us
    ppermute x4, starting transfers between devices, combine_stats(): lax.ppermute(jnp.stack([top, total, picked]), 'vocab', [(k, k ^ bit) for...  6.74 us
    dynamic_slice x3, local copies, waits for them, and re-layouts, halving_scatter(): keep = lax.dynamic_index_in_dim(halves, mine, 2, keepdims=False)  6.43 us
    ppermute x4, starting transfers between devices, halving_scatter(): lax.ppermute(send.astype(jnp.bfloat16), 'vocab', [(k, k ^ bit) for k in r...  6.38 us
    ppermute x4, waiting for transfers between devices, combine_stats(): lax.ppermute(jnp.stack([top, total, picked]), 'vocab', [(k, k ^ bit) for...  6.33 us
    dot_general x1, matrix products, shards(): jnp.einsum('str,tsd->rd', placed, halves, preferred_element_type=jnp.floa...  6.25 us
    gather x1, local copies, waits for them, and re-layouts, shards(): jnp.take(blocks, jnp.maximum(local, 0).reshape(-1), axis=0, mode='clip')  6.21 us
  transfers between devices with their start and end apart: 12, of which 7 were waited for; matrix products, arithmetic and copies ran while one was open for 18% of the time, Pallas kernels for 0%

profile of v6, /device:TPU:0, one launch (start us, length us, event | category | flops | bytes accessed | tf_op | source)
XLA Modules:
  0.0 164.0 jit_solution(16031209665292470154)
XLA Ops:
  7.2 1.7 %copy.45 = bf16[128,512]{0,1:T(8,128)(2,1)} copy(bf16[128,512]{1,0:T(8,128)(2,1)} %param.5) | data formatting | bytes 262144 | tf_op args[0]
  8.9 0.7 fusion.38
  10.7 6.2 %gather_fusion = bf16[4,128,4096]{2,1,0:T(8,128)(2,1)} fusion(bf16[8,128,4096]{2,1,0:T(8,128)(2,1)} %bitcast.196, s32[1024]{0:T(1024)S(1)} %pad_clamp_fusion), kind=kCustom, calls=%fused_computation | custom fusion | bytes 8388624 | tf_op jit(solution)/shard_map/jit(_take)/gather | solution.py:87
  16.9 5.8 %all-to-all-start = ((bf16[2,256,4096]{2,1,0:T(8,128)(2,1)}), bf16[2,256,4096]{2,1,0:T(8,128)(2,1)}, u32[]{:S(2)}, u32[]{:S(2)}) async-start(bf16[2,256,4096]{2,1,0:T(8,128)(2,1)} %bitcast.189), calls=%async_computation | async-start | bytes 8388608 | tf_op jit(solution)/shard_map/all_to_all | solution.py:95
  23.2 2.8 %select_reduce_fusion = f32[128,256]{1,0:T(8,128)S(1)} fusion(f32[128,64]{1,0:T(8,128)S(1)} %copy.64, s32[128,64]{1,0:T(8,128)S(1)} %copy.47), kind=kLoop, calls=%fused_computation.2 | loop fusion | flops 6258688 | bytes 196608
  26.2 45.4 %all-to-all-done = bf16[2,256,4096]{2,1,0:T(8,128)(2,1)} async-done(((bf16[2,256,4096]{2,1,0:T(8,128)(2,1)}), bf16[2,256,4096]{2,1,0:T(8,128)(2,1)}, u32[]{:S(2)}, u32[]{:S(2)}) %all-to-all-start) | async-done | bytes 4194336 | tf_op jit(solution)/shard_map/all_to_all | solution.py:95
  71.6 4.1 %select_reduce_fusion.2 = (f32[128]{0:T(128)S(1)}, f32[128,256]{0,1:T(8,128)S(1)}) fusion(pred[256]{0:T(512)(128)(4,1)S(1)} %broadcast_bitcast_fusion.2, bf16[2,256,4096]{2,1,0:T(8,128)(2,1)} %all-to-all-done, bf16[128,2,4096]{0,2,1:T(8,128)(2,1)} %bitcast.192), kind=kOutput, calls=%fused_computation.23 | convolution fusion | flops 536936320 | bytes 6423296 | tf_op jit(solution)/shard_map/tkd,krd->tr/dot_general | solution.py:96
  76.0 1.1 collective-permute-done
  77.1 1.8 %collective-permute-start.1 = (f32[3,128]{1,0:T(4,128)S(1)}, f32[3,128]{1,0:T(4,128)S(1)}, u32[]{:S(2)}, u32[]{:S(2)}) collective-permute-start(f32[3,128]{1,0:T(4,128)S(1)} %pad_maximum_fusion.1), channel_id=1, source_target_pairs={{0,2},{1,3},{2,0},{3,1},{4,6},{5,7},{6,4},{7,5},{8,10},{9,11},{10,... | collective-permute-start | bytes 4616 | tf_op jit(solution)/shard_map/ppermute | solution.py:30
  79.0 1.8 %collective-permute-done.1 = f32[3,128]{1,0:T(4,128)S(1)} collective-permute-done((f32[3,128]{1,0:T(4,128)S(1)}, f32[3,128]{1,0:T(4,128)S(1)}, u32[]{:S(2)}, u32[]{:S(2)}) %collective-permute-start.1) | collective-permute-done | bytes 1568 | tf_op jit(solution)/shard_map/ppermute | solution.py:30
  80.8 1.9 %collective-permute-start.2 = (f32[3,128]{1,0:T(4,128)S(1)}, f32[3,128]{1,0:T(4,128)S(1)}, u32[]{:S(2)}, u32[]{:S(2)}) collective-permute-start(f32[3,128]{1,0:T(4,128)S(1)} %pad_maximum_fusion.2), channel_id=1, source_target_pairs={{0,4},{1,5},{2,6},{3,7},{4,0},{5,1},{6,2},{7,3},{8,12},{9,13},{10,... | collective-permute-start | bytes 4616 | tf_op jit(solution)/shard_map/ppermute | solution.py:30
  82.7 1.7 %collective-permute-done.2 = f32[3,128]{1,0:T(4,128)S(1)} collective-permute-done((f32[3,128]{1,0:T(4,128)S(1)}, f32[3,128]{1,0:T(4,128)S(1)}, u32[]{:S(2)}, u32[]{:S(2)}) %collective-permute-start.2) | collective-permute-done | bytes 1568 | tf_op jit(solution)/shard_map/ppermute | solution.py:30
  84.5 2.9 %collective-permute-start.3 = (f32[3,128]{1,0:T(4,128)S(1)}, f32[3,128]{1,0:T(4,128)S(1)}, u32[]{:S(2)}, u32[]{:S(2)}) collective-permute-start(f32[3,128]{1,0:T(4,128)S(1)} %pad_maximum_fusion.3), channel_id=1, source_target_pairs={{0,8},{1,9},{2,10},{3,11},{4,12},{5,13},{6,14},{7,15},{8,0},{9,1},... | collective-permute-start | bytes 4616 | tf_op jit(solution)/shard_map/ppermute | solution.py:30
  87.4 1.6 collective-permute-done.3
  89.7 4.0 %fusion.5 = f32[128,2,4096]{0,2,1:T(8,128)S(1)} fusion(bf16[2,256,4096]{2,1,0:T(8,128)(2,1)} %all-to-all-done, bf16[128,256]{0,1:T(8,128)(2,1)S(1)} %subtract_convert_fusion), kind=kOutput, calls=%fused_computation.29 | convolution fusion | flops 536870912 | bytes 8454144 | tf_op jit(solution)/shard_map/tr,krd->tkd/dot_general | solution.py:116
  93.7 2.0 %copy-done = f32[128,2,4096]{0,2,1:T(8,128)} copy-done((f32[128,2,4096]{0,2,1:T(8,128)}, f32[128,2,4096]{0,2,1:T(8,128)S(1)}, u32[]{:S(2)}) %copy-start) | copy-done | bytes 4194328
  95.8 1.7 %copy.51 = bf16[128,8,1,512]{3,1,0,2:T(8,128)(2,1)} copy(bf16[128,8,1,512]{0,3,2,1:T(8,128)(2,1)S(1)} %dynamic-slice_convert_fusion) | data formatting | bytes 2097152 | tf_op jit(solution)/shard_map/convert_element_type | solution.py:54
  97.9 3.1 %constant_dynamic-slice_fusion.2 = f32[128,8,1,512]{0,3,2,1:T(8,128)} fusion(f32[128,8,2,512]{0,3,2,1:T(8,128)} %bitcast.191, s32[]{:T(128)S(6)} %select_n.142), kind=kLoop, calls=%fused_computation.50 | loop fusion | bytes 4194308 | tf_op jit(solution)/shard_map/jit(dynamic_index_in_dim)/dynamic_slice | solution.py:52
  101.0 2.2 %copy.50 = f32[128,8,1,512]{3,1,0,2:T(8,128)S(1)} copy(f32[128,8,1,512]{0,3,2,1:T(8,128)} %constant_dynamic-slice_fusion.2) | data formatting | bytes 4194304 | tf_op jit(solution)/shard_map/jit(dynamic_index_in_dim)/dynamic_slice | solution.py:52
  103.3 1.6 %bitcast_add_fusion = f32[128,8,512]{2,1,0:T(8,128)} fusion(f32[128,8,1,512]{3,1,0,2:T(8,128)S(1)} %copy.50, bf16[128,8,512]{2,1,0:T(8,128)(2,1)S(1)} %collective-permute-done.4), kind=kLoop, calls=%fused_computation.4 | loop fusion | flops 1048576 | bytes 5242880 | tf_op jit(solution)/shard_map/add | solution.py:55
  104.9 2.5 %reshape.241 = f32[128,4,2,512]{3,2,1,0:T(2,128)S(1)} reshape(f32[128,8,512]{2,1,0:T(8,128)} %bitcast_add_fusion) | data formatting | bytes 4194304 | tf_op jit(solution)/shard_map/reshape | solution.py:50
  107.4 1.1 constant_dynamic-slice_fusion
  108.8 1.8 %collective-permute-start.5 = (bf16[128,4,512]{2,0,1:T(8,128)(2,1)S(1)}, bf16[128,4,512]{2,0,1:T(8,128)(2,1)S(1)}, u32[]{:S(2)}, u32[]{:S(2)}) collective-permute-start(bf16[128,4,512]{2,0,1:T(8,128)(2,1)S(1)} %bitcast.199), channel_id=1, source_target_pairs={{0,2},{1,3},{2,0},{3,1},{4,6},{5,7},{6,4},{7,5},{8,10},{9,11},{10,... | collective-permute-start | bytes 1572872 | tf_op jit(solution)/shard_map/ppermute | solution.py:54
  110.8 4.1 %copy.54 = bf16[128,2,4096]{2,0,1:T(8,128)(2,1)} copy(bf16[128,2,4096]{0,2,1:T(8,128)(2,1)} %bitcast.193) | data formatting | bytes 4194304 | tf_op jit(solution)/shard_map/reshape | solution.py:91
  114.9 5.0 %all-to-all-start.1 = ((bf16[128,2,4096]{2,0,1:T(8,128)(2,1)}), bf16[128,2,4096]{2,0,1:T(8,128)(2,1)}, u32[]{:S(2)}, u32[]{:S(2)}) async-start(bf16[128,2,4096]{2,0,1:T(8,128)(2,1)} %copy.54), calls=%async_computation.1 | async-start | bytes 4194304 | tf_op jit(solution)/shard_map/all_to_all | solution.py:92
  119.9 1.8 %collective-permute-start.8 = (bf16[1,128,256]{1,2,0:T(8,128)(2,1)S(1)}, bf16[1,128,256]{1,2,0:T(8,128)(2,1)S(1)}, u32[]{:S(2)}, u32[]{:S(2)}) collective-permute-start(bf16[1,128,256]{1,2,0:T(8,128)(2,1)S(1)} %bitcast.197), channel_id=1, source_target_pairs={{0,16},{16,0},{1,17},{17,1},{2,18},{18,2},{3,19},{19,3},{4,20},{20... | collective-permute-start | bytes 196616 | tf_op jit(solution)/shard_map/ppermute | solution.py:68
  121.8 1.1 constant_dynamic-slice_fusion.1
  123.6 1.9 %collective-permute-start.6 = (bf16[128,2,512]{2,0,1:T(8,128)(2,1)S(1)}, bf16[128,2,512]{2,0,1:T(8,128)(2,1)S(1)}, u32[]{:S(2)}, u32[]{:S(2)}) collective-permute-start(bf16[128,2,512]{2,0,1:T(8,128)(2,1)S(1)} %fusion.2), channel_id=1, source_target_pairs={{0,4},{1,5},{2,6},{3,7},{4,0},{5,1},{6,2},{7,3},{8,12},{9,13},{10,... | collective-permute-start | bytes 786440 | tf_op jit(solution)/shard_map/ppermute | solution.py:54
  125.5 21.1 %collective-permute-done.8 = bf16[1,128,256]{1,2,0:T(8,128)(2,1)S(1)} collective-permute-done((bf16[1,128,256]{1,2,0:T(8,128)(2,1)S(1)}, bf16[1,128,256]{1,2,0:T(8,128)(2,1)S(1)}, u32[]{:S(2)}, u32[]{:S(2)}) %collective-permute-start.8) | collective-permute-done | bytes 65568 | tf_op jit(solution)/shard_map/ppermute | solution.py:68
  146.7 0.7 fusion.1
  147.5 2.7 %collective-permute-start.7 = (bf16[128,1,512]{2,0,1:T(8,128)(2,1)S(1)}, bf16[128,1,512]{2,0,1:T(8,128)(2,1)S(1)}, u32[]{:S(2)}, u32[]{:S(2)}) collective-permute-start(bf16[128,1,512]{2,0,1:T(8,128)(2,1)S(1)} %dynamic-slice_convert_fusion.2), channel_id=1, source_target_pairs={{0,8},{1,9},{2,10},{3,11},{4,12},{5,13},{6,14},{7,15},{8,0},{9,1},... | collective-permute-start | bytes 393224 | tf_op jit(solution)/shard_map/ppermute | solution.py:54
  150.2 6.2 %bitcast_convert_fusion = bf16[1024,4096]{1,0:T(8,128)(2,1)} fusion(bf16[2,128,1024]{1,2,0:T(8,128)(2,1)S(1)} %fusion.1, bf16[128,2,4096]{2,0,1:T(8,128)(2,1)} %all-to-all-done.1), kind=kOutput, calls=%fused_computation.1 | convolution fusion | flops 2151677952 | bytes 11010048 | tf_op jit(solution)/shard_map/str,tsd->rd/dot_general | solution.py:128
  (59 shorter events, 5.3 us)
Async XLA Ops:
  7.2 64.4 %all-gather.2.cloned.1.call-start = ((), (), s32[]{:S(2)}) async-start(), calls=%async_computation.2 | async-start | bytes 2228224 | tf_op jit(solution)/shard_map/all_gather | solution.py:90
  16.9 5.8 %copy-start.1 = (f32[128,64]{0,1:T(8,128)S(1)}, f32[128,64]{0,1:T(8,128)}, u32[]{:S(2)}) copy-start(f32[128,64]{0,1:T(8,128)} %param.8) | copy-start | bytes 98308
  16.9 5.9 %copy-start.2 = (s32[128,64]{0,1:T(8,128)S(1)}, s32[128,64]{0,1:T(8,128)}, u32[]{:S(2)}) copy-start(s32[128,64]{0,1:T(8,128)} %param.7) | copy-start | bytes 98308
  16.9 54.7 %all-to-all-start = ((bf16[2,256,4096]{2,1,0:T(8,128)(2,1)}), bf16[2,256,4096]{2,1,0:T(8,128)(2,1)}, u32[]{:S(2)}, u32[]{:S(2)}) async-start(bf16[2,256,4096]{2,1,0:T(8,128)(2,1)} %bitcast.189), calls=%async_computation | async-start | bytes 8388608 | tf_op jit(solution)/shard_map/all_to_all | solution.py:95
  75.9 1.2 collective-permute-start
  77.1 3.7 %collective-permute-start.1 = (f32[3,128]{1,0:T(4,128)S(1)}, f32[3,128]{1,0:T(4,128)S(1)}, u32[]{:S(2)}, u32[]{:S(2)}) collective-permute-start(f32[3,128]{1,0:T(4,128)S(1)} %pad_maximum_fusion.1), channel_id=1, source_target_pairs={{0,2},{1,3},{2,0},{3,1},{4,6},{5,7},{6,4},{7,5},{8,10},{9,11},{10,... | collective-permute-start | bytes 4616 | tf_op jit(solution)/shard_map/ppermute | solution.py:30
  80.8 3.7 %collective-permute-start.2 = (f32[3,128]{1,0:T(4,128)S(1)}, f32[3,128]{1,0:T(4,128)S(1)}, u32[]{:S(2)}, u32[]{:S(2)}) collective-permute-start(f32[3,128]{1,0:T(4,128)S(1)} %pad_maximum_fusion.2), channel_id=1, source_target_pairs={{0,4},{1,5},{2,6},{3,7},{4,0},{5,1},{6,2},{7,3},{8,12},{9,13},{10,... | collective-permute-start | bytes 4616 | tf_op jit(solution)/shard_map/ppermute | solution.py:30
  84.5 4.5 %collective-permute-start.3 = (f32[3,128]{1,0:T(4,128)S(1)}, f32[3,128]{1,0:T(4,128)S(1)}, u32[]{:S(2)}, u32[]{:S(2)}) collective-permute-start(f32[3,128]{1,0:T(4,128)S(1)} %pad_maximum_fusion.3), channel_id=1, source_target_pairs={{0,8},{1,9},{2,10},{3,11},{4,12},{5,13},{6,14},{7,15},{8,0},{9,1},... | collective-permute-start | bytes 4616 | tf_op jit(solution)/shard_map/ppermute | solution.py:30
  93.7 2.0 %copy-start = (f32[128,2,4096]{0,2,1:T(8,128)}, f32[128,2,4096]{0,2,1:T(8,128)S(1)}, u32[]{:S(2)}) copy-start(f32[128,2,4096]{0,2,1:T(8,128)S(1)} %fusion.5) | copy-start | bytes 12582916
  97.6 5.7 %collective-permute-start.4 = (bf16[128,8,512]{2,1,0:T(8,128)(2,1)}, bf16[128,8,512]{2,1,0:T(8,128)(2,1)S(1)}, u32[]{:S(2)}, u32[]{:S(2)}) collective-permute-start(bf16[128,8,512]{2,1,0:T(8,128)(2,1)} %bitcast.26), channel_id=1, source_target_pairs={{0,1},{1,0},{2,3},{3,2},{4,5},{5,4},{6,7},{7,6},{8,9},{9,8},{10,11... | collective-permute-start | bytes 3145736 | tf_op jit(solution)/shard_map/ppermute | solution.py:54
  108.8 14.4 %collective-permute-start.5 = (bf16[128,4,512]{2,0,1:T(8,128)(2,1)S(1)}, bf16[128,4,512]{2,0,1:T(8,128)(2,1)S(1)}, u32[]{:S(2)}, u32[]{:S(2)}) collective-permute-start(bf16[128,4,512]{2,0,1:T(8,128)(2,1)S(1)} %bitcast.199), channel_id=1, source_target_pairs={{0,2},{1,3},{2,0},{3,1},{4,6},{5,7},{6,4},{7,5},{8,10},{9,11},{10,... | collective-permute-start | bytes 1572872 | tf_op jit(solution)/shard_map/ppermute | solution.py:54
  114.9 35.3 %all-to-all-start.1 = ((bf16[128,2,4096]{2,0,1:T(8,128)(2,1)}), bf16[128,2,4096]{2,0,1:T(8,128)(2,1)}, u32[]{:S(2)}, u32[]{:S(2)}) async-start(bf16[128,2,4096]{2,0,1:T(8,128)(2,1)} %copy.54), calls=%async_computation.1 | async-start | bytes 4194304 | tf_op jit(solution)/shard_map/all_to_all | solution.py:92
  119.9 26.7 %collective-permute-start.8 = (bf16[1,128,256]{1,2,0:T(8,128)(2,1)S(1)}, bf16[1,128,256]{1,2,0:T(8,128)(2,1)S(1)}, u32[]{:S(2)}, u32[]{:S(2)}) collective-permute-start(bf16[1,128,256]{1,2,0:T(8,128)(2,1)S(1)} %bitcast.197), channel_id=1, source_target_pairs={{0,16},{16,0},{1,17},{17,1},{2,18},{18,2},{3,19},{19,3},{4,20},{20... | collective-permute-start | bytes 196616 | tf_op jit(solution)/shard_map/ppermute | solution.py:68
  123.6 23.8 %collective-permute-start.6 = (bf16[128,2,512]{2,0,1:T(8,128)(2,1)S(1)}, bf16[128,2,512]{2,0,1:T(8,128)(2,1)S(1)}, u32[]{:S(2)}, u32[]{:S(2)}) collective-permute-start(bf16[128,2,512]{2,0,1:T(8,128)(2,1)S(1)} %fusion.2), channel_id=1, source_target_pairs={{0,4},{1,5},{2,6},{3,7},{4,0},{5,1},{6,2},{7,3},{8,12},{9,13},{10,... | collective-permute-start | bytes 786440 | tf_op jit(solution)/shard_map/ppermute | solution.py:54
  147.5 8.9 %collective-permute-start.7 = (bf16[128,1,512]{2,0,1:T(8,128)(2,1)S(1)}, bf16[128,1,512]{2,0,1:T(8,128)(2,1)S(1)}, u32[]{:S(2)}, u32[]{:S(2)}) collective-permute-start(bf16[128,1,512]{2,0,1:T(8,128)(2,1)S(1)} %dynamic-slice_convert_fusion.2), channel_id=1, source_target_pairs={{0,8},{1,9},{2,10},{3,11},{4,12},{5,13},{6,14},{7,15},{8,0},{9,1},... | collective-permute-start | bytes 393224 | tf_op jit(solution)/shard_map/ppermute | solution.py:54
Sparse Core Ops, SparseCore 0:
  10.7 44.1 all-gather.1

commit v7 on v6

--- a/solution.py
+++ b/solution.py
@@ -72,6 +72,18 @@
     return held
 
 
+def shift_exchange(wide):
+    n = lax.axis_size("dp")
+    me = lax.axis_index("dp")
+    own = lax.dynamic_index_in_dim(wide, me, 1, keepdims=True)
+    pieces = [own]
+    for shift in range(1, n):
+        send = lax.dynamic_index_in_dim(wide, (me + shift) % n, 1, keepdims=True)
+        pieces.append(lax.ppermute(send, "dp", [(k, (k + shift) % n) for k in range(n)]))
+    held = jnp.concatenate(pieces, axis=1)
+    return jnp.take(held, (me - jnp.arange(n)) % n, axis=1, mode="clip")
+
+
 def shards(hidden, weight, teacher_ids, teacher_logp, union_blocks):
     tokens_here = hidden.shape[0]
     n_groups = lax.axis_size("dp")
@@ -89,7 +101,7 @@
     )
     full_rows = lax.all_gather(hidden, "vocab", axis=1, tiled=True)
     wide = full_rows.reshape(tokens_here, n_groups, piece)
-    halves = lax.all_to_all(wide, "dp", split_axis=1, concat_axis=1, tiled=True)
+    halves = shift_exchange(wide)
     own_slots = lax.dynamic_index_in_dim(table, dp_row, 0, keepdims=False)
     col_mask = jnp.repeat(own_slots >= 0, BLOCK)
     rows_w = lax.all_to_all(chosen, "dp", split_axis=0, concat_axis=0, tiled=True)

time: 165 us -> 158 us (0.958)
  waiting for transfers between devices: 73.2 us -> 64.5 us
  starting transfers between devices: 25.8 us -> 19.8 us
  other arithmetic: 9.32 us -> 15 us
  local copies, waits for them, and re-layouts: 27 us -> 28.7 us
    ppermute x1, waiting for transfers between devices: 21.1 us -> 12 us  [doubling_gather(): got = lax.ppermute(held, 'dp', [(k, k ^ bit) for k in range(n)])]
    all_to_all x1 -> x0, starting transfers between devices: 5 us -> none  [shards(): halves = lax.all_to_all(wide, 'dp', split_axis=1, concat_axis=1, tiled=True)]
    reshape x1 -> x0, local copies, waits for them, and re-layouts: 4.08 us -> none  [shards(): wide = full_rows.reshape(tokens_here, n_groups, piece)]
    unnamed x13 -> x21, local copies, waits for them, and re-layouts: 4.24 us -> 7.24 us
    concatenate x0 -> x1, other arithmetic: none -> 2.74 us  [shift_exchange(): held = jnp.concatenate(pieces, axis=1)]
    gather x0 -> x1, local copies, waits for them, and re-layouts: none -> 2.63 us  [shift_exchange(): return jnp.take(held, (me - jnp.arange(n)) % n, axis=1, mode='clip')]
    add x3, other arithmetic: 2.08 us -> 4.34 us  [halving_scatter(): part = keep + got.astype(jnp.float32)]
  transfers between devices with their start and end apart: 12 -> 12, of which waited for: 7 -> 7; matrix products, arithmetic and copies ran while one was open for 18% -> 26% of each run, Pallas kernels for 0% -> 0%
where the time goes in v7:
time: 158 us; the launch traced here: 157 us
  waiting for transfers between devices  64.5 us (41%)
  local copies, waits for them, and re-layouts  28.7 us (18%)
  starting transfers between devices  19.8 us (13%)
  other arithmetic  15 us (9%)
  matrix products  14.9 us (9%)
  between operations  14.3 us (9%)
    all_to_all x1, waiting for transfers between devices, shards(): lax.all_to_all(chosen, 'dp', split_axis=0, concat_axis=0, tiled=True)  45.4 us
    ppermute x1, waiting for transfers between devices, doubling_gather(): got = lax.ppermute(held, 'dp', [(k, k ^ bit) for k in range(n)])  12 us
    unnamed x21, local copies, waits for them, and re-layouts  7.24 us
    dot_general x1, matrix products, shards(): jnp.einsum('str,tsd->rd', placed, halves, preferred_element_type=jnp.floa...  6.82 us
    ppermute x4, starting transfers between devices, combine_stats(): lax.ppermute(jnp.stack([top, total, picked]), 'vocab', [(k, k ^ bit) for...  6.7 us
    ppermute x4, starting transfers between devices, halving_scatter(): lax.ppermute(send.astype(jnp.bfloat16), 'vocab', [(k, k ^ bit) for k in r...  6.41 us
    gather x1, local copies, waits for them, and re-layouts, shards(): jnp.take(blocks, jnp.maximum(local, 0).reshape(-1), axis=0, mode='clip')  6.21 us
    ppermute x4, waiting for transfers between devices, combine_stats(): lax.ppermute(jnp.stack([top, total, picked]), 'vocab', [(k, k ^ bit) for...  6.05 us
  transfers between devices with their start and end apart: 12, of which 7 were waited for; matrix products, arithmetic and copies ran while one was open for 26% of the time, Pallas kernels for 0%

profile of v7, /device:TPU:0, one launch (start us, length us, event | category | flops | bytes accessed | tf_op | source)
XLA Modules:
  0.0 157.3 jit_solution(11057757628581756959)
XLA Ops:
  7.2 1.7 %copy.45 = bf16[128,512]{0,1:T(8,128)(2,1)} copy(bf16[128,512]{1,0:T(8,128)(2,1)} %param.5) | data formatting | bytes 262144 | tf_op args[0]
  10.7 6.2 %gather_fusion = bf16[4,128,4096]{2,1,0:T(8,128)(2,1)} fusion(bf16[8,128,4096]{2,1,0:T(8,128)(2,1)} %bitcast.200, s32[1024]{0:T(1024)S(1)} %pad_clamp_fusion.1), kind=kCustom, calls=%fused_computation | custom fusion | bytes 8388624 | tf_op jit(solution)/shard_map/jit(_take)/gather | solution.py:99
  16.9 5.8 %all-to-all-start = ((bf16[2,256,4096]{2,1,0:T(8,128)(2,1)}), bf16[2,256,4096]{2,1,0:T(8,128)(2,1)}, u32[]{:S(2)}, u32[]{:S(2)}) async-start(bf16[2,256,4096]{2,1,0:T(8,128)(2,1)} %bitcast.193), calls=%async_computation | async-start | bytes 8388608 | tf_op jit(solution)/shard_map/all_to_all | solution.py:107
  23.2 2.8 %select_reduce_fusion = f32[128,256]{1,0:T(8,128)S(1)} fusion(f32[128,64]{1,0:T(8,128)S(1)} %copy.65, s32[128,64]{1,0:T(8,128)S(1)} %copy.47), kind=kLoop, calls=%fused_computation.3 | loop fusion | flops 6258688 | bytes 196608
  26.2 45.4 %all-to-all-done = bf16[2,256,4096]{2,1,0:T(8,128)(2,1)} async-done(((bf16[2,256,4096]{2,1,0:T(8,128)(2,1)}), bf16[2,256,4096]{2,1,0:T(8,128)(2,1)}, u32[]{:S(2)}, u32[]{:S(2)}) %all-to-all-start) | async-done | bytes 4194336 | tf_op jit(solution)/shard_map/all_to_all | solution.py:107
  71.6 4.1 %select_reduce_fusion.2 = (f32[128]{0:T(128)S(1)}, f32[128,256]{0,1:T(8,128)S(1)}) fusion(pred[256]{0:T(512)(128)(4,1)S(1)} %broadcast_bitcast_fusion.2, bf16[2,256,4096]{2,1,0:T(8,128)(2,1)} %all-to-all-done, bf16[128,2,4096]{0,2,1:T(8,128)(2,1)} %bitcast.196), kind=kOutput, calls=%fused_computation.26 | convolution fusion | flops 536936320 | bytes 6423296 | tf_op jit(solution)/shard_map/tkd,krd->tr/dot_general | solution.py:108
  76.0 1.1 collective-permute-done
  77.1 1.8 %collective-permute-start.1 = (f32[3,128]{1,0:T(4,128)S(1)}, f32[3,128]{1,0:T(4,128)S(1)}, u32[]{:S(2)}, u32[]{:S(2)}) collective-permute-start(f32[3,128]{1,0:T(4,128)S(1)} %pad_maximum_fusion.2), channel_id=1, source_target_pairs={{0,2},{1,3},{2,0},{3,1},{4,6},{5,7},{6,4},{7,5},{8,10},{9,11},{10,... | collective-permute-start | bytes 4616 | tf_op jit(solution)/shard_map/ppermute | solution.py:30
  79.1 1.7 %collective-permute-done.1 = f32[3,128]{1,0:T(4,128)S(1)} collective-permute-done((f32[3,128]{1,0:T(4,128)S(1)}, f32[3,128]{1,0:T(4,128)S(1)}, u32[]{:S(2)}, u32[]{:S(2)}) %collective-permute-start.1) | collective-permute-done | bytes 1568 | tf_op jit(solution)/shard_map/ppermute | solution.py:30
  80.8 1.9 %collective-permute-start.2 = (f32[3,128]{1,0:T(4,128)S(1)}, f32[3,128]{1,0:T(4,128)S(1)}, u32[]{:S(2)}, u32[]{:S(2)}) collective-permute-start(f32[3,128]{1,0:T(4,128)S(1)} %pad_maximum_fusion.3), channel_id=1, source_target_pairs={{0,4},{1,5},{2,6},{3,7},{4,0},{5,1},{6,2},{7,3},{8,12},{9,13},{10,... | collective-permute-start | bytes 4616 | tf_op jit(solution)/shard_map/ppermute | solution.py:30
  82.8 1.7 %collective-permute-done.2 = f32[3,128]{1,0:T(4,128)S(1)} collective-permute-done((f32[3,128]{1,0:T(4,128)S(1)}, f32[3,128]{1,0:T(4,128)S(1)}, u32[]{:S(2)}, u32[]{:S(2)}) %collective-permute-start.2) | collective-permute-done | bytes 1568 | tf_op jit(solution)/shard_map/ppermute | solution.py:30
  84.5 2.9 %collective-permute-start.3 = (f32[3,128]{1,0:T(4,128)S(1)}, f32[3,128]{1,0:T(4,128)S(1)}, u32[]{:S(2)}, u32[]{:S(2)}) collective-permute-start(f32[3,128]{1,0:T(4,128)S(1)} %pad_maximum_fusion.4), channel_id=1, source_target_pairs={{0,8},{1,9},{2,10},{3,11},{4,12},{5,13},{6,14},{7,15},{8,0},{9,1},... | collective-permute-start | bytes 4616 | tf_op jit(solution)/shard_map/ppermute | solution.py:30
  87.5 1.6 collective-permute-done.3
  89.7 4.0 %fusion.6 = f32[128,2,4096]{0,2,1:T(8,128)S(1)} fusion(bf16[2,256,4096]{2,1,0:T(8,128)(2,1)} %all-to-all-done, bf16[128,256]{0,1:T(8,128)(2,1)S(1)} %subtract_convert_fusion), kind=kOutput, calls=%fused_computation.32 | convolution fusion | flops 536870912 | bytes 8454144 | tf_op jit(solution)/shard_map/tr,krd->tkd/dot_general | solution.py:128
  93.7 2.0 %copy-done = f32[128,2,4096]{0,2,1:T(8,128)} copy-done((f32[128,2,4096]{0,2,1:T(8,128)}, f32[128,2,4096]{0,2,1:T(8,128)S(1)}, u32[]{:S(2)}) %copy-start) | copy-done | bytes 4194328
  95.9 1.7 %copy.51 = bf16[128,8,1,512]{3,1,0,2:T(8,128)(2,1)} copy(bf16[128,8,1,512]{0,3,2,1:T(8,128)(2,1)S(1)} %dynamic-slice_convert_fusion) | data formatting | bytes 2097152 | tf_op jit(solution)/shard_map/convert_element_type | solution.py:54
  97.7 1.1 constant_dynamic-slice_fusion.1
  99.1 1.2 copy-done.1
  100.3 1.5 constant_dynamic-slice_fusion.4
  101.8 2.2 %copy.50 = f32[128,8,1,512]{3,1,0,2:T(8,128)S(1)} copy(f32[128,8,1,512]{0,3,2,1:T(8,128)} %constant_dynamic-slice_fusion.4) | data formatting | bytes 4194304 | tf_op jit(solution)/shard_map/jit(dynamic_index_in_dim)/dynamic_slice | solution.py:52
  104.7 2.9 %bitcast_add_fusion = f32[128,8,512]{2,1,0:T(8,128)} fusion(f32[128,8,1,512]{3,1,0,2:T(8,128)S(1)} %copy.50, bf16[128,8,512]{2,1,0:T(8,128)(2,1)} %collective-permute-done.4), kind=kLoop, calls=%fused_computation.7 | loop fusion | flops 1048576 | bytes 5242880 | tf_op jit(solution)/shard_map/add | solution.py:55
  107.5 2.5 %reshape.281 = f32[128,4,2,512]{3,2,1,0:T(2,128)S(1)} reshape(f32[128,8,512]{2,1,0:T(8,128)} %bitcast_add_fusion) | data formatting | bytes 4194304 | tf_op jit(solution)/shard_map/reshape | solution.py:50
  111.1 1.1 copy.74
  112.2 1.8 %collective-permute-start.5 = (bf16[128,4,512]{2,0,1:T(8,128)(2,1)}, bf16[128,4,512]{2,0,1:T(8,128)(2,1)}, u32[]{:S(2)}, u32[]{:S(2)}) collective-permute-start(bf16[128,4,512]{2,0,1:T(8,128)(2,1)} %bitcast.190), channel_id=1, source_target_pairs={{0,2},{1,3},{2,0},{3,1},{4,6},{5,7},{6,4},{7,5},{8,10},{9,11},{10,... | collective-permute-start | bytes 1572872 | tf_op jit(solution)/shard_map/ppermute | solution.py:54
  114.0 12.0 %collective-permute-done.8 = bf16[1,128,256]{1,2,0:T(8,128)(2,1)S(1)} collective-permute-done((bf16[1,128,256]{1,2,0:T(8,128)(2,1)S(1)}, bf16[1,128,256]{1,2,0:T(8,128)(2,1)S(1)}, u32[]{:S(2)}, u32[]{:S(2)}) %collective-permute-start.8) | collective-permute-done | bytes 65568 | tf_op jit(solution)/shard_map/ppermute | solution.py:68
  126.1 1.4 fusion.2
  128.6 1.4 bitcast_add_fusion.1
  131.7 1.8 %collective-permute-start.6 = (bf16[128,2,512]{2,0,1:T(8,128)(2,1)}, bf16[128,2,512]{2,0,1:T(8,128)(2,1)S(1)}, u32[]{:S(2)}, u32[]{:S(2)}) collective-permute-start(bf16[128,2,512]{2,0,1:T(8,128)(2,1)} %fusion.3), channel_id=1, source_target_pairs={{0,4},{1,5},{2,6},{3,7},{4,0},{5,1},{6,2},{7,3},{8,12},{9,13},{10,... | collective-permute-start | bytes 786440 | tf_op jit(solution)/shard_map/ppermute | solution.py:54
  133.6 2.7 %pad_maximum_fusion = bf16[128,2,4096]{0,2,1:T(8,128)(2,1)} fusion(bf16[128,1,4096]{0,2,1:T(8,128)(2,1)} %collective-permute-done.9, bf16[128,1,4096]{0,2,1:T(8,128)(2,1)S(1)} %get-tuple-element.19), kind=kLoop, calls=%fused_computation.5 | loop fusion | flops 1048576 | bytes 4194304 | tf_op jit(solution)/shard_map/concatenate | solution.py:83
  136.3 2.6 %gather_fusion.1 = bf16[2,128,4096]{1,2,0:T(8,128)(2,1)S(1)} fusion(bf16[128,2,4096]{0,2,1:T(8,128)(2,1)} %pad_maximum_fusion, s32[1024]{0:T(1024)S(1)} %pad_clamp_fusion), kind=kCustom, calls=%fused_computation.1 | custom fusion | bytes 4194312 | tf_op jit(solution)/shard_map/jit(_take)/gather | solution.py:84
  140.1 2.8 %collective-permute-start.7 = (bf16[128,1,512]{2,0,1:T(8,128)(2,1)S(1)}, bf16[128,1,512]{2,0,1:T(8,128)(2,1)S(1)}, u32[]{:S(2)}, u32[]{:S(2)}) collective-permute-start(bf16[128,1,512]{2,0,1:T(8,128)(2,1)S(1)} %dynamic-slice_convert_fusion.2), channel_id=1, source_target_pairs={{0,8},{1,9},{2,10},{3,11},{4,12},{5,13},{6,14},{7,15},{8,0},{9,1},... | collective-permute-start | bytes 393224 | tf_op jit(solution)/shard_map/ppermute | solution.py:54
  142.9 6.8 %bitcast_convert_fusion = bf16[1024,4096]{1,0:T(8,128)(2,1)} fusion(bf16[2,128,1024]{1,2,0:T(8,128)(2,1)} %fusion.2, bf16[2,128,4096]{1,2,0:T(8,128)(2,1)S(1)} %gather_fusion.1), kind=kOutput, calls=%fused_computation.2 | convolution fusion | flops 2151677952 | bytes 11010048 | tf_op jit(solution)/shard_map/str,tsd->rd/dot_general | solution.py:140
  (71 shorter events, 10.7 us)
Async XLA Ops:
  7.2 64.5 %all-gather.2.cloned.1.call-start = ((), (), s32[]{:S(2)}) async-start(), calls=%async_computation.1 | async-start | bytes 2228224 | tf_op jit(solution)/shard_map/all_gather | solution.py:102
  16.9 5.8 %copy-start.5 = (f32[128,64]{0,1:T(8,128)S(1)}, f32[128,64]{0,1:T(8,128)}, u32[]{:S(2)}) copy-start(f32[128,64]{0,1:T(8,128)} %param.8) | copy-start | bytes 98308
  16.9 5.9 %copy-start.6 = (s32[128,64]{0,1:T(8,128)S(1)}, s32[128,64]{0,1:T(8,128)}, u32[]{:S(2)}) copy-start(s32[128,64]{0,1:T(8,128)} %param.7) | copy-start | bytes 98308
  16.9 54.7 %all-to-all-start = ((bf16[2,256,4096]{2,1,0:T(8,128)(2,1)}), bf16[2,256,4096]{2,1,0:T(8,128)(2,1)}, u32[]{:S(2)}, u32[]{:S(2)}) async-start(bf16[2,256,4096]{2,1,0:T(8,128)(2,1)} %bitcast.193), calls=%async_computation | async-start | bytes 8388608 | tf_op jit(solution)/shard_map/all_to_all | solution.py:107
  75.9 1.2 collective-permute-start
  77.1 3.7 %collective-permute-start.1 = (f32[3,128]{1,0:T(4,128)S(1)}, f32[3,128]{1,0:T(4,128)S(1)}, u32[]{:S(2)}, u32[]{:S(2)}) collective-permute-start(f32[3,128]{1,0:T(4,128)S(1)} %pad_maximum_fusion.2), channel_id=1, source_target_pairs={{0,2},{1,3},{2,0},{3,1},{4,6},{5,7},{6,4},{7,5},{8,10},{9,11},{10,... | collective-permute-start | bytes 4616 | tf_op jit(solution)/shard_map/ppermute | solution.py:30
  80.8 3.7 %collective-permute-start.2 = (f32[3,128]{1,0:T(4,128)S(1)}, f32[3,128]{1,0:T(4,128)S(1)}, u32[]{:S(2)}, u32[]{:S(2)}) collective-permute-start(f32[3,128]{1,0:T(4,128)S(1)} %pad_maximum_fusion.3), channel_id=1, source_target_pairs={{0,4},{1,5},{2,6},{3,7},{4,0},{5,1},{6,2},{7,3},{8,12},{9,13},{10,... | collective-permute-start | bytes 4616 | tf_op jit(solution)/shard_map/ppermute | solution.py:30
  84.5 4.5 %collective-permute-start.3 = (f32[3,128]{1,0:T(4,128)S(1)}, f32[3,128]{1,0:T(4,128)S(1)}, u32[]{:S(2)}, u32[]{:S(2)}) collective-permute-start(f32[3,128]{1,0:T(4,128)S(1)} %pad_maximum_fusion.4), channel_id=1, source_target_pairs={{0,8},{1,9},{2,10},{3,11},{4,12},{5,13},{6,14},{7,15},{8,0},{9,1},... | collective-permute-start | bytes 4616 | tf_op jit(solution)/shard_map/ppermute | solution.py:30
  93.7 2.0 %copy-start = (f32[128,2,4096]{0,2,1:T(8,128)}, f32[128,2,4096]{0,2,1:T(8,128)S(1)}, u32[]{:S(2)}) copy-start(f32[128,2,4096]{0,2,1:T(8,128)S(1)} %fusion.6) | copy-start | bytes 12582916
  95.7 2.0 %copy-start.2 = (bf16[128,8192]{0,1:T(8,128)(2,1)S(1)}, bf16[128,8192]{0,1:T(8,128)(2,1)}, u32[]{:S(2)}) copy-start(bf16[128,8192]{0,1:T(8,128)(2,1)} %all-gather.2.cloned.1.call-done) | copy-start | bytes 6291460
  97.6 7.1 %collective-permute-start.4 = (bf16[128,8,512]{2,1,0:T(8,128)(2,1)}, bf16[128,8,512]{2,1,0:T(8,128)(2,1)}, u32[]{:S(2)}, u32[]{:S(2)}) collective-permute-start(bf16[128,8,512]{2,1,0:T(8,128)(2,1)} %bitcast.201), channel_id=1, source_target_pairs={{0,1},{1,0},{2,3},{3,2},{4,5},{5,4},{6,7},{7,6},{8,9},{9,8},{10,11... | collective-permute-start | bytes 3145736 | tf_op jit(solution)/shard_map/ppermute | solution.py:54
  97.7 2.6 %copy-start.1 = (f32[128,2,4096]{0,2,1:T(8,128)S(1)}, f32[128,2,4096]{0,2,1:T(8,128)}, u32[]{:S(2)}) copy-start(f32[128,2,4096]{0,2,1:T(8,128)} %copy-done) | copy-start | bytes 12582916
  98.9 34.7 %collective-permute-start.9 = (bf16[128,1,4096]{0,2,1:T(8,128)(2,1)}, bf16[128,1,4096]{0,2,1:T(8,128)(2,1)}, u32[]{:S(2)}, u32[]{:S(2)}) collective-permute-start(bf16[128,1,4096]{0,2,1:T(8,128)(2,1)} %get-tuple-element.20), channel_id=1, source_target_pairs={{0,16},{16,0},{1,17},{17,1},{2,18},{18,2},{3,19},{19,3},{4,20},{20... | collective-permute-start | bytes 3145736 | tf_op jit(solution)/shard_map/ppermute | solution.py:82
  104.0 22.0 %collective-permute-start.8 = (bf16[1,128,256]{1,2,0:T(8,128)(2,1)S(1)}, bf16[1,128,256]{1,2,0:T(8,128)(2,1)S(1)}, u32[]{:S(2)}, u32[]{:S(2)}) collective-permute-start(bf16[1,128,256]{1,2,0:T(8,128)(2,1)S(1)} %bitcast.202), channel_id=1, source_target_pairs={{0,16},{16,0},{1,17},{17,1},{2,18},{18,2},{3,19},{19,3},{4,20},{20... | collective-permute-start | bytes 196616 | tf_op jit(solution)/shard_map/ppermute | solution.py:68
  112.2 16.4 %collective-permute-start.5 = (bf16[128,4,512]{2,0,1:T(8,128)(2,1)}, bf16[128,4,512]{2,0,1:T(8,128)(2,1)}, u32[]{:S(2)}, u32[]{:S(2)}) collective-permute-start(bf16[128,4,512]{2,0,1:T(8,128)(2,1)} %bitcast.190), channel_id=1, source_target_pairs={{0,2},{1,3},{2,0},{3,1},{4,6},{5,7},{6,4},{7,5},{8,10},{9,11},{10,... | collective-permute-start | bytes 1572872 | tf_op jit(solution)/shard_map/ppermute | solution.py:54
  130.0 1.0 copy-start.3
  131.7 8.3 %collective-permute-start.6 = (bf16[128,2,512]{2,0,1:T(8,128)(2,1)}, bf16[128,2,512]{2,0,1:T(8,128)(2,1)S(1)}, u32[]{:S(2)}, u32[]{:S(2)}) collective-permute-start(bf16[128,2,512]{2,0,1:T(8,128)(2,1)} %fusion.3), channel_id=1, source_target_pairs={{0,4},{1,5},{2,6},{3,7},{4,0},{5,1},{6,2},{7,3},{8,12},{9,13},{10,... | collective-permute-start | bytes 786440 | tf_op jit(solution)/shard_map/ppermute | solution.py:54
  136.3 3.7 %copy-start.4 = (f32[128,4,512]{2,0,1:T(8,128)S(1)}, f32[128,4,512]{2,0,1:T(8,128)}, u32[]{:S(2)}) copy-start(f32[128,4,512]{2,0,1:T(8,128)} %copy-done.3) | copy-start | bytes 3145732
  140.1 9.6 %collective-permute-start.7 = (bf16[128,1,512]{2,0,1:T(8,128)(2,1)S(1)}, bf16[128,1,512]{2,0,1:T(8,128)(2,1)S(1)}, u32[]{:S(2)}, u32[]{:S(2)}) collective-permute-start(bf16[128,1,512]{2,0,1:T(8,128)(2,1)S(1)} %dynamic-slice_convert_fusion.2), channel_id=1, source_target_pairs={{0,8},{1,9},{2,10},{3,11},{4,12},{5,13},{6,14},{7,15},{8,0},{9,1},... | collective-permute-start | bytes 393224 | tf_op jit(solution)/shard_map/ppermute | solution.py:54
Sparse Core Ops, SparseCore 0:
  10.7 44.1 all-gather.1

commit v8 on v7

--- a/solution.py
+++ b/solution.py
@@ -57,6 +57,24 @@
     return part.reshape(rows, width // n)
 
 
+def doubling_rows(block):
+    n = lax.axis_size("vocab")
+    if n & (n - 1):
+        return lax.all_gather(block, "vocab", axis=1, tiled=True)
+    me = lax.axis_index("vocab")
+    rows, width = block.shape
+    held = block[:, None, :]
+    bit = n // 2
+    while bit >= 1:
+        got = lax.ppermute(held, "vocab", [(k, k ^ bit) for k in range(n)])
+        clear = (me // bit) % 2 == 0
+        low = jnp.where(clear, held, got)
+        high = jnp.where(clear, got, held)
+        held = jnp.stack([low, high], axis=2).reshape(rows, 2 * held.shape[1], width)
+        bit //= 2
+    return held.reshape(rows, n * width)
+
+
 def doubling_gather(piece):
     n = lax.axis_size("dp")
     if n & (n - 1):
@@ -99,7 +117,7 @@
     chosen = jnp.take(blocks, jnp.maximum(local, 0).reshape(-1), axis=0, mode="clip").reshape(
         n_groups, width, piece
     )
-    full_rows = lax.all_gather(hidden, "vocab", axis=1, tiled=True)
+    full_rows = doubling_rows(hidden)
     wide = full_rows.reshape(tokens_here, n_groups, piece)
     halves = shift_exchange(wide)
     own_slots = lax.dynamic_index_in_dim(table, dp_row, 0, keepdims=False)

time: 158 us -> 160 us (1.013)
  between operations: 14.3 us -> 1.12 us
  starting transfers between devices: 19.8 us -> 26.6 us
  waiting for transfers between devices: 64.5 us -> 69.3 us
  local copies, waits for them, and re-layouts: 28.7 us -> 30.7 us
    ppermute x0 -> x4, waiting for transfers between devices: none -> 11.4 us  [doubling_rows(): got = lax.ppermute(held, 'vocab', [(k, k ^ bit) for k in range(n)])]
    all_to_all x1, waiting for transfers between devices: 45.4 us -> 38 us  [shards(): lax.all_to_all(chosen, 'dp', split_axis=0, concat_axis=0, tiled=True)]
    ppermute x0 -> x4, starting transfers between devices: none -> 6.49 us  [doubling_rows(): got = lax.ppermute(held, 'vocab', [(k, k ^ bit) for k in range(n)])]
    another operation x0 -> x2, local copies, waits for them, and re-layouts: none -> 3.1 us  [doubling_rows(): jnp.stack([low, high], axis=2).reshape(rows, 2 * held.shape[1], width)]
    unnamed x21 -> x15, local copies, waits for them, and re-layouts: 7.24 us -> 4.23 us
    another operation x0 -> x7, other arithmetic: none -> 2.92 us  [doubling_rows(): jnp.stack([low, high], axis=2).reshape(rows, 2 * held.shape[1], width)]
    unnamed x1 -> x0, other arithmetic: 2.83 us -> none
    dot_general x0 -> x1, matrix products: none -> 1.98 us  [shards(): target = jnp.einsum('tk,tkr->tr', teacher_q, onehot)]
  transfers between devices with their start and end apart: 12 -> 15, of which waited for: 7 -> 9; matrix products, arithmetic and copies ran while one was open for 26% -> 30% of each run, Pallas kernels for 0% -> 0%
where the time goes in v8:
time: 160 us; the launch traced here: 159 us
  waiting for transfers between devices  69.3 us (43%)
  local copies, waits for them, and re-layouts  30.7 us (19%)
  starting transfers between devices  26.6 us (17%)
  matrix products  16.5 us (10%)
  other arithmetic  15.2 us (10%)
    all_to_all x1, waiting for transfers between devices, shards(): lax.all_to_all(chosen, 'dp', split_axis=0, concat_axis=0, tiled=True)  38 us
    ppermute x1, waiting for transfers between devices, doubling_gather(): got = lax.ppermute(held, 'dp', [(k, k ^ bit) for k in range(n)])  11.6 us
    ppermute x4, waiting for transfers between devices, doubling_rows(): got = lax.ppermute(held, 'vocab', [(k, k ^ bit) for k in range(n)])  11.4 us
    ppermute x4, starting transfers between devices, combine_stats(): lax.ppermute(jnp.stack([top, total, picked]), 'vocab', [(k, k ^ bit) for...  7.26 us
    ppermute x4, waiting for transfers between devices, combine_stats(): lax.ppermute(jnp.stack([top, total, picked]), 'vocab', [(k, k ^ bit) for...  6.96 us
    dot_general x1, matrix products, shards(): jnp.einsum('str,tsd->rd', placed, halves, preferred_element_type=jnp.floa...  6.82 us
    ppermute x4, starting transfers between devices, doubling_rows(): got = lax.ppermute(held, 'vocab', [(k, k ^ bit) for k in range(n)])  6.49 us
    dynamic_slice x3, local copies, waits for them, and re-layouts, halving_scatter(): keep = lax.dynamic_index_in_dim(halves, mine, 2, keepdims=False)  6.43 us
  transfers between devices with their start and end apart: 15, of which 9 were waited for; matrix products, arithmetic and copies ran while one was open for 30% of the time, Pallas kernels for 0%

profile of v8, /device:TPU:0, one launch (start us, length us, event | category | flops | bytes accessed | tf_op | source)
XLA Modules:
  0.0 159.5 jit_solution(15392180363496747221)
XLA Ops:
  0.6 4.1 %collective-permute-start = (bf16[128,1,512]{2,0,1:T(8,128)(2,1)}, bf16[128,1,512]{2,0,1:T(8,128)(2,1)S(1)}, u32[]{:S(2)}, u32[]{:S(2)}) collective-permute-start(bf16[128,1,512]{2,0,1:T(8,128)(2,1)} %bitcast.251), channel_id=1, source_target_pairs={{0,8},{1,9},{2,10},{3,11},{4,12},{5,13},{6,14},{7,15},{8,0},{9,1},... | collective-permute-start | bytes 393224 | tf_op jit(solution)/shard_map/ppermute | solution.py:69
  6.3 5.0 %collective-permute-done = bf16[128,1,512]{2,0,1:T(8,128)(2,1)S(1)} collective-permute-done((bf16[128,1,512]{2,0,1:T(8,128)(2,1)}, bf16[128,1,512]{2,0,1:T(8,128)(2,1)S(1)}, u32[]{:S(2)}, u32[]{:S(2)}) %collective-permute-start) | collective-permute-done | bytes 131104 | tf_op jit(solution)/shard_map/ppermute | solution.py:69
  13.4 6.4 %collective-permute-done.1 = bf16[128,2,512]{2,0,1:T(8,128)(2,1)S(1)} collective-permute-done((bf16[128,2,512]{2,0,1:T(8,128)(2,1)S(1)}, bf16[128,2,512]{2,0,1:T(8,128)(2,1)S(1)}, u32[]{:S(2)}, u32[]{:S(2)}) %collective-permute-start.1) | collective-permute-done | bytes 262176 | tf_op jit(solution)/shard_map/ppermute | solution.py:69
  19.9 1.4 collective-permute-start.2
  21.3 6.2 %gather_fusion = bf16[4,128,4096]{2,1,0:T(8,128)(2,1)} fusion(bf16[8,128,4096]{2,1,0:T(8,128)(2,1)} %bitcast.248, s32[1024]{0:T(1024)S(1)} %pad_clamp_fusion.1), kind=kCustom, calls=%fused_computation | custom fusion | bytes 8388624 | tf_op jit(solution)/shard_map/jit(_take)/gather | solution.py:117
  27.5 5.8 %all-to-all-start = ((bf16[2,256,4096]{2,1,0:T(8,128)(2,1)}), bf16[2,256,4096]{2,1,0:T(8,128)(2,1)}, u32[]{:S(2)}, u32[]{:S(2)}) async-start(bf16[2,256,4096]{2,1,0:T(8,128)(2,1)} %bitcast.241), calls=%async_computation | async-start | bytes 8388608 | tf_op jit(solution)/shard_map/all_to_all | solution.py:125
  34.5 2.0 %fusion = f32[128,1,256]{2,1,0:T(1,128)S(1)} fusion(bf16[128,64,1]{1,2,0:T(2,128)(2,1)S(1)} %copy.89, s32[128,64]{1,0:T(8,128)S(1)} %copy.75), kind=kOutput, calls=%fused_computation.4 | convolution fusion | flops 6291456 | bytes 180224 | tf_op jit(solution)/shard_map/tk,tkr->tr/dot_general | solution.py:136
  36.7 1.5 pad_maximum_fusion
  38.2 3.0 %copy.73 = bf16[128,8,2,512]{0,3,2,1:T(8,128)(2,1)S(1)} copy(bf16[128,8,2,512]{3,0,1,2:T(8,128)(2,1)} %pad_maximum_fusion) | data formatting | bytes 4194304 | tf_op jit(solution)/shard_map/stack | solution.py:73
  41.3 38.0 %all-to-all-done = bf16[2,256,4096]{2,1,0:T(8,128)(2,1)} async-done(((bf16[2,256,4096]{2,1,0:T(8,128)(2,1)}), bf16[2,256,4096]{2,1,0:T(8,128)(2,1)}, u32[]{:S(2)}, u32[]{:S(2)}) %all-to-all-start) | async-done | bytes 4194336 | tf_op jit(solution)/shard_map/all_to_all | solution.py:125
  79.2 3.8 %select_reduce_fusion.1 = (f32[128]{0:T(128)S(1)}, f32[128,256]{1,0:T(8,128)S(1)}) fusion(pred[256]{0:T(512)(128)(4,1)S(1)} %broadcast_bitcast_fusion.2, bf16[128,2,4096]{0,2,1:T(8,128)(2,1)S(1)} %bitcast.239, bf16[2,256,4096]{2,1,0:T(8,128)(2,1)} %all-to-all-done), kind=kOutput, calls=%fused_computation.41 | convolution fusion | flops 536936320 | bytes 6423296 | tf_op jit(solution)/shard_map/tkd,krd->tr/dot_general | solution.py:126
  85.3 2.8 %collective-permute-done.5 = f32[3,128]{1,0:T(4,128)S(1)} collective-permute-done((f32[3,128]{1,0:T(4,128)S(1)}, f32[3,128]{1,0:T(4,128)S(1)}, u32[]{:S(2)}, u32[]{:S(2)}) %collective-permute-start.5) | collective-permute-done | bytes 1568 | tf_op jit(solution)/shard_map/ppermute | solution.py:30
  88.2 2.5 %collective-permute-start.6 = (f32[3,128]{1,0:T(4,128)S(1)}, f32[3,128]{1,0:T(4,128)S(1)}, u32[]{:S(2)}, u32[]{:S(2)}) collective-permute-start(f32[3,128]{1,0:T(4,128)S(1)} %pad_maximum_fusion.6), channel_id=1, source_target_pairs={{0,4},{1,5},{2,6},{3,7},{4,0},{5,1},{6,2},{7,3},{8,12},{9,13},{10,... | collective-permute-start | bytes 4616 | tf_op jit(solution)/shard_map/ppermute | solution.py:30
  90.8 1.5 collective-permute-done.6
  92.3 3.9 %collective-permute-start.7 = (f32[3,128]{1,0:T(4,128)S(1)}, f32[3,128]{1,0:T(4,128)S(1)}, u32[]{:S(2)}, u32[]{:S(2)}) collective-permute-start(f32[3,128]{1,0:T(4,128)S(1)} %pad_maximum_fusion.7), channel_id=1, source_target_pairs={{0,8},{1,9},{2,10},{3,11},{4,12},{5,13},{6,14},{7,15},{8,0},{9,1},... | collective-permute-start | bytes 4616 | tf_op jit(solution)/shard_map/ppermute | solution.py:30
  96.2 1.6 collective-permute-done.7
  98.4 4.0 %fusion.10 = f32[128,2,4096]{0,2,1:T(8,128)S(1)} fusion(bf16[2,256,4096]{2,1,0:T(8,128)(2,1)} %all-to-all-done, bf16[128,256]{1,0:T(8,128)(2,1)S(1)} %fusion.8), kind=kOutput, calls=%fused_computation.48 | convolution fusion | flops 536870912 | bytes 8454144 | tf_op jit(solution)/shard_map/tr,krd->tkd/dot_general | solution.py:146
  102.4 2.0 %copy-done = f32[128,2,4096]{0,2,1:T(8,128)} copy-done((f32[128,2,4096]{0,2,1:T(8,128)}, f32[128,2,4096]{0,2,1:T(8,128)S(1)}, u32[]{:S(2)}) %copy-start) | copy-done | bytes 4194328
  104.6 1.7 %copy.78 = bf16[128,8,1,512]{3,1,0,2:T(8,128)(2,1)} copy(bf16[128,8,1,512]{0,3,2,1:T(8,128)(2,1)S(1)} %dynamic-slice_convert_fusion) | data formatting | bytes 2097152 | tf_op jit(solution)/shard_map/convert_element_type | solution.py:54
  107.9 3.1 %constant_dynamic-slice_fusion.4 = f32[128,8,1,512]{0,3,2,1:T(8,128)} fusion(f32[128,8,2,512]{0,3,2,1:T(8,128)} %bitcast.243, s32[]{:T(128)S(6)} %select_n.242), kind=kLoop, calls=%fused_computation.72 | loop fusion | bytes 4194308 | tf_op jit(solution)/shard_map/jit(dynamic_index_in_dim)/dynamic_slice | solution.py:52
  111.0 2.2 %copy.77 = f32[128,8,1,512]{3,1,0,2:T(8,128)S(1)} copy(f32[128,8,1,512]{0,3,2,1:T(8,128)} %constant_dynamic-slice_fusion.4) | data formatting | bytes 4194304 | tf_op jit(solution)/shard_map/jit(dynamic_index_in_dim)/dynamic_slice | solution.py:52
  113.2 1.8 %collective-permute-start.12 = (bf16[1,128,256]{2,1,0:T(8,128)(2,1)S(1)}, bf16[1,128,256]{2,1,0:T(8,128)(2,1)S(1)}, u32[]{:S(2)}, u32[]{:S(2)}) collective-permute-start(bf16[1,128,256]{2,1,0:T(8,128)(2,1)S(1)} %bitcast.250), channel_id=1, source_target_pairs={{0,16},{16,0},{1,17},{17,1},{2,18},{18,2},{3,19},{19,3},{4,20},{20... | collective-permute-start | bytes 196616 | tf_op jit(solution)/shard_map/ppermute | solution.py:86
  115.1 2.9 %bitcast_add_fusion = f32[128,8,512]{2,1,0:T(8,128)} fusion(f32[128,8,1,512]{3,1,0,2:T(8,128)S(1)} %copy.77, bf16[128,8,512]{2,1,0:T(8,128)(2,1)} %collective-permute-done.8), kind=kLoop, calls=%fused_computation.9 | loop fusion | flops 1048576 | bytes 5242880 | tf_op jit(solution)/shard_map/add | solution.py:55
  117.9 2.5 %reshape.289 = f32[128,4,2,512]{3,2,1,0:T(2,128)S(1)} reshape(f32[128,8,512]{2,1,0:T(8,128)} %bitcast_add_fusion) | data formatting | bytes 4194304 | tf_op jit(solution)/shard_map/reshape | solution.py:50
  123.1 11.6 %collective-permute-done.12 = bf16[1,128,256]{2,1,0:T(8,128)(2,1)S(1)} collective-permute-done((bf16[1,128,256]{2,1,0:T(8,128)(2,1)S(1)}, bf16[1,128,256]{2,1,0:T(8,128)(2,1)S(1)}, u32[]{:S(2)}, u32[]{:S(2)}) %collective-permute-start.12) | collective-permute-done | bytes 65568 | tf_op jit(solution)/shard_map/ppermute | solution.py:86
  135.1 1.4 fusion.4
  137.6 1.4 bitcast_add_fusion.1
  140.7 1.5 collective-permute-start.10
  142.1 2.7 %pad_maximum_fusion.1 = bf16[128,2,4096]{0,2,1:T(8,128)(2,1)} fusion(bf16[128,1,4096]{0,2,1:T(8,128)(2,1)} %collective-permute-done.13, bf16[128,1,4096]{0,2,1:T(8,128)(2,1)S(1)} %get-tuple-element.19), kind=kLoop, calls=%fused_computation.7 | loop fusion | flops 1048576 | bytes 4194304 | tf_op jit(solution)/shard_map/concatenate | solution.py:101
  144.9 2.6 %gather_fusion.1 = bf16[2,128,4096]{1,2,0:T(8,128)(2,1)S(1)} fusion(bf16[128,2,4096]{0,2,1:T(8,128)(2,1)} %pad_maximum_fusion.1, s32[1024]{0:T(1024)S(1)} %pad_clamp_fusion), kind=kCustom, calls=%fused_computation.1 | custom fusion | bytes 4194312 | tf_op jit(solution)/shard_map/jit(_take)/gather | solution.py:102
  149.0 3.0 %collective-permute-start.11 = (bf16[128,1,512]{2,0,1:T(8,128)(2,1)S(1)}, bf16[128,1,512]{2,0,1:T(8,128)(2,1)S(1)}, u32[]{:S(2)}, u32[]{:S(2)}) collective-permute-start(bf16[128,1,512]{2,0,1:T(8,128)(2,1)S(1)} %dynamic-slice_convert_fusion.2), channel_id=1, source_target_pairs={{0,8},{1,9},{2,10},{3,11},{4,12},{5,13},{6,14},{7,15},{8,0},{9,1},... | collective-permute-start | bytes 393224 | tf_op jit(solution)/shard_map/ppermute | solution.py:54
  152.0 6.8 %bitcast_convert_fusion = bf16[1024,4096]{1,0:T(8,128)(2,1)} fusion(bf16[2,128,1024]{1,2,0:T(8,128)(2,1)} %fusion.4, bf16[2,128,4096]{1,2,0:T(8,128)(2,1)S(1)} %gather_fusion.1), kind=kOutput, calls=%fused_computation.2 | convolution fusion | flops 2151677952 | bytes 11010048 | tf_op jit(solution)/shard_map/str,tsd->rd/dot_general | solution.py:158
  (85 shorter events, 17.7 us)
Async XLA Ops:
  0.6 10.6 %collective-permute-start = (bf16[128,1,512]{2,0,1:T(8,128)(2,1)}, bf16[128,1,512]{2,0,1:T(8,128)(2,1)S(1)}, u32[]{:S(2)}, u32[]{:S(2)}) collective-permute-start(bf16[128,1,512]{2,0,1:T(8,128)(2,1)} %bitcast.251), channel_id=1, source_target_pairs={{0,8},{1,9},{2,10},{3,11},{4,12},{5,13},{6,14},{7,15},{8,0},{9,1},... | collective-permute-start | bytes 393224 | tf_op jit(solution)/shard_map/ppermute | solution.py:69
  12.2 7.5 %collective-permute-start.1 = (bf16[128,2,512]{2,0,1:T(8,128)(2,1)S(1)}, bf16[128,2,512]{2,0,1:T(8,128)(2,1)S(1)}, u32[]{:S(2)}, u32[]{:S(2)}) collective-permute-start(bf16[128,2,512]{2,0,1:T(8,128)(2,1)S(1)} %maximum_bitcast_fusion), channel_id=1, source_target_pairs={{0,4},{1,5},{2,6},{3,7},{4,0},{5,1},{6,2},{7,3},{8,12},{9,13},{10,... | collective-permute-start | bytes 786440 | tf_op jit(solution)/shard_map/ppermute | solution.py:69
  19.9 13.6 %collective-permute-start.2 = (bf16[128,4,512]{2,0,1:T(8,128)(2,1)S(1)}, bf16[128,4,512]{2,0,1:T(8,128)(2,1)S(1)}, u32[]{:S(2)}, u32[]{:S(2)}) collective-permute-start(bf16[128,4,512]{2,0,1:T(8,128)(2,1)S(1)} %bitcast.247), channel_id=1, source_target_pairs={{0,2},{1,3},{2,0},{3,1},{4,6},{5,7},{6,4},{7,5},{8,10},{9,11},{10,... | collective-permute-start | bytes 1572872 | tf_op jit(solution)/shard_map/ppermute | solution.py:69
  27.5 5.8 %copy-start.4 = (s32[128,64]{0,1:T(8,128)S(1)}, s32[128,64]{0,1:T(8,128)}, u32[]{:S(2)}) copy-start(s32[128,64]{0,1:T(8,128)} %param.7) | copy-start | bytes 98308
  27.5 6.0 %copy-start.3 = (f32[128,64]{0,1:T(8,128)S(1)}, f32[128,64]{0,1:T(8,128)}, u32[]{:S(2)}) copy-start(f32[128,64]{0,1:T(8,128)} %param.8) | copy-start | bytes 98308
  27.5 51.7 %all-to-all-start = ((bf16[2,256,4096]{2,1,0:T(8,128)(2,1)}), bf16[2,256,4096]{2,1,0:T(8,128)(2,1)}, u32[]{:S(2)}, u32[]{:S(2)}) async-start(bf16[2,256,4096]{2,1,0:T(8,128)(2,1)} %bitcast.241), calls=%async_computation | async-start | bytes 8388608 | tf_op jit(solution)/shard_map/all_to_all | solution.py:125
  33.8 2.7 %collective-permute-start.3 = (bf16[128,8,512]{2,0,1:T(8,128)(2,1)S(1)}, bf16[128,8,512]{2,0,1:T(8,128)(2,1)S(1)}, u32[]{:S(2)}, u32[]{:S(2)}) collective-permute-start(bf16[128,8,512]{2,0,1:T(8,128)(2,1)S(1)} %bitcast.244), channel_id=1, source_target_pairs={{0,1},{1,0},{2,3},{3,2},{4,5},{5,4},{6,7},{7,6},{8,9},{9,8},{10,11... | collective-permute-start | bytes 3145736 | tf_op jit(solution)/shard_map/ppermute | solution.py:69
  83.2 1.2 collective-permute-start.4
  84.5 3.7 %collective-permute-start.5 = (f32[3,128]{1,0:T(4,128)S(1)}, f32[3,128]{1,0:T(4,128)S(1)}, u32[]{:S(2)}, u32[]{:S(2)}) collective-permute-start(f32[3,128]{1,0:T(4,128)S(1)} %pad_maximum_fusion.5), channel_id=1, source_target_pairs={{0,2},{1,3},{2,0},{3,1},{4,6},{5,7},{6,4},{7,5},{8,10},{9,11},{10,... | collective-permute-start | bytes 4616 | tf_op jit(solution)/shard_map/ppermute | solution.py:30
  88.2 4.1 %collective-permute-start.6 = (f32[3,128]{1,0:T(4,128)S(1)}, f32[3,128]{1,0:T(4,128)S(1)}, u32[]{:S(2)}, u32[]{:S(2)}) collective-permute-start(f32[3,128]{1,0:T(4,128)S(1)} %pad_maximum_fusion.6), channel_id=1, source_target_pairs={{0,4},{1,5},{2,6},{3,7},{4,0},{5,1},{6,2},{7,3},{8,12},{9,13},{10,... | collective-permute-start | bytes 4616 | tf_op jit(solution)/shard_map/ppermute | solution.py:30
  92.3 5.5 %collective-permute-start.7 = (f32[3,128]{1,0:T(4,128)S(1)}, f32[3,128]{1,0:T(4,128)S(1)}, u32[]{:S(2)}, u32[]{:S(2)}) collective-permute-start(f32[3,128]{1,0:T(4,128)S(1)} %pad_maximum_fusion.7), channel_id=1, source_target_pairs={{0,8},{1,9},{2,10},{3,11},{4,12},{5,13},{6,14},{7,15},{8,0},{9,1},... | collective-permute-start | bytes 4616 | tf_op jit(solution)/shard_map/ppermute | solution.py:30
  102.4 2.0 %copy-start = (f32[128,2,4096]{0,2,1:T(8,128)}, f32[128,2,4096]{0,2,1:T(8,128)S(1)}, u32[]{:S(2)}) copy-start(f32[128,2,4096]{0,2,1:T(8,128)S(1)} %fusion.10) | copy-start | bytes 12582916
  106.2 8.8 %collective-permute-start.8 = (bf16[128,8,512]{2,1,0:T(8,128)(2,1)}, bf16[128,8,512]{2,1,0:T(8,128)(2,1)}, u32[]{:S(2)}, u32[]{:S(2)}) collective-permute-start(bf16[128,8,512]{2,1,0:T(8,128)(2,1)} %bitcast.249), channel_id=1, source_target_pairs={{0,1},{1,0},{2,3},{3,2},{4,5},{5,4},{6,7},{7,6},{8,9},{9,8},{10,11... | collective-permute-start | bytes 3145736 | tf_op jit(solution)/shard_map/ppermute | solution.py:54
  107.6 34.6 %collective-permute-start.13 = (bf16[128,1,4096]{0,2,1:T(8,128)(2,1)}, bf16[128,1,4096]{0,2,1:T(8,128)(2,1)}, u32[]{:S(2)}, u32[]{:S(2)}) collective-permute-start(bf16[128,1,4096]{0,2,1:T(8,128)(2,1)} %get-tuple-element.20), channel_id=1, source_target_pairs={{0,16},{16,0},{1,17},{17,1},{2,18},{18,2},{3,19},{19,3},{4,20},{20... | collective-permute-start | bytes 3145736 | tf_op jit(solution)/shard_map/ppermute | solution.py:100
  113.2 21.5 %collective-permute-start.12 = (bf16[1,128,256]{2,1,0:T(8,128)(2,1)S(1)}, bf16[1,128,256]{2,1,0:T(8,128)(2,1)S(1)}, u32[]{:S(2)}, u32[]{:S(2)}) collective-permute-start(bf16[1,128,256]{2,1,0:T(8,128)(2,1)S(1)} %bitcast.250), channel_id=1, source_target_pairs={{0,16},{16,0},{1,17},{17,1},{2,18},{18,2},{3,19},{19,3},{4,20},{20... | collective-permute-start | bytes 196616 | tf_op jit(solution)/shard_map/ppermute | solution.py:86
  122.6 15.0 %collective-permute-start.9 = (bf16[128,4,512]{2,0,1:T(8,128)(2,1)}, bf16[128,4,512]{2,0,1:T(8,128)(2,1)}, u32[]{:S(2)}, u32[]{:S(2)}) collective-permute-start(bf16[128,4,512]{2,0,1:T(8,128)(2,1)} %bitcast.236), channel_id=1, source_target_pairs={{0,2},{1,3},{2,0},{3,1},{4,6},{5,7},{6,4},{7,5},{8,10},{9,11},{10,... | collective-permute-start | bytes 1572872 | tf_op jit(solution)/shard_map/ppermute | solution.py:54
  139.0 1.0 copy-start.1
  140.7 8.2 %collective-permute-start.10 = (bf16[128,2,512]{2,0,1:T(8,128)(2,1)}, bf16[128,2,512]{2,0,1:T(8,128)(2,1)S(1)}, u32[]{:S(2)}, u32[]{:S(2)}) collective-permute-start(bf16[128,2,512]{2,0,1:T(8,128)(2,1)} %fusion.5), channel_id=1, source_target_pairs={{0,4},{1,5},{2,6},{3,7},{4,0},{5,1},{6,2},{7,3},{8,12},{9,13},{10,... | collective-permute-start | bytes 786440 | tf_op jit(solution)/shard_map/ppermute | solution.py:54
  144.9 4.0 %copy-start.2 = (f32[128,4,512]{2,0,1:T(8,128)S(1)}, f32[128,4,512]{2,0,1:T(8,128)}, u32[]{:S(2)}) copy-start(f32[128,4,512]{2,0,1:T(8,128)} %copy-done.1) | copy-start | bytes 3145732
  149.0 9.8 %collective-permute-start.11 = (bf16[128,1,512]{2,0,1:T(8,128)(2,1)S(1)}, bf16[128,1,512]{2,0,1:T(8,128)(2,1)S(1)}, u32[]{:S(2)}, u32[]{:S(2)}) collective-permute-start(bf16[128,1,512]{2,0,1:T(8,128)(2,1)S(1)} %dynamic-slice_convert_fusion.2), channel_id=1, source_target_pairs={{0,8},{1,9},{2,10},{3,11},{4,12},{5,13},{6,14},{7,15},{8,0},{9,1},... | collective-permute-start | bytes 393224 | tf_op jit(solution)/shard_map/ppermute | solution.py:54

commit v9 on v8

--- a/solution.py
+++ b/solution.py
@@ -90,16 +90,16 @@
     return held
 
 
-def shift_exchange(wide):
+def shift_exchange(wide, axis):
     n = lax.axis_size("dp")
     me = lax.axis_index("dp")
-    own = lax.dynamic_index_in_dim(wide, me, 1, keepdims=True)
+    own = lax.dynamic_index_in_dim(wide, me, axis, keepdims=True)
     pieces = [own]
     for shift in range(1, n):
-        send = lax.dynamic_index_in_dim(wide, (me + shift) % n, 1, keepdims=True)
+        send = lax.dynamic_index_in_dim(wide, (me + shift) % n, axis, keepdims=True)
         pieces.append(lax.ppermute(send, "dp", [(k, (k + shift) % n) for k in range(n)]))
-    held = jnp.concatenate(pieces, axis=1)
-    return jnp.take(held, (me - jnp.arange(n)) % n, axis=1, mode="clip")
+    held = jnp.concatenate(pieces, axis=axis)
+    return jnp.take(held, (me - jnp.arange(n)) % n, axis=axis, mode="clip")
 
 
 def shards(hidden, weight, teacher_ids, teacher_logp, union_blocks):
@@ -119,10 +119,10 @@
     )
     full_rows = doubling_rows(hidden)
     wide = full_rows.reshape(tokens_here, n_groups, piece)
-    halves = shift_exchange(wide)
+    halves = shift_exchange(wide, 1)
     own_slots = lax.dynamic_index_in_dim(table, dp_row, 0, keepdims=False)
     col_mask = jnp.repeat(own_slots >= 0, BLOCK)
-    rows_w = lax.all_to_all(chosen, "dp", split_axis=0, concat_axis=0, tiled=True)
+    rows_w = shift_exchange(chosen, 0)
     logits = jnp.einsum("tkd,krd->tr", wide, rows_w, preferred_element_type=jnp.float32)
     offsets = teacher_ids % BLOCK
     match = (teacher_ids // BLOCK)[:, :, None] == own_slots[None, None, :]

time: 160 us -> 162 us (1.012)
  local copies, waits for them, and re-layouts: 30.7 us -> 48.9 us
  waiting for transfers between devices: 69.3 us -> 58.3 us
  starting transfers between devices: 26.6 us -> 18 us
  other arithmetic: 15.2 us -> 18.1 us
    all_to_all x1 -> x0, waiting for transfers between devices: 38 us -> none  [shards(): lax.all_to_all(chosen, 'dp', split_axis=0, concat_axis=0, tiled=True)]
    ppermute x1 -> x2, waiting for transfers between devices: 0.01 us -> 24.8 us  [shift_exchange(): lax.ppermute(send, 'dp', [(k, (k + shift) % n) for k in range(n)])]
    gather x1 -> x3, local copies, waits for them, and re-layouts: 2.63 us -> 9.77 us  [shift_exchange(): return jnp.take(held, (me - jnp.arange(n)) % n, axis=axis, mode='clip')]
    unnamed x15 -> x19, local copies, waits for them, and re-layouts: 4.23 us -> 10.6 us
    all_to_all x1 -> x0, starting transfers between devices: 5.75 us -> none  [shards(): lax.all_to_all(chosen, 'dp', split_axis=0, concat_axis=0, tiled=True)]
    dynamic_slice x1 -> x2, local copies, waits for them, and re-layouts: 1.15 us -> 5.79 us  [the longest x1 4.66 us: shift_exchange(): send = lax.dynamic_index_in_dim(wide, (me + shift) % n, axis, keepdims=True)]
    concatenate x1 -> x2, other arithmetic: 2.74 us -> 6.51 us  [shift_exchange(): held = jnp.concatenate(pieces, axis=axis)]
    ppermute x4, starting transfers between devices: 7.26 us -> 3.6 us  [combine_stats(): lax.ppermute(jnp.stack([top, total, picked]), 'vocab', [(k, k ^ bit) for...]
  transfers between devices with their start and end apart: 15 -> 15, of which waited for: 9 -> 9; matrix products, arithmetic and copies ran while one was open for 30% -> 32% of each run, Pallas kernels for 0% -> 0%
where the time goes in v9:
time: 162 us; the launch traced here: 161 us
  waiting for transfers between devices  58.3 us (36%)
  local copies, waits for them, and re-layouts  48.9 us (30%)
  other arithmetic  18.1 us (11%)
  starting transfers between devices  18 us (11%)
  matrix products  16.5 us (10%)
    ppermute x2, waiting for transfers between devices, shift_exchange(): lax.ppermute(send, 'dp', [(k, (k + shift) % n) for k in range(n)])  24.8 us
    ppermute x4, waiting for transfers between devices, doubling_rows(): got = lax.ppermute(held, 'vocab', [(k, k ^ bit) for k in range(n)])  11.4 us
    ppermute x1, waiting for transfers between devices, doubling_gather(): got = lax.ppermute(held, 'dp', [(k, k ^ bit) for k in range(n)])  10.7 us
    unnamed x19, local copies, waits for them, and re-layouts  10.6 us
    gather x3, local copies, waits for them, and re-layouts, shift_exchange(): return jnp.take(held, (me - jnp.arange(n)) % n, axis=axis, mode='clip')  9.77 us
    ppermute x4, waiting for transfers between devices, combine_stats(): lax.ppermute(jnp.stack([top, total, picked]), 'vocab', [(k, k ^ bit) for...  9.13 us
    ppermute x4, starting transfers between devices, doubling_rows(): got = lax.ppermute(held, 'vocab', [(k, k ^ bit) for k in range(n)])  7.4 us
    dot_general x1, matrix products, shards(): jnp.einsum('str,tsd->rd', placed, halves, preferred_element_type=jnp.floa...  6.82 us
  transfers between devices with their start and end apart: 15, of which 9 were waited for; matrix products, arithmetic and copies ran while one was open for 32% of the time, Pallas kernels for 0%

profile of v9, /device:TPU:0, one launch (start us, length us, event | category | flops | bytes accessed | tf_op | source)
XLA Modules:
  0.0 161.0 jit_solution(9224045362716158677)
XLA Ops:
  0.6 4.1 %collective-permute-start = (bf16[128,1,512]{2,0,1:T(8,128)(2,1)}, bf16[128,1,512]{2,0,1:T(8,128)(2,1)S(1)}, u32[]{:S(2)}, u32[]{:S(2)}) collective-permute-start(bf16[128,1,512]{2,0,1:T(8,128)(2,1)} %bitcast.251), channel_id=1, source_target_pairs={{0,8},{1,9},{2,10},{3,11},{4,12},{5,13},{6,14},{7,15},{8,0},{9,1},... | collective-permute-start | bytes 393224 | tf_op jit(solution)/shard_map/ppermute | solution.py:69
  6.6 6.2 %gather_fusion = bf16[4,128,4096]{2,1,0:T(8,128)(2,1)} fusion(bf16[8,128,4096]{2,1,0:T(8,128)(2,1)} %bitcast.248, s32[1024]{0:T(1024)S(1)} %pad_clamp_fusion.1), kind=kCustom, calls=%fused_computation | custom fusion | bytes 8388624 | tf_op jit(solution)/shard_map/jit(_take)/gather | solution.py:117
  12.9 1.6 %collective-permute-start.1 = (bf16[128,2,512]{2,0,1:T(8,128)(2,1)S(1)}, bf16[128,2,512]{2,0,1:T(8,128)(2,1)S(1)}, u32[]{:S(2)}, u32[]{:S(2)}) collective-permute-start(bf16[128,2,512]{2,0,1:T(8,128)(2,1)S(1)} %maximum_bitcast_fusion), channel_id=1, source_target_pairs={{0,4},{1,5},{2,6},{3,7},{4,0},{5,1},{6,2},{7,3},{8,12},{9,13},{10,... | collective-permute-start | bytes 786440 | tf_op jit(solution)/shard_map/ppermute | solution.py:69
  14.6 4.7 %constant_dynamic-slice_fusion.5 = (bf16[1,256,4096]{2,1,0:T(8,128)(2,1)}, bf16[1,256,4096]{2,1,0:T(8,128)(2,1)}) fusion(bf16[2,256,4096]{2,1,0:T(8,128)(2,1)} %bitcast.241, s32[]{:T(128)S(6)} %select_n.244, s32[]{:T(128)S(6)} %select_n.222), kind=kLoop, calls=%fused_computation.81 | loop fusion | bytes 8388616 | tf_op jit(solution)/shard_map/jit(dynamic_index_in_dim)/dynamic_slice | solution.py:99
  19.2 1.5 collective-permute-start.4
  20.9 1.6 collective-permute-start.2
  22.7 11.1 %collective-permute-done.2 = bf16[128,4,512]{2,0,1:T(8,128)(2,1)S(1)} collective-permute-done((bf16[128,4,512]{2,0,1:T(8,128)(2,1)S(1)}, bf16[128,4,512]{2,0,1:T(8,128)(2,1)S(1)}, u32[]{:S(2)}, u32[]{:S(2)}) %collective-permute-start.2) | collective-permute-done | bytes 524320 | tf_op jit(solution)/shard_map/ppermute | solution.py:69
  34.6 2.0 %fusion = f32[128,1,256]{2,1,0:T(1,128)S(1)} fusion(bf16[128,64,1]{1,2,0:T(2,128)(2,1)S(1)} %copy.89, s32[128,64]{1,0:T(8,128)S(1)} %copy.75), kind=kOutput, calls=%fused_computation.6 | convolution fusion | flops 6291456 | bytes 180224 | tf_op jit(solution)/shard_map/tk,tkr->tr/dot_general | solution.py:136
  38.5 3.0 %copy.73 = bf16[128,8,2,512]{0,3,2,1:T(8,128)(2,1)S(1)} copy(bf16[128,8,2,512]{3,0,1,2:T(8,128)(2,1)} %pad_maximum_fusion.1) | data formatting | bytes 4194304 | tf_op jit(solution)/shard_map/stack | solution.py:73
  41.6 24.8 %collective-permute-done.4 = bf16[1,256,4096]{2,1,0:T(8,128)(2,1)} collective-permute-done((bf16[1,256,4096]{2,1,0:T(8,128)(2,1)}, bf16[1,256,4096]{2,1,0:T(8,128)(2,1)}, u32[]{:S(2)}, u32[]{:S(2)}) %collective-permute-start.4) | collective-permute-done | bytes 2097184 | tf_op jit(solution)/shard_map/ppermute | solution.py:100
  66.4 3.8 %pad_maximum_fusion = (bf16[2,256,2048]{2,1,0:T(8,128)(2,1)}, bf16[2,256,2048]{2,1,0:T(8,128)(2,1)}) fusion(bf16[1,256,4096]{2,1,0:T(8,128)(2,1)} %collective-permute-done.4, bf16[1,256,4096]{2,1,0:T(8,128)(2,1)} %get-tuple-element.22), kind=kLoop, calls=%fused_computation.11 | loop fusion | flops 8388608 | bytes 8388608 | tf_op jit(solution)/shard_map/concatenate | solution.py:101
  70.1 3.6 %gather_fusion.2 = bf16[2,256,2048]{2,1,0:T(8,128)(2,1)} fusion(bf16[2,256,2048]{2,1,0:T(8,128)(2,1)} %get-tuple-element.20, s32[1024]{0:T(1024)S(1)} %pad_clamp_fusion), kind=kCustom, calls=%fused_computation.2 | custom fusion | bytes 4194312 | tf_op jit(solution)/shard_map/jit(_take)/gather | solution.py:102
  73.7 3.2 %constant_dynamic-update-slice_fusion.1 = bf16[2,256,4096]{2,1,0:T(8,128)(2,1)} fusion(bf16[2,256,2048]{2,1,0:T(8,128)(2,1)} %gather_fusion.2), kind=kLoop, calls=%fused_computation.72 | loop fusion | bytes 4194304
  76.9 3.6 %gather_fusion.3 = bf16[2,256,2048]{2,1,0:T(8,128)(2,1)} fusion(bf16[2,256,2048]{2,1,0:T(8,128)(2,1)} %get-tuple-element.19, s32[1024]{0:T(1024)S(1)} %pad_clamp_fusion), kind=kCustom, calls=%fused_computation.3 | custom fusion | bytes 4194312 | tf_op jit(solution)/shard_map/jit(_take)/gather | solution.py:102
  80.5 3.2 %constant_dynamic-update-slice_fusion = bf16[2,256,4096]{2,1,0:T(8,128)(2,1)} fusion(bf16[2,256,4096]{2,1,0:T(8,128)(2,1)} %constant_dynamic-update-slice_fusion.1, bf16[2,256,2048]{2,1,0:T(8,128)(2,1)} %gather_fusion.3), kind=kLoop, calls=%fused_computation.71 | loop fusion | bytes 4194304
  83.6 3.8 %select_reduce_fusion.1 = (f32[128]{0:T(128)S(1)}, f32[128,256]{1,0:T(8,128)S(1)}) fusion(pred[256]{0:T(512)(128)(4,1)S(1)} %broadcast_bitcast_fusion.2, bf16[128,2,4096]{0,2,1:T(8,128)(2,1)S(1)} %bitcast.239, bf16[2,256,4096]{2,1,0:T(8,128)(2,1)} %constant_dynamic-update-slice_fusion), kind=kOutput, calls=%fused_computation.47 | convolution fusion | flops 536936320 | bytes 6423296 | tf_op jit(solution)/shard_map/tkd,krd->tr/dot_general | solution.py:126
  88.9 1.6 collective-permute-start.6
  90.6 1.9 %collective-permute-done.6 = f32[3,128]{1,0:T(4,128)S(1)} collective-permute-done((f32[3,128]{1,0:T(4,128)S(1)}, f32[3,128]{1,0:T(4,128)S(1)}, u32[]{:S(2)}, u32[]{:S(2)}) %collective-permute-start.6) | collective-permute-done | bytes 1568 | tf_op jit(solution)/shard_map/ppermute | solution.py:30
  93.1 3.1 %collective-permute-done.7 = f32[3,128]{1,0:T(4,128)S(1)} collective-permute-done((f32[3,128]{1,0:T(4,128)S(1)}, f32[3,128]{1,0:T(4,128)S(1)}, u32[]{:S(2)}, u32[]{:S(2)}) %collective-permute-start.7) | collective-permute-done | bytes 1568 | tf_op jit(solution)/shard_map/ppermute | solution.py:30
  97.8 3.0 %collective-permute-done.8 = f32[3,128]{1,0:T(4,128)S(1)} collective-permute-done((f32[3,128]{1,0:T(4,128)S(1)}, f32[3,128]{1,0:T(4,128)S(1)}, u32[]{:S(2)}, u32[]{:S(2)}) %collective-permute-start.8) | collective-permute-done | bytes 1568 | tf_op jit(solution)/shard_map/ppermute | solution.py:30
  101.4 4.0 %fusion.11 = f32[128,2,4096]{0,2,1:T(8,128)S(1)} fusion(bf16[2,256,4096]{2,1,0:T(8,128)(2,1)} %constant_dynamic-update-slice_fusion, bf16[128,256]{1,0:T(8,128)(2,1)S(1)} %fusion.9), kind=kOutput, calls=%fused_computation.54 | convolution fusion | flops 536870912 | bytes 8454144 | tf_op jit(solution)/shard_map/tr,krd->tkd/dot_general | solution.py:146
  105.4 2.0 %copy-done = f32[128,2,4096]{0,2,1:T(8,128)} copy-done((f32[128,2,4096]{0,2,1:T(8,128)}, f32[128,2,4096]{0,2,1:T(8,128)S(1)}, u32[]{:S(2)}) %copy-start) | copy-done | bytes 4194328
  107.6 1.7 %copy.78 = bf16[128,8,1,512]{3,1,0,2:T(8,128)(2,1)} copy(bf16[128,8,1,512]{0,3,2,1:T(8,128)(2,1)S(1)} %dynamic-slice_convert_fusion) | data formatting | bytes 2097152 | tf_op jit(solution)/shard_map/convert_element_type | solution.py:54
  112.1 3.1 %constant_dynamic-slice_fusion.4 = f32[128,8,1,512]{0,3,2,1:T(8,128)} fusion(f32[128,8,2,512]{0,3,2,1:T(8,128)} %bitcast.243, s32[]{:T(128)S(6)} %select_n.252), kind=kLoop, calls=%fused_computation.80 | loop fusion | bytes 4194308 | tf_op jit(solution)/shard_map/jit(dynamic_index_in_dim)/dynamic_slice | solution.py:52
  115.2 2.2 %copy.77 = f32[128,8,1,512]{3,1,0,2:T(8,128)S(1)} copy(f32[128,8,1,512]{0,3,2,1:T(8,128)} %constant_dynamic-slice_fusion.4) | data formatting | bytes 4194304 | tf_op jit(solution)/shard_map/jit(dynamic_index_in_dim)/dynamic_slice | solution.py:52
  118.1 2.9 %bitcast_add_fusion = f32[128,8,512]{2,1,0:T(8,128)} fusion(f32[128,8,1,512]{3,1,0,2:T(8,128)S(1)} %copy.77, bf16[128,8,512]{2,1,0:T(8,128)(2,1)} %collective-permute-done.9), kind=kLoop, calls=%fused_computation.15 | loop fusion | flops 1048576 | bytes 5242880 | tf_op jit(solution)/shard_map/add | solution.py:55
  121.0 2.5 %reshape.289 = f32[128,4,2,512]{3,2,1,0:T(2,128)S(1)} reshape(f32[128,8,512]{2,1,0:T(8,128)} %bitcast_add_fusion) | data formatting | bytes 4194304 | tf_op jit(solution)/shard_map/reshape | solution.py:50
  127.1 10.7 %collective-permute-done.13 = bf16[1,128,256]{2,1,0:T(8,128)(2,1)S(1)} collective-permute-done((bf16[1,128,256]{2,1,0:T(8,128)(2,1)S(1)}, bf16[1,128,256]{2,1,0:T(8,128)(2,1)S(1)}, u32[]{:S(2)}, u32[]{:S(2)}) %collective-permute-start.13) | collective-permute-done | bytes 65568 | tf_op jit(solution)/shard_map/ppermute | solution.py:86
  144.2 2.7 %pad_maximum_fusion.2 = bf16[128,2,4096]{0,2,1:T(8,128)(2,1)} fusion(bf16[128,1,4096]{0,2,1:T(8,128)(2,1)} %collective-permute-done.14, bf16[128,1,4096]{0,2,1:T(8,128)(2,1)S(1)} %get-tuple-element.23), kind=kLoop, calls=%fused_computation.13 | loop fusion | flops 1048576 | bytes 4194304 | tf_op jit(solution)/shard_map/concatenate | solution.py:101
  146.9 2.6 %gather_fusion.1 = bf16[2,128,4096]{1,2,0:T(8,128)(2,1)S(1)} fusion(bf16[128,2,4096]{0,2,1:T(8,128)(2,1)} %pad_maximum_fusion.2, s32[1024]{0:T(1024)S(1)} %pad_clamp_fusion), kind=kCustom, calls=%fused_computation.1 | custom fusion | bytes 4194312 | tf_op jit(solution)/shard_map/jit(_take)/gather | solution.py:102
  149.5 2.3 %collective-permute-done.11 = bf16[128,2,512]{2,0,1:T(8,128)(2,1)S(1)} collective-permute-done((bf16[128,2,512]{2,0,1:T(8,128)(2,1)}, bf16[128,2,512]{2,0,1:T(8,128)(2,1)S(1)}, u32[]{:S(2)}, u32[]{:S(2)}) %collective-permute-start.11) | collective-permute-done | bytes 262176 | tf_op jit(solution)/shard_map/ppermute | solution.py:54
  153.5 6.8 %bitcast_convert_fusion = bf16[1024,4096]{1,0:T(8,128)(2,1)} fusion(bf16[2,128,1024]{1,2,0:T(8,128)(2,1)} %fusion.5, bf16[2,128,4096]{1,2,0:T(8,128)(2,1)S(1)} %gather_fusion.1), kind=kOutput, calls=%fused_computation.4 | convolution fusion | flops 2151677952 | bytes 11010048 | tf_op jit(solution)/shard_map/str,tsd->rd/dot_general | solution.py:158
  (93 shorter events, 25.0 us)
Async XLA Ops:
  0.6 12.2 %collective-permute-start = (bf16[128,1,512]{2,0,1:T(8,128)(2,1)}, bf16[128,1,512]{2,0,1:T(8,128)(2,1)S(1)}, u32[]{:S(2)}, u32[]{:S(2)}) collective-permute-start(bf16[128,1,512]{2,0,1:T(8,128)(2,1)} %bitcast.251), channel_id=1, source_target_pairs={{0,8},{1,9},{2,10},{3,11},{4,12},{5,13},{6,14},{7,15},{8,0},{9,1},... | collective-permute-start | bytes 393224 | tf_op jit(solution)/shard_map/ppermute | solution.py:69
  6.6 6.3 %copy-start.4 = (bf16[128,512]{1,0:T(8,128)(2,1)S(1)}, bf16[128,512]{1,0:T(8,128)(2,1)}, u32[]{:S(2)}) copy-start(bf16[128,512]{1,0:T(8,128)(2,1)} %param.5) | copy-start | bytes 393220
  12.9 7.9 %collective-permute-start.1 = (bf16[128,2,512]{2,0,1:T(8,128)(2,1)S(1)}, bf16[128,2,512]{2,0,1:T(8,128)(2,1)S(1)}, u32[]{:S(2)}, u32[]{:S(2)}) collective-permute-start(bf16[128,2,512]{2,0,1:T(8,128)(2,1)S(1)} %maximum_bitcast_fusion), channel_id=1, source_target_pairs={{0,4},{1,5},{2,6},{3,7},{4,0},{5,1},{6,2},{7,3},{8,12},{9,13},{10,... | collective-permute-start | bytes 786440 | tf_op jit(solution)/shard_map/ppermute | solution.py:69
  14.6 6.2 %copy-start.3 = (f32[128,64]{0,1:T(8,128)S(1)}, f32[128,64]{0,1:T(8,128)}, u32[]{:S(2)}) copy-start(f32[128,64]{0,1:T(8,128)} %param.8) | copy-start | bytes 98308
  19.2 3.2 %copy-start.5 = (s32[128,64]{0,1:T(8,128)S(1)}, s32[128,64]{0,1:T(8,128)}, u32[]{:S(2)}) copy-start(s32[128,64]{0,1:T(8,128)} %param.7) | copy-start | bytes 98308
  19.2 47.1 %collective-permute-start.4 = (bf16[1,256,4096]{2,1,0:T(8,128)(2,1)}, bf16[1,256,4096]{2,1,0:T(8,128)(2,1)}, u32[]{:S(2)}, u32[]{:S(2)}) collective-permute-start(bf16[1,256,4096]{2,1,0:T(8,128)(2,1)} %get-tuple-element.21), channel_id=1, source_target_pairs={{0,16},{16,0},{1,17},{17,1},{2,18},{18,2},{3,19},{19,3},{4,20},{20... | collective-permute-start | bytes 6291464 | tf_op jit(solution)/shard_map/ppermute | solution.py:100
  20.9 12.9 %collective-permute-start.2 = (bf16[128,4,512]{2,0,1:T(8,128)(2,1)S(1)}, bf16[128,4,512]{2,0,1:T(8,128)(2,1)S(1)}, u32[]{:S(2)}, u32[]{:S(2)}) collective-permute-start(bf16[128,4,512]{2,0,1:T(8,128)(2,1)S(1)} %bitcast.247), channel_id=1, source_target_pairs={{0,2},{1,3},{2,0},{3,1},{4,6},{5,7},{6,4},{7,5},{8,10},{9,11},{10,... | collective-permute-start | bytes 1572872 | tf_op jit(solution)/shard_map/ppermute | solution.py:69
  34.1 2.7 %collective-permute-start.3 = (bf16[128,8,512]{2,0,1:T(8,128)(2,1)S(1)}, bf16[128,8,512]{2,0,1:T(8,128)(2,1)S(1)}, u32[]{:S(2)}, u32[]{:S(2)}) collective-permute-start(bf16[128,8,512]{2,0,1:T(8,128)(2,1)S(1)} %bitcast.244), channel_id=1, source_target_pairs={{0,1},{1,0},{2,3},{3,2},{4,5},{5,4},{6,7},{7,6},{8,9},{9,8},{10,11... | collective-permute-start | bytes 3145736 | tf_op jit(solution)/shard_map/ppermute | solution.py:69
  87.6 1.2 collective-permute-start.5
  88.9 3.7 %collective-permute-start.6 = (f32[3,128]{1,0:T(4,128)S(1)}, f32[3,128]{1,0:T(4,128)S(1)}, u32[]{:S(2)}, u32[]{:S(2)}) collective-permute-start(f32[3,128]{1,0:T(4,128)S(1)} %pad_maximum_fusion.6), channel_id=1, source_target_pairs={{0,2},{1,3},{2,0},{3,1},{4,6},{5,7},{6,4},{7,5},{8,10},{9,11},{10,... | collective-permute-start | bytes 4616 | tf_op jit(solution)/shard_map/ppermute | solution.py:30
  92.5 3.7 %collective-permute-start.7 = (f32[3,128]{1,0:T(4,128)S(1)}, f32[3,128]{1,0:T(4,128)S(1)}, u32[]{:S(2)}, u32[]{:S(2)}) collective-permute-start(f32[3,128]{1,0:T(4,128)S(1)} %pad_maximum_fusion.7), channel_id=1, source_target_pairs={{0,4},{1,5},{2,6},{3,7},{4,0},{5,1},{6,2},{7,3},{8,12},{9,13},{10,... | collective-permute-start | bytes 4616 | tf_op jit(solution)/shard_map/ppermute | solution.py:30
  96.2 4.5 %collective-permute-start.8 = (f32[3,128]{1,0:T(4,128)S(1)}, f32[3,128]{1,0:T(4,128)S(1)}, u32[]{:S(2)}, u32[]{:S(2)}) collective-permute-start(f32[3,128]{1,0:T(4,128)S(1)} %pad_maximum_fusion.8), channel_id=1, source_target_pairs={{0,8},{1,9},{2,10},{3,11},{4,12},{5,13},{6,14},{7,15},{8,0},{9,1},... | collective-permute-start | bytes 4616 | tf_op jit(solution)/shard_map/ppermute | solution.py:30
  105.4 2.0 %copy-start = (f32[128,2,4096]{0,2,1:T(8,128)}, f32[128,2,4096]{0,2,1:T(8,128)S(1)}, u32[]{:S(2)}) copy-start(f32[128,2,4096]{0,2,1:T(8,128)S(1)} %fusion.11) | copy-start | bytes 12582916
  109.3 8.8 %collective-permute-start.9 = (bf16[128,8,512]{2,1,0:T(8,128)(2,1)}, bf16[128,8,512]{2,1,0:T(8,128)(2,1)}, u32[]{:S(2)}, u32[]{:S(2)}) collective-permute-start(bf16[128,8,512]{2,1,0:T(8,128)(2,1)} %bitcast.249), channel_id=1, source_target_pairs={{0,1},{1,0},{2,3},{3,2},{4,5},{5,4},{6,7},{7,6},{8,9},{9,8},{10,11... | collective-permute-start | bytes 3145736 | tf_op jit(solution)/shard_map/ppermute | solution.py:54
  110.6 33.6 %collective-permute-start.14 = (bf16[128,1,4096]{0,2,1:T(8,128)(2,1)}, bf16[128,1,4096]{0,2,1:T(8,128)(2,1)}, u32[]{:S(2)}, u32[]{:S(2)}) collective-permute-start(bf16[128,1,4096]{0,2,1:T(8,128)(2,1)} %get-tuple-element.24), channel_id=1, source_target_pairs={{0,16},{16,0},{1,17},{17,1},{2,18},{18,2},{3,19},{19,3},{4,20},{20... | collective-permute-start | bytes 3145736 | tf_op jit(solution)/shard_map/ppermute | solution.py:100
  117.5 20.3 %collective-permute-start.13 = (bf16[1,128,256]{2,1,0:T(8,128)(2,1)S(1)}, bf16[1,128,256]{2,1,0:T(8,128)(2,1)S(1)}, u32[]{:S(2)}, u32[]{:S(2)}) collective-permute-start(bf16[1,128,256]{2,1,0:T(8,128)(2,1)S(1)} %bitcast.250), channel_id=1, source_target_pairs={{0,16},{16,0},{1,17},{17,1},{2,18},{18,2},{3,19},{19,3},{4,20},{20... | collective-permute-start | bytes 196616 | tf_op jit(solution)/shard_map/ppermute | solution.py:86
  125.6 15.0 %collective-permute-start.10 = (bf16[128,4,512]{2,0,1:T(8,128)(2,1)}, bf16[128,4,512]{2,0,1:T(8,128)(2,1)}, u32[]{:S(2)}, u32[]{:S(2)}) collective-permute-start(bf16[128,4,512]{2,0,1:T(8,128)(2,1)} %bitcast.236), channel_id=1, source_target_pairs={{0,2},{1,3},{2,0},{3,1},{4,6},{5,7},{6,4},{7,5},{8,10},{9,11},{10,... | collective-permute-start | bytes 1572872 | tf_op jit(solution)/shard_map/ppermute | solution.py:54
  142.0 1.0 copy-start.1
  143.7 8.2 %collective-permute-start.11 = (bf16[128,2,512]{2,0,1:T(8,128)(2,1)}, bf16[128,2,512]{2,0,1:T(8,128)(2,1)S(1)}, u32[]{:S(2)}, u32[]{:S(2)}) collective-permute-start(bf16[128,2,512]{2,0,1:T(8,128)(2,1)} %fusion.6), channel_id=1, source_target_pairs={{0,4},{1,5},{2,6},{3,7},{4,0},{5,1},{6,2},{7,3},{8,12},{9,13},{10,... | collective-permute-start | bytes 786440 | tf_op jit(solution)/shard_map/ppermute | solution.py:54
  146.9 5.0 %copy-start.2 = (f32[128,4,512]{2,0,1:T(8,128)S(1)}, f32[128,4,512]{2,0,1:T(8,128)}, u32[]{:S(2)}) copy-start(f32[128,4,512]{2,0,1:T(8,128)} %copy-done.1) | copy-start | bytes 3145732
  152.0 8.3 %collective-permute-start.12 = (bf16[128,1,512]{2,0,1:T(8,128)(2,1)S(1)}, bf16[128,1,512]{2,0,1:T(8,128)(2,1)S(1)}, u32[]{:S(2)}, u32[]{:S(2)}) collective-permute-start(bf16[128,1,512]{2,0,1:T(8,128)(2,1)S(1)} %dynamic-slice_convert_fusion.2), channel_id=1, source_target_pairs={{0,8},{1,9},{2,10},{3,11},{4,12},{5,13},{6,14},{7,15},{8,0},{9,1},... | collective-permute-start | bytes 393224 | tf_op jit(solution)/shard_map/ppermute | solution.py:54

commit v10 on v9

--- a/solution.py
+++ b/solution.py
@@ -38,11 +38,11 @@
     return top, total, picked
 
 
-def halving_scatter(terms):
+def halving_scatter(terms, flip=0):
     n = lax.axis_size("vocab")
     if n & (n - 1):
         return lax.psum_scatter(terms, "vocab", scatter_dimension=1, tiled=True)
-    me = lax.axis_index("vocab")
+    me = lax.axis_index("vocab") ^ flip
     rows, width = terms.shape
     part = terms.reshape(rows, n, width // n)
     bit = 1
@@ -119,11 +119,32 @@
     )
     full_rows = doubling_rows(hidden)
     wide = full_rows.reshape(tokens_here, n_groups, piece)
-    halves = shift_exchange(wide, 1)
+    n_vocab = lax.axis_size("vocab")
+    pair = n_groups == 2 and n_vocab % 2 == 0 and not n_vocab & (n_vocab - 1)
+    if pair:
+        own_half = lax.dynamic_index_in_dim(wide, dp_row, 1, keepdims=False)
+        other_half = lax.dynamic_index_in_dim(wide, 1 - dp_row, 1, keepdims=False)
+        got_half = lax.ppermute(other_half, "dp", [(0, 1), (1, 0)])
+    else:
+        halves = shift_exchange(wide, 1)
     own_slots = lax.dynamic_index_in_dim(table, dp_row, 0, keepdims=False)
     col_mask = jnp.repeat(own_slots >= 0, BLOCK)
-    rows_w = shift_exchange(chosen, 0)
-    logits = jnp.einsum("tkd,krd->tr", wide, rows_w, preferred_element_type=jnp.float32)
+    if pair:
+        own_w = lax.dynamic_index_in_dim(chosen, dp_row, 0, keepdims=False)
+        got_w = lax.ppermute(
+            lax.dynamic_index_in_dim(chosen, 1 - dp_row, 0, keepdims=False),
+            "dp",
+            [(0, 1), (1, 0)],
+        )
+        held_w = jnp.stack([own_w, got_w])
+    else:
+        rows_w = shift_exchange(chosen, 0)
+    if pair:
+        logits = jnp.einsum(
+            "td,rd->tr", own_half, own_w, preferred_element_type=jnp.float32
+        ) + jnp.einsum("td,rd->tr", other_half, got_w, preferred_element_type=jnp.float32)
+    else:
+        logits = jnp.einsum("tkd,krd->tr", wide, rows_w, preferred_element_type=jnp.float32)
     offsets = teacher_ids % BLOCK
     match = (teacher_ids // BLOCK)[:, :, None] == own_slots[None, None, :]
     starts = jnp.arange(SLOTS, dtype=jnp.int32) * BLOCK
@@ -143,9 +164,14 @@
     loss = lse - picked
     probs = jnp.where(col_mask[None, :], jnp.exp(logits - lse[:, None]), 0.0)
     dlog = (probs - target).astype(jnp.bfloat16)
-    hidden_terms = jnp.einsum("tr,krd->tkd", dlog, rows_w, preferred_element_type=jnp.float32)
+    if pair:
+        hidden_terms = jnp.einsum("tr,krd->tkd", dlog, held_w, preferred_element_type=jnp.float32)
+        flip = dp_row * (lax.axis_size("vocab") // 2)
+    else:
+        hidden_terms = jnp.einsum("tr,krd->tkd", dlog, rows_w, preferred_element_type=jnp.float32)
+        flip = 0
     hidden_terms = hidden_terms.reshape(tokens_here, n_groups * piece)
-    grad_hidden = halving_scatter(hidden_terms).astype(jnp.bfloat16)
+    grad_hidden = halving_scatter(hidden_terms, flip).astype(jnp.bfloat16)
     dlog_all = doubling_gather(dlog).reshape(n_groups, tokens_here, SLOTS, BLOCK)
     block_ids = jnp.arange(per_dev, dtype=jnp.int32)
     placed = jnp.zeros((n_groups, tokens_here, per_dev, BLOCK), jnp.bfloat16)
@@ -155,9 +181,17 @@
             hit_q[:, None, :, None], dlog_all[:, :, q, :][:, :, None, :], jnp.zeros((), jnp.bfloat16)
         )
     placed = placed.reshape(n_groups, tokens_here, per_dev * BLOCK)
-    grad_weight = jnp.einsum(
-        "str,tsd->rd", placed, halves, preferred_element_type=jnp.float32
-    ).astype(jnp.bfloat16)
+    if pair:
+        mine_p = lax.dynamic_index_in_dim(placed, dp_row, 0, keepdims=False)
+        other_p = lax.dynamic_index_in_dim(placed, 1 - dp_row, 0, keepdims=False)
+        grad_weight = (
+            jnp.einsum("tr,td->rd", mine_p, own_half, preferred_element_type=jnp.float32)
+            + jnp.einsum("tr,td->rd", other_p, got_half, preferred_element_type=jnp.float32)
+        ).astype(jnp.bfloat16)
+    else:
+        grad_weight = jnp.einsum(
+            "str,tsd->rd", placed, halves, preferred_element_type=jnp.float32
+        ).astype(jnp.bfloat16)
     return (loss, grad_hidden, grad_weight)
 
 

time: 162 us -> 180 us (1.11)
  waiting for transfers between devices: 58.3 us -> 74.8 us
  matrix products: 16.5 us -> 30.9 us
  local copies, waits for them, and re-layouts: 48.9 us -> 40.8 us
  other arithmetic: 18.1 us -> 11.8 us
  starting transfers between devices: 18 us -> 20.4 us
    dot_general x3 -> x5, matrix products: 14.6 us -> 28.9 us  [the longest x1 11.9 us: shards(): jnp.einsum('tr,td->rd', other_p, got_half, preferred_element_type=jnp.flo...]
    gather x3 -> x0, local copies, waits for them, and re-layouts: 9.77 us -> none  [shift_exchange(): return jnp.take(held, (me - jnp.arange(n)) % n, axis=axis, mode='clip')]
    ppermute x1, waiting for transfers between devices: 10.7 us -> 18.9 us  [doubling_gather(): got = lax.ppermute(held, 'dp', [(k, k ^ bit) for k in range(n)])]
    unnamed x19 -> x11, local copies, waits for them, and re-layouts: 10.6 us -> 3.56 us
    concatenate x2 -> x0, other arithmetic: 6.51 us -> none  [shift_exchange(): held = jnp.concatenate(pieces, axis=axis)]
    ppermute x4, waiting for transfers between devices: 2.35 us -> 7.95 us  [halving_scatter(): lax.ppermute(send.astype(jnp.bfloat16), 'vocab', [(k, k ^ bit) for k in r...]
    ppermute x2, waiting for transfers between devices: 24.8 us -> 29.4 us  [the longest x1 29.4 us: shards(): lax.ppermute(lax.dynamic_index_in_dim(chosen, 1 - dp_row, 0, keepdims=Fal...]
    dynamic_slice x3, local copies, waits for them, and re-layouts: 6.42 us -> 8.8 us  [halving_scatter(): keep = lax.dynamic_index_in_dim(halves, mine, 2, keepdims=False)]
  transfers between devices with their start and end apart: 15 -> 15, of which waited for: 9 -> 10; matrix products, arithmetic and copies ran while one was open for 32% -> 38% of each run, Pallas kernels for 0% -> 0%
where the time goes in v10:
time: 180 us
  waiting for transfers between devices  74.8 us (42%)
  local copies, waits for them, and re-layouts  40.8 us (23%)
  matrix products  30.9 us (17%)
  starting transfers between devices  20.4 us (11%)
  other arithmetic  11.8 us (7%)
    ppermute x1, waiting for transfers between devices, shards(): lax.ppermute(lax.dynamic_index_in_dim(chosen, 1 - dp_row, 0, keepdims=Fal...  29.4 us
    ppermute x1, waiting for transfers between devices, doubling_gather(): got = lax.ppermute(held, 'dp', [(k, k ^ bit) for k in range(n)])  18.9 us
    dot_general x1, matrix products, shards(): jnp.einsum('tr,td->rd', other_p, got_half, preferred_element_type=jnp.flo...  11.9 us
    ppermute x4, waiting for transfers between devices, doubling_rows(): got = lax.ppermute(held, 'vocab', [(k, k ^ bit) for k in range(n)])  10.8 us
    dynamic_slice x3, local copies, waits for them, and re-layouts, halving_scatter(): keep = lax.dynamic_index_in_dim(halves, mine, 2, keepdims=False)  8.8 us
    dot_general x1, matrix products, shards(): jnp.einsum('tr,td->rd', mine_p, own_half, preferred_element_type=jnp.floa...  8.11 us
    ppermute x4, waiting for transfers between devices, halving_scatter(): lax.ppermute(send.astype(jnp.bfloat16), 'vocab', [(k, k ^ bit) for k in r...  7.95 us
    ppermute x4, waiting for transfers between devices, combine_stats(): lax.ppermute(jnp.stack([top, total, picked]), 'vocab', [(k, k ^ bit) for...  7.76 us
  transfers between devices with their start and end apart: 15, of which 10 were waited for; matrix products, arithmetic and copies ran while one was open for 38% of the time, Pallas kernels for 0%

profile of v10, /device:TPU:0, one launch (start us, length us, event | category | flops | bytes accessed | tf_op | source)
XLA Modules:
  0.0 179.7 jit_solution(7999716303958997957)
XLA Ops:
  0.6 4.1 %collective-permute-start = (bf16[128,1,512]{2,0,1:T(8,128)(2,1)}, bf16[128,1,512]{2,0,1:T(8,128)(2,1)S(1)}, u32[]{:S(2)}, u32[]{:S(2)}) collective-permute-start(bf16[128,1,512]{2,0,1:T(8,128)(2,1)} %bitcast.264), channel_id=1, source_target_pairs={{0,8},{1,9},{2,10},{3,11},{4,12},{5,13},{6,14},{7,15},{8,0},{9,1},... | collective-permute-start | bytes 393224 | tf_op jit(solution)/shard_map/ppermute | solution.py:69
  6.5 4.8 %collective-permute-done = bf16[128,1,512]{2,0,1:T(8,128)(2,1)S(1)} collective-permute-done((bf16[128,1,512]{2,0,1:T(8,128)(2,1)}, bf16[128,1,512]{2,0,1:T(8,128)(2,1)S(1)}, u32[]{:S(2)}, u32[]{:S(2)}) %collective-permute-start) | collective-permute-done | bytes 131104 | tf_op jit(solution)/shard_map/ppermute | solution.py:69
  13.2 6.2 %gather_fusion = bf16[4,128,4096]{2,1,0:T(8,128)(2,1)} fusion(bf16[8,128,4096]{2,1,0:T(8,128)(2,1)} %bitcast.260, s32[1024]{0:T(1024)S(1)} %pad_clamp_fusion), kind=kCustom, calls=%fused_computation | custom fusion | bytes 8388624 | tf_op jit(solution)/shard_map/jit(_take)/gather | solution.py:117
  21.3 4.7 %constant_dynamic-slice_fusion.4 = (bf16[1,256,4096]{2,1,0:T(8,128)(2,1)}, bf16[256,4096]{1,0:T(8,128)(2,1)}) fusion(bf16[2,256,4096]{2,1,0:T(8,128)(2,1)} %bitcast.251, s32[]{:T(128)S(6)} %select_n.218, s32[]{:T(128)S(6)} %select_n.239), kind=kLoop, calls=%fused_computation.84 | loop fusion | bytes 8388616 | tf_op jit(solution)/shard_map/jit(dynamic_index_in_dim)/dynamic_slice | solution.py:133
  25.9 1.5 collective-permute-start.4
  27.5 5.7 %collective-permute-done.2 = bf16[128,4,512]{2,0,1:T(8,128)(2,1)S(1)} collective-permute-done((bf16[128,4,512]{2,0,1:T(8,128)(2,1)S(1)}, bf16[128,4,512]{2,0,1:T(8,128)(2,1)S(1)}, u32[]{:S(2)}, u32[]{:S(2)}) %collective-permute-start.2) | collective-permute-done | bytes 524320 | tf_op jit(solution)/shard_map/ppermute | solution.py:69
  34.4 2.0 %fusion = f32[128,1,256]{2,1,0:T(1,128)S(1)} fusion(bf16[128,64,1]{1,2,0:T(2,128)(2,1)S(1)} %copy.78, s32[128,64]{1,0:T(8,128)S(1)} %copy.68), kind=kOutput, calls=%fused_computation.3 | convolution fusion | flops 6291456 | bytes 180224 | tf_op jit(solution)/shard_map/tk,tkr->tr/dot_general | solution.py:157
  36.6 1.5 pad_maximum_fusion
  38.1 3.0 %copy.65 = bf16[128,8,2,512]{0,3,2,1:T(8,128)(2,1)S(1)} copy(bf16[128,8,2,512]{3,0,1,2:T(8,128)(2,1)} %pad_maximum_fusion) | data formatting | bytes 4194304 | tf_op jit(solution)/shard_map/stack | solution.py:73
  41.2 2.4 %fusion.6 = f32[128,256]{1,0:T(8,128)S(1)} fusion(bf16[128,2,4096]{0,2,1:T(8,128)(2,1)S(1)} %bitcast.253, s32[]{:T(128)S(6)} %select_n.218, bf16[2,256,4096]{2,1,0:T(8,128)(2,1)} %bitcast.252), kind=kOutput, calls=%fused_computation.11 | convolution fusion | flops 268435456 | bytes 3277824 | tf_op jit(solution)/shard_map/td,rd->tr/dot_general | solution.py:143
  43.7 29.4 %collective-permute-done.4 = bf16[256,4096]{1,0:T(8,128)(2,1)} collective-permute-done((bf16[256,4096]{1,0:T(8,128)(2,1)}, bf16[256,4096]{1,0:T(8,128)(2,1)}, u32[]{:S(2)}, u32[]{:S(2)}) %collective-permute-start.4) | collective-permute-done | bytes 2097184 | tf_op jit(solution)/shard_map/ppermute | solution.py:134
  73.1 2.5 %select_reduce_fusion.1 = (f32[128]{0:T(128)S(1)}, f32[128,256]{1,0:T(8,128)S(1)}) fusion(pred[256]{0:T(512)(128)(4,1)S(1)} %broadcast_bitcast_fusion.2, f32[128,256]{1,0:T(8,128)S(1)} %fusion.6, bf16[256,4096]{1,0:T(8,128)(2,1)} %collective-permute-done.4, bf16[128,1,4096]{0,2,1:T(8,128)(2,1)S(1)} %constant_dynamic-slice_fusion.3), kind=kOutput, calls=%fused_computation.53 | convolution fusion | flops 268533632 | bytes 3408640 | tf_op jit(solution)/shard_map/td,rd->tr/dot_general | solution.py:145
  77.6 3.0 %collective-permute-done.6 = f32[3,128]{1,0:T(4,128)S(1)} collective-permute-done((f32[3,128]{1,0:T(4,128)S(1)}, f32[3,128]{1,0:T(4,128)S(1)}, u32[]{:S(2)}, u32[]{:S(2)}) %collective-permute-start.6) | collective-permute-done | bytes 1568 | tf_op jit(solution)/shard_map/ppermute | solution.py:30
  82.3 2.1 %collective-permute-done.7 = f32[3,128]{1,0:T(4,128)S(1)} collective-permute-done((f32[3,128]{1,0:T(4,128)S(1)}, f32[3,128]{1,0:T(4,128)S(1)}, u32[]{:S(2)}, u32[]{:S(2)}) %collective-permute-start.7) | collective-permute-done | bytes 1568 | tf_op jit(solution)/shard_map/ppermute | solution.py:30
  84.4 3.3 %collective-permute-start.8 = (f32[3,128]{1,0:T(4,128)S(1)}, f32[3,128]{1,0:T(4,128)S(1)}, u32[]{:S(2)}, u32[]{:S(2)}) collective-permute-start(f32[3,128]{1,0:T(4,128)S(1)} %pad_maximum_fusion.6), channel_id=1, source_target_pairs={{0,8},{1,9},{2,10},{3,11},{4,12},{5,13},{6,14},{7,15},{8,0},{9,1},... | collective-permute-start | bytes 4616 | tf_op jit(solution)/shard_map/ppermute | solution.py:30
  87.8 1.5 collective-permute-done.8
  89.9 4.0 %fusion.1 = f32[128,2,4096]{0,2,1:T(8,128)S(1)} fusion(bf16[1,256,4096]{2,1,0:T(8,128)(2,1)} %bitcast.41, bf16[1,256,4096]{2,1,0:T(8,128)(2,1)} %get-tuple-element.19, bf16[128,256]{1,0:T(8,128)(2,1)S(1)} %fusion.22), kind=kOutput, calls=%fused_computation.4 | convolution fusion | flops 545259520 | bytes 8454144 | tf_op jit(solution)/shard_map/tr,krd->tkd/dot_general | solution.py:168
  94.0 2.0 %copy-done = f32[128,2,4096]{0,2,1:T(8,128)} copy-done((f32[128,2,4096]{0,2,1:T(8,128)}, f32[128,2,4096]{0,2,1:T(8,128)S(1)}, u32[]{:S(2)}) %copy-start) | copy-done | bytes 4194328
  97.1 2.7 %copy.71 = bf16[128,8,1,512]{3,1,0,2:T(8,128)(2,1)} copy(bf16[128,8,1,512]{0,3,2,1:T(8,128)(2,1)} %dynamic-slice_convert_fusion) | data formatting | bytes 2097152 | tf_op jit(solution)/shard_map/convert_element_type | solution.py:54
  101.5 1.5 collective-permute-start.14
  103.5 3.1 %constant_dynamic-slice_fusion.2 = f32[128,8,1,512]{0,3,2,1:T(8,128)} fusion(f32[128,8,2,512]{0,3,2,1:T(8,128)} %bitcast.250, s32[]{:T(128)S(6)} %select_n.247), kind=kLoop, calls=%fused_computation.82 | loop fusion | bytes 4194308 | tf_op jit(solution)/shard_map/jit(dynamic_index_in_dim)/dynamic_slice | solution.py:52
  106.6 3.0 %copy.70 = f32[128,8,1,512]{3,1,0,2:T(8,128)} copy(f32[128,8,1,512]{0,3,2,1:T(8,128)} %constant_dynamic-slice_fusion.2) | data formatting | bytes 4194304 | tf_op jit(solution)/shard_map/jit(dynamic_index_in_dim)/dynamic_slice | solution.py:52
  109.7 18.9 %collective-permute-done.13 = bf16[1,128,256]{2,1,0:T(8,128)(2,1)S(1)} collective-permute-done((bf16[1,128,256]{2,1,0:T(8,128)(2,1)S(1)}, bf16[1,128,256]{2,1,0:T(8,128)(2,1)S(1)}, u32[]{:S(2)}, u32[]{:S(2)}) %collective-permute-start.13) | collective-permute-done | bytes 65568 | tf_op jit(solution)/shard_map/ppermute | solution.py:86
  128.6 3.5 %bitcast_add_fusion = f32[128,8,512]{2,1,0:T(8,128)} fusion(f32[128,8,1,512]{3,1,0,2:T(8,128)} %copy.70, bf16[128,8,512]{2,1,0:T(8,128)(2,1)} %collective-permute-done.9), kind=kLoop, calls=%fused_computation.10 | loop fusion | flops 1048576 | bytes 5242880 | tf_op jit(solution)/shard_map/add | solution.py:55
  132.1 3.5 %reshape.249 = f32[128,4,2,512]{3,2,1,0:T(2,128)} reshape(f32[128,8,512]{2,1,0:T(8,128)} %bitcast_add_fusion) | data formatting | bytes 4194304 | tf_op jit(solution)/shard_map/reshape | solution.py:50
  135.6 2.7 %constant_dynamic-slice_fusion = bf16[128,4,1,512]{3,2,1,0:T(2,128)(2,1)S(1)} fusion(f32[128,4,2,512]{3,2,1,0:T(2,128)} %reshape.249, s32[]{:T(128)S(6)} %select_n.252), kind=kLoop, calls=%fused_computation.80 | loop fusion | bytes 1048580 | tf_op jit(solution)/shard_map/jit(dynamic_index_in_dim)/dynamic_slice | solution.py:53
  142.5 2.7 %constant_dynamic-slice_fusion.1 = f32[128,4,1,512]{3,2,1,0:T(1,128)S(1)} fusion(f32[128,4,2,512]{3,2,1,0:T(2,128)} %reshape.249, s32[]{:T(128)S(6)} %select_n.251), kind=kLoop, calls=%fused_computation.81 | loop fusion | bytes 2097156 | tf_op jit(solution)/shard_map/jit(dynamic_index_in_dim)/dynamic_slice | solution.py:52
  145.2 7.9 %collective-permute-done.10 = bf16[128,4,512]{2,0,1:T(8,128)(2,1)} collective-permute-done((bf16[128,4,512]{2,0,1:T(8,128)(2,1)}, bf16[128,4,512]{2,0,1:T(8,128)(2,1)}, u32[]{:S(2)}, u32[]{:S(2)}) %collective-permute-start.10) | collective-permute-done | bytes 524320 | tf_op jit(solution)/shard_map/ppermute | solution.py:54
  154.5 1.4 collective-permute-start.11
  156.0 8.1 %fusion.9 = f32[1024,4096]{1,0:T(8,128)} fusion(bf16[128,2,4096]{0,2,1:T(8,128)(2,1)S(1)} %bitcast.255, s32[]{:T(128)S(6)} %select_n.218, bf16[2,128,1024]{2,1,0:T(8,128)(2,1)S(1)} %select_add_fusion), kind=kOutput, calls=%fused_computation.18 | convolution fusion | flops 1073741824 | bytes 18088960 | tf_op jit(solution)/shard_map/tr,td->rd/dot_general | solution.py:188
  164.2 3.0 %collective-permute-start.12 = (bf16[128,1,512]{2,0,1:T(8,128)(2,1)S(1)}, bf16[128,1,512]{2,0,1:T(8,128)(2,1)S(1)}, u32[]{:S(2)}, u32[]{:S(2)}) collective-permute-start(bf16[128,1,512]{2,0,1:T(8,128)(2,1)S(1)} %dynamic-slice_convert_fusion.2), channel_id=1, source_target_pairs={{0,8},{1,9},{2,10},{3,11},{4,12},{5,13},{6,14},{7,15},{8,0},{9,1},... | collective-permute-start | bytes 393224 | tf_op jit(solution)/shard_map/ppermute | solution.py:54
  167.2 11.9 %add_convert_fusion = bf16[1024,4096]{1,0:T(8,128)(2,1)} fusion(f32[1024,4096]{1,0:T(8,128)} %fusion.9, bf16[128,4096]{1,0:T(8,128)(2,1)} %collective-permute-done.14, bf16[2,128,1024]{2,1,0:T(8,128)(2,1)S(1)} %select_add_fusion, s32[]{:T(128)S(6)} %select_n.239), kind=kOutput, calls=%fused_computation.1 | convolution fusion | flops 1082130432 | bytes 26476548 | tf_op jit(solution)/shard_map/tr,td->rd/dot_general | solution.py:189
  (83 shorter events, 21.0 us)
Async XLA Ops:
  0.6 10.6 %collective-permute-start = (bf16[128,1,512]{2,0,1:T(8,128)(2,1)}, bf16[128,1,512]{2,0,1:T(8,128)(2,1)S(1)}, u32[]{:S(2)}, u32[]{:S(2)}) collective-permute-start(bf16[128,1,512]{2,0,1:T(8,128)(2,1)} %bitcast.264), channel_id=1, source_target_pairs={{0,8},{1,9},{2,10},{3,11},{4,12},{5,13},{6,14},{7,15},{8,0},{9,1},... | collective-permute-start | bytes 393224 | tf_op jit(solution)/shard_map/ppermute | solution.py:69
  12.2 7.5 %collective-permute-start.1 = (bf16[128,2,512]{2,0,1:T(8,128)(2,1)S(1)}, bf16[128,2,512]{2,0,1:T(8,128)(2,1)S(1)}, u32[]{:S(2)}, u32[]{:S(2)}) collective-permute-start(bf16[128,2,512]{2,0,1:T(8,128)(2,1)S(1)} %maximum_bitcast_fusion), channel_id=1, source_target_pairs={{0,4},{1,5},{2,6},{3,7},{4,0},{5,1},{6,2},{7,3},{8,12},{9,13},{10,... | collective-permute-start | bytes 786440 | tf_op jit(solution)/shard_map/ppermute | solution.py:69
  19.9 13.3 %collective-permute-start.2 = (bf16[128,4,512]{2,0,1:T(8,128)(2,1)S(1)}, bf16[128,4,512]{2,0,1:T(8,128)(2,1)S(1)}, u32[]{:S(2)}, u32[]{:S(2)}) collective-permute-start(bf16[128,4,512]{2,0,1:T(8,128)(2,1)S(1)} %bitcast.259), channel_id=1, source_target_pairs={{0,2},{1,3},{2,0},{3,1},{4,6},{5,7},{6,4},{7,5},{8,10},{9,11},{10,... | collective-permute-start | bytes 1572872 | tf_op jit(solution)/shard_map/ppermute | solution.py:69
  21.3 6.2 %copy-start.2 = (s32[128,64]{0,1:T(8,128)S(1)}, s32[128,64]{0,1:T(8,128)}, u32[]{:S(2)}) copy-start(s32[128,64]{0,1:T(8,128)} %param.7) | copy-start | bytes 98308
  25.9 47.1 %collective-permute-start.4 = (bf16[256,4096]{1,0:T(8,128)(2,1)}, bf16[256,4096]{1,0:T(8,128)(2,1)}, u32[]{:S(2)}, u32[]{:S(2)}) collective-permute-start(bf16[256,4096]{1,0:T(8,128)(2,1)} %get-tuple-element.20), channel_id=1, source_target_pairs={{0,16},{16,0},{1,17},{17,1},{2,18},{18,2},{3,19},{19,3},{4,20},{20... | collective-permute-start | bytes 6291464 | tf_op jit(solution)/shard_map/ppermute | solution.py:134
  33.3 0.8 copy-start.1
  33.5 2.9 %collective-permute-start.3 = (bf16[128,8,512]{2,0,1:T(8,128)(2,1)S(1)}, bf16[128,8,512]{2,0,1:T(8,128)(2,1)S(1)}, u32[]{:S(2)}, u32[]{:S(2)}) collective-permute-start(bf16[128,8,512]{2,0,1:T(8,128)(2,1)S(1)} %bitcast.256), channel_id=1, source_target_pairs={{0,1},{1,0},{2,3},{3,2},{4,5},{5,4},{6,7},{7,6},{8,9},{9,8},{10,11... | collective-permute-start | bytes 3145736 | tf_op jit(solution)/shard_map/ppermute | solution.py:69
  75.8 1.2 collective-permute-start.5
  77.0 3.7 %collective-permute-start.6 = (f32[3,128]{1,0:T(4,128)S(1)}, f32[3,128]{1,0:T(4,128)S(1)}, u32[]{:S(2)}, u32[]{:S(2)}) collective-permute-start(f32[3,128]{1,0:T(4,128)S(1)} %pad_maximum_fusion.4), channel_id=1, source_target_pairs={{0,2},{1,3},{2,0},{3,1},{4,6},{5,7},{6,4},{7,5},{8,10},{9,11},{10,... | collective-permute-start | bytes 4616 | tf_op jit(solution)/shard_map/ppermute | solution.py:30
  80.7 3.7 %collective-permute-start.7 = (f32[3,128]{1,0:T(4,128)S(1)}, f32[3,128]{1,0:T(4,128)S(1)}, u32[]{:S(2)}, u32[]{:S(2)}) collective-permute-start(f32[3,128]{1,0:T(4,128)S(1)} %pad_maximum_fusion.5), channel_id=1, source_target_pairs={{0,4},{1,5},{2,6},{3,7},{4,0},{5,1},{6,2},{7,3},{8,12},{9,13},{10,... | collective-permute-start | bytes 4616 | tf_op jit(solution)/shard_map/ppermute | solution.py:30
  84.4 4.9 %collective-permute-start.8 = (f32[3,128]{1,0:T(4,128)S(1)}, f32[3,128]{1,0:T(4,128)S(1)}, u32[]{:S(2)}, u32[]{:S(2)}) collective-permute-start(f32[3,128]{1,0:T(4,128)S(1)} %pad_maximum_fusion.6), channel_id=1, source_target_pairs={{0,8},{1,9},{2,10},{3,11},{4,12},{5,13},{6,14},{7,15},{8,0},{9,1},... | collective-permute-start | bytes 4616 | tf_op jit(solution)/shard_map/ppermute | solution.py:30
  94.0 2.0 %copy-start = (f32[128,2,4096]{0,2,1:T(8,128)}, f32[128,2,4096]{0,2,1:T(8,128)S(1)}, u32[]{:S(2)}) copy-start(f32[128,2,4096]{0,2,1:T(8,128)S(1)} %fusion.1) | copy-start | bytes 12582916
  99.8 28.8 %collective-permute-start.9 = (bf16[128,8,512]{2,1,0:T(8,128)(2,1)}, bf16[128,8,512]{2,1,0:T(8,128)(2,1)}, u32[]{:S(2)}, u32[]{:S(2)}) collective-permute-start(bf16[128,8,512]{2,1,0:T(8,128)(2,1)} %bitcast.261), channel_id=1, source_target_pairs={{0,1},{1,0},{2,3},{3,2},{4,5},{5,4},{6,7},{7,6},{8,9},{9,8},{10,11... | collective-permute-start | bytes 3145736 | tf_op jit(solution)/shard_map/ppermute | solution.py:54
  101.5 65.7 %collective-permute-start.14 = (bf16[128,4096]{1,0:T(8,128)(2,1)}, bf16[128,4096]{1,0:T(8,128)(2,1)}, u32[]{:S(2)}, u32[]{:S(2)}) collective-permute-start(bf16[128,4096]{1,0:T(8,128)(2,1)} %bitcast.262), channel_id=1, source_target_pairs={{0,16},{16,0},{1,17},{17,1},{2,18},{18,2},{3,19},{19,3},{4,20},{20... | collective-permute-start | bytes 3145736 | tf_op jit(solution)/shard_map/ppermute | solution.py:127
  103.0 25.6 %collective-permute-start.13 = (bf16[1,128,256]{2,1,0:T(8,128)(2,1)S(1)}, bf16[1,128,256]{2,1,0:T(8,128)(2,1)S(1)}, u32[]{:S(2)}, u32[]{:S(2)}) collective-permute-start(bf16[1,128,256]{2,1,0:T(8,128)(2,1)S(1)} %bitcast.263), channel_id=1, source_target_pairs={{0,16},{16,0},{1,17},{17,1},{2,18},{18,2},{3,19},{19,3},{4,20},{20... | collective-permute-start | bytes 196616 | tf_op jit(solution)/shard_map/ppermute | solution.py:86
  139.4 13.7 %collective-permute-start.10 = (bf16[128,4,512]{2,0,1:T(8,128)(2,1)}, bf16[128,4,512]{2,0,1:T(8,128)(2,1)}, u32[]{:S(2)}, u32[]{:S(2)}) collective-permute-start(bf16[128,4,512]{2,0,1:T(8,128)(2,1)} %bitcast.246), channel_id=1, source_target_pairs={{0,2},{1,3},{2,0},{3,1},{4,6},{5,7},{6,4},{7,5},{8,10},{9,11},{10,... | collective-permute-start | bytes 1572872 | tf_op jit(solution)/shard_map/ppermute | solution.py:54
  154.5 9.5 %collective-permute-start.11 = (bf16[128,2,512]{2,0,1:T(8,128)(2,1)S(1)}, bf16[128,2,512]{2,0,1:T(8,128)(2,1)S(1)}, u32[]{:S(2)}, u32[]{:S(2)}) collective-permute-start(bf16[128,2,512]{2,0,1:T(8,128)(2,1)S(1)} %fusion.15), channel_id=1, source_target_pairs={{0,4},{1,5},{2,6},{3,7},{4,0},{5,1},{6,2},{7,3},{8,12},{9,13},{10,... | collective-permute-start | bytes 786440 | tf_op jit(solution)/shard_map/ppermute | solution.py:54
  164.2 14.9 %collective-permute-start.12 = (bf16[128,1,512]{2,0,1:T(8,128)(2,1)S(1)}, bf16[128,1,512]{2,0,1:T(8,128)(2,1)S(1)}, u32[]{:S(2)}, u32[]{:S(2)}) collective-permute-start(bf16[128,1,512]{2,0,1:T(8,128)(2,1)S(1)} %dynamic-slice_convert_fusion.2), channel_id=1, source_target_pairs={{0,8},{1,9},{2,10},{3,11},{4,12},{5,13},{6,14},{7,15},{8,0},{9,1},... | collective-permute-start | bytes 393224 | tf_op jit(solution)/shard_map/ppermute | solution.py:54

commit v11 on v10

--- a/solution.py
+++ b/solution.py
@@ -130,12 +130,14 @@
     own_slots = lax.dynamic_index_in_dim(table, dp_row, 0, keepdims=False)
     col_mask = jnp.repeat(own_slots >= 0, BLOCK)
     if pair:
-        own_w = lax.dynamic_index_in_dim(chosen, dp_row, 0, keepdims=False)
-        got_w = lax.ppermute(
-            lax.dynamic_index_in_dim(chosen, 1 - dp_row, 0, keepdims=False),
-            "dp",
-            [(0, 1), (1, 0)],
-        )
+        slot_rows = jnp.maximum(local, 0)
+
+        def rows_of(tile):
+            picks = lax.dynamic_index_in_dim(slot_rows, tile, 0, keepdims=False)
+            return jnp.take(blocks, picks, axis=0, mode="clip").reshape(width, piece)
+
+        got_w = lax.ppermute(rows_of(1 - dp_row), "dp", [(0, 1), (1, 0)])
+        own_w = rows_of(dp_row)
         held_w = jnp.stack([own_w, got_w])
     else:
         rows_w = shift_exchange(chosen, 0)
@@ -184,9 +186,11 @@
     if pair:
         mine_p = lax.dynamic_index_in_dim(placed, dp_row, 0, keepdims=False)
         other_p = lax.dynamic_index_in_dim(placed, 1 - dp_row, 0, keepdims=False)
-        grad_weight = (
-            jnp.einsum("tr,td->rd", mine_p, own_half, preferred_element_type=jnp.float32)
-            + jnp.einsum("tr,td->rd", other_p, got_half, preferred_element_type=jnp.float32)
+        grad_weight = jnp.einsum(
+            "tr,td->rd",
+            jnp.concatenate([mine_p, other_p]),
+            jnp.concatenate([own_half, got_half]),
+            preferred_element_type=jnp.float32,
         ).astype(jnp.bfloat16)
     else:
         grad_weight = jnp.einsum(

time: 180 us -> 155 us (0.86)
  matrix products: 30.9 us -> 15.7 us
  waiting for transfers between devices: 74.8 us -> 63.9 us
  starting transfers between devices: 20.4 us -> 22.5 us
    dot_general x2 -> x1, matrix products: 20 us -> 7.01 us  [shards(): jnp.einsum('tr,td->rd', jnp.concatenate([mine_p, other_p]), jnp.concatena...]
    ppermute x1, waiting for transfers between devices: 18.9 us -> 11.5 us  [doubling_gather(): got = lax.ppermute(held, 'dp', [(k, k ^ bit) for k in range(n)])]
    ppermute x1, waiting for transfers between devices: 29.4 us -> 23.8 us  [shards(): got_w = lax.ppermute(rows_of(1 - dp_row), 'dp', [(0, 1), (1, 0)])]
    ppermute x4, waiting for transfers between devices: 10.8 us -> 15.3 us  [doubling_rows(): got = lax.ppermute(held, 'vocab', [(k, k ^ bit) for k in range(n)])]
    dynamic_slice x1, local copies, waits for them, and re-layouts: 4.67 us -> 0.52 us  [shards(): own_half = lax.dynamic_index_in_dim(wide, dp_row, 1, keepdims=False)]
    broadcast_in_dim x5, local copies, waits for them, and re-layouts: 2.45 us -> 5.85 us  [shards(): jnp.where(hit_q[:, None, :, None], dlog_all[:, :, q, :][:, :, None, :], j...]
    gather x1 -> x2, local copies, waits for them, and re-layouts: 6.21 us -> 9.47 us  [rows_of(): return jnp.take(blocks, picks, axis=0, mode='clip').reshape(width, piece)]
    dynamic_slice x3, local copies, waits for them, and re-layouts: 8.8 us -> 6.39 us  [halving_scatter(): keep = lax.dynamic_index_in_dim(halves, mine, 2, keepdims=False)]
  transfers between devices with their start and end apart: 15 -> 15, of which waited for: 10 -> 10; matrix products, arithmetic and copies ran while one was open for 38% -> 35% of each run, Pallas kernels for 0% -> 0%
where the time goes in v11:
time: 155 us
  waiting for transfers between devices  63.9 us (41%)
  local copies, waits for them, and re-layouts  39.2 us (25%)
  starting transfers between devices  22.5 us (15%)
  matrix products  15.7 us (10%)
  other arithmetic  12.4 us (8%)
    ppermute x1, waiting for transfers between devices, shards(): got_w = lax.ppermute(rows_of(1 - dp_row), 'dp', [(0, 1), (1, 0)])  23.8 us
    ppermute x4, waiting for transfers between devices, doubling_rows(): got = lax.ppermute(held, 'vocab', [(k, k ^ bit) for k in range(n)])  15.3 us
    ppermute x1, waiting for transfers between devices, doubling_gather(): got = lax.ppermute(held, 'dp', [(k, k ^ bit) for k in range(n)])  11.5 us
    gather x2, local copies, waits for them, and re-layouts, rows_of(): return jnp.take(blocks, picks, axis=0, mode='clip').reshape(width, piece)  9.47 us
    ppermute x4, starting transfers between devices, combine_stats(): lax.ppermute(jnp.stack([top, total, picked]), 'vocab', [(k, k ^ bit) for...  7.26 us
    dot_general x1, matrix products, shards(): jnp.einsum('tr,td->rd', jnp.concatenate([mine_p, other_p]), jnp.concatena...  7.01 us
    ppermute x4, waiting for transfers between devices, combine_stats(): lax.ppermute(jnp.stack([top, total, picked]), 'vocab', [(k, k ^ bit) for...  6.99 us
    ppermute x4, starting transfers between devices, doubling_rows(): got = lax.ppermute(held, 'vocab', [(k, k ^ bit) for k in range(n)])  6.49 us
  transfers between devices with their start and end apart: 15, of which 10 were waited for; matrix products, arithmetic and copies ran while one was open for 35% of the time, Pallas kernels for 0%

profile of v11, /device:TPU:0, one launch (start us, length us, event | category | flops | bytes accessed | tf_op | source)
XLA Modules:
  0.0 154.7 jit_solution(9887922121527350498)
XLA Ops:
  0.6 4.1 %collective-permute-start = (bf16[128,1,512]{2,0,1:T(8,128)(2,1)}, bf16[128,1,512]{2,0,1:T(8,128)(2,1)S(1)}, u32[]{:S(2)}, u32[]{:S(2)}) collective-permute-start(bf16[128,1,512]{2,0,1:T(8,128)(2,1)} %bitcast.259), channel_id=1, source_target_pairs={{0,8},{1,9},{2,10},{3,11},{4,12},{5,13},{6,14},{7,15},{8,0},{9,1},... | collective-permute-start | bytes 393224 | tf_op jit(solution)/shard_map/ppermute | solution.py:69
  6.5 4.8 %collective-permute-done = bf16[128,1,512]{2,0,1:T(8,128)(2,1)S(1)} collective-permute-done((bf16[128,1,512]{2,0,1:T(8,128)(2,1)}, bf16[128,1,512]{2,0,1:T(8,128)(2,1)S(1)}, u32[]{:S(2)}, u32[]{:S(2)}) %collective-permute-start) | collective-permute-done | bytes 131104 | tf_op jit(solution)/shard_map/ppermute | solution.py:69
  13.1 6.6 %collective-permute-done.1 = bf16[128,2,512]{2,0,1:T(8,128)(2,1)S(1)} collective-permute-done((bf16[128,2,512]{2,0,1:T(8,128)(2,1)S(1)}, bf16[128,2,512]{2,0,1:T(8,128)(2,1)S(1)}, u32[]{:S(2)}, u32[]{:S(2)}) %collective-permute-start.1) | collective-permute-done | bytes 262176 | tf_op jit(solution)/shard_map/ppermute | solution.py:69
  21.3 5.4 %gather_fusion.1 = bf16[2,128,4096]{2,1,0:T(8,128)(2,1)} fusion(bf16[8,128,4096]{2,1,0:T(8,128)(2,1)} %bitcast.255, s32[1024]{0:T(1024)S(1)} %pad_clamp_fusion), kind=kCustom, calls=%fused_computation.1 | custom fusion | bytes 4194312 | tf_op jit(solution)/shard_map/jit(_take)/gather | solution.py:137
  26.7 1.5 collective-permute-start.4
  28.4 3.8 %collective-permute-done.2 = bf16[128,4,512]{2,0,1:T(8,128)(2,1)S(1)} collective-permute-done((bf16[128,4,512]{2,0,1:T(8,128)(2,1)S(1)}, bf16[128,4,512]{2,0,1:T(8,128)(2,1)S(1)}, u32[]{:S(2)}, u32[]{:S(2)}) %collective-permute-start.2) | collective-permute-done | bytes 524320 | tf_op jit(solution)/shard_map/ppermute | solution.py:69
  33.4 4.1 %gather_fusion = bf16[2,128,4096]{2,1,0:T(8,128)(2,1)S(1)} fusion(bf16[8,128,4096]{2,1,0:T(8,128)(2,1)} %bitcast.256, s32[1024]{0:T(1024)S(1)} %pad_clamp_fusion.1), kind=kCustom, calls=%fused_computation | custom fusion | bytes 4194312 | tf_op jit(solution)/shard_map/jit(_take)/gather | solution.py:137
  37.6 2.0 %fusion = f32[128,1,256]{2,1,0:T(1,128)S(1)} fusion(bf16[128,64,1]{1,2,0:T(2,128)(2,1)S(1)} %copy.75, s32[128,64]{1,0:T(8,128)S(1)} %copy.65), kind=kOutput, calls=%fused_computation.3 | convolution fusion | flops 6291456 | bytes 180224 | tf_op jit(solution)/shard_map/tk,tkr->tr/dot_general | solution.py:159
  42.4 3.9 %copy.62 = bf16[128,8,2,512]{0,3,2,1:T(8,128)(2,1)} copy(bf16[128,8,2,512]{3,0,1,2:T(8,128)(2,1)} %pad_maximum_fusion) | data formatting | bytes 4194304 | tf_op jit(solution)/shard_map/stack | solution.py:73
  46.3 1.7 %constant_dynamic-slice_fusion.4 = (bf16[128,1,4096]{0,2,1:T(8,128)(2,1)S(1)}, bf16[128,1,4096]{0,2,1:T(8,128)(2,1)S(1)}) fusion(bf16[128,2,4096]{0,2,1:T(8,128)(2,1)} %bitcast.249, s32[]{:T(128)S(6)} %select_n.230, s32[]{:T(128)S(6)} %select_n.209), kind=kLoop, calls=%fused_computation.82 | loop fusion | bytes 4194312 | tf_op jit(solution)/shard_map/jit(dynamic_index_in_dim)/dynamic_slice | solution.py:126
  48.9 23.8 %collective-permute-done.4 = bf16[256,4096]{1,0:T(8,128)(2,1)} collective-permute-done((bf16[256,4096]{1,0:T(8,128)(2,1)}, bf16[256,4096]{1,0:T(8,128)(2,1)}, u32[]{:S(2)}, u32[]{:S(2)}) %collective-permute-start.4) | collective-permute-done | bytes 2097184 | tf_op jit(solution)/shard_map/ppermute | solution.py:139
  72.7 2.5 %select_reduce_fusion.1 = (f32[128]{0:T(128)S(1)}, f32[128,256]{1,0:T(8,128)S(1)}) fusion(pred[256]{0:T(512)(128)(4,1)S(1)} %broadcast_bitcast_fusion.2, f32[128,256]{1,0:T(8,128)S(1)} %fusion.10, bf16[256,4096]{1,0:T(8,128)(2,1)} %collective-permute-done.4, bf16[128,1,4096]{0,2,1:T(8,128)(2,1)S(1)} %get-tuple-element.19), kind=kOutput, calls=%fused_computation.52 | convolution fusion | flops 268533632 | bytes 3408640 | tf_op jit(solution)/shard_map/td,rd->tr/dot_general | solution.py:147
  77.4 2.9 %collective-permute-done.6 = f32[3,128]{1,0:T(4,128)S(1)} collective-permute-done((f32[3,128]{1,0:T(4,128)S(1)}, f32[3,128]{1,0:T(4,128)S(1)}, u32[]{:S(2)}, u32[]{:S(2)}) %collective-permute-start.6) | collective-permute-done | bytes 1568 | tf_op jit(solution)/shard_map/ppermute | solution.py:30
  80.3 2.5 %collective-permute-start.7 = (f32[3,128]{1,0:T(4,128)S(1)}, f32[3,128]{1,0:T(4,128)S(1)}, u32[]{:S(2)}, u32[]{:S(2)}) collective-permute-start(f32[3,128]{1,0:T(4,128)S(1)} %pad_maximum_fusion.5), channel_id=1, source_target_pairs={{0,4},{1,5},{2,6},{3,7},{4,0},{5,1},{6,2},{7,3},{8,12},{9,13},{10,... | collective-permute-start | bytes 4616 | tf_op jit(solution)/shard_map/ppermute | solution.py:30
  82.9 1.6 %collective-permute-done.7 = f32[3,128]{1,0:T(4,128)S(1)} collective-permute-done((f32[3,128]{1,0:T(4,128)S(1)}, f32[3,128]{1,0:T(4,128)S(1)}, u32[]{:S(2)}, u32[]{:S(2)}) %collective-permute-start.7) | collective-permute-done | bytes 1568 | tf_op jit(solution)/shard_map/ppermute | solution.py:30
  84.5 3.9 %collective-permute-start.8 = (f32[3,128]{1,0:T(4,128)S(1)}, f32[3,128]{1,0:T(4,128)S(1)}, u32[]{:S(2)}, u32[]{:S(2)}) collective-permute-start(f32[3,128]{1,0:T(4,128)S(1)} %pad_maximum_fusion.6), channel_id=1, source_target_pairs={{0,8},{1,9},{2,10},{3,11},{4,12},{5,13},{6,14},{7,15},{8,0},{9,1},... | collective-permute-start | bytes 4616 | tf_op jit(solution)/shard_map/ppermute | solution.py:30
  88.4 1.6 %collective-permute-done.8 = f32[3,128]{1,0:T(4,128)S(1)} collective-permute-done((f32[3,128]{1,0:T(4,128)S(1)}, f32[3,128]{1,0:T(4,128)S(1)}, u32[]{:S(2)}, u32[]{:S(2)}) %collective-permute-start.8) | collective-permute-done | bytes 1568 | tf_op jit(solution)/shard_map/ppermute | solution.py:30
  90.6 3.4 %fusion.1 = f32[128,2,4096]{0,2,1:T(8,128)S(1)} fusion(bf16[1,256,4096]{2,1,0:T(8,128)(2,1)} %bitcast.43, bf16[1,256,4096]{2,1,0:T(8,128)(2,1)S(1)} %bitcast.248, bf16[128,256]{1,0:T(8,128)(2,1)S(1)} %fusion.19), kind=kOutput, calls=%fused_computation.5 | convolution fusion | flops 545259520 | bytes 8454144 | tf_op jit(solution)/shard_map/tr,krd->tkd/dot_general | solution.py:170
  94.0 2.0 %copy-done = f32[128,2,4096]{0,2,1:T(8,128)} copy-done((f32[128,2,4096]{0,2,1:T(8,128)}, f32[128,2,4096]{0,2,1:T(8,128)S(1)}, u32[]{:S(2)}) %copy-start) | copy-done | bytes 4194328
  96.2 1.7 %copy.68 = bf16[128,8,1,512]{3,1,0,2:T(8,128)(2,1)} copy(bf16[128,8,1,512]{0,3,2,1:T(8,128)(2,1)S(1)} %dynamic-slice_convert_fusion) | data formatting | bytes 2097152 | tf_op jit(solution)/shard_map/convert_element_type | solution.py:54
  100.1 1.6 %collective-permute-start.14 = (bf16[128,4096]{1,0:T(8,128)(2,1)}, bf16[128,4096]{1,0:T(8,128)(2,1)}, u32[]{:S(2)}, u32[]{:S(2)}) collective-permute-start(bf16[128,4096]{1,0:T(8,128)(2,1)} %bitcast.21), channel_id=1, source_target_pairs={{0,16},{16,0},{1,17},{17,1},{2,18},{18,2},{3,19},{19,3},{4,20},{20... | collective-permute-start | bytes 3145736 | tf_op jit(solution)/shard_map/ppermute | solution.py:127
  102.3 3.1 %constant_dynamic-slice_fusion.2 = f32[128,8,1,512]{0,3,2,1:T(8,128)} fusion(f32[128,8,2,512]{0,3,2,1:T(8,128)} %bitcast.246, s32[]{:T(128)S(6)} %select_n.238), kind=kLoop, calls=%fused_computation.80 | loop fusion | bytes 4194308 | tf_op jit(solution)/shard_map/jit(dynamic_index_in_dim)/dynamic_slice | solution.py:52
  105.4 2.2 %copy.67 = f32[128,8,1,512]{3,1,0,2:T(8,128)S(1)} copy(f32[128,8,1,512]{0,3,2,1:T(8,128)} %constant_dynamic-slice_fusion.2) | data formatting | bytes 4194304 | tf_op jit(solution)/shard_map/jit(dynamic_index_in_dim)/dynamic_slice | solution.py:52
  107.6 2.9 %bitcast_add_fusion = f32[128,8,512]{2,1,0:T(8,128)} fusion(f32[128,8,1,512]{3,1,0,2:T(8,128)S(1)} %copy.67, bf16[128,8,512]{2,1,0:T(8,128)(2,1)} %collective-permute-done.9), kind=kLoop, calls=%fused_computation.14 | loop fusion | flops 1048576 | bytes 5242880 | tf_op jit(solution)/shard_map/add | solution.py:55
  110.5 2.7 %reshape.221 = f32[128,4,2,512]{3,2,1,0:T(2,128)S(1)} reshape(f32[128,8,512]{2,1,0:T(8,128)} %bitcast_add_fusion) | data formatting | bytes 4194304 | tf_op jit(solution)/shard_map/reshape | solution.py:50
  115.9 11.5 %collective-permute-done.13 = bf16[1,128,256]{2,1,0:T(8,128)(2,1)S(1)} collective-permute-done((bf16[1,128,256]{2,1,0:T(8,128)(2,1)S(1)}, bf16[1,128,256]{2,1,0:T(8,128)(2,1)S(1)}, u32[]{:S(2)}, u32[]{:S(2)}) %collective-permute-start.13) | collective-permute-done | bytes 65568 | tf_op jit(solution)/shard_map/ppermute | solution.py:86
  128.3 2.1 %broadcast_in_dim.140 = bf16[2,128,1024]{2,1,0:T(8,128)(2,1)} reshape(bf16[2,128,8,128]{3,2,1,0:T(8,128)(2,1)} %broadcast_in_dim.139) | data formatting | bytes 1048576 | tf_op jit(solution)/shard_map/jit(_where)/broadcast_in_dim | solution.py:182
  131.2 2.1 %broadcast_in_dim.147 = bf16[2,128,1024]{2,1,0:T(8,128)(2,1)} reshape(bf16[2,128,8,128]{3,2,1,0:T(8,128)(2,1)} %broadcast_in_dim.146) | data formatting | bytes 1048576 | tf_op jit(solution)/shard_map/jit(_where)/broadcast_in_dim | solution.py:182
  135.9 1.5 collective-permute-start.11
  137.6 6.4 %collective-permute-done.11 = bf16[128,2,512]{2,0,1:T(8,128)(2,1)S(1)} collective-permute-done((bf16[128,2,512]{2,0,1:T(8,128)(2,1)S(1)}, bf16[128,2,512]{2,0,1:T(8,128)(2,1)S(1)}, u32[]{:S(2)}, u32[]{:S(2)}) %collective-permute-start.11) | collective-permute-done | bytes 262176 | tf_op jit(solution)/shard_map/ppermute | solution.py:54
  144.0 3.0 %collective-permute-start.12 = (bf16[128,1,512]{2,0,1:T(8,128)(2,1)S(1)}, bf16[128,1,512]{2,0,1:T(8,128)(2,1)S(1)}, u32[]{:S(2)}, u32[]{:S(2)}) collective-permute-start(bf16[128,1,512]{2,0,1:T(8,128)(2,1)S(1)} %dynamic-slice_convert_fusion.2), channel_id=1, source_target_pairs={{0,8},{1,9},{2,10},{3,11},{4,12},{5,13},{6,14},{7,15},{8,0},{9,1},... | collective-permute-start | bytes 393224 | tf_op jit(solution)/shard_map/ppermute | solution.py:54
  147.0 7.0 %convolution_convert_fusion = bf16[1024,4096]{1,0:T(8,128)(2,1)} fusion(bf16[128,4096]{1,0:T(8,128)(2,1)} %collective-permute-done.14, bf16[128,4096]{1,0:T(8,128)(2,1)S(1)} %bitcast.251, bf16[128,1024]{1,0:T(8,128)(2,1)S(1)} %get-tuple-element.26, bf16[128,1024]{1,0:T(8,128)(2,1)S(1)} %get-tuple-element.25), kind=kOutput, calls=%fused_computation.4 | convolution fusion | flops 2156920832 | bytes 11010048 | tf_op jit(solution)/shard_map/tr,td->rd/dot_general | solution.py:189
  (93 shorter events, 23.9 us)
Async XLA Ops:
  0.6 10.6 %collective-permute-start = (bf16[128,1,512]{2,0,1:T(8,128)(2,1)}, bf16[128,1,512]{2,0,1:T(8,128)(2,1)S(1)}, u32[]{:S(2)}, u32[]{:S(2)}) collective-permute-start(bf16[128,1,512]{2,0,1:T(8,128)(2,1)} %bitcast.259), channel_id=1, source_target_pairs={{0,8},{1,9},{2,10},{3,11},{4,12},{5,13},{6,14},{7,15},{8,0},{9,1},... | collective-permute-start | bytes 393224 | tf_op jit(solution)/shard_map/ppermute | solution.py:69
  12.2 7.5 %collective-permute-start.1 = (bf16[128,2,512]{2,0,1:T(8,128)(2,1)S(1)}, bf16[128,2,512]{2,0,1:T(8,128)(2,1)S(1)}, u32[]{:S(2)}, u32[]{:S(2)}) collective-permute-start(bf16[128,2,512]{2,0,1:T(8,128)(2,1)S(1)} %maximum_bitcast_fusion), channel_id=1, source_target_pairs={{0,4},{1,5},{2,6},{3,7},{4,0},{5,1},{6,2},{7,3},{8,12},{9,13},{10,... | collective-permute-start | bytes 786440 | tf_op jit(solution)/shard_map/ppermute | solution.py:69
  19.9 12.3 %collective-permute-start.2 = (bf16[128,4,512]{2,0,1:T(8,128)(2,1)S(1)}, bf16[128,4,512]{2,0,1:T(8,128)(2,1)S(1)}, u32[]{:S(2)}, u32[]{:S(2)}) collective-permute-start(bf16[128,4,512]{2,0,1:T(8,128)(2,1)S(1)} %bitcast.254), channel_id=1, source_target_pairs={{0,2},{1,3},{2,0},{3,1},{4,6},{5,7},{6,4},{7,5},{8,10},{9,11},{10,... | collective-permute-start | bytes 1572872 | tf_op jit(solution)/shard_map/ppermute | solution.py:69
  21.3 6.9 %copy-start.6 = (s32[128,64]{0,1:T(8,128)S(1)}, s32[128,64]{0,1:T(8,128)}, u32[]{:S(2)}) copy-start(s32[128,64]{0,1:T(8,128)} %param.7) | copy-start | bytes 98308
  26.7 46.0 %collective-permute-start.4 = (bf16[256,4096]{1,0:T(8,128)(2,1)}, bf16[256,4096]{1,0:T(8,128)(2,1)}, u32[]{:S(2)}, u32[]{:S(2)}) collective-permute-start(bf16[256,4096]{1,0:T(8,128)(2,1)} %bitcast.23), channel_id=1, source_target_pairs={{0,16},{16,0},{1,17},{17,1},{2,18},{18,2},{3,19},{19,3},{4,20},{20... | collective-permute-start | bytes 6291464 | tf_op jit(solution)/shard_map/ppermute | solution.py:139
  32.3 0.8 copy-start.5
  32.5 7.1 %collective-permute-start.3 = (bf16[128,8,512]{2,0,1:T(8,128)(2,1)S(1)}, bf16[128,8,512]{2,0,1:T(8,128)(2,1)}, u32[]{:S(2)}, u32[]{:S(2)}) collective-permute-start(bf16[128,8,512]{2,0,1:T(8,128)(2,1)S(1)} %bitcast.250), channel_id=1, source_target_pairs={{0,1},{1,0},{2,3},{3,2},{4,5},{5,4},{6,7},{7,6},{8,9},{9,8},{10,11... | collective-permute-start | bytes 3145736 | tf_op jit(solution)/shard_map/ppermute | solution.py:69
  48.0 27.2 %copy-start.1 = (bf16[128,1,4096]{0,2,1:T(8,128)(2,1)}, bf16[128,1,4096]{0,2,1:T(8,128)(2,1)S(1)}, u32[]{:S(2)}) copy-start(bf16[128,1,4096]{0,2,1:T(8,128)(2,1)S(1)} %get-tuple-element.19) | copy-start | bytes 3145732
  75.4 1.2 collective-permute-start.5
  76.7 3.7 %collective-permute-start.6 = (f32[3,128]{1,0:T(4,128)S(1)}, f32[3,128]{1,0:T(4,128)S(1)}, u32[]{:S(2)}, u32[]{:S(2)}) collective-permute-start(f32[3,128]{1,0:T(4,128)S(1)} %pad_maximum_fusion.4), channel_id=1, source_target_pairs={{0,2},{1,3},{2,0},{3,1},{4,6},{5,7},{6,4},{7,5},{8,10},{9,11},{10,... | collective-permute-start | bytes 4616 | tf_op jit(solution)/shard_map/ppermute | solution.py:30
  80.3 4.1 %collective-permute-start.7 = (f32[3,128]{1,0:T(4,128)S(1)}, f32[3,128]{1,0:T(4,128)S(1)}, u32[]{:S(2)}, u32[]{:S(2)}) collective-permute-start(f32[3,128]{1,0:T(4,128)S(1)} %pad_maximum_fusion.5), channel_id=1, source_target_pairs={{0,4},{1,5},{2,6},{3,7},{4,0},{5,1},{6,2},{7,3},{8,12},{9,13},{10,... | collective-permute-start | bytes 4616 | tf_op jit(solution)/shard_map/ppermute | solution.py:30
  84.5 5.5 %collective-permute-start.8 = (f32[3,128]{1,0:T(4,128)S(1)}, f32[3,128]{1,0:T(4,128)S(1)}, u32[]{:S(2)}, u32[]{:S(2)}) collective-permute-start(f32[3,128]{1,0:T(4,128)S(1)} %pad_maximum_fusion.6), channel_id=1, source_target_pairs={{0,8},{1,9},{2,10},{3,11},{4,12},{5,13},{6,14},{7,15},{8,0},{9,1},... | collective-permute-start | bytes 4616 | tf_op jit(solution)/shard_map/ppermute | solution.py:30
  94.0 2.0 %copy-start = (f32[128,2,4096]{0,2,1:T(8,128)}, f32[128,2,4096]{0,2,1:T(8,128)S(1)}, u32[]{:S(2)}) copy-start(f32[128,2,4096]{0,2,1:T(8,128)S(1)} %fusion.1) | copy-start | bytes 12582916
  96.0 2.3 %copy-start.2 = (bf16[128,1,4096]{0,2,1:T(8,128)(2,1)S(1)}, bf16[128,1,4096]{0,2,1:T(8,128)(2,1)}, u32[]{:S(2)}) copy-start(bf16[128,1,4096]{0,2,1:T(8,128)(2,1)} %copy-done.1) | copy-start | bytes 3145732
  97.9 9.7 %collective-permute-start.9 = (bf16[128,8,512]{2,1,0:T(8,128)(2,1)}, bf16[128,8,512]{2,1,0:T(8,128)(2,1)}, u32[]{:S(2)}, u32[]{:S(2)}) collective-permute-start(bf16[128,8,512]{2,1,0:T(8,128)(2,1)} %bitcast.257), channel_id=1, source_target_pairs={{0,1},{1,0},{2,3},{3,2},{4,5},{5,4},{6,7},{7,6},{8,9},{9,8},{10,11... | collective-permute-start | bytes 3145736 | tf_op jit(solution)/shard_map/ppermute | solution.py:54
  100.1 46.9 %collective-permute-start.14 = (bf16[128,4096]{1,0:T(8,128)(2,1)}, bf16[128,4096]{1,0:T(8,128)(2,1)}, u32[]{:S(2)}, u32[]{:S(2)}) collective-permute-start(bf16[128,4096]{1,0:T(8,128)(2,1)} %bitcast.21), channel_id=1, source_target_pairs={{0,16},{16,0},{1,17},{17,1},{2,18},{18,2},{3,19},{19,3},{4,20},{20... | collective-permute-start | bytes 3145736 | tf_op jit(solution)/shard_map/ppermute | solution.py:127
  101.7 25.6 %collective-permute-start.13 = (bf16[1,128,256]{2,1,0:T(8,128)(2,1)S(1)}, bf16[1,128,256]{2,1,0:T(8,128)(2,1)S(1)}, u32[]{:S(2)}, u32[]{:S(2)}) collective-permute-start(bf16[1,128,256]{2,1,0:T(8,128)(2,1)S(1)} %bitcast.258), channel_id=1, source_target_pairs={{0,16},{16,0},{1,17},{17,1},{2,18},{18,2},{3,19},{19,3},{4,20},{20... | collective-permute-start | bytes 196616 | tf_op jit(solution)/shard_map/ppermute | solution.py:86
  115.3 19.0 %collective-permute-start.10 = (bf16[128,4,512]{2,0,1:T(8,128)(2,1)}, bf16[128,4,512]{2,0,1:T(8,128)(2,1)}, u32[]{:S(2)}, u32[]{:S(2)}) collective-permute-start(bf16[128,4,512]{2,0,1:T(8,128)(2,1)} %bitcast.242), channel_id=1, source_target_pairs={{0,2},{1,3},{2,0},{3,1},{4,6},{5,7},{6,4},{7,5},{8,10},{9,11},{10,... | collective-permute-start | bytes 1572872 | tf_op jit(solution)/shard_map/ppermute | solution.py:54
  134.3 3.1 %copy-start.3 = (bf16[2,128,1024]{2,1,0:T(8,128)(2,1)S(1)}, bf16[2,128,1024]{2,1,0:T(8,128)(2,1)}, u32[]{:S(2)}) copy-start(bf16[2,128,1024]{2,1,0:T(8,128)(2,1)} %broadcast_in_dim.140) | copy-start | bytes 1572868
  134.3 3.1 %copy-start.4 = (bf16[2,128,1024]{2,1,0:T(8,128)(2,1)S(1)}, bf16[2,128,1024]{2,1,0:T(8,128)(2,1)}, u32[]{:S(2)}) copy-start(bf16[2,128,1024]{2,1,0:T(8,128)(2,1)} %broadcast_in_dim.147) | copy-start | bytes 1572868
  135.9 8.0 %collective-permute-start.11 = (bf16[128,2,512]{2,0,1:T(8,128)(2,1)S(1)}, bf16[128,2,512]{2,0,1:T(8,128)(2,1)S(1)}, u32[]{:S(2)}, u32[]{:S(2)}) collective-permute-start(bf16[128,2,512]{2,0,1:T(8,128)(2,1)S(1)} %fusion.16), channel_id=1, source_target_pairs={{0,4},{1,5},{2,6},{3,7},{4,0},{5,1},{6,2},{7,3},{8,12},{9,13},{10,... | collective-permute-start | bytes 786440 | tf_op jit(solution)/shard_map/ppermute | solution.py:54
  144.0 10.0 %collective-permute-start.12 = (bf16[128,1,512]{2,0,1:T(8,128)(2,1)S(1)}, bf16[128,1,512]{2,0,1:T(8,128)(2,1)S(1)}, u32[]{:S(2)}, u32[]{:S(2)}) collective-permute-start(bf16[128,1,512]{2,0,1:T(8,128)(2,1)S(1)} %dynamic-slice_convert_fusion.2), channel_id=1, source_target_pairs={{0,8},{1,9},{2,10},{3,11},{4,12},{5,13},{6,14},{7,15},{8,0},{9,1},... | collective-permute-start | bytes 393224 | tf_op jit(solution)/shard_map/ppermute | solution.py:54

commit v12 on v11

--- a/solution.py
+++ b/solution.py
@@ -51,7 +51,9 @@
         mine = (me // bit) % 2
         keep = lax.dynamic_index_in_dim(halves, mine, 2, keepdims=False)
         send = lax.dynamic_index_in_dim(halves, 1 - mine, 2, keepdims=False)
-        got = lax.ppermute(send.astype(jnp.bfloat16), "vocab", [(k, k ^ bit) for k in range(n)])
+        got = lax.ppermute(
+            send.astype(jnp.bfloat16), "vocab", [(k, k ^ bit) for k in range(n)]
+        )
         part = keep + got.astype(jnp.float32)
         bit *= 2
     return part.reshape(rows, width // n)
@@ -183,7 +185,14 @@
             hit_q[:, None, :, None], dlog_all[:, :, q, :][:, :, None, :], jnp.zeros((), jnp.bfloat16)
         )
     placed = placed.reshape(n_groups, tokens_here, per_dev * BLOCK)
-    if pair:
+    grad_weight = weight_grad(pair, placed, dp_row, halves if not pair else None,
+                              (own_half, got_half) if pair else None)
+    return (loss, grad_hidden, grad_weight)
+
+
+def weight_grad(pair, placed, dp_row, halves, pieces):
+    if pair:
+        own_half, got_half = pieces
         mine_p = lax.dynamic_index_in_dim(placed, dp_row, 0, keepdims=False)
         other_p = lax.dynamic_index_in_dim(placed, 1 - dp_row, 0, keepdims=False)
         grad_weight = jnp.einsum(
@@ -196,7 +205,7 @@
         grad_weight = jnp.einsum(
             "str,tsd->rd", placed, halves, preferred_element_type=jnp.float32
         ).astype(jnp.bfloat16)
-    return (loss, grad_hidden, grad_weight)
+    return grad_weight
 
 
 def solution(mesh):

time: 155 us -> 155 us (level)
  no operation moved by 1% of the time
where the time goes in v12:
time: 155 us
  waiting for transfers between devices  63.9 us (41%)
  local copies, waits for them, and re-layouts  39.2 us (25%)
  starting transfers between devices  22.5 us (15%)
  matrix products  15.7 us (10%)
  other arithmetic  12.4 us (8%)
    ppermute x1, waiting for transfers between devices, shards(): got_w = lax.ppermute(rows_of(1 - dp_row), 'dp', [(0, 1), (1, 0)])  23.8 us
    ppermute x4, waiting for transfers between devices, doubling_rows(): got = lax.ppermute(held, 'vocab', [(k, k ^ bit) for k in range(n)])  15.3 us
    ppermute x1, waiting for transfers between devices, doubling_gather(): got = lax.ppermute(held, 'dp', [(k, k ^ bit) for k in range(n)])  11.5 us
    gather x2, local copies, waits for them, and re-layouts, rows_of(): return jnp.take(blocks, picks, axis=0, mode='clip').reshape(width, piece)  9.47 us
    ppermute x4, starting transfers between devices, combine_stats(): lax.ppermute(jnp.stack([top, total, picked]), 'vocab', [(k, k ^ bit) for...  7.26 us
    dot_general x1, matrix products, weight_grad(): jnp.einsum('tr,td->rd', jnp.concatenate([mine_p, other_p]), jnp.concatena...  7.01 us
    ppermute x4, waiting for transfers between devices, combine_stats(): lax.ppermute(jnp.stack([top, total, picked]), 'vocab', [(k, k ^ bit) for...  6.99 us
    ppermute x4, starting transfers between devices, doubling_rows(): got = lax.ppermute(held, 'vocab', [(k, k ^ bit) for k in range(n)])  6.49 us
  transfers between devices with their start and end apart: 15, of which 10 were waited for; matrix products, arithmetic and copies ran while one was open for 35% of the time, Pallas kernels for 0%

profile of v12, /device:TPU:0, one launch (start us, length us, event | category | flops | bytes accessed | tf_op | source)
XLA Modules:
  0.0 154.7 jit_solution(9887922121527350498)
XLA Ops:
  0.6 4.1 %collective-permute-start = (bf16[128,1,512]{2,0,1:T(8,128)(2,1)}, bf16[128,1,512]{2,0,1:T(8,128)(2,1)S(1)}, u32[]{:S(2)}, u32[]{:S(2)}) collective-permute-start(bf16[128,1,512]{2,0,1:T(8,128)(2,1)} %bitcast.259), channel_id=1, source_target_pairs={{0,8},{1,9},{2,10},{3,11},{4,12},{5,13},{6,14},{7,15},{8,0},{9,1},... | collective-permute-start | bytes 393224 | tf_op jit(solution)/shard_map/ppermute | solution.py:71
  6.5 4.8 %collective-permute-done = bf16[128,1,512]{2,0,1:T(8,128)(2,1)S(1)} collective-permute-done((bf16[128,1,512]{2,0,1:T(8,128)(2,1)}, bf16[128,1,512]{2,0,1:T(8,128)(2,1)S(1)}, u32[]{:S(2)}, u32[]{:S(2)}) %collective-permute-start) | collective-permute-done | bytes 131104 | tf_op jit(solution)/shard_map/ppermute | solution.py:71
  13.1 6.6 %collective-permute-done.1 = bf16[128,2,512]{2,0,1:T(8,128)(2,1)S(1)} collective-permute-done((bf16[128,2,512]{2,0,1:T(8,128)(2,1)S(1)}, bf16[128,2,512]{2,0,1:T(8,128)(2,1)S(1)}, u32[]{:S(2)}, u32[]{:S(2)}) %collective-permute-start.1) | collective-permute-done | bytes 262176 | tf_op jit(solution)/shard_map/ppermute | solution.py:71
  21.3 5.4 %gather_fusion.1 = bf16[2,128,4096]{2,1,0:T(8,128)(2,1)} fusion(bf16[8,128,4096]{2,1,0:T(8,128)(2,1)} %bitcast.255, s32[1024]{0:T(1024)S(1)} %pad_clamp_fusion), kind=kCustom, calls=%fused_computation.1 | custom fusion | bytes 4194312 | tf_op jit(solution)/shard_map/jit(_take)/gather | solution.py:139
  26.7 1.5 collective-permute-start.4
  28.4 3.8 %collective-permute-done.2 = bf16[128,4,512]{2,0,1:T(8,128)(2,1)S(1)} collective-permute-done((bf16[128,4,512]{2,0,1:T(8,128)(2,1)S(1)}, bf16[128,4,512]{2,0,1:T(8,128)(2,1)S(1)}, u32[]{:S(2)}, u32[]{:S(2)}) %collective-permute-start.2) | collective-permute-done | bytes 524320 | tf_op jit(solution)/shard_map/ppermute | solution.py:71
  33.4 4.1 %gather_fusion = bf16[2,128,4096]{2,1,0:T(8,128)(2,1)S(1)} fusion(bf16[8,128,4096]{2,1,0:T(8,128)(2,1)} %bitcast.256, s32[1024]{0:T(1024)S(1)} %pad_clamp_fusion.1), kind=kCustom, calls=%fused_computation | custom fusion | bytes 4194312 | tf_op jit(solution)/shard_map/jit(_take)/gather | solution.py:139
  37.6 2.0 %fusion = f32[128,1,256]{2,1,0:T(1,128)S(1)} fusion(bf16[128,64,1]{1,2,0:T(2,128)(2,1)S(1)} %copy.75, s32[128,64]{1,0:T(8,128)S(1)} %copy.65), kind=kOutput, calls=%fused_computation.3 | convolution fusion | flops 6291456 | bytes 180224 | tf_op jit(solution)/shard_map/tk,tkr->tr/dot_general | solution.py:161
  42.4 3.9 %copy.62 = bf16[128,8,2,512]{0,3,2,1:T(8,128)(2,1)} copy(bf16[128,8,2,512]{3,0,1,2:T(8,128)(2,1)} %pad_maximum_fusion) | data formatting | bytes 4194304 | tf_op jit(solution)/shard_map/stack | solution.py:75
  46.3 1.7 %constant_dynamic-slice_fusion.4 = (bf16[128,1,4096]{0,2,1:T(8,128)(2,1)S(1)}, bf16[128,1,4096]{0,2,1:T(8,128)(2,1)S(1)}) fusion(bf16[128,2,4096]{0,2,1:T(8,128)(2,1)} %bitcast.249, s32[]{:T(128)S(6)} %select_n.230, s32[]{:T(128)S(6)} %select_n.209), kind=kLoop, calls=%fused_computation.82 | loop fusion | bytes 4194312 | tf_op jit(solution)/shard_map/jit(dynamic_index_in_dim)/dynamic_slice | solution.py:128
  48.9 23.8 %collective-permute-done.4 = bf16[256,4096]{1,0:T(8,128)(2,1)} collective-permute-done((bf16[256,4096]{1,0:T(8,128)(2,1)}, bf16[256,4096]{1,0:T(8,128)(2,1)}, u32[]{:S(2)}, u32[]{:S(2)}) %collective-permute-start.4) | collective-permute-done | bytes 2097184 | tf_op jit(solution)/shard_map/ppermute | solution.py:141
  72.7 2.5 %select_reduce_fusion.1 = (f32[128]{0:T(128)S(1)}, f32[128,256]{1,0:T(8,128)S(1)}) fusion(pred[256]{0:T(512)(128)(4,1)S(1)} %broadcast_bitcast_fusion.2, f32[128,256]{1,0:T(8,128)S(1)} %fusion.10, bf16[256,4096]{1,0:T(8,128)(2,1)} %collective-permute-done.4, bf16[128,1,4096]{0,2,1:T(8,128)(2,1)S(1)} %get-tuple-element.19), kind=kOutput, calls=%fused_computation.52 | convolution fusion | flops 268533632 | bytes 3408640 | tf_op jit(solution)/shard_map/td,rd->tr/dot_general | solution.py:149
  77.4 2.9 %collective-permute-done.6 = f32[3,128]{1,0:T(4,128)S(1)} collective-permute-done((f32[3,128]{1,0:T(4,128)S(1)}, f32[3,128]{1,0:T(4,128)S(1)}, u32[]{:S(2)}, u32[]{:S(2)}) %collective-permute-start.6) | collective-permute-done | bytes 1568 | tf_op jit(solution)/shard_map/ppermute | solution.py:30
  80.3 2.5 %collective-permute-start.7 = (f32[3,128]{1,0:T(4,128)S(1)}, f32[3,128]{1,0:T(4,128)S(1)}, u32[]{:S(2)}, u32[]{:S(2)}) collective-permute-start(f32[3,128]{1,0:T(4,128)S(1)} %pad_maximum_fusion.5), channel_id=1, source_target_pairs={{0,4},{1,5},{2,6},{3,7},{4,0},{5,1},{6,2},{7,3},{8,12},{9,13},{10,... | collective-permute-start | bytes 4616 | tf_op jit(solution)/shard_map/ppermute | solution.py:30
  82.9 1.6 %collective-permute-done.7 = f32[3,128]{1,0:T(4,128)S(1)} collective-permute-done((f32[3,128]{1,0:T(4,128)S(1)}, f32[3,128]{1,0:T(4,128)S(1)}, u32[]{:S(2)}, u32[]{:S(2)}) %collective-permute-start.7) | collective-permute-done | bytes 1568 | tf_op jit(solution)/shard_map/ppermute | solution.py:30
  84.5 3.9 %collective-permute-start.8 = (f32[3,128]{1,0:T(4,128)S(1)}, f32[3,128]{1,0:T(4,128)S(1)}, u32[]{:S(2)}, u32[]{:S(2)}) collective-permute-start(f32[3,128]{1,0:T(4,128)S(1)} %pad_maximum_fusion.6), channel_id=1, source_target_pairs={{0,8},{1,9},{2,10},{3,11},{4,12},{5,13},{6,14},{7,15},{8,0},{9,1},... | collective-permute-start | bytes 4616 | tf_op jit(solution)/shard_map/ppermute | solution.py:30
  88.4 1.6 %collective-permute-done.8 = f32[3,128]{1,0:T(4,128)S(1)} collective-permute-done((f32[3,128]{1,0:T(4,128)S(1)}, f32[3,128]{1,0:T(4,128)S(1)}, u32[]{:S(2)}, u32[]{:S(2)}) %collective-permute-start.8) | collective-permute-done | bytes 1568 | tf_op jit(solution)/shard_map/ppermute | solution.py:30
  90.6 3.4 %fusion.1 = f32[128,2,4096]{0,2,1:T(8,128)S(1)} fusion(bf16[1,256,4096]{2,1,0:T(8,128)(2,1)} %bitcast.43, bf16[1,256,4096]{2,1,0:T(8,128)(2,1)S(1)} %bitcast.248, bf16[128,256]{1,0:T(8,128)(2,1)S(1)} %fusion.19), kind=kOutput, calls=%fused_computation.5 | convolution fusion | flops 545259520 | bytes 8454144 | tf_op jit(solution)/shard_map/tr,krd->tkd/dot_general | solution.py:172
  94.0 2.0 %copy-done = f32[128,2,4096]{0,2,1:T(8,128)} copy-done((f32[128,2,4096]{0,2,1:T(8,128)}, f32[128,2,4096]{0,2,1:T(8,128)S(1)}, u32[]{:S(2)}) %copy-start) | copy-done | bytes 4194328
  96.2 1.7 %copy.68 = bf16[128,8,1,512]{3,1,0,2:T(8,128)(2,1)} copy(bf16[128,8,1,512]{0,3,2,1:T(8,128)(2,1)S(1)} %dynamic-slice_convert_fusion) | data formatting | bytes 2097152 | tf_op jit(solution)/shard_map/convert_element_type | solution.py:55
  100.1 1.6 %collective-permute-start.14 = (bf16[128,4096]{1,0:T(8,128)(2,1)}, bf16[128,4096]{1,0:T(8,128)(2,1)}, u32[]{:S(2)}, u32[]{:S(2)}) collective-permute-start(bf16[128,4096]{1,0:T(8,128)(2,1)} %bitcast.21), channel_id=1, source_target_pairs={{0,16},{16,0},{1,17},{17,1},{2,18},{18,2},{3,19},{19,3},{4,20},{20... | collective-permute-start | bytes 3145736 | tf_op jit(solution)/shard_map/ppermute | solution.py:129
  102.3 3.1 %constant_dynamic-slice_fusion.2 = f32[128,8,1,512]{0,3,2,1:T(8,128)} fusion(f32[128,8,2,512]{0,3,2,1:T(8,128)} %bitcast.246, s32[]{:T(128)S(6)} %select_n.238), kind=kLoop, calls=%fused_computation.80 | loop fusion | bytes 4194308 | tf_op jit(solution)/shard_map/jit(dynamic_index_in_dim)/dynamic_slice | solution.py:52
  105.4 2.2 %copy.67 = f32[128,8,1,512]{3,1,0,2:T(8,128)S(1)} copy(f32[128,8,1,512]{0,3,2,1:T(8,128)} %constant_dynamic-slice_fusion.2) | data formatting | bytes 4194304 | tf_op jit(solution)/shard_map/jit(dynamic_index_in_dim)/dynamic_slice | solution.py:52
  107.6 2.9 %bitcast_add_fusion = f32[128,8,512]{2,1,0:T(8,128)} fusion(f32[128,8,1,512]{3,1,0,2:T(8,128)S(1)} %copy.67, bf16[128,8,512]{2,1,0:T(8,128)(2,1)} %collective-permute-done.9), kind=kLoop, calls=%fused_computation.14 | loop fusion | flops 1048576 | bytes 5242880 | tf_op jit(solution)/shard_map/add | solution.py:57
  110.5 2.7 %reshape.221 = f32[128,4,2,512]{3,2,1,0:T(2,128)S(1)} reshape(f32[128,8,512]{2,1,0:T(8,128)} %bitcast_add_fusion) | data formatting | bytes 4194304 | tf_op jit(solution)/shard_map/reshape | solution.py:50
  115.9 11.5 %collective-permute-done.13 = bf16[1,128,256]{2,1,0:T(8,128)(2,1)S(1)} collective-permute-done((bf16[1,128,256]{2,1,0:T(8,128)(2,1)S(1)}, bf16[1,128,256]{2,1,0:T(8,128)(2,1)S(1)}, u32[]{:S(2)}, u32[]{:S(2)}) %collective-permute-start.13) | collective-permute-done | bytes 65568 | tf_op jit(solution)/shard_map/ppermute | solution.py:88
  128.3 2.1 %broadcast_in_dim.140 = bf16[2,128,1024]{2,1,0:T(8,128)(2,1)} reshape(bf16[2,128,8,128]{3,2,1,0:T(8,128)(2,1)} %broadcast_in_dim.139) | data formatting | bytes 1048576 | tf_op jit(solution)/shard_map/jit(_where)/broadcast_in_dim | solution.py:184
  131.2 2.1 %broadcast_in_dim.147 = bf16[2,128,1024]{2,1,0:T(8,128)(2,1)} reshape(bf16[2,128,8,128]{3,2,1,0:T(8,128)(2,1)} %broadcast_in_dim.146) | data formatting | bytes 1048576 | tf_op jit(solution)/shard_map/jit(_where)/broadcast_in_dim | solution.py:184
  135.9 1.5 collective-permute-start.11
  137.6 6.4 %collective-permute-done.11 = bf16[128,2,512]{2,0,1:T(8,128)(2,1)S(1)} collective-permute-done((bf16[128,2,512]{2,0,1:T(8,128)(2,1)S(1)}, bf16[128,2,512]{2,0,1:T(8,128)(2,1)S(1)}, u32[]{:S(2)}, u32[]{:S(2)}) %collective-permute-start.11) | collective-permute-done | bytes 262176 | tf_op jit(solution)/shard_map/ppermute | solution.py:54
  144.0 3.0 %collective-permute-start.12 = (bf16[128,1,512]{2,0,1:T(8,128)(2,1)S(1)}, bf16[128,1,512]{2,0,1:T(8,128)(2,1)S(1)}, u32[]{:S(2)}, u32[]{:S(2)}) collective-permute-start(bf16[128,1,512]{2,0,1:T(8,128)(2,1)S(1)} %dynamic-slice_convert_fusion.2), channel_id=1, source_target_pairs={{0,8},{1,9},{2,10},{3,11},{4,12},{5,13},{6,14},{7,15},{8,0},{9,1},... | collective-permute-start | bytes 393224 | tf_op jit(solution)/shard_map/ppermute | solution.py:54
  147.0 7.0 %convolution_convert_fusion = bf16[1024,4096]{1,0:T(8,128)(2,1)} fusion(bf16[128,4096]{1,0:T(8,128)(2,1)} %collective-permute-done.14, bf16[128,4096]{1,0:T(8,128)(2,1)S(1)} %bitcast.251, bf16[128,1024]{1,0:T(8,128)(2,1)S(1)} %get-tuple-element.26, bf16[128,1024]{1,0:T(8,128)(2,1)S(1)} %get-tuple-element.25), kind=kOutput, calls=%fused_computation.4 | convolution fusion | flops 2156920832 | bytes 11010048 | tf_op jit(solution)/shard_map/tr,td->rd/dot_general | solution.py:198
  (93 shorter events, 23.9 us)
Async XLA Ops:
  0.6 10.6 %collective-permute-start = (bf16[128,1,512]{2,0,1:T(8,128)(2,1)}, bf16[128,1,512]{2,0,1:T(8,128)(2,1)S(1)}, u32[]{:S(2)}, u32[]{:S(2)}) collective-permute-start(bf16[128,1,512]{2,0,1:T(8,128)(2,1)} %bitcast.259), channel_id=1, source_target_pairs={{0,8},{1,9},{2,10},{3,11},{4,12},{5,13},{6,14},{7,15},{8,0},{9,1},... | collective-permute-start | bytes 393224 | tf_op jit(solution)/shard_map/ppermute | solution.py:71
  12.2 7.5 %collective-permute-start.1 = (bf16[128,2,512]{2,0,1:T(8,128)(2,1)S(1)}, bf16[128,2,512]{2,0,1:T(8,128)(2,1)S(1)}, u32[]{:S(2)}, u32[]{:S(2)}) collective-permute-start(bf16[128,2,512]{2,0,1:T(8,128)(2,1)S(1)} %maximum_bitcast_fusion), channel_id=1, source_target_pairs={{0,4},{1,5},{2,6},{3,7},{4,0},{5,1},{6,2},{7,3},{8,12},{9,13},{10,... | collective-permute-start | bytes 786440 | tf_op jit(solution)/shard_map/ppermute | solution.py:71
  19.9 12.3 %collective-permute-start.2 = (bf16[128,4,512]{2,0,1:T(8,128)(2,1)S(1)}, bf16[128,4,512]{2,0,1:T(8,128)(2,1)S(1)}, u32[]{:S(2)}, u32[]{:S(2)}) collective-permute-start(bf16[128,4,512]{2,0,1:T(8,128)(2,1)S(1)} %bitcast.254), channel_id=1, source_target_pairs={{0,2},{1,3},{2,0},{3,1},{4,6},{5,7},{6,4},{7,5},{8,10},{9,11},{10,... | collective-permute-start | bytes 1572872 | tf_op jit(solution)/shard_map/ppermute | solution.py:71
  21.3 6.9 %copy-start.6 = (s32[128,64]{0,1:T(8,128)S(1)}, s32[128,64]{0,1:T(8,128)}, u32[]{:S(2)}) copy-start(s32[128,64]{0,1:T(8,128)} %param.7) | copy-start | bytes 98308
  26.7 46.0 %collective-permute-start.4 = (bf16[256,4096]{1,0:T(8,128)(2,1)}, bf16[256,4096]{1,0:T(8,128)(2,1)}, u32[]{:S(2)}, u32[]{:S(2)}) collective-permute-start(bf16[256,4096]{1,0:T(8,128)(2,1)} %bitcast.23), channel_id=1, source_target_pairs={{0,16},{16,0},{1,17},{17,1},{2,18},{18,2},{3,19},{19,3},{4,20},{20... | collective-permute-start | bytes 6291464 | tf_op jit(solution)/shard_map/ppermute | solution.py:141
  32.3 0.8 copy-start.5
  32.5 7.1 %collective-permute-start.3 = (bf16[128,8,512]{2,0,1:T(8,128)(2,1)S(1)}, bf16[128,8,512]{2,0,1:T(8,128)(2,1)}, u32[]{:S(2)}, u32[]{:S(2)}) collective-permute-start(bf16[128,8,512]{2,0,1:T(8,128)(2,1)S(1)} %bitcast.250), channel_id=1, source_target_pairs={{0,1},{1,0},{2,3},{3,2},{4,5},{5,4},{6,7},{7,6},{8,9},{9,8},{10,11... | collective-permute-start | bytes 3145736 | tf_op jit(solution)/shard_map/ppermute | solution.py:71
  48.0 27.2 %copy-start.1 = (bf16[128,1,4096]{0,2,1:T(8,128)(2,1)}, bf16[128,1,4096]{0,2,1:T(8,128)(2,1)S(1)}, u32[]{:S(2)}) copy-start(bf16[128,1,4096]{0,2,1:T(8,128)(2,1)S(1)} %get-tuple-element.19) | copy-start | bytes 3145732
  75.4 1.2 collective-permute-start.5
  76.7 3.7 %collective-permute-start.6 = (f32[3,128]{1,0:T(4,128)S(1)}, f32[3,128]{1,0:T(4,128)S(1)}, u32[]{:S(2)}, u32[]{:S(2)}) collective-permute-start(f32[3,128]{1,0:T(4,128)S(1)} %pad_maximum_fusion.4), channel_id=1, source_target_pairs={{0,2},{1,3},{2,0},{3,1},{4,6},{5,7},{6,4},{7,5},{8,10},{9,11},{10,... | collective-permute-start | bytes 4616 | tf_op jit(solution)/shard_map/ppermute | solution.py:30
  80.3 4.1 %collective-permute-start.7 = (f32[3,128]{1,0:T(4,128)S(1)}, f32[3,128]{1,0:T(4,128)S(1)}, u32[]{:S(2)}, u32[]{:S(2)}) collective-permute-start(f32[3,128]{1,0:T(4,128)S(1)} %pad_maximum_fusion.5), channel_id=1, source_target_pairs={{0,4},{1,5},{2,6},{3,7},{4,0},{5,1},{6,2},{7,3},{8,12},{9,13},{10,... | collective-permute-start | bytes 4616 | tf_op jit(solution)/shard_map/ppermute | solution.py:30
  84.5 5.5 %collective-permute-start.8 = (f32[3,128]{1,0:T(4,128)S(1)}, f32[3,128]{1,0:T(4,128)S(1)}, u32[]{:S(2)}, u32[]{:S(2)}) collective-permute-start(f32[3,128]{1,0:T(4,128)S(1)} %pad_maximum_fusion.6), channel_id=1, source_target_pairs={{0,8},{1,9},{2,10},{3,11},{4,12},{5,13},{6,14},{7,15},{8,0},{9,1},... | collective-permute-start | bytes 4616 | tf_op jit(solution)/shard_map/ppermute | solution.py:30
  94.0 2.0 %copy-start = (f32[128,2,4096]{0,2,1:T(8,128)}, f32[128,2,4096]{0,2,1:T(8,128)S(1)}, u32[]{:S(2)}) copy-start(f32[128,2,4096]{0,2,1:T(8,128)S(1)} %fusion.1) | copy-start | bytes 12582916
  96.0 2.3 %copy-start.2 = (bf16[128,1,4096]{0,2,1:T(8,128)(2,1)S(1)}, bf16[128,1,4096]{0,2,1:T(8,128)(2,1)}, u32[]{:S(2)}) copy-start(bf16[128,1,4096]{0,2,1:T(8,128)(2,1)} %copy-done.1) | copy-start | bytes 3145732
  97.9 9.7 %collective-permute-start.9 = (bf16[128,8,512]{2,1,0:T(8,128)(2,1)}, bf16[128,8,512]{2,1,0:T(8,128)(2,1)}, u32[]{:S(2)}, u32[]{:S(2)}) collective-permute-start(bf16[128,8,512]{2,1,0:T(8,128)(2,1)} %bitcast.257), channel_id=1, source_target_pairs={{0,1},{1,0},{2,3},{3,2},{4,5},{5,4},{6,7},{7,6},{8,9},{9,8},{10,11... | collective-permute-start | bytes 3145736 | tf_op jit(solution)/shard_map/ppermute | solution.py:54
  100.1 46.9 %collective-permute-start.14 = (bf16[128,4096]{1,0:T(8,128)(2,1)}, bf16[128,4096]{1,0:T(8,128)(2,1)}, u32[]{:S(2)}, u32[]{:S(2)}) collective-permute-start(bf16[128,4096]{1,0:T(8,128)(2,1)} %bitcast.21), channel_id=1, source_target_pairs={{0,16},{16,0},{1,17},{17,1},{2,18},{18,2},{3,19},{19,3},{4,20},{20... | collective-permute-start | bytes 3145736 | tf_op jit(solution)/shard_map/ppermute | solution.py:129
  101.7 25.6 %collective-permute-start.13 = (bf16[1,128,256]{2,1,0:T(8,128)(2,1)S(1)}, bf16[1,128,256]{2,1,0:T(8,128)(2,1)S(1)}, u32[]{:S(2)}, u32[]{:S(2)}) collective-permute-start(bf16[1,128,256]{2,1,0:T(8,128)(2,1)S(1)} %bitcast.258), channel_id=1, source_target_pairs={{0,16},{16,0},{1,17},{17,1},{2,18},{18,2},{3,19},{19,3},{4,20},{20... | collective-permute-start | bytes 196616 | tf_op jit(solution)/shard_map/ppermute | solution.py:88
  115.3 19.0 %collective-permute-start.10 = (bf16[128,4,512]{2,0,1:T(8,128)(2,1)}, bf16[128,4,512]{2,0,1:T(8,128)(2,1)}, u32[]{:S(2)}, u32[]{:S(2)}) collective-permute-start(bf16[128,4,512]{2,0,1:T(8,128)(2,1)} %bitcast.242), channel_id=1, source_target_pairs={{0,2},{1,3},{2,0},{3,1},{4,6},{5,7},{6,4},{7,5},{8,10},{9,11},{10,... | collective-permute-start | bytes 1572872 | tf_op jit(solution)/shard_map/ppermute | solution.py:54
  134.3 3.1 %copy-start.3 = (bf16[2,128,1024]{2,1,0:T(8,128)(2,1)S(1)}, bf16[2,128,1024]{2,1,0:T(8,128)(2,1)}, u32[]{:S(2)}) copy-start(bf16[2,128,1024]{2,1,0:T(8,128)(2,1)} %broadcast_in_dim.140) | copy-start | bytes 1572868
  134.3 3.1 %copy-start.4 = (bf16[2,128,1024]{2,1,0:T(8,128)(2,1)S(1)}, bf16[2,128,1024]{2,1,0:T(8,128)(2,1)}, u32[]{:S(2)}) copy-start(bf16[2,128,1024]{2,1,0:T(8,128)(2,1)} %broadcast_in_dim.147) | copy-start | bytes 1572868
  135.9 8.0 %collective-permute-start.11 = (bf16[128,2,512]{2,0,1:T(8,128)(2,1)S(1)}, bf16[128,2,512]{2,0,1:T(8,128)(2,1)S(1)}, u32[]{:S(2)}, u32[]{:S(2)}) collective-permute-start(bf16[128,2,512]{2,0,1:T(8,128)(2,1)S(1)} %fusion.16), channel_id=1, source_target_pairs={{0,4},{1,5},{2,6},{3,7},{4,0},{5,1},{6,2},{7,3},{8,12},{9,13},{10,... | collective-permute-start | bytes 786440 | tf_op jit(solution)/shard_map/ppermute | solution.py:54
  144.0 10.0 %collective-permute-start.12 = (bf16[128,1,512]{2,0,1:T(8,128)(2,1)S(1)}, bf16[128,1,512]{2,0,1:T(8,128)(2,1)S(1)}, u32[]{:S(2)}, u32[]{:S(2)}) collective-permute-start(bf16[128,1,512]{2,0,1:T(8,128)(2,1)S(1)} %dynamic-slice_convert_fusion.2), channel_id=1, source_target_pairs={{0,8},{1,9},{2,10},{3,11},{4,12},{5,13},{6,14},{7,15},{8,0},{9,1},... | collective-permute-start | bytes 393224 | tf_op jit(solution)/shard_map/ppermute | solution.py:54

commit v13 on v12

--- a/solution.py
+++ b/solution.py
@@ -48,9 +48,9 @@
     bit = 1
     while bit < n:
         halves = part.reshape(rows, part.shape[1] // 2, 2, width // n)
-        mine = (me // bit) % 2
-        keep = lax.dynamic_index_in_dim(halves, mine, 2, keepdims=False)
-        send = lax.dynamic_index_in_dim(halves, 1 - mine, 2, keepdims=False)
+        low = (me // bit) % 2 == 0
+        keep = jnp.where(low, halves[:, :, 0], halves[:, :, 1])
+        send = jnp.where(low, halves[:, :, 1], halves[:, :, 0])
         got = lax.ppermute(
             send.astype(jnp.bfloat16), "vocab", [(k, k ^ bit) for k in range(n)]
         )

time: 155 us -> 150 us (0.968)
  local copies, waits for them, and re-layouts: 39.2 us -> 25.1 us
  waiting for transfers between devices: 63.9 us -> 70.6 us
  other arithmetic: 12.4 us -> 14 us
    dynamic_slice x4 -> x0, local copies, waits for them, and re-layouts: 7.46 us -> none  [the longest x3 6.39 us: halving_scatter(): keep = lax.dynamic_index_in_dim(halves, mine, 2, keepdims=False)]
    ppermute x1, waiting for transfers between devices: 11.5 us -> 18.2 us  [doubling_gather(): got = lax.ppermute(held, 'dp', [(k, k ^ bit) for k in range(n)])]
    broadcast_in_dim x5, local copies, waits for them, and re-layouts: 5.85 us -> 2.17 us  [shards(): jnp.where(hit_q[:, None, :, None], dlog_all[:, :, q, :][:, :, None, :], j...]
    reshape x1 -> x0, local copies, waits for them, and re-layouts: 2.67 us -> none  [halving_scatter(): halves = part.reshape(rows, part.shape[1] // 2, 2, width // n)]
    convert_element_type x4 -> x0, local copies, waits for them, and re-layouts: 1.95 us -> none  [halving_scatter(): send.astype(jnp.bfloat16)]
    add x0 -> x1, local copies, waits for them, and re-layouts: none -> 1.92 us  [halving_scatter(): part = keep + got.astype(jnp.float32)]
    add x3 -> x2, other arithmetic: 4.43 us -> 5.56 us  [halving_scatter(): part = keep + got.astype(jnp.float32)]
    unnamed x19 -> x20, local copies, waits for them, and re-layouts: 3.76 us -> 2.64 us
  transfers between devices with their start and end apart: 15 -> 15, of which waited for: 10 -> 10; matrix products, arithmetic and copies ran while one was open for 35% -> 29% of each run, Pallas kernels for 0% -> 0%
where the time goes in v13:
time: 150 us; the launch traced here: 149 us
  waiting for transfers between devices  70.6 us (47%)
  local copies, waits for them, and re-layouts  25.1 us (17%)
  starting transfers between devices  22.6 us (15%)
  matrix products  15.7 us (10%)
  other arithmetic  14 us (9%)
    ppermute x1, waiting for transfers between devices, shards(): got_w = lax.ppermute(rows_of(1 - dp_row), 'dp', [(0, 1), (1, 0)])  23.8 us
    ppermute x1, waiting for transfers between devices, doubling_gather(): got = lax.ppermute(held, 'dp', [(k, k ^ bit) for k in range(n)])  18.2 us
    ppermute x4, waiting for transfers between devices, doubling_rows(): got = lax.ppermute(held, 'vocab', [(k, k ^ bit) for k in range(n)])  15.3 us
    gather x2, local copies, waits for them, and re-layouts, rows_of(): return jnp.take(blocks, picks, axis=0, mode='clip').reshape(width, piece)  9.47 us
    ppermute x4, starting transfers between devices, combine_stats(): lax.ppermute(jnp.stack([top, total, picked]), 'vocab', [(k, k ^ bit) for...  7.26 us
    ppermute x4, waiting for transfers between devices, combine_stats(): lax.ppermute(jnp.stack([top, total, picked]), 'vocab', [(k, k ^ bit) for...  7.19 us
    dot_general x1, matrix products, weight_grad(): jnp.einsum('tr,td->rd', jnp.concatenate([mine_p, other_p]), jnp.concatena...  7.01 us
    ppermute x4, starting transfers between devices, doubling_rows(): got = lax.ppermute(held, 'vocab', [(k, k ^ bit) for k in range(n)])  6.49 us
  transfers between devices with their start and end apart: 15, of which 10 were waited for; matrix products, arithmetic and copies ran while one was open for 29% of the time, Pallas kernels for 0%

profile of v13, /device:TPU:0, one launch (start us, length us, event | category | flops | bytes accessed | tf_op | source)
XLA Modules:
  0.0 149.0 jit_solution(17903079067721709329)
XLA Ops:
  0.6 4.1 %collective-permute-start = (bf16[128,1,512]{2,0,1:T(8,128)(2,1)}, bf16[128,1,512]{2,0,1:T(8,128)(2,1)S(1)}, u32[]{:S(2)}, u32[]{:S(2)}) collective-permute-start(bf16[128,1,512]{2,0,1:T(8,128)(2,1)} %bitcast.291), channel_id=1, source_target_pairs={{0,8},{1,9},{2,10},{3,11},{4,12},{5,13},{6,14},{7,15},{8,0},{9,1},... | collective-permute-start | bytes 393224 | tf_op jit(solution)/shard_map/ppermute | solution.py:71
  6.5 4.8 %collective-permute-done = bf16[128,1,512]{2,0,1:T(8,128)(2,1)S(1)} collective-permute-done((bf16[128,1,512]{2,0,1:T(8,128)(2,1)}, bf16[128,1,512]{2,0,1:T(8,128)(2,1)S(1)}, u32[]{:S(2)}, u32[]{:S(2)}) %collective-permute-start) | collective-permute-done | bytes 131104 | tf_op jit(solution)/shard_map/ppermute | solution.py:71
  13.1 6.6 %collective-permute-done.1 = bf16[128,2,512]{2,0,1:T(8,128)(2,1)S(1)} collective-permute-done((bf16[128,2,512]{2,0,1:T(8,128)(2,1)S(1)}, bf16[128,2,512]{2,0,1:T(8,128)(2,1)S(1)}, u32[]{:S(2)}, u32[]{:S(2)}) %collective-permute-start.1) | collective-permute-done | bytes 262176 | tf_op jit(solution)/shard_map/ppermute | solution.py:71
  19.9 1.4 collective-permute-start.2
  21.3 5.4 %gather_fusion.1 = bf16[2,128,4096]{2,1,0:T(8,128)(2,1)} fusion(bf16[8,128,4096]{2,1,0:T(8,128)(2,1)} %bitcast.288, s32[1024]{0:T(1024)S(1)} %pad_clamp_fusion), kind=kCustom, calls=%fused_computation.1 | custom fusion | bytes 4194312 | tf_op jit(solution)/shard_map/jit(_take)/gather | solution.py:139
  26.7 1.5 %collective-permute-start.4 = (bf16[256,4096]{1,0:T(8,128)(2,1)}, bf16[256,4096]{1,0:T(8,128)(2,1)}, u32[]{:S(2)}, u32[]{:S(2)}) collective-permute-start(bf16[256,4096]{1,0:T(8,128)(2,1)} %bitcast.23), channel_id=1, source_target_pairs={{0,16},{16,0},{1,17},{17,1},{2,18},{18,2},{3,19},{19,3},{4,20},{20... | collective-permute-start | bytes 6291464 | tf_op jit(solution)/shard_map/ppermute | solution.py:141
  28.3 3.8 %collective-permute-done.2 = bf16[128,4,512]{2,0,1:T(8,128)(2,1)S(1)} collective-permute-done((bf16[128,4,512]{2,0,1:T(8,128)(2,1)S(1)}, bf16[128,4,512]{2,0,1:T(8,128)(2,1)S(1)}, u32[]{:S(2)}, u32[]{:S(2)}) %collective-permute-start.2) | collective-permute-done | bytes 524320 | tf_op jit(solution)/shard_map/ppermute | solution.py:71
  33.5 4.1 %gather_fusion = bf16[2,128,4096]{2,1,0:T(8,128)(2,1)S(1)} fusion(bf16[8,128,4096]{2,1,0:T(8,128)(2,1)} %bitcast.289, s32[1024]{0:T(1024)S(1)} %pad_clamp_fusion.1), kind=kCustom, calls=%fused_computation | custom fusion | bytes 4194312 | tf_op jit(solution)/shard_map/jit(_take)/gather | solution.py:139
  37.6 2.0 %fusion = f32[128,1,256]{2,1,0:T(1,128)S(1)} fusion(bf16[128,64,1]{1,2,0:T(2,128)(2,1)S(1)} %copy.94, s32[128,64]{1,0:T(8,128)S(1)} %copy.81), kind=kOutput, calls=%fused_computation.3 | convolution fusion | flops 6291456 | bytes 180224 | tf_op jit(solution)/shard_map/tk,tkr->tr/dot_general | solution.py:161
  39.6 1.4 select_bitcast_fusion.1
  40.9 1.5 %pad_maximum_fusion = bf16[128,8,2,512]{3,0,1,2:T(8,128)(2,1)} fusion(bf16[128,8,1,512]{3,0,1,2:T(8,128)(2,1)S(1)} %get-tuple-element.22, bf16[128,8,1,512]{3,0,1,2:T(8,128)(2,1)S(1)} %get-tuple-element.21), kind=kLoop, calls=%fused_computation.10 | loop fusion | flops 1048576 | bytes 4194304 | tf_op jit(solution)/shard_map/stack | solution.py:75
  42.4 3.9 %copy.78 = bf16[128,8,2,512]{0,3,2,1:T(8,128)(2,1)} copy(bf16[128,8,2,512]{3,0,1,2:T(8,128)(2,1)} %pad_maximum_fusion) | data formatting | bytes 4194304 | tf_op jit(solution)/shard_map/stack | solution.py:75
  46.4 1.7 %constant_dynamic-slice_fusion.1 = (bf16[128,1,4096]{0,2,1:T(8,128)(2,1)S(1)}, bf16[128,1,4096]{0,2,1:T(8,128)(2,1)S(1)}) fusion(bf16[128,2,4096]{0,2,1:T(8,128)(2,1)} %bitcast.282, s32[]{:T(128)S(6)} %select_n.282, s32[]{:T(128)S(6)} %select_n.261), kind=kLoop, calls=%fused_computation.92 | loop fusion | bytes 4194312 | tf_op jit(solution)/shard_map/jit(dynamic_index_in_dim)/dynamic_slice | solution.py:128
  48.9 23.8 %collective-permute-done.4 = bf16[256,4096]{1,0:T(8,128)(2,1)} collective-permute-done((bf16[256,4096]{1,0:T(8,128)(2,1)}, bf16[256,4096]{1,0:T(8,128)(2,1)}, u32[]{:S(2)}, u32[]{:S(2)}) %collective-permute-start.4) | collective-permute-done | bytes 2097184 | tf_op jit(solution)/shard_map/ppermute | solution.py:141
  72.7 2.5 %select_reduce_fusion.1 = (f32[128]{0:T(128)S(1)}, f32[128,256]{1,0:T(8,128)S(1)}) fusion(pred[256]{0:T(512)(128)(4,1)S(1)} %broadcast_bitcast_fusion.2, f32[128,256]{1,0:T(8,128)S(1)} %fusion.11, bf16[256,4096]{1,0:T(8,128)(2,1)} %collective-permute-done.4, bf16[128,1,4096]{0,2,1:T(8,128)(2,1)S(1)} %get-tuple-element.19), kind=kOutput, calls=%fused_computation.58 | convolution fusion | flops 268533632 | bytes 3408640 | tf_op jit(solution)/shard_map/td,rd->tr/dot_general | solution.py:149
  77.4 2.9 %collective-permute-done.6 = f32[3,128]{1,0:T(4,128)S(1)} collective-permute-done((f32[3,128]{1,0:T(4,128)S(1)}, f32[3,128]{1,0:T(4,128)S(1)}, u32[]{:S(2)}, u32[]{:S(2)}) %collective-permute-start.6) | collective-permute-done | bytes 1568 | tf_op jit(solution)/shard_map/ppermute | solution.py:30
  80.3 2.5 %collective-permute-start.7 = (f32[3,128]{1,0:T(4,128)S(1)}, f32[3,128]{1,0:T(4,128)S(1)}, u32[]{:S(2)}, u32[]{:S(2)}) collective-permute-start(f32[3,128]{1,0:T(4,128)S(1)} %pad_maximum_fusion.5), channel_id=1, source_target_pairs={{0,4},{1,5},{2,6},{3,7},{4,0},{5,1},{6,2},{7,3},{8,12},{9,13},{10,... | collective-permute-start | bytes 4616 | tf_op jit(solution)/shard_map/ppermute | solution.py:30
  82.9 1.6 %collective-permute-done.7 = f32[3,128]{1,0:T(4,128)S(1)} collective-permute-done((f32[3,128]{1,0:T(4,128)S(1)}, f32[3,128]{1,0:T(4,128)S(1)}, u32[]{:S(2)}, u32[]{:S(2)}) %collective-permute-start.7) | collective-permute-done | bytes 1568 | tf_op jit(solution)/shard_map/ppermute | solution.py:30
  84.5 3.9 %collective-permute-start.8 = (f32[3,128]{1,0:T(4,128)S(1)}, f32[3,128]{1,0:T(4,128)S(1)}, u32[]{:S(2)}, u32[]{:S(2)}) collective-permute-start(f32[3,128]{1,0:T(4,128)S(1)} %pad_maximum_fusion.6), channel_id=1, source_target_pairs={{0,8},{1,9},{2,10},{3,11},{4,12},{5,13},{6,14},{7,15},{8,0},{9,1},... | collective-permute-start | bytes 4616 | tf_op jit(solution)/shard_map/ppermute | solution.py:30
  88.4 1.6 %collective-permute-done.8 = f32[3,128]{1,0:T(4,128)S(1)} collective-permute-done((f32[3,128]{1,0:T(4,128)S(1)}, f32[3,128]{1,0:T(4,128)S(1)}, u32[]{:S(2)}, u32[]{:S(2)}) %collective-permute-start.8) | collective-permute-done | bytes 1568 | tf_op jit(solution)/shard_map/ppermute | solution.py:30
  90.6 3.4 %fusion.1 = f32[128,2,4096]{0,2,1:T(8,128)S(1)} fusion(bf16[1,256,4096]{2,1,0:T(8,128)(2,1)} %bitcast.43, bf16[1,256,4096]{2,1,0:T(8,128)(2,1)S(1)} %bitcast.279, bf16[128,256]{1,0:T(8,128)(2,1)S(1)} %fusion.25), kind=kOutput, calls=%fused_computation.5 | convolution fusion | flops 545259520 | bytes 8454144 | tf_op jit(solution)/shard_map/tr,krd->tkd/dot_general | solution.py:172
  94.0 2.0 %copy-done = f32[128,2,4096]{0,2,1:T(8,128)} copy-done((f32[128,2,4096]{0,2,1:T(8,128)}, f32[128,2,4096]{0,2,1:T(8,128)S(1)}, u32[]{:S(2)}) %copy-start) | copy-done | bytes 4194328
  96.9 1.4 copy.80
  99.6 1.5 %collective-permute-start.14 = (bf16[128,4096]{1,0:T(8,128)(2,1)}, bf16[128,4096]{1,0:T(8,128)(2,1)}, u32[]{:S(2)}, u32[]{:S(2)}) collective-permute-start(bf16[128,4096]{1,0:T(8,128)(2,1)} %bitcast.21), channel_id=1, source_target_pairs={{0,16},{16,0},{1,17},{17,1},{2,18},{18,2},{3,19},{19,3},{4,20},{20... | collective-permute-start | bytes 3145736 | tf_op jit(solution)/shard_map/ppermute | solution.py:129
  101.7 4.1 %bitcast_add_fusion = f32[128,8,512]{0,2,1:T(8,128)} fusion(bf16[128,8,512]{0,2,1:T(8,128)(2,1)} %collective-permute-done.9, f32[128,8,2,512]{0,3,2,1:T(8,128)} %bitcast.277, pred[]{:T(512)S(6)} %eq.140), kind=kLoop, calls=%fused_computation.14 | loop fusion | flops 1572864 | bytes 7340033 | tf_op jit(solution)/shard_map/add | solution.py:57
  105.9 1.9 %copy.85 = f32[128,8,512]{2,0,1:T(8,128)S(1)} copy(f32[128,8,512]{0,2,1:T(8,128)} %bitcast_add_fusion) | data formatting | bytes 4194304 | tf_op jit(solution)/shard_map/add | solution.py:57
  108.5 18.2 %collective-permute-done.13 = bf16[1,128,256]{2,1,0:T(8,128)(2,1)S(1)} collective-permute-done((bf16[1,128,256]{2,1,0:T(8,128)(2,1)S(1)}, bf16[1,128,256]{2,1,0:T(8,128)(2,1)S(1)}, u32[]{:S(2)}, u32[]{:S(2)}) %collective-permute-start.13) | collective-permute-done | bytes 65568 | tf_op jit(solution)/shard_map/ppermute | solution.py:88
  128.9 1.4 bitcast_add_fusion.1
  130.3 1.5 %collective-permute-start.11 = (bf16[128,2,512]{2,0,1:T(8,128)(2,1)S(1)}, bf16[128,2,512]{2,0,1:T(8,128)(2,1)S(1)}, u32[]{:S(2)}, u32[]{:S(2)}) collective-permute-start(bf16[128,2,512]{2,0,1:T(8,128)(2,1)S(1)} %fusion.20), channel_id=1, source_target_pairs={{0,4},{1,5},{2,6},{3,7},{4,0},{5,1},{6,2},{7,3},{8,12},{9,13},{10,... | collective-permute-start | bytes 786440 | tf_op jit(solution)/shard_map/ppermute | solution.py:54
  132.0 6.1 %collective-permute-done.11 = bf16[128,2,512]{2,0,1:T(8,128)(2,1)S(1)} collective-permute-done((bf16[128,2,512]{2,0,1:T(8,128)(2,1)S(1)}, bf16[128,2,512]{2,0,1:T(8,128)(2,1)S(1)}, u32[]{:S(2)}, u32[]{:S(2)}) %collective-permute-start.11) | collective-permute-done | bytes 262176 | tf_op jit(solution)/shard_map/ppermute | solution.py:54
  138.3 3.0 %collective-permute-start.12 = (bf16[128,1,512]{2,0,1:T(8,128)(2,1)S(1)}, bf16[128,1,512]{2,0,1:T(8,128)(2,1)S(1)}, u32[]{:S(2)}, u32[]{:S(2)}) collective-permute-start(bf16[128,1,512]{2,0,1:T(8,128)(2,1)S(1)} %fusion.22), channel_id=1, source_target_pairs={{0,8},{1,9},{2,10},{3,11},{4,12},{5,13},{6,14},{7,15},{8,0},{9,1},... | collective-permute-start | bytes 393224 | tf_op jit(solution)/shard_map/ppermute | solution.py:54
  141.3 7.0 %convolution_convert_fusion = bf16[1024,4096]{1,0:T(8,128)(2,1)} fusion(bf16[128,4096]{1,0:T(8,128)(2,1)} %collective-permute-done.14, bf16[128,4096]{1,0:T(8,128)(2,1)S(1)} %bitcast.286, bf16[128,1024]{1,0:T(8,128)(2,1)S(1)} %get-tuple-element.26, bf16[128,1024]{1,0:T(8,128)(2,1)S(1)} %get-tuple-element.25), kind=kOutput, calls=%fused_computation.4 | convolution fusion | flops 2156920832 | bytes 11010048 | tf_op jit(solution)/shard_map/tr,td->rd/dot_general | solution.py:198
  (90 shorter events, 15.4 us)
Async XLA Ops:
  0.6 10.6 %collective-permute-start = (bf16[128,1,512]{2,0,1:T(8,128)(2,1)}, bf16[128,1,512]{2,0,1:T(8,128)(2,1)S(1)}, u32[]{:S(2)}, u32[]{:S(2)}) collective-permute-start(bf16[128,1,512]{2,0,1:T(8,128)(2,1)} %bitcast.291), channel_id=1, source_target_pairs={{0,8},{1,9},{2,10},{3,11},{4,12},{5,13},{6,14},{7,15},{8,0},{9,1},... | collective-permute-start | bytes 393224 | tf_op jit(solution)/shard_map/ppermute | solution.py:71
  12.2 7.5 %collective-permute-start.1 = (bf16[128,2,512]{2,0,1:T(8,128)(2,1)S(1)}, bf16[128,2,512]{2,0,1:T(8,128)(2,1)S(1)}, u32[]{:S(2)}, u32[]{:S(2)}) collective-permute-start(bf16[128,2,512]{2,0,1:T(8,128)(2,1)S(1)} %maximum_bitcast_fusion), channel_id=1, source_target_pairs={{0,4},{1,5},{2,6},{3,7},{4,0},{5,1},{6,2},{7,3},{8,12},{9,13},{10,... | collective-permute-start | bytes 786440 | tf_op jit(solution)/shard_map/ppermute | solution.py:71
  19.9 12.3 %collective-permute-start.2 = (bf16[128,4,512]{2,0,1:T(8,128)(2,1)S(1)}, bf16[128,4,512]{2,0,1:T(8,128)(2,1)S(1)}, u32[]{:S(2)}, u32[]{:S(2)}) collective-permute-start(bf16[128,4,512]{2,0,1:T(8,128)(2,1)S(1)} %bitcast.287), channel_id=1, source_target_pairs={{0,2},{1,3},{2,0},{3,1},{4,6},{5,7},{6,4},{7,5},{8,10},{9,11},{10,... | collective-permute-start | bytes 1572872 | tf_op jit(solution)/shard_map/ppermute | solution.py:71
  21.3 6.9 %copy-start.7 = (s32[128,64]{0,1:T(8,128)S(1)}, s32[128,64]{0,1:T(8,128)}, u32[]{:S(2)}) copy-start(s32[128,64]{0,1:T(8,128)} %param.7) | copy-start | bytes 98308
  26.7 46.0 %collective-permute-start.4 = (bf16[256,4096]{1,0:T(8,128)(2,1)}, bf16[256,4096]{1,0:T(8,128)(2,1)}, u32[]{:S(2)}, u32[]{:S(2)}) collective-permute-start(bf16[256,4096]{1,0:T(8,128)(2,1)} %bitcast.23), channel_id=1, source_target_pairs={{0,16},{16,0},{1,17},{17,1},{2,18},{18,2},{3,19},{19,3},{4,20},{20... | collective-permute-start | bytes 6291464 | tf_op jit(solution)/shard_map/ppermute | solution.py:141
  32.3 0.8 copy-start.6
  32.5 7.1 %collective-permute-start.3 = (bf16[128,8,512]{2,0,1:T(8,128)(2,1)S(1)}, bf16[128,8,512]{2,0,1:T(8,128)(2,1)}, u32[]{:S(2)}, u32[]{:S(2)}) collective-permute-start(bf16[128,8,512]{2,0,1:T(8,128)(2,1)S(1)} %bitcast.285), channel_id=1, source_target_pairs={{0,1},{1,0},{2,3},{3,2},{4,5},{5,4},{6,7},{7,6},{8,9},{9,8},{10,11... | collective-permute-start | bytes 3145736 | tf_op jit(solution)/shard_map/ppermute | solution.py:71
  48.0 27.2 %copy-start.1 = (bf16[128,1,4096]{0,2,1:T(8,128)(2,1)}, bf16[128,1,4096]{0,2,1:T(8,128)(2,1)S(1)}, u32[]{:S(2)}) copy-start(bf16[128,1,4096]{0,2,1:T(8,128)(2,1)S(1)} %get-tuple-element.19) | copy-start | bytes 3145732
  75.4 1.2 collective-permute-start.5
  76.7 3.7 %collective-permute-start.6 = (f32[3,128]{1,0:T(4,128)S(1)}, f32[3,128]{1,0:T(4,128)S(1)}, u32[]{:S(2)}, u32[]{:S(2)}) collective-permute-start(f32[3,128]{1,0:T(4,128)S(1)} %pad_maximum_fusion.4), channel_id=1, source_target_pairs={{0,2},{1,3},{2,0},{3,1},{4,6},{5,7},{6,4},{7,5},{8,10},{9,11},{10,... | collective-permute-start | bytes 4616 | tf_op jit(solution)/shard_map/ppermute | solution.py:30
  80.3 4.1 %collective-permute-start.7 = (f32[3,128]{1,0:T(4,128)S(1)}, f32[3,128]{1,0:T(4,128)S(1)}, u32[]{:S(2)}, u32[]{:S(2)}) collective-permute-start(f32[3,128]{1,0:T(4,128)S(1)} %pad_maximum_fusion.5), channel_id=1, source_target_pairs={{0,4},{1,5},{2,6},{3,7},{4,0},{5,1},{6,2},{7,3},{8,12},{9,13},{10,... | collective-permute-start | bytes 4616 | tf_op jit(solution)/shard_map/ppermute | solution.py:30
  84.5 5.5 %collective-permute-start.8 = (f32[3,128]{1,0:T(4,128)S(1)}, f32[3,128]{1,0:T(4,128)S(1)}, u32[]{:S(2)}, u32[]{:S(2)}) collective-permute-start(f32[3,128]{1,0:T(4,128)S(1)} %pad_maximum_fusion.6), channel_id=1, source_target_pairs={{0,8},{1,9},{2,10},{3,11},{4,12},{5,13},{6,14},{7,15},{8,0},{9,1},... | collective-permute-start | bytes 4616 | tf_op jit(solution)/shard_map/ppermute | solution.py:30
  94.0 2.0 %copy-start = (f32[128,2,4096]{0,2,1:T(8,128)}, f32[128,2,4096]{0,2,1:T(8,128)S(1)}, u32[]{:S(2)}) copy-start(f32[128,2,4096]{0,2,1:T(8,128)S(1)} %fusion.1) | copy-start | bytes 12582916
  94.0 2.9 %copy-start.2 = (bf16[128,1,4096]{0,2,1:T(8,128)(2,1)S(1)}, bf16[128,1,4096]{0,2,1:T(8,128)(2,1)}, u32[]{:S(2)}) copy-start(bf16[128,1,4096]{0,2,1:T(8,128)(2,1)} %copy-done.1) | copy-start | bytes 3145732
  96.2 5.5 %collective-permute-start.9 = (bf16[128,8,512]{0,2,1:T(8,128)(2,1)S(1)}, bf16[128,8,512]{0,2,1:T(8,128)(2,1)}, u32[]{:S(2)}, u32[]{:S(2)}) collective-permute-start(bf16[128,8,512]{0,2,1:T(8,128)(2,1)S(1)} %fusion.9), channel_id=1, source_target_pairs={{0,1},{1,0},{2,3},{3,2},{4,5},{5,4},{6,7},{7,6},{8,9},{9,8},{10,11... | collective-permute-start | bytes 3145736 | tf_op jit(solution)/shard_map/ppermute | solution.py:54
  99.6 41.7 %collective-permute-start.14 = (bf16[128,4096]{1,0:T(8,128)(2,1)}, bf16[128,4096]{1,0:T(8,128)(2,1)}, u32[]{:S(2)}, u32[]{:S(2)}) collective-permute-start(bf16[128,4096]{1,0:T(8,128)(2,1)} %bitcast.21), channel_id=1, source_target_pairs={{0,16},{16,0},{1,17},{17,1},{2,18},{18,2},{3,19},{19,3},{4,20},{20... | collective-permute-start | bytes 3145736 | tf_op jit(solution)/shard_map/ppermute | solution.py:129
  101.1 25.5 %collective-permute-start.13 = (bf16[1,128,256]{2,1,0:T(8,128)(2,1)S(1)}, bf16[1,128,256]{2,1,0:T(8,128)(2,1)S(1)}, u32[]{:S(2)}, u32[]{:S(2)}) collective-permute-start(bf16[1,128,256]{2,1,0:T(8,128)(2,1)S(1)} %bitcast.290), channel_id=1, source_target_pairs={{0,16},{16,0},{1,17},{17,1},{2,18},{18,2},{3,19},{19,3},{4,20},{20... | collective-permute-start | bytes 196616 | tf_op jit(solution)/shard_map/ppermute | solution.py:88
  107.9 21.0 %collective-permute-start.10 = (bf16[128,4,512]{2,0,1:T(8,128)(2,1)S(1)}, bf16[128,4,512]{2,0,1:T(8,128)(2,1)}, u32[]{:S(2)}, u32[]{:S(2)}) collective-permute-start(bf16[128,4,512]{2,0,1:T(8,128)(2,1)S(1)} %fusion.13), channel_id=1, source_target_pairs={{0,2},{1,3},{2,0},{3,1},{4,6},{5,7},{6,4},{7,5},{8,10},{9,11},{10,... | collective-permute-start | bytes 1572872 | tf_op jit(solution)/shard_map/ppermute | solution.py:54
  128.8 3.0 %copy-start.4 = (bf16[2,128,1024]{2,1,0:T(8,128)(2,1)S(1)}, bf16[2,128,1024]{2,1,0:T(8,128)(2,1)}, u32[]{:S(2)}) copy-start(bf16[2,128,1024]{2,1,0:T(8,128)(2,1)} %broadcast_in_dim.140) | copy-start | bytes 1572868
  128.9 3.0 %copy-start.5 = (bf16[2,128,1024]{2,1,0:T(8,128)(2,1)S(1)}, bf16[2,128,1024]{2,1,0:T(8,128)(2,1)}, u32[]{:S(2)}) copy-start(bf16[2,128,1024]{2,1,0:T(8,128)(2,1)} %broadcast_in_dim.147) | copy-start | bytes 1572868
  130.3 7.8 %collective-permute-start.11 = (bf16[128,2,512]{2,0,1:T(8,128)(2,1)S(1)}, bf16[128,2,512]{2,0,1:T(8,128)(2,1)S(1)}, u32[]{:S(2)}, u32[]{:S(2)}) collective-permute-start(bf16[128,2,512]{2,0,1:T(8,128)(2,1)S(1)} %fusion.20), channel_id=1, source_target_pairs={{0,4},{1,5},{2,6},{3,7},{4,0},{5,1},{6,2},{7,3},{8,12},{9,13},{10,... | collective-permute-start | bytes 786440 | tf_op jit(solution)/shard_map/ppermute | solution.py:54
  131.9 9.4 %copy-start.3 = (bf16[128,1,4096]{2,0,1:T(8,128)(2,1)S(1)}, bf16[128,1,4096]{2,0,1:T(8,128)(2,1)}, u32[]{:S(2)}) copy-start(bf16[128,1,4096]{2,0,1:T(8,128)(2,1)} %copy.79) | copy-start | bytes 3145732
  138.3 10.0 %collective-permute-start.12 = (bf16[128,1,512]{2,0,1:T(8,128)(2,1)S(1)}, bf16[128,1,512]{2,0,1:T(8,128)(2,1)S(1)}, u32[]{:S(2)}, u32[]{:S(2)}) collective-permute-start(bf16[128,1,512]{2,0,1:T(8,128)(2,1)S(1)} %fusion.22), channel_id=1, source_target_pairs={{0,8},{1,9},{2,10},{3,11},{4,12},{5,13},{6,14},{7,15},{8,0},{9,1},... | collective-permute-start | bytes 393224 | tf_op jit(solution)/shard_map/ppermute | solution.py:54

commit v14 on v13

--- a/solution.py
+++ b/solution.py
@@ -124,8 +124,9 @@
     n_vocab = lax.axis_size("vocab")
     pair = n_groups == 2 and n_vocab % 2 == 0 and not n_vocab & (n_vocab - 1)
     if pair:
-        own_half = lax.dynamic_index_in_dim(wide, dp_row, 1, keepdims=False)
-        other_half = lax.dynamic_index_in_dim(wide, 1 - dp_row, 1, keepdims=False)
+        first = dp_row == 0
+        own_half = jnp.where(first, wide[:, 0], wide[:, 1])
+        other_half = jnp.where(first, wide[:, 1], wide[:, 0])
         got_half = lax.ppermute(other_half, "dp", [(0, 1), (1, 0)])
     else:
         halves = shift_exchange(wide, 1)
@@ -193,8 +194,8 @@
 def weight_grad(pair, placed, dp_row, halves, pieces):
     if pair:
         own_half, got_half = pieces
-        mine_p = lax.dynamic_index_in_dim(placed, dp_row, 0, keepdims=False)
-        other_p = lax.dynamic_index_in_dim(placed, 1 - dp_row, 0, keepdims=False)
+        mine_p = jnp.where(dp_row == 0, placed[0], placed[1])
+        other_p = jnp.where(dp_row == 0, placed[1], placed[0])
         grad_weight = jnp.einsum(
             "tr,td->rd",
             jnp.concatenate([mine_p, other_p]),

time: 150 us -> 144 us (0.960)
  local copies, waits for them, and re-layouts: 25.1 us -> 18.5 us
    dynamic_slice x3 -> x0, local copies, waits for them, and re-layouts: 4.37 us -> none  [the longest x2 3.04 us: shards(): other_half = lax.dynamic_index_in_dim(wide, 1 - dp_row, 1, keepdims=False)]
    select_n x0 -> x2, other arithmetic: none -> 2.72 us  [the longest x1 2.68 us: shards(): other_half = jnp.where(first, wide[:, 1], wide[:, 0])]
    broadcast_in_dim x5 -> x1, local copies, waits for them, and re-layouts: 2.17 us -> 0.01 us  [shards(): jnp.where(hit_q[:, None, :, None], dlog_all[:, :, q, :][:, :, None, :], j...]
  transfers between devices with their start and end apart: 15 -> 15, of which waited for: 10 -> 11; matrix products, arithmetic and copies ran while one was open for 29% -> 27% of each run, Pallas kernels for 0% -> 0%
where the time goes in v14:
time: 144 us; the launch traced here: 143 us
  waiting for transfers between devices  69.7 us (48%)
  starting transfers between devices  22.6 us (16%)
  local copies, waits for them, and re-layouts  18.5 us (13%)
  matrix products  16 us (11%)
  other arithmetic  15.3 us (11%)
    ppermute x1, waiting for transfers between devices, shards(): got_w = lax.ppermute(rows_of(1 - dp_row), 'dp', [(0, 1), (1, 0)])  22.8 us
    ppermute x1, waiting for transfers between devices, doubling_gather(): got = lax.ppermute(held, 'dp', [(k, k ^ bit) for k in range(n)])  18.3 us
    ppermute x4, waiting for transfers between devices, doubling_rows(): got = lax.ppermute(held, 'vocab', [(k, k ^ bit) for k in range(n)])  15.3 us
    gather x2, local copies, waits for them, and re-layouts, rows_of(): return jnp.take(blocks, picks, axis=0, mode='clip').reshape(width, piece)  9.48 us
    ppermute x4, starting transfers between devices, combine_stats(): lax.ppermute(jnp.stack([top, total, picked]), 'vocab', [(k, k ^ bit) for...  7.25 us
    ppermute x4, waiting for transfers between devices, combine_stats(): lax.ppermute(jnp.stack([top, total, picked]), 'vocab', [(k, k ^ bit) for...  7.19 us
    dot_general x1, matrix products, weight_grad(): jnp.einsum('tr,td->rd', jnp.concatenate([mine_p, other_p]), jnp.concatena...  7.03 us
    ppermute x4, starting transfers between devices, doubling_rows(): got = lax.ppermute(held, 'vocab', [(k, k ^ bit) for k in range(n)])  6.49 us
  transfers between devices with their start and end apart: 15, of which 11 were waited for; matrix products, arithmetic and copies ran while one was open for 27% of the time, Pallas kernels for 0%

profile of v14, /device:TPU:0, one launch (start us, length us, event | category | flops | bytes accessed | tf_op | source)
XLA Modules:
  0.0 143.2 jit_solution(7490445401148878318)
XLA Ops:
  0.6 4.1 %collective-permute-start = (bf16[128,1,512]{2,0,1:T(8,128)(2,1)}, bf16[128,1,512]{2,0,1:T(8,128)(2,1)S(1)}, u32[]{:S(2)}, u32[]{:S(2)}) collective-permute-start(bf16[128,1,512]{2,0,1:T(8,128)(2,1)} %bitcast.284), channel_id=1, source_target_pairs={{0,8},{1,9},{2,10},{3,11},{4,12},{5,13},{6,14},{7,15},{8,0},{9,1},... | collective-permute-start | bytes 393224 | tf_op jit(solution)/shard_map/ppermute | solution.py:71
  6.3 4.9 %collective-permute-done = bf16[128,1,512]{2,0,1:T(8,128)(2,1)S(1)} collective-permute-done((bf16[128,1,512]{2,0,1:T(8,128)(2,1)}, bf16[128,1,512]{2,0,1:T(8,128)(2,1)S(1)}, u32[]{:S(2)}, u32[]{:S(2)}) %collective-permute-start) | collective-permute-done | bytes 131104 | tf_op jit(solution)/shard_map/ppermute | solution.py:71
  11.3 0.9 select_bitcast_fusion.9
  13.3 6.5 %collective-permute-done.1 = bf16[128,2,512]{2,0,1:T(8,128)(2,1)S(1)} collective-permute-done((bf16[128,2,512]{2,0,1:T(8,128)(2,1)S(1)}, bf16[128,2,512]{2,0,1:T(8,128)(2,1)S(1)}, u32[]{:S(2)}, u32[]{:S(2)}) %collective-permute-start.1) | collective-permute-done | bytes 262176 | tf_op jit(solution)/shard_map/ppermute | solution.py:71
  19.9 1.4 collective-permute-start.2
  21.3 5.4 %gather_fusion.1 = bf16[2,128,4096]{2,1,0:T(8,128)(2,1)} fusion(bf16[8,128,4096]{2,1,0:T(8,128)(2,1)} %bitcast.277, s32[1024]{0:T(1024)S(1)} %get-tuple-element.45), kind=kCustom, calls=%fused_computation.1 | custom fusion | bytes 4194312 | tf_op jit(solution)/shard_map/jit(_take)/gather | solution.py:140
  26.7 1.5 %collective-permute-start.4 = (bf16[256,4096]{1,0:T(8,128)(2,1)}, bf16[256,4096]{1,0:T(8,128)(2,1)}, u32[]{:S(2)}, u32[]{:S(2)}) collective-permute-start(bf16[256,4096]{1,0:T(8,128)(2,1)} %bitcast.23), channel_id=1, source_target_pairs={{0,16},{16,0},{1,17},{17,1},{2,18},{18,2},{3,19},{19,3},{4,20},{20... | collective-permute-start | bytes 6291464 | tf_op jit(solution)/shard_map/ppermute | solution.py:142
  28.3 3.9 %collective-permute-done.2 = bf16[128,4,512]{2,0,1:T(8,128)(2,1)S(1)} collective-permute-done((bf16[128,4,512]{2,0,1:T(8,128)(2,1)S(1)}, bf16[128,4,512]{2,0,1:T(8,128)(2,1)S(1)}, u32[]{:S(2)}, u32[]{:S(2)}) %collective-permute-start.2) | collective-permute-done | bytes 524320 | tf_op jit(solution)/shard_map/ppermute | solution.py:71
  33.6 4.1 %gather_fusion = bf16[2,128,4096]{2,1,0:T(8,128)(2,1)S(1)} fusion(bf16[8,128,4096]{2,1,0:T(8,128)(2,1)} %bitcast.278, s32[1024]{0:T(1024)S(1)} %get-tuple-element.46), kind=kCustom, calls=%fused_computation | custom fusion | bytes 4194312 | tf_op jit(solution)/shard_map/jit(_take)/gather | solution.py:140
  37.7 2.0 %fusion = f32[128,1,256]{2,1,0:T(1,128)S(1)} fusion(bf16[128,64,1]{1,2,0:T(2,128)(2,1)S(1)} %copy.97, s32[128,64]{1,0:T(8,128)S(1)} %copy.83), kind=kOutput, calls=%fused_computation.3 | convolution fusion | flops 6291456 | bytes 180224 | tf_op jit(solution)/shard_map/tk,tkr->tr/dot_general | solution.py:162
  39.7 1.4 select_bitcast_fusion.3
  41.0 1.5 %pad_maximum_fusion = bf16[128,8,2,512]{3,0,1,2:T(8,128)(2,1)} fusion(bf16[128,8,1,512]{3,0,1,2:T(8,128)(2,1)S(1)} %get-tuple-element.22, bf16[128,8,1,512]{3,0,1,2:T(8,128)(2,1)S(1)} %get-tuple-element.21), kind=kLoop, calls=%fused_computation.10 | loop fusion | flops 1048576 | bytes 4194304 | tf_op jit(solution)/shard_map/stack | solution.py:75
  42.5 3.9 %copy.81 = bf16[128,8,2,512]{0,3,2,1:T(8,128)(2,1)} copy(bf16[128,8,2,512]{3,0,1,2:T(8,128)(2,1)} %pad_maximum_fusion) | data formatting | bytes 4194304 | tf_op jit(solution)/shard_map/stack | solution.py:75
  46.4 2.7 %select_bitcast_fusion = (bf16[128,4096]{0,1:T(8,128)(2,1)}, bf16[128,4096]{0,1:T(8,128)(2,1)S(1)}) fusion(pred[]{:T(512)S(6)} %eq.132, bf16[128,2,4096]{0,2,1:T(8,128)(2,1)} %bitcast.272), kind=kLoop, calls=%fused_computation.21 | loop fusion | flops 1048576 | bytes 4194305 | tf_op jit(solution)/shard_map/jit(_where)/select_n | solution.py:129
  50.0 22.8 %collective-permute-done.4 = bf16[256,4096]{1,0:T(8,128)(2,1)} collective-permute-done((bf16[256,4096]{1,0:T(8,128)(2,1)}, bf16[256,4096]{1,0:T(8,128)(2,1)}, u32[]{:S(2)}, u32[]{:S(2)}) %collective-permute-start.4) | collective-permute-done | bytes 2097184 | tf_op jit(solution)/shard_map/ppermute | solution.py:142
  72.7 2.8 %select_reduce_fusion.1 = (f32[128]{0:T(128)S(1)}, f32[128,256]{1,0:T(8,128)S(1)}) fusion(pred[256]{0:T(512)(128)(4,1)S(1)} %broadcast_bitcast_fusion, f32[128,256]{1,0:T(8,128)S(1)} %fusion.62, bf16[128,4096]{0,1:T(8,128)(2,1)} %get-tuple-element.19, bf16[256,4096]{1,0:T(8,128)(2,1)} %collective-permute-done.4), kind=kOutput, calls=%fused_computation.59 | convolution fusion | flops 268533632 | bytes 3408640 | tf_op jit(solution)/shard_map/td,rd->tr/dot_general | solution.py:150
  75.8 1.1 collective-permute-done.5
  77.7 2.9 %collective-permute-done.6 = f32[3,128]{1,0:T(4,128)S(1)} collective-permute-done((f32[3,128]{1,0:T(4,128)S(1)}, f32[3,128]{1,0:T(4,128)S(1)}, u32[]{:S(2)}, u32[]{:S(2)}) %collective-permute-start.6) | collective-permute-done | bytes 1568 | tf_op jit(solution)/shard_map/ppermute | solution.py:30
  80.7 2.5 %collective-permute-start.7 = (f32[3,128]{1,0:T(4,128)S(1)}, f32[3,128]{1,0:T(4,128)S(1)}, u32[]{:S(2)}, u32[]{:S(2)}) collective-permute-start(f32[3,128]{1,0:T(4,128)S(1)} %pad_maximum_fusion.5), channel_id=1, source_target_pairs={{0,4},{1,5},{2,6},{3,7},{4,0},{5,1},{6,2},{7,3},{8,12},{9,13},{10,... | collective-permute-start | bytes 4616 | tf_op jit(solution)/shard_map/ppermute | solution.py:30
  83.2 1.6 %collective-permute-done.7 = f32[3,128]{1,0:T(4,128)S(1)} collective-permute-done((f32[3,128]{1,0:T(4,128)S(1)}, f32[3,128]{1,0:T(4,128)S(1)}, u32[]{:S(2)}, u32[]{:S(2)}) %collective-permute-start.7) | collective-permute-done | bytes 1568 | tf_op jit(solution)/shard_map/ppermute | solution.py:30
  84.8 3.9 %collective-permute-start.8 = (f32[3,128]{1,0:T(4,128)S(1)}, f32[3,128]{1,0:T(4,128)S(1)}, u32[]{:S(2)}, u32[]{:S(2)}) collective-permute-start(f32[3,128]{1,0:T(4,128)S(1)} %pad_maximum_fusion.6), channel_id=1, source_target_pairs={{0,8},{1,9},{2,10},{3,11},{4,12},{5,13},{6,14},{7,15},{8,0},{9,1},... | collective-permute-start | bytes 4616 | tf_op jit(solution)/shard_map/ppermute | solution.py:30
  88.7 1.6 %collective-permute-done.8 = f32[3,128]{1,0:T(4,128)S(1)} collective-permute-done((f32[3,128]{1,0:T(4,128)S(1)}, f32[3,128]{1,0:T(4,128)S(1)}, u32[]{:S(2)}, u32[]{:S(2)}) %collective-permute-start.8) | collective-permute-done | bytes 1568 | tf_op jit(solution)/shard_map/ppermute | solution.py:30
  90.9 3.4 %fusion.1 = f32[128,2,4096]{0,2,1:T(8,128)S(1)} fusion(bf16[1,256,4096]{2,1,0:T(8,128)(2,1)} %bitcast.43, bf16[1,256,4096]{2,1,0:T(8,128)(2,1)S(1)} %bitcast.269, bf16[128,256]{1,0:T(8,128)(2,1)S(1)} %fusion.22), kind=kOutput, calls=%fused_computation.5 | convolution fusion | flops 545259520 | bytes 8454144 | tf_op jit(solution)/shard_map/tr,krd->tkd/dot_general | solution.py:173
  94.3 2.0 %copy-done = f32[128,2,4096]{0,2,1:T(8,128)} copy-done((f32[128,2,4096]{0,2,1:T(8,128)}, f32[128,2,4096]{0,2,1:T(8,128)S(1)}, u32[]{:S(2)}) %copy-start) | copy-done | bytes 4194328
  96.9 1.5 %collective-permute-start.14 = (bf16[128,4096]{0,1:T(8,128)(2,1)}, bf16[128,4096]{0,1:T(8,128)(2,1)}, u32[]{:S(2)}, u32[]{:S(2)}) collective-permute-start(bf16[128,4096]{0,1:T(8,128)(2,1)} %get-tuple-element.19), channel_id=1, source_target_pairs={{0,16},{16,0},{1,17},{17,1},{2,18},{18,2},{3,19},{19,3},{4,20},{20... | collective-permute-start | bytes 3145736 | tf_op jit(solution)/shard_map/ppermute | solution.py:130
  99.2 3.8 %bitcast_add_fusion = f32[128,8,512]{0,2,1:T(8,128)} fusion(bf16[128,8,512]{0,2,1:T(8,128)(2,1)S(1)} %collective-permute-done.9, f32[128,8,2,512]{0,3,2,1:T(8,128)} %bitcast.267, pred[]{:T(512)S(6)} %eq.146), kind=kLoop, calls=%fused_computation.14 | loop fusion | flops 1572864 | bytes 7340033 | tf_op jit(solution)/shard_map/add | solution.py:57
  103.1 1.9 %copy.87 = f32[128,8,512]{2,0,1:T(8,128)S(1)} copy(f32[128,8,512]{0,2,1:T(8,128)} %bitcast_add_fusion) | data formatting | bytes 4194304 | tf_op jit(solution)/shard_map/add | solution.py:57
  105.7 18.3 %collective-permute-done.13 = bf16[1,128,256]{2,1,0:T(8,128)(2,1)S(1)} collective-permute-done((bf16[1,128,256]{2,1,0:T(8,128)(2,1)S(1)}, bf16[1,128,256]{2,1,0:T(8,128)(2,1)S(1)}, u32[]{:S(2)}, u32[]{:S(2)}) %collective-permute-start.13) | collective-permute-done | bytes 65568 | tf_op jit(solution)/shard_map/ppermute | solution.py:88
  124.4 1.5 %collective-permute-start.11 = (bf16[128,2,512]{2,0,1:T(8,128)(2,1)S(1)}, bf16[128,2,512]{2,0,1:T(8,128)(2,1)S(1)}, u32[]{:S(2)}, u32[]{:S(2)}) collective-permute-start(bf16[128,2,512]{2,0,1:T(8,128)(2,1)S(1)} %fusion.17), channel_id=1, source_target_pairs={{0,4},{1,5},{2,6},{3,7},{4,0},{5,1},{6,2},{7,3},{8,12},{9,13},{10,... | collective-permute-start | bytes 786440 | tf_op jit(solution)/shard_map/ppermute | solution.py:54
  126.3 6.0 %collective-permute-done.11 = bf16[128,2,512]{2,0,1:T(8,128)(2,1)S(1)} collective-permute-done((bf16[128,2,512]{2,0,1:T(8,128)(2,1)S(1)}, bf16[128,2,512]{2,0,1:T(8,128)(2,1)S(1)}, u32[]{:S(2)}, u32[]{:S(2)}) %collective-permute-start.11) | collective-permute-done | bytes 262176 | tf_op jit(solution)/shard_map/ppermute | solution.py:54
  132.4 3.0 %collective-permute-start.12 = (bf16[128,1,512]{2,0,1:T(8,128)(2,1)S(1)}, bf16[128,1,512]{2,0,1:T(8,128)(2,1)S(1)}, u32[]{:S(2)}, u32[]{:S(2)}) collective-permute-start(bf16[128,1,512]{2,0,1:T(8,128)(2,1)S(1)} %fusion.19), channel_id=1, source_target_pairs={{0,8},{1,9},{2,10},{3,11},{4,12},{5,13},{6,14},{7,15},{8,0},{9,1},... | collective-permute-start | bytes 393224 | tf_op jit(solution)/shard_map/ppermute | solution.py:54
  135.4 7.0 %convolution_convert_fusion = bf16[1024,4096]{1,0:T(8,128)(2,1)} fusion(bf16[128,4096]{0,1:T(8,128)(2,1)} %collective-permute-done.14, bf16[128,4096]{0,1:T(8,128)(2,1)S(1)} %get-tuple-element.20, bf16[128,1024]{1,0:T(8,128)(2,1)S(1)} %bitcast.280, bf16[128,1024]{1,0:T(8,128)(2,1)S(1)} %bitcast.279), kind=kOutput, calls=%fused_computation.4 | convolution fusion | flops 2156920832 | bytes 11010048 | tf_op jit(solution)/shard_map/tr,td->rd/dot_general | solution.py:199
  (71 shorter events, 10.2 us)
Async XLA Ops:
  0.6 10.6 %collective-permute-start = (bf16[128,1,512]{2,0,1:T(8,128)(2,1)}, bf16[128,1,512]{2,0,1:T(8,128)(2,1)S(1)}, u32[]{:S(2)}, u32[]{:S(2)}) collective-permute-start(bf16[128,1,512]{2,0,1:T(8,128)(2,1)} %bitcast.284), channel_id=1, source_target_pairs={{0,8},{1,9},{2,10},{3,11},{4,12},{5,13},{6,14},{7,15},{8,0},{9,1},... | collective-permute-start | bytes 393224 | tf_op jit(solution)/shard_map/ppermute | solution.py:71
  12.2 7.5 %collective-permute-start.1 = (bf16[128,2,512]{2,0,1:T(8,128)(2,1)S(1)}, bf16[128,2,512]{2,0,1:T(8,128)(2,1)S(1)}, u32[]{:S(2)}, u32[]{:S(2)}) collective-permute-start(bf16[128,2,512]{2,0,1:T(8,128)(2,1)S(1)} %maximum_bitcast_fusion), channel_id=1, source_target_pairs={{0,4},{1,5},{2,6},{3,7},{4,0},{5,1},{6,2},{7,3},{8,12},{9,13},{10,... | collective-permute-start | bytes 786440 | tf_op jit(solution)/shard_map/ppermute | solution.py:71
  19.9 12.3 %collective-permute-start.2 = (bf16[128,4,512]{2,0,1:T(8,128)(2,1)S(1)}, bf16[128,4,512]{2,0,1:T(8,128)(2,1)S(1)}, u32[]{:S(2)}, u32[]{:S(2)}) collective-permute-start(bf16[128,4,512]{2,0,1:T(8,128)(2,1)S(1)} %bitcast.276), channel_id=1, source_target_pairs={{0,2},{1,3},{2,0},{3,1},{4,6},{5,7},{6,4},{7,5},{8,10},{9,11},{10,... | collective-permute-start | bytes 1572872 | tf_op jit(solution)/shard_map/ppermute | solution.py:71
  21.3 7.0 %copy-start.2 = (s32[128,64]{0,1:T(8,128)S(1)}, s32[128,64]{0,1:T(8,128)}, u32[]{:S(2)}) copy-start(s32[128,64]{0,1:T(8,128)} %param.7) | copy-start | bytes 98308
  26.7 46.0 %collective-permute-start.4 = (bf16[256,4096]{1,0:T(8,128)(2,1)}, bf16[256,4096]{1,0:T(8,128)(2,1)}, u32[]{:S(2)}, u32[]{:S(2)}) collective-permute-start(bf16[256,4096]{1,0:T(8,128)(2,1)} %bitcast.23), channel_id=1, source_target_pairs={{0,16},{16,0},{1,17},{17,1},{2,18},{18,2},{3,19},{19,3},{4,20},{20... | collective-permute-start | bytes 6291464 | tf_op jit(solution)/shard_map/ppermute | solution.py:142
  32.3 0.8 copy-start.1
  32.5 7.1 %collective-permute-start.3 = (bf16[128,8,512]{2,0,1:T(8,128)(2,1)S(1)}, bf16[128,8,512]{2,0,1:T(8,128)(2,1)}, u32[]{:S(2)}, u32[]{:S(2)}) collective-permute-start(bf16[128,8,512]{2,0,1:T(8,128)(2,1)S(1)} %bitcast.275), channel_id=1, source_target_pairs={{0,1},{1,0},{2,3},{3,2},{4,5},{5,4},{6,7},{7,6},{8,9},{9,8},{10,11... | collective-permute-start | bytes 3145736 | tf_op jit(solution)/shard_map/ppermute | solution.py:71
  75.7 1.2 collective-permute-start.5
  77.0 3.7 %collective-permute-start.6 = (f32[3,128]{1,0:T(4,128)S(1)}, f32[3,128]{1,0:T(4,128)S(1)}, u32[]{:S(2)}, u32[]{:S(2)}) collective-permute-start(f32[3,128]{1,0:T(4,128)S(1)} %pad_maximum_fusion.4), channel_id=1, source_target_pairs={{0,2},{1,3},{2,0},{3,1},{4,6},{5,7},{6,4},{7,5},{8,10},{9,11},{10,... | collective-permute-start | bytes 4616 | tf_op jit(solution)/shard_map/ppermute | solution.py:30
  80.7 4.1 %collective-permute-start.7 = (f32[3,128]{1,0:T(4,128)S(1)}, f32[3,128]{1,0:T(4,128)S(1)}, u32[]{:S(2)}, u32[]{:S(2)}) collective-permute-start(f32[3,128]{1,0:T(4,128)S(1)} %pad_maximum_fusion.5), channel_id=1, source_target_pairs={{0,4},{1,5},{2,6},{3,7},{4,0},{5,1},{6,2},{7,3},{8,12},{9,13},{10,... | collective-permute-start | bytes 4616 | tf_op jit(solution)/shard_map/ppermute | solution.py:30
  84.8 5.5 %collective-permute-start.8 = (f32[3,128]{1,0:T(4,128)S(1)}, f32[3,128]{1,0:T(4,128)S(1)}, u32[]{:S(2)}, u32[]{:S(2)}) collective-permute-start(f32[3,128]{1,0:T(4,128)S(1)} %pad_maximum_fusion.6), channel_id=1, source_target_pairs={{0,8},{1,9},{2,10},{3,11},{4,12},{5,13},{6,14},{7,15},{8,0},{9,1},... | collective-permute-start | bytes 4616 | tf_op jit(solution)/shard_map/ppermute | solution.py:30
  94.3 2.0 %copy-start = (f32[128,2,4096]{0,2,1:T(8,128)}, f32[128,2,4096]{0,2,1:T(8,128)S(1)}, u32[]{:S(2)}) copy-start(f32[128,2,4096]{0,2,1:T(8,128)S(1)} %fusion.1) | copy-start | bytes 12582916
  96.5 2.7 %collective-permute-start.9 = (bf16[128,8,512]{0,2,1:T(8,128)(2,1)S(1)}, bf16[128,8,512]{0,2,1:T(8,128)(2,1)S(1)}, u32[]{:S(2)}, u32[]{:S(2)}) collective-permute-start(bf16[128,8,512]{0,2,1:T(8,128)(2,1)S(1)} %fusion.9), channel_id=1, source_target_pairs={{0,1},{1,0},{2,3},{3,2},{4,5},{5,4},{6,7},{7,6},{8,9},{9,8},{10,11... | collective-permute-start | bytes 3145736 | tf_op jit(solution)/shard_map/ppermute | solution.py:54
  96.9 38.5 %collective-permute-start.14 = (bf16[128,4096]{0,1:T(8,128)(2,1)}, bf16[128,4096]{0,1:T(8,128)(2,1)}, u32[]{:S(2)}, u32[]{:S(2)}) collective-permute-start(bf16[128,4096]{0,1:T(8,128)(2,1)} %get-tuple-element.19), channel_id=1, source_target_pairs={{0,16},{16,0},{1,17},{17,1},{2,18},{18,2},{3,19},{19,3},{4,20},{20... | collective-permute-start | bytes 3145736 | tf_op jit(solution)/shard_map/ppermute | solution.py:130
  98.5 25.5 %collective-permute-start.13 = (bf16[1,128,256]{2,1,0:T(8,128)(2,1)S(1)}, bf16[1,128,256]{2,1,0:T(8,128)(2,1)S(1)}, u32[]{:S(2)}, u32[]{:S(2)}) collective-permute-start(bf16[1,128,256]{2,1,0:T(8,128)(2,1)S(1)} %bitcast.283), channel_id=1, source_target_pairs={{0,16},{16,0},{1,17},{17,1},{2,18},{18,2},{3,19},{19,3},{4,20},{20... | collective-permute-start | bytes 196616 | tf_op jit(solution)/shard_map/ppermute | solution.py:88
  105.1 19.0 %collective-permute-start.10 = (bf16[128,4,512]{2,0,1:T(8,128)(2,1)S(1)}, bf16[128,4,512]{2,0,1:T(8,128)(2,1)S(1)}, u32[]{:S(2)}, u32[]{:S(2)}) collective-permute-start(bf16[128,4,512]{2,0,1:T(8,128)(2,1)S(1)} %fusion.10), channel_id=1, source_target_pairs={{0,2},{1,3},{2,0},{3,1},{4,6},{5,7},{6,4},{7,5},{8,10},{9,11},{10,... | collective-permute-start | bytes 1572872 | tf_op jit(solution)/shard_map/ppermute | solution.py:54
  124.4 7.8 %collective-permute-start.11 = (bf16[128,2,512]{2,0,1:T(8,128)(2,1)S(1)}, bf16[128,2,512]{2,0,1:T(8,128)(2,1)S(1)}, u32[]{:S(2)}, u32[]{:S(2)}) collective-permute-start(bf16[128,2,512]{2,0,1:T(8,128)(2,1)S(1)} %fusion.17), channel_id=1, source_target_pairs={{0,4},{1,5},{2,6},{3,7},{4,0},{5,1},{6,2},{7,3},{8,12},{9,13},{10,... | collective-permute-start | bytes 786440 | tf_op jit(solution)/shard_map/ppermute | solution.py:54
  132.4 10.0 %collective-permute-start.12 = (bf16[128,1,512]{2,0,1:T(8,128)(2,1)S(1)}, bf16[128,1,512]{2,0,1:T(8,128)(2,1)S(1)}, u32[]{:S(2)}, u32[]{:S(2)}) collective-permute-start(bf16[128,1,512]{2,0,1:T(8,128)(2,1)S(1)} %fusion.19), channel_id=1, source_target_pairs={{0,8},{1,9},{2,10},{3,11},{4,12},{5,13},{6,14},{7,15},{8,0},{9,1},... | collective-permute-start | bytes 393224 | tf_op jit(solution)/shard_map/ppermute | solution.py:54

commit v15 on v14

--- a/solution.py
+++ b/solution.py
@@ -139,7 +139,15 @@
             picks = lax.dynamic_index_in_dim(slot_rows, tile, 0, keepdims=False)
             return jnp.take(blocks, picks, axis=0, mode="clip").reshape(width, piece)
 
-        got_w = lax.ppermute(rows_of(1 - dp_row), "dp", [(0, 1), (1, 0)])
+        partner_slots = lax.dynamic_index_in_dim(slot_rows, 1 - dp_row, 0, keepdims=False)
+        got_w = jnp.concatenate([
+            lax.ppermute(
+                lax.dynamic_index_in_dim(blocks, partner_slots[q], 0, keepdims=False),
+                "dp",
+                [(0, 1), (1, 0)],
+            )
+            for q in range(SLOTS)
+        ])
         own_w = rows_of(dp_row)
         held_w = jnp.stack([own_w, got_w])
     else:

time: 144 us -> 144 us (level)
  between operations: 1.11 us -> 5.02 us
  starting transfers between devices: 22.6 us -> 18.8 us
  local copies, waits for them, and re-layouts: 18.5 us -> 20.9 us
  waiting for transfers between devices: 69.7 us -> 68.1 us
    gather x2 -> x1, local copies, waits for them, and re-layouts: 9.48 us -> 4.06 us  [rows_of(): return jnp.take(blocks, picks, axis=0, mode='clip').reshape(width, piece)]
    ppermute x4, starting transfers between devices: 7.25 us -> 3.65 us  [combine_stats(): lax.ppermute(jnp.stack([top, total, picked]), 'vocab', [(k, k ^ bit) for...]
    squeeze x0 -> x1, local copies, waits for them, and re-layouts: none -> 3.11 us  [shards(): lax.dynamic_index_in_dim(blocks, partner_slots[q], 0, keepdims=False)]
    concatenate x0 -> x1, local copies, waits for them, and re-layouts: none -> 2.34 us  [shards(): jnp.concatenate([lax.ppermute(lax.dynamic_index_in_dim(blocks, partner_sl...]
    ppermute x4, waiting for transfers between devices: 7.19 us -> 9.42 us  [combine_stats(): lax.ppermute(jnp.stack([top, total, picked]), 'vocab', [(k, k ^ bit) for...]
    unnamed x8 -> x11, local copies, waits for them, and re-layouts: 2.53 us -> 4.4 us
    ppermute x1 -> x2, waiting for transfers between devices: 22.8 us -> 21.1 us  [shards(): lax.ppermute(lax.dynamic_index_in_dim(blocks, partner_slots[q], 0, keepdi...]
    ppermute x4, starting transfers between devices: 5.2 us -> 3.65 us  [halving_scatter(): lax.ppermute(send.astype(jnp.bfloat16), 'vocab', [(k, k ^ bit) for k in r...]
  transfers between devices with their start and end apart: 15 -> 16, of which waited for: 11 -> 11; matrix products, arithmetic and copies ran while one was open for 27% -> 22% of each run, Pallas kernels for 0% -> 0%
where the time goes in v15:
time: 144 us; the launch traced here: 143 us
  waiting for transfers between devices  68.1 us (47%)
  local copies, waits for them, and re-layouts  20.9 us (15%)
  starting transfers between devices  18.8 us (13%)
  matrix products  16 us (11%)
  other arithmetic  14.4 us (10%)
  between operations  5.02 us (3%)
    ppermute x2, waiting for transfers between devices, shards(): lax.ppermute(lax.dynamic_index_in_dim(blocks, partner_slots[q], 0, keepdi...  21.1 us
    ppermute x1, waiting for transfers between devices, doubling_gather(): got = lax.ppermute(held, 'dp', [(k, k ^ bit) for k in range(n)])  17.4 us
    ppermute x4, waiting for transfers between devices, doubling_rows(): got = lax.ppermute(held, 'vocab', [(k, k ^ bit) for k in range(n)])  13.8 us
    ppermute x4, waiting for transfers between devices, combine_stats(): lax.ppermute(jnp.stack([top, total, picked]), 'vocab', [(k, k ^ bit) for...  9.42 us
    ppermute x4, starting transfers between devices, doubling_rows(): got = lax.ppermute(held, 'vocab', [(k, k ^ bit) for k in range(n)])  7.4 us
    dot_general x1, matrix products, weight_grad(): jnp.einsum('tr,td->rd', jnp.concatenate([mine_p, other_p]), jnp.concatena...  7.04 us
    ppermute x4, waiting for transfers between devices, halving_scatter(): lax.ppermute(send.astype(jnp.bfloat16), 'vocab', [(k, k ^ bit) for k in r...  6.42 us
    unnamed x11, local copies, waits for them, and re-layouts  4.4 us
  transfers between devices with their start and end apart: 16, of which 11 were waited for; matrix products, arithmetic and copies ran while one was open for 22% of the time, Pallas kernels for 0%

profile of v15, /device:TPU:0, one launch (start us, length us, event | category | flops | bytes accessed | tf_op | source)
XLA Modules:
  0.0 143.3 jit_solution(2253054468910676395)
XLA Ops:
  0.6 4.1 %collective-permute-start = (bf16[128,1,512]{2,0,1:T(8,128)(2,1)}, bf16[128,1,512]{2,0,1:T(8,128)(2,1)S(1)}, u32[]{:S(2)}, u32[]{:S(2)}) collective-permute-start(bf16[128,1,512]{2,0,1:T(8,128)(2,1)} %bitcast.287), channel_id=1, source_target_pairs={{0,8},{1,9},{2,10},{3,11},{4,12},{5,13},{6,14},{7,15},{8,0},{9,1},... | collective-permute-start | bytes 393224 | tf_op jit(solution)/shard_map/ppermute | solution.py:71
  11.0 3.1 %dynamic-slice_bitcast_fusion = (bf16[128,4096]{1,0:T(8,128)(2,1)}, bf16[128,4096]{1,0:T(8,128)(2,1)}) fusion(bf16[8,128,4096]{2,1,0:T(8,128)(2,1)} %bitcast.280, s32[]{:T(128)S(6)} %select_n.325, s32[]{:T(128)S(6)} %select_n.324), kind=kLoop, calls=%fused_computation.20 | loop fusion | bytes 4194312 | tf_op jit(solution)/shard_map/jit(dynamic_index_in_dim)/squeeze | solution.py:145
  14.1 1.5 %collective-permute-start.5 = (bf16[128,4096]{1,0:T(8,128)(2,1)}, bf16[128,4096]{1,0:T(8,128)(2,1)}, u32[]{:S(2)}, u32[]{:S(2)}) collective-permute-start(bf16[128,4096]{1,0:T(8,128)(2,1)} %get-tuple-element.19), channel_id=1, source_target_pairs={{0,16},{16,0},{1,17},{17,1},{2,18},{18,2},{3,19},{19,3},{4,20},{20... | collective-permute-start | bytes 3145736 | tf_op jit(solution)/shard_map/ppermute | solution.py:144
  16.5 1.6 %collective-permute-start.1 = (bf16[128,2,512]{2,0,1:T(8,128)(2,1)S(1)}, bf16[128,2,512]{2,0,1:T(8,128)(2,1)S(1)}, u32[]{:S(2)}, u32[]{:S(2)}) collective-permute-start(bf16[128,2,512]{2,0,1:T(8,128)(2,1)S(1)} %maximum_bitcast_fusion), channel_id=1, source_target_pairs={{0,4},{1,5},{2,6},{3,7},{4,0},{5,1},{6,2},{7,3},{8,12},{9,13},{10,... | collective-permute-start | bytes 786440 | tf_op jit(solution)/shard_map/ppermute | solution.py:71
  18.1 5.6 %collective-permute-done.1 = bf16[128,2,512]{2,0,1:T(8,128)(2,1)S(1)} collective-permute-done((bf16[128,2,512]{2,0,1:T(8,128)(2,1)S(1)}, bf16[128,2,512]{2,0,1:T(8,128)(2,1)S(1)}, u32[]{:S(2)}, u32[]{:S(2)}) %collective-permute-start.1) | collective-permute-done | bytes 262176 | tf_op jit(solution)/shard_map/ppermute | solution.py:71
  23.9 1.6 %collective-permute-start.2 = (bf16[128,4,512]{2,0,1:T(8,128)(2,1)S(1)}, bf16[128,4,512]{2,0,1:T(8,128)(2,1)S(1)}, u32[]{:S(2)}, u32[]{:S(2)}) collective-permute-start(bf16[128,4,512]{2,0,1:T(8,128)(2,1)S(1)} %bitcast.279), channel_id=1, source_target_pairs={{0,2},{1,3},{2,0},{3,1},{4,6},{5,7},{6,4},{7,5},{8,10},{9,11},{10,... | collective-permute-start | bytes 1572872 | tf_op jit(solution)/shard_map/ppermute | solution.py:71
  25.7 2.0 %fusion = f32[128,1,256]{2,1,0:T(1,128)S(1)} fusion(bf16[128,64,1]{1,2,0:T(2,128)(2,1)S(1)} %copy.97, s32[128,64]{1,0:T(8,128)S(1)} %copy.83), kind=kOutput, calls=%fused_computation.2 | convolution fusion | flops 6291456 | bytes 180224 | tf_op jit(solution)/shard_map/tk,tkr->tr/dot_general | solution.py:170
  27.8 8.2 %collective-permute-done.2 = bf16[128,4,512]{2,0,1:T(8,128)(2,1)S(1)} collective-permute-done((bf16[128,4,512]{2,0,1:T(8,128)(2,1)S(1)}, bf16[128,4,512]{2,0,1:T(8,128)(2,1)S(1)}, u32[]{:S(2)}, u32[]{:S(2)}) %collective-permute-start.2) | collective-permute-done | bytes 524320 | tf_op jit(solution)/shard_map/ppermute | solution.py:71
  36.4 4.1 %gather_fusion = bf16[2,128,4096]{2,1,0:T(8,128)(2,1)S(1)} fusion(bf16[8,128,4096]{2,1,0:T(8,128)(2,1)} %bitcast.281, s32[1024]{0:T(1024)S(1)} %pad_clamp_fusion), kind=kCustom, calls=%fused_computation | custom fusion | bytes 4194312 | tf_op jit(solution)/shard_map/jit(_take)/gather | solution.py:140
  40.4 21.1 %collective-permute-done.4 = bf16[128,4096]{1,0:T(8,128)(2,1)} collective-permute-done((bf16[128,4096]{1,0:T(8,128)(2,1)}, bf16[128,4096]{1,0:T(8,128)(2,1)}, u32[]{:S(2)}, u32[]{:S(2)}) %collective-permute-start.4) | collective-permute-done | bytes 1048608 | tf_op jit(solution)/shard_map/ppermute | solution.py:144
  61.5 2.3 %constant_dynamic-update-slice_fusion.1 = bf16[256,4096]{1,0:T(8,128)(2,1)} fusion(bf16[128,4096]{1,0:T(8,128)(2,1)} %collective-permute-done.4), kind=kLoop, calls=%fused_computation.81 | loop fusion | bytes 2097152
  63.8 2.3 %constant_dynamic-update-slice_fusion = bf16[256,4096]{1,0:T(8,128)(2,1)} fusion(bf16[256,4096]{1,0:T(8,128)(2,1)} %constant_dynamic-update-slice_fusion.1, bf16[128,4096]{1,0:T(8,128)(2,1)} %collective-permute-done.5), kind=kLoop, calls=%fused_computation.80 | loop fusion | bytes 2097152 | tf_op jit(solution)/shard_map/concatenate | solution.py:143
  66.2 1.4 select_bitcast_fusion.3
  67.5 1.5 %pad_maximum_fusion = bf16[128,8,2,512]{3,0,1,2:T(8,128)(2,1)} fusion(bf16[128,8,1,512]{3,0,1,2:T(8,128)(2,1)S(1)} %get-tuple-element.24, bf16[128,8,1,512]{3,0,1,2:T(8,128)(2,1)S(1)} %get-tuple-element.23), kind=kLoop, calls=%fused_computation.9 | loop fusion | flops 1048576 | bytes 4194304 | tf_op jit(solution)/shard_map/stack | solution.py:75
  69.0 3.9 %copy.81 = bf16[128,8,2,512]{0,3,2,1:T(8,128)(2,1)} copy(bf16[128,8,2,512]{3,0,1,2:T(8,128)(2,1)} %pad_maximum_fusion) | data formatting | bytes 4194304 | tf_op jit(solution)/shard_map/stack | solution.py:75
  72.9 2.6 %select_bitcast_fusion = (bf16[128,4096]{0,1:T(8,128)(2,1)}, bf16[128,4096]{0,1:T(8,128)(2,1)S(1)}) fusion(pred[]{:T(512)S(6)} %eq.132, bf16[128,2,4096]{0,2,1:T(8,128)(2,1)} %bitcast.275), kind=kLoop, calls=%fused_computation.22 | loop fusion | flops 1048576 | bytes 4194305 | tf_op jit(solution)/shard_map/jit(_where)/select_n | solution.py:129
  76.4 2.8 %select_reduce_fusion.1 = (f32[128]{0:T(128)S(1)}, f32[128,256]{1,0:T(8,128)S(1)}) fusion(pred[256]{0:T(512)(128)(4,1)S(1)} %broadcast_bitcast_fusion, f32[128,256]{1,0:T(8,128)S(1)} %fusion.62, bf16[128,4096]{0,1:T(8,128)(2,1)} %get-tuple-element.21, bf16[256,4096]{1,0:T(8,128)(2,1)} %constant_dynamic-update-slice_fusion), kind=kOutput, calls=%fused_computation.60 | convolution fusion | flops 268533632 | bytes 3408640 | tf_op jit(solution)/shard_map/td,rd->tr/dot_general | solution.py:158
  80.7 1.6 %collective-permute-start.7 = (f32[3,128]{1,0:T(4,128)S(1)}, f32[3,128]{1,0:T(4,128)S(1)}, u32[]{:S(2)}, u32[]{:S(2)}) collective-permute-start(f32[3,128]{1,0:T(4,128)S(1)} %pad_maximum_fusion.4), channel_id=1, source_target_pairs={{0,2},{1,3},{2,0},{3,1},{4,6},{5,7},{6,4},{7,5},{8,10},{9,11},{10,... | collective-permute-start | bytes 4616 | tf_op jit(solution)/shard_map/ppermute | solution.py:30
  82.3 2.1 %collective-permute-done.7 = f32[3,128]{1,0:T(4,128)S(1)} collective-permute-done((f32[3,128]{1,0:T(4,128)S(1)}, f32[3,128]{1,0:T(4,128)S(1)}, u32[]{:S(2)}, u32[]{:S(2)}) %collective-permute-start.7) | collective-permute-done | bytes 1568 | tf_op jit(solution)/shard_map/ppermute | solution.py:30
  84.4 1.6 %collective-permute-start.8 = (f32[3,128]{1,0:T(4,128)S(1)}, f32[3,128]{1,0:T(4,128)S(1)}, u32[]{:S(2)}, u32[]{:S(2)}) collective-permute-start(f32[3,128]{1,0:T(4,128)S(1)} %pad_maximum_fusion.5), channel_id=1, source_target_pairs={{0,4},{1,5},{2,6},{3,7},{4,0},{5,1},{6,2},{7,3},{8,12},{9,13},{10,... | collective-permute-start | bytes 4616 | tf_op jit(solution)/shard_map/ppermute | solution.py:30
  86.0 2.0 %collective-permute-done.8 = f32[3,128]{1,0:T(4,128)S(1)} collective-permute-done((f32[3,128]{1,0:T(4,128)S(1)}, f32[3,128]{1,0:T(4,128)S(1)}, u32[]{:S(2)}, u32[]{:S(2)}) %collective-permute-start.8) | collective-permute-done | bytes 1568 | tf_op jit(solution)/shard_map/ppermute | solution.py:30
  88.4 4.2 %collective-permute-done.9 = f32[3,128]{1,0:T(4,128)S(1)} collective-permute-done((f32[3,128]{1,0:T(4,128)S(1)}, f32[3,128]{1,0:T(4,128)S(1)}, u32[]{:S(2)}, u32[]{:S(2)}) %collective-permute-start.9) | collective-permute-done | bytes 1568 | tf_op jit(solution)/shard_map/ppermute | solution.py:30
  93.2 3.4 %fusion.1 = f32[128,2,4096]{0,2,1:T(8,128)S(1)} fusion(bf16[1,256,4096]{2,1,0:T(8,128)(2,1)} %bitcast.45, bf16[1,256,4096]{2,1,0:T(8,128)(2,1)S(1)} %bitcast.272, bf16[128,256]{1,0:T(8,128)(2,1)S(1)} %fusion.22), kind=kOutput, calls=%fused_computation.4 | convolution fusion | flops 545259520 | bytes 8454144 | tf_op jit(solution)/shard_map/tr,krd->tkd/dot_general | solution.py:181
  96.6 2.0 %copy-done = f32[128,2,4096]{0,2,1:T(8,128)} copy-done((f32[128,2,4096]{0,2,1:T(8,128)}, f32[128,2,4096]{0,2,1:T(8,128)S(1)}, u32[]{:S(2)}) %copy-start) | copy-done | bytes 4194328
  99.3 1.5 %collective-permute-start.15 = (bf16[128,4096]{0,1:T(8,128)(2,1)}, bf16[128,4096]{0,1:T(8,128)(2,1)}, u32[]{:S(2)}, u32[]{:S(2)}) collective-permute-start(bf16[128,4096]{0,1:T(8,128)(2,1)} %get-tuple-element.21), channel_id=1, source_target_pairs={{0,16},{16,0},{1,17},{17,1},{2,18},{18,2},{3,19},{19,3},{4,20},{20... | collective-permute-start | bytes 3145736 | tf_op jit(solution)/shard_map/ppermute | solution.py:130
  101.5 3.8 %bitcast_add_fusion = f32[128,8,512]{0,2,1:T(8,128)} fusion(bf16[128,8,512]{0,2,1:T(8,128)(2,1)S(1)} %collective-permute-done.10, f32[128,8,2,512]{0,3,2,1:T(8,128)} %bitcast.270, pred[]{:T(512)S(6)} %eq.146), kind=kLoop, calls=%fused_computation.13 | loop fusion | flops 1572864 | bytes 7340033 | tf_op jit(solution)/shard_map/add | solution.py:57
  105.4 1.9 %copy.87 = f32[128,8,512]{2,0,1:T(8,128)S(1)} copy(f32[128,8,512]{0,2,1:T(8,128)} %bitcast_add_fusion) | data formatting | bytes 4194304 | tf_op jit(solution)/shard_map/add | solution.py:57
  107.4 1.6 %collective-permute-start.11 = (bf16[128,4,512]{2,0,1:T(8,128)(2,1)S(1)}, bf16[128,4,512]{2,0,1:T(8,128)(2,1)S(1)}, u32[]{:S(2)}, u32[]{:S(2)}) collective-permute-start(bf16[128,4,512]{2,0,1:T(8,128)(2,1)S(1)} %fusion.10), channel_id=1, source_target_pairs={{0,2},{1,3},{2,0},{3,1},{4,6},{5,7},{6,4},{7,5},{8,10},{9,11},{10,... | collective-permute-start | bytes 1572872 | tf_op jit(solution)/shard_map/ppermute | solution.py:54
  109.0 17.4 %collective-permute-done.14 = bf16[1,128,256]{2,1,0:T(8,128)(2,1)S(1)} collective-permute-done((bf16[1,128,256]{2,1,0:T(8,128)(2,1)S(1)}, bf16[1,128,256]{2,1,0:T(8,128)(2,1)S(1)}, u32[]{:S(2)}, u32[]{:S(2)}) %collective-permute-start.14) | collective-permute-done | bytes 65568 | tf_op jit(solution)/shard_map/ppermute | solution.py:88
  126.8 1.6 %collective-permute-start.12 = (bf16[128,2,512]{2,0,1:T(8,128)(2,1)S(1)}, bf16[128,2,512]{2,0,1:T(8,128)(2,1)S(1)}, u32[]{:S(2)}, u32[]{:S(2)}) collective-permute-start(bf16[128,2,512]{2,0,1:T(8,128)(2,1)S(1)} %fusion.17), channel_id=1, source_target_pairs={{0,4},{1,5},{2,6},{3,7},{4,0},{5,1},{6,2},{7,3},{8,12},{9,13},{10,... | collective-permute-start | bytes 786440 | tf_op jit(solution)/shard_map/ppermute | solution.py:54
  128.7 5.8 %collective-permute-done.12 = bf16[128,2,512]{2,0,1:T(8,128)(2,1)S(1)} collective-permute-done((bf16[128,2,512]{2,0,1:T(8,128)(2,1)S(1)}, bf16[128,2,512]{2,0,1:T(8,128)(2,1)S(1)}, u32[]{:S(2)}, u32[]{:S(2)}) %collective-permute-start.12) | collective-permute-done | bytes 262176 | tf_op jit(solution)/shard_map/ppermute | solution.py:54
  135.1 7.0 %convolution_convert_fusion = bf16[1024,4096]{1,0:T(8,128)(2,1)} fusion(bf16[128,4096]{0,1:T(8,128)(2,1)} %collective-permute-done.15, bf16[128,4096]{0,1:T(8,128)(2,1)S(1)} %get-tuple-element.22, bf16[128,1024]{1,0:T(8,128)(2,1)S(1)} %bitcast.283, bf16[128,1024]{1,0:T(8,128)(2,1)S(1)} %bitcast.282), kind=kOutput, calls=%fused_computation.3 | convolution fusion | flops 2156920832 | bytes 11010048 | tf_op jit(solution)/shard_map/tr,td->rd/dot_general | solution.py:207
  (78 shorter events, 10.9 us)
Async XLA Ops:
  0.6 15.8 %collective-permute-start = (bf16[128,1,512]{2,0,1:T(8,128)(2,1)}, bf16[128,1,512]{2,0,1:T(8,128)(2,1)S(1)}, u32[]{:S(2)}, u32[]{:S(2)}) collective-permute-start(bf16[128,1,512]{2,0,1:T(8,128)(2,1)} %bitcast.287), channel_id=1, source_target_pairs={{0,8},{1,9},{2,10},{3,11},{4,12},{5,13},{6,14},{7,15},{8,0},{9,1},... | collective-permute-start | bytes 393224 | tf_op jit(solution)/shard_map/ppermute | solution.py:71
  11.0 5.2 %copy-start.1 = (f32[128,64]{0,1:T(8,128)S(1)}, f32[128,64]{0,1:T(8,128)}, u32[]{:S(2)}) copy-start(f32[128,64]{0,1:T(8,128)} %param.8) | copy-start | bytes 98308
  11.0 5.2 %copy-start.3 = (s32[128,64]{0,1:T(8,128)S(1)}, s32[128,64]{0,1:T(8,128)}, u32[]{:S(2)}) copy-start(s32[128,64]{0,1:T(8,128)} %param.7) | copy-start | bytes 98308
  11.0 5.4 %copy-start.2 = (bf16[128,512]{1,0:T(8,128)(2,1)S(1)}, bf16[128,512]{1,0:T(8,128)(2,1)}, u32[]{:S(2)}) copy-start(bf16[128,512]{1,0:T(8,128)(2,1)} %param.5) | copy-start | bytes 393220
  14.1 49.7 %collective-permute-start.5 = (bf16[128,4096]{1,0:T(8,128)(2,1)}, bf16[128,4096]{1,0:T(8,128)(2,1)}, u32[]{:S(2)}, u32[]{:S(2)}) collective-permute-start(bf16[128,4096]{1,0:T(8,128)(2,1)} %get-tuple-element.19), channel_id=1, source_target_pairs={{0,16},{16,0},{1,17},{17,1},{2,18},{18,2},{3,19},{19,3},{4,20},{20... | collective-permute-start | bytes 3145736 | tf_op jit(solution)/shard_map/ppermute | solution.py:144
  15.6 45.9 %collective-permute-start.4 = (bf16[128,4096]{1,0:T(8,128)(2,1)}, bf16[128,4096]{1,0:T(8,128)(2,1)}, u32[]{:S(2)}, u32[]{:S(2)}) collective-permute-start(bf16[128,4096]{1,0:T(8,128)(2,1)} %get-tuple-element.20), channel_id=1, source_target_pairs={{0,16},{16,0},{1,17},{17,1},{2,18},{18,2},{3,19},{19,3},{4,20},{20... | collective-permute-start | bytes 3145736 | tf_op jit(solution)/shard_map/ppermute | solution.py:144
  16.5 7.3 %collective-permute-start.1 = (bf16[128,2,512]{2,0,1:T(8,128)(2,1)S(1)}, bf16[128,2,512]{2,0,1:T(8,128)(2,1)S(1)}, u32[]{:S(2)}, u32[]{:S(2)}) collective-permute-start(bf16[128,2,512]{2,0,1:T(8,128)(2,1)S(1)} %maximum_bitcast_fusion), channel_id=1, source_target_pairs={{0,4},{1,5},{2,6},{3,7},{4,0},{5,1},{6,2},{7,3},{8,12},{9,13},{10,... | collective-permute-start | bytes 786440 | tf_op jit(solution)/shard_map/ppermute | solution.py:71
  23.9 12.1 %collective-permute-start.2 = (bf16[128,4,512]{2,0,1:T(8,128)(2,1)S(1)}, bf16[128,4,512]{2,0,1:T(8,128)(2,1)S(1)}, u32[]{:S(2)}, u32[]{:S(2)}) collective-permute-start(bf16[128,4,512]{2,0,1:T(8,128)(2,1)S(1)} %bitcast.279), channel_id=1, source_target_pairs={{0,2},{1,3},{2,0},{3,1},{4,6},{5,7},{6,4},{7,5},{8,10},{9,11},{10,... | collective-permute-start | bytes 1572872 | tf_op jit(solution)/shard_map/ppermute | solution.py:71
  36.3 29.9 %collective-permute-start.3 = (bf16[128,8,512]{2,0,1:T(8,128)(2,1)S(1)}, bf16[128,8,512]{2,0,1:T(8,128)(2,1)}, u32[]{:S(2)}, u32[]{:S(2)}) collective-permute-start(bf16[128,8,512]{2,0,1:T(8,128)(2,1)S(1)} %bitcast.278), channel_id=1, source_target_pairs={{0,1},{1,0},{2,3},{3,2},{4,5},{5,4},{6,7},{7,6},{8,9},{9,8},{10,11... | collective-permute-start | bytes 3145736 | tf_op jit(solution)/shard_map/ppermute | solution.py:71
  79.4 1.2 collective-permute-start.6
  80.7 3.7 %collective-permute-start.7 = (f32[3,128]{1,0:T(4,128)S(1)}, f32[3,128]{1,0:T(4,128)S(1)}, u32[]{:S(2)}, u32[]{:S(2)}) collective-permute-start(f32[3,128]{1,0:T(4,128)S(1)} %pad_maximum_fusion.4), channel_id=1, source_target_pairs={{0,2},{1,3},{2,0},{3,1},{4,6},{5,7},{6,4},{7,5},{8,10},{9,11},{10,... | collective-permute-start | bytes 4616 | tf_op jit(solution)/shard_map/ppermute | solution.py:30
  84.4 3.7 %collective-permute-start.8 = (f32[3,128]{1,0:T(4,128)S(1)}, f32[3,128]{1,0:T(4,128)S(1)}, u32[]{:S(2)}, u32[]{:S(2)}) collective-permute-start(f32[3,128]{1,0:T(4,128)S(1)} %pad_maximum_fusion.5), channel_id=1, source_target_pairs={{0,4},{1,5},{2,6},{3,7},{4,0},{5,1},{6,2},{7,3},{8,12},{9,13},{10,... | collective-permute-start | bytes 4616 | tf_op jit(solution)/shard_map/ppermute | solution.py:30
  88.0 4.5 %collective-permute-start.9 = (f32[3,128]{1,0:T(4,128)S(1)}, f32[3,128]{1,0:T(4,128)S(1)}, u32[]{:S(2)}, u32[]{:S(2)}) collective-permute-start(f32[3,128]{1,0:T(4,128)S(1)} %pad_maximum_fusion.6), channel_id=1, source_target_pairs={{0,8},{1,9},{2,10},{3,11},{4,12},{5,13},{6,14},{7,15},{8,0},{9,1},... | collective-permute-start | bytes 4616 | tf_op jit(solution)/shard_map/ppermute | solution.py:30
  96.6 2.0 %copy-start = (f32[128,2,4096]{0,2,1:T(8,128)}, f32[128,2,4096]{0,2,1:T(8,128)S(1)}, u32[]{:S(2)}) copy-start(f32[128,2,4096]{0,2,1:T(8,128)S(1)} %fusion.1) | copy-start | bytes 12582916
  98.8 2.7 %collective-permute-start.10 = (bf16[128,8,512]{0,2,1:T(8,128)(2,1)S(1)}, bf16[128,8,512]{0,2,1:T(8,128)(2,1)S(1)}, u32[]{:S(2)}, u32[]{:S(2)}) collective-permute-start(bf16[128,8,512]{0,2,1:T(8,128)(2,1)S(1)} %fusion.9), channel_id=1, source_target_pairs={{0,1},{1,0},{2,3},{3,2},{4,5},{5,4},{6,7},{7,6},{8,9},{9,8},{10,11... | collective-permute-start | bytes 3145736 | tf_op jit(solution)/shard_map/ppermute | solution.py:54
  99.3 35.8 %collective-permute-start.15 = (bf16[128,4096]{0,1:T(8,128)(2,1)}, bf16[128,4096]{0,1:T(8,128)(2,1)}, u32[]{:S(2)}, u32[]{:S(2)}) collective-permute-start(bf16[128,4096]{0,1:T(8,128)(2,1)} %get-tuple-element.21), channel_id=1, source_target_pairs={{0,16},{16,0},{1,17},{17,1},{2,18},{18,2},{3,19},{19,3},{4,20},{20... | collective-permute-start | bytes 3145736 | tf_op jit(solution)/shard_map/ppermute | solution.py:130
  100.8 25.5 %collective-permute-start.14 = (bf16[1,128,256]{2,1,0:T(8,128)(2,1)S(1)}, bf16[1,128,256]{2,1,0:T(8,128)(2,1)S(1)}, u32[]{:S(2)}, u32[]{:S(2)}) collective-permute-start(bf16[1,128,256]{2,1,0:T(8,128)(2,1)S(1)} %bitcast.286), channel_id=1, source_target_pairs={{0,16},{16,0},{1,17},{17,1},{2,18},{18,2},{3,19},{19,3},{4,20},{20... | collective-permute-start | bytes 196616 | tf_op jit(solution)/shard_map/ppermute | solution.py:88
  107.4 19.0 %collective-permute-start.11 = (bf16[128,4,512]{2,0,1:T(8,128)(2,1)S(1)}, bf16[128,4,512]{2,0,1:T(8,128)(2,1)S(1)}, u32[]{:S(2)}, u32[]{:S(2)}) collective-permute-start(bf16[128,4,512]{2,0,1:T(8,128)(2,1)S(1)} %fusion.10), channel_id=1, source_target_pairs={{0,2},{1,3},{2,0},{3,1},{4,6},{5,7},{6,4},{7,5},{8,10},{9,11},{10,... | collective-permute-start | bytes 1572872 | tf_op jit(solution)/shard_map/ppermute | solution.py:54
  126.8 7.8 %collective-permute-start.12 = (bf16[128,2,512]{2,0,1:T(8,128)(2,1)S(1)}, bf16[128,2,512]{2,0,1:T(8,128)(2,1)S(1)}, u32[]{:S(2)}, u32[]{:S(2)}) collective-permute-start(bf16[128,2,512]{2,0,1:T(8,128)(2,1)S(1)} %fusion.17), channel_id=1, source_target_pairs={{0,4},{1,5},{2,6},{3,7},{4,0},{5,1},{6,2},{7,3},{8,12},{9,13},{10,... | collective-permute-start | bytes 786440 | tf_op jit(solution)/shard_map/ppermute | solution.py:54
  134.7 7.8 %collective-permute-start.13 = (bf16[128,1,512]{2,0,1:T(8,128)(2,1)S(1)}, bf16[128,1,512]{2,0,1:T(8,128)(2,1)S(1)}, u32[]{:S(2)}, u32[]{:S(2)}) collective-permute-start(bf16[128,1,512]{2,0,1:T(8,128)(2,1)S(1)} %fusion.19), channel_id=1, source_target_pairs={{0,8},{1,9},{2,10},{3,11},{4,12},{5,13},{6,14},{7,15},{8,0},{9,1},... | collective-permute-start | bytes 393224 | tf_op jit(solution)/shard_map/ppermute | solution.py:54

commit v16 on v14

--- a/solution.py
+++ b/solution.py
@@ -141,7 +141,6 @@
 
         got_w = lax.ppermute(rows_of(1 - dp_row), "dp", [(0, 1), (1, 0)])
         own_w = rows_of(dp_row)
-        held_w = jnp.stack([own_w, got_w])
     else:
         rows_w = shift_exchange(chosen, 0)
     if pair:
@@ -170,7 +169,13 @@
     probs = jnp.where(col_mask[None, :], jnp.exp(logits - lse[:, None]), 0.0)
     dlog = (probs - target).astype(jnp.bfloat16)
     if pair:
-        hidden_terms = jnp.einsum("tr,krd->tkd", dlog, held_w, preferred_element_type=jnp.float32)
+        hidden_terms = jnp.stack(
+            [
+                jnp.einsum("tr,rd->td", dlog, own_w, preferred_element_type=jnp.float32),
+                jnp.einsum("tr,rd->td", dlog, got_w, preferred_element_type=jnp.float32),
+            ],
+            axis=1,
+        )
         flip = dp_row * (lax.axis_size("vocab") // 2)
     else:
         hidden_terms = jnp.einsum("tr,krd->tkd", dlog, rows_w, preferred_element_type=jnp.float32)

time: 144 us -> 151 us (1.049)
  other arithmetic: 15.3 us -> 19.8 us
  local copies, waits for them, and re-layouts: 18.5 us -> 22 us
    another operation x0 -> x1, local copies, waits for them, and re-layouts: none -> 5.6 us  [shards(): jnp.stack([jnp.einsum('tr,rd->td', dlog, own_w, preferred_element_type=jn...]
    another operation x0 -> x1, other arithmetic: none -> 2.3 us  [shards(): jnp.stack([jnp.einsum('tr,rd->td', dlog, own_w, preferred_element_type=jn...]
    convert_element_type x4, other arithmetic: 0.36 us -> 2.58 us  [halving_scatter(): send.astype(jnp.bfloat16)]
    unnamed x8 -> x6, local copies, waits for them, and re-layouts: 2.53 us -> 0.52 us
    dot_general x1 -> x2, matrix products: 3.36 us -> 2.49 us  [the longest x1 2.04 us: shards(): jnp.einsum('tr,rd->td', dlog, got_w, preferred_element_type=jnp.float32)]
  transfers between devices with their start and end apart: 15 -> 15, of which waited for: 11 -> 11; matrix products, arithmetic and copies ran while one was open for 27% -> 25% of each run, Pallas kernels for 0% -> 0%
where the time goes in v16:
time: 151 us; the launch traced here: 150 us
  waiting for transfers between devices  69.7 us (46%)
  starting transfers between devices  22.6 us (15%)
  local copies, waits for them, and re-layouts  22 us (15%)
  other arithmetic  19.8 us (13%)
  matrix products  15.2 us (10%)
    ppermute x1, waiting for transfers between devices, shards(): got_w = lax.ppermute(rows_of(1 - dp_row), 'dp', [(0, 1), (1, 0)])  22.8 us
    ppermute x1, waiting for transfers between devices, doubling_gather(): got = lax.ppermute(held, 'dp', [(k, k ^ bit) for k in range(n)])  18.4 us
    ppermute x4, waiting for transfers between devices, doubling_rows(): got = lax.ppermute(held, 'vocab', [(k, k ^ bit) for k in range(n)])  15.3 us
    gather x2, local copies, waits for them, and re-layouts, rows_of(): return jnp.take(blocks, picks, axis=0, mode='clip').reshape(width, piece)  9.47 us
    ppermute x4, starting transfers between devices, combine_stats(): lax.ppermute(jnp.stack([top, total, picked]), 'vocab', [(k, k ^ bit) for...  7.27 us
    ppermute x4, waiting for transfers between devices, combine_stats(): lax.ppermute(jnp.stack([top, total, picked]), 'vocab', [(k, k ^ bit) for...  7.18 us
    dot_general x1, matrix products, weight_grad(): jnp.einsum('tr,td->rd', jnp.concatenate([mine_p, other_p]), jnp.concatena...  7.04 us
    ppermute x4, starting transfers between devices, doubling_rows(): got = lax.ppermute(held, 'vocab', [(k, k ^ bit) for k in range(n)])  6.49 us
  transfers between devices with their start and end apart: 15, of which 11 were waited for; matrix products, arithmetic and copies ran while one was open for 25% of the time, Pallas kernels for 0%

profile of v16, /device:TPU:0, one launch (start us, length us, event | category | flops | bytes accessed | tf_op | source)
XLA Modules:
  0.0 150.4 jit_solution(13269643190893809756)
XLA Ops:
  0.6 4.1 %collective-permute-start = (bf16[128,1,512]{2,0,1:T(8,128)(2,1)}, bf16[128,1,512]{2,0,1:T(8,128)(2,1)S(1)}, u32[]{:S(2)}, u32[]{:S(2)}) collective-permute-start(bf16[128,1,512]{2,0,1:T(8,128)(2,1)} %bitcast.287), channel_id=1, source_target_pairs={{0,8},{1,9},{2,10},{3,11},{4,12},{5,13},{6,14},{7,15},{8,0},{9,1},... | collective-permute-start | bytes 393224 | tf_op jit(solution)/shard_map/ppermute | solution.py:71
  6.3 4.9 %collective-permute-done = bf16[128,1,512]{2,0,1:T(8,128)(2,1)S(1)} collective-permute-done((bf16[128,1,512]{2,0,1:T(8,128)(2,1)}, bf16[128,1,512]{2,0,1:T(8,128)(2,1)S(1)}, u32[]{:S(2)}, u32[]{:S(2)}) %collective-permute-start) | collective-permute-done | bytes 131104 | tf_op jit(solution)/shard_map/ppermute | solution.py:71
  13.3 6.5 %collective-permute-done.1 = bf16[128,2,512]{2,0,1:T(8,128)(2,1)S(1)} collective-permute-done((bf16[128,2,512]{2,0,1:T(8,128)(2,1)S(1)}, bf16[128,2,512]{2,0,1:T(8,128)(2,1)S(1)}, u32[]{:S(2)}, u32[]{:S(2)}) %collective-permute-start.1) | collective-permute-done | bytes 262176 | tf_op jit(solution)/shard_map/ppermute | solution.py:71
  19.9 1.4 collective-permute-start.2
  21.3 5.4 %gather_fusion.1 = bf16[2,128,4096]{2,1,0:T(8,128)(2,1)} fusion(bf16[8,128,4096]{2,1,0:T(8,128)(2,1)} %bitcast.280, s32[1024]{0:T(1024)S(1)} %get-tuple-element.45), kind=kCustom, calls=%fused_computation.1 | custom fusion | bytes 4194312 | tf_op jit(solution)/shard_map/jit(_take)/gather | solution.py:140
  26.7 1.5 %collective-permute-start.4 = (bf16[256,4096]{1,0:T(8,128)(2,1)}, bf16[256,4096]{1,0:T(8,128)(2,1)}, u32[]{:S(2)}, u32[]{:S(2)}) collective-permute-start(bf16[256,4096]{1,0:T(8,128)(2,1)} %bitcast.23), channel_id=1, source_target_pairs={{0,16},{16,0},{1,17},{17,1},{2,18},{18,2},{3,19},{19,3},{4,20},{20... | collective-permute-start | bytes 6291464 | tf_op jit(solution)/shard_map/ppermute | solution.py:142
  28.3 3.9 %collective-permute-done.2 = bf16[128,4,512]{2,0,1:T(8,128)(2,1)S(1)} collective-permute-done((bf16[128,4,512]{2,0,1:T(8,128)(2,1)S(1)}, bf16[128,4,512]{2,0,1:T(8,128)(2,1)S(1)}, u32[]{:S(2)}, u32[]{:S(2)}) %collective-permute-start.2) | collective-permute-done | bytes 524320 | tf_op jit(solution)/shard_map/ppermute | solution.py:71
  33.6 4.1 %gather_fusion = bf16[2,128,4096]{2,1,0:T(8,128)(2,1)S(1)} fusion(bf16[8,128,4096]{2,1,0:T(8,128)(2,1)} %bitcast.281, s32[1024]{0:T(1024)S(1)} %get-tuple-element.46), kind=kCustom, calls=%fused_computation | custom fusion | bytes 4194312 | tf_op jit(solution)/shard_map/jit(_take)/gather | solution.py:140
  37.7 2.0 %fusion = f32[128,1,256]{2,1,0:T(1,128)S(1)} fusion(bf16[128,64,1]{1,2,0:T(2,128)(2,1)S(1)} %copy.97, s32[128,64]{1,0:T(8,128)S(1)} %copy.83), kind=kOutput, calls=%fused_computation.3 | convolution fusion | flops 6291456 | bytes 180224 | tf_op jit(solution)/shard_map/tk,tkr->tr/dot_general | solution.py:161
  39.7 1.4 select_bitcast_fusion.3
  41.0 1.5 pad_maximum_fusion.1
  42.5 3.9 %copy.81 = bf16[128,8,2,512]{0,3,2,1:T(8,128)(2,1)} copy(bf16[128,8,2,512]{3,0,1,2:T(8,128)(2,1)} %pad_maximum_fusion.1) | data formatting | bytes 4194304 | tf_op jit(solution)/shard_map/stack | solution.py:75
  46.4 2.7 %select_bitcast_fusion = (bf16[128,4096]{0,1:T(8,128)(2,1)}, bf16[128,4096]{0,1:T(8,128)(2,1)S(1)}) fusion(pred[]{:T(512)S(6)} %eq.132, bf16[128,2,4096]{0,2,1:T(8,128)(2,1)} %bitcast.275), kind=kLoop, calls=%fused_computation.20 | loop fusion | flops 1048576 | bytes 4194305 | tf_op jit(solution)/shard_map/jit(_where)/select_n | solution.py:129
  49.9 22.8 %collective-permute-done.4 = bf16[256,4096]{1,0:T(8,128)(2,1)} collective-permute-done((bf16[256,4096]{1,0:T(8,128)(2,1)}, bf16[256,4096]{1,0:T(8,128)(2,1)}, u32[]{:S(2)}, u32[]{:S(2)}) %collective-permute-start.4) | collective-permute-done | bytes 2097184 | tf_op jit(solution)/shard_map/ppermute | solution.py:142
  72.7 2.8 %select_reduce_fusion.1 = (f32[128]{0:T(128)S(1)}, f32[128,256]{1,0:T(8,128)S(1)}) fusion(pred[256]{0:T(512)(128)(4,1)S(1)} %broadcast_bitcast_fusion, f32[128,256]{1,0:T(8,128)S(1)} %fusion.56, bf16[128,4096]{0,1:T(8,128)(2,1)} %get-tuple-element.19, bf16[256,4096]{1,0:T(8,128)(2,1)} %collective-permute-done.4), kind=kOutput, calls=%fused_computation.58 | convolution fusion | flops 268533632 | bytes 3408640 | tf_op jit(solution)/shard_map/td,rd->tr/dot_general | solution.py:149
  77.7 2.9 %collective-permute-done.6 = f32[3,128]{1,0:T(4,128)S(1)} collective-permute-done((f32[3,128]{1,0:T(4,128)S(1)}, f32[3,128]{1,0:T(4,128)S(1)}, u32[]{:S(2)}, u32[]{:S(2)}) %collective-permute-start.6) | collective-permute-done | bytes 1568 | tf_op jit(solution)/shard_map/ppermute | solution.py:30
  80.7 2.5 %collective-permute-start.7 = (f32[3,128]{1,0:T(4,128)S(1)}, f32[3,128]{1,0:T(4,128)S(1)}, u32[]{:S(2)}, u32[]{:S(2)}) collective-permute-start(f32[3,128]{1,0:T(4,128)S(1)} %pad_maximum_fusion.6), channel_id=1, source_target_pairs={{0,4},{1,5},{2,6},{3,7},{4,0},{5,1},{6,2},{7,3},{8,12},{9,13},{10,... | collective-permute-start | bytes 4616 | tf_op jit(solution)/shard_map/ppermute | solution.py:30
  83.2 1.6 %collective-permute-done.7 = f32[3,128]{1,0:T(4,128)S(1)} collective-permute-done((f32[3,128]{1,0:T(4,128)S(1)}, f32[3,128]{1,0:T(4,128)S(1)}, u32[]{:S(2)}, u32[]{:S(2)}) %collective-permute-start.7) | collective-permute-done | bytes 1568 | tf_op jit(solution)/shard_map/ppermute | solution.py:30
  84.8 3.9 %collective-permute-start.8 = (f32[3,128]{1,0:T(4,128)S(1)}, f32[3,128]{1,0:T(4,128)S(1)}, u32[]{:S(2)}, u32[]{:S(2)}) collective-permute-start(f32[3,128]{1,0:T(4,128)S(1)} %pad_maximum_fusion.7), channel_id=1, source_target_pairs={{0,8},{1,9},{2,10},{3,11},{4,12},{5,13},{6,14},{7,15},{8,0},{9,1},... | collective-permute-start | bytes 4616 | tf_op jit(solution)/shard_map/ppermute | solution.py:30
  88.7 1.6 %collective-permute-done.8 = f32[3,128]{1,0:T(4,128)S(1)} collective-permute-done((f32[3,128]{1,0:T(4,128)S(1)}, f32[3,128]{1,0:T(4,128)S(1)}, u32[]{:S(2)}, u32[]{:S(2)}) %collective-permute-start.8) | collective-permute-done | bytes 1568 | tf_op jit(solution)/shard_map/ppermute | solution.py:30
  91.4 2.0 %convolution_bitcast_fusion = f32[128,1,4096]{2,0,1:T(8,128)S(1)} fusion(bf16[128,256]{1,0:T(8,128)(2,1)S(1)} %fusion.18, bf16[256,4096]{1,0:T(8,128)(2,1)} %collective-permute-done.4), kind=kOutput, calls=%fused_computation.5 | convolution fusion | flops 268435456 | bytes 4259840 | tf_op jit(solution)/shard_map/tr,rd->td/dot_general | solution.py:175
  93.4 2.3 %pad_maximum_fusion = f32[128,2,4096]{2,0,1:T(8,128)} fusion(f32[128,1,4096]{2,0,1:T(8,128)S(1)} %convolution_bitcast_fusion, f32[128,1,4096]{2,0,1:T(8,128)S(1)} %convolution_bitcast_fusion.1), kind=kLoop, calls=%fused_computation.7 | loop fusion | flops 1048576 | bytes 8388608 | tf_op jit(solution)/shard_map/stack | solution.py:172
  95.7 5.6 %copy.84 = f32[128,2,4096]{0,2,1:T(8,128)} copy(f32[128,2,4096]{2,0,1:T(8,128)} %pad_maximum_fusion) | data formatting | bytes 8388608 | tf_op jit(solution)/shard_map/stack | solution.py:172
  101.3 2.4 %fusion.5 = bf16[128,8,512]{0,2,1:T(8,128)(2,1)S(1)} fusion(f32[128,8,2,512]{0,3,2,1:T(8,128)} %bitcast.269, pred[]{:T(512)S(6)} %eq.146), kind=kLoop, calls=%fused_computation.16 | loop fusion | flops 524288 | bytes 3145729 | tf_op jit(solution)/shard_map/convert_element_type | solution.py:55
  104.2 1.5 %collective-permute-start.14 = (bf16[128,4096]{0,1:T(8,128)(2,1)}, bf16[128,4096]{0,1:T(8,128)(2,1)}, u32[]{:S(2)}, u32[]{:S(2)}) collective-permute-start(bf16[128,4096]{0,1:T(8,128)(2,1)} %get-tuple-element.19), channel_id=1, source_target_pairs={{0,16},{16,0},{1,17},{17,1},{2,18},{18,2},{3,19},{19,3},{4,20},{20... | collective-permute-start | bytes 3145736 | tf_op jit(solution)/shard_map/ppermute | solution.py:130
  106.4 3.8 %bitcast_add_fusion = f32[128,8,512]{0,2,1:T(8,128)} fusion(bf16[128,8,512]{0,2,1:T(8,128)(2,1)S(1)} %collective-permute-done.9, f32[128,8,2,512]{0,3,2,1:T(8,128)} %bitcast.270, pred[]{:T(512)S(6)} %eq.146), kind=kLoop, calls=%fused_computation.13 | loop fusion | flops 1572864 | bytes 7340033 | tf_op jit(solution)/shard_map/add | solution.py:57
  110.2 1.9 %copy.87 = f32[128,8,512]{2,0,1:T(8,128)S(1)} copy(f32[128,8,512]{0,2,1:T(8,128)} %bitcast_add_fusion) | data formatting | bytes 4194304 | tf_op jit(solution)/shard_map/add | solution.py:57
  112.9 18.4 %collective-permute-done.13 = bf16[1,128,256]{2,1,0:T(8,128)(2,1)S(1)} collective-permute-done((bf16[1,128,256]{2,1,0:T(8,128)(2,1)S(1)}, bf16[1,128,256]{2,1,0:T(8,128)(2,1)S(1)}, u32[]{:S(2)}, u32[]{:S(2)}) %collective-permute-start.13) | collective-permute-done | bytes 65568 | tf_op jit(solution)/shard_map/ppermute | solution.py:88
  131.7 1.5 %collective-permute-start.11 = (bf16[128,2,512]{2,0,1:T(8,128)(2,1)S(1)}, bf16[128,2,512]{2,0,1:T(8,128)(2,1)S(1)}, u32[]{:S(2)}, u32[]{:S(2)}) collective-permute-start(bf16[128,2,512]{2,0,1:T(8,128)(2,1)S(1)} %fusion.13), channel_id=1, source_target_pairs={{0,4},{1,5},{2,6},{3,7},{4,0},{5,1},{6,2},{7,3},{8,12},{9,13},{10,... | collective-permute-start | bytes 786440 | tf_op jit(solution)/shard_map/ppermute | solution.py:54
  133.5 6.0 %collective-permute-done.11 = bf16[128,2,512]{2,0,1:T(8,128)(2,1)S(1)} collective-permute-done((bf16[128,2,512]{2,0,1:T(8,128)(2,1)S(1)}, bf16[128,2,512]{2,0,1:T(8,128)(2,1)S(1)}, u32[]{:S(2)}, u32[]{:S(2)}) %collective-permute-start.11) | collective-permute-done | bytes 262176 | tf_op jit(solution)/shard_map/ppermute | solution.py:54
  139.6 3.0 %collective-permute-start.12 = (bf16[128,1,512]{2,0,1:T(8,128)(2,1)S(1)}, bf16[128,1,512]{2,0,1:T(8,128)(2,1)S(1)}, u32[]{:S(2)}, u32[]{:S(2)}) collective-permute-start(bf16[128,1,512]{2,0,1:T(8,128)(2,1)S(1)} %fusion.15), channel_id=1, source_target_pairs={{0,8},{1,9},{2,10},{3,11},{4,12},{5,13},{6,14},{7,15},{8,0},{9,1},... | collective-permute-start | bytes 393224 | tf_op jit(solution)/shard_map/ppermute | solution.py:54
  142.6 7.0 %convolution_convert_fusion = bf16[1024,4096]{1,0:T(8,128)(2,1)} fusion(bf16[128,4096]{0,1:T(8,128)(2,1)} %collective-permute-done.14, bf16[128,4096]{0,1:T(8,128)(2,1)S(1)} %get-tuple-element.20, bf16[128,1024]{1,0:T(8,128)(2,1)S(1)} %bitcast.284, bf16[128,1024]{1,0:T(8,128)(2,1)S(1)} %bitcast.283), kind=kOutput, calls=%fused_computation.4 | convolution fusion | flops 2156920832 | bytes 11010048 | tf_op jit(solution)/shard_map/tr,td->rd/dot_general | solution.py:204
  (72 shorter events, 12.5 us)
Async XLA Ops:
  0.6 10.6 %collective-permute-start = (bf16[128,1,512]{2,0,1:T(8,128)(2,1)}, bf16[128,1,512]{2,0,1:T(8,128)(2,1)S(1)}, u32[]{:S(2)}, u32[]{:S(2)}) collective-permute-start(bf16[128,1,512]{2,0,1:T(8,128)(2,1)} %bitcast.287), channel_id=1, source_target_pairs={{0,8},{1,9},{2,10},{3,11},{4,12},{5,13},{6,14},{7,15},{8,0},{9,1},... | collective-permute-start | bytes 393224 | tf_op jit(solution)/shard_map/ppermute | solution.py:71
  12.2 7.5 %collective-permute-start.1 = (bf16[128,2,512]{2,0,1:T(8,128)(2,1)S(1)}, bf16[128,2,512]{2,0,1:T(8,128)(2,1)S(1)}, u32[]{:S(2)}, u32[]{:S(2)}) collective-permute-start(bf16[128,2,512]{2,0,1:T(8,128)(2,1)S(1)} %maximum_bitcast_fusion), channel_id=1, source_target_pairs={{0,4},{1,5},{2,6},{3,7},{4,0},{5,1},{6,2},{7,3},{8,12},{9,13},{10,... | collective-permute-start | bytes 786440 | tf_op jit(solution)/shard_map/ppermute | solution.py:71
  19.9 12.3 %collective-permute-start.2 = (bf16[128,4,512]{2,0,1:T(8,128)(2,1)S(1)}, bf16[128,4,512]{2,0,1:T(8,128)(2,1)S(1)}, u32[]{:S(2)}, u32[]{:S(2)}) collective-permute-start(bf16[128,4,512]{2,0,1:T(8,128)(2,1)S(1)} %bitcast.279), channel_id=1, source_target_pairs={{0,2},{1,3},{2,0},{3,1},{4,6},{5,7},{6,4},{7,5},{8,10},{9,11},{10,... | collective-permute-start | bytes 1572872 | tf_op jit(solution)/shard_map/ppermute | solution.py:71
  21.3 7.0 %copy-start.1 = (s32[128,64]{0,1:T(8,128)S(1)}, s32[128,64]{0,1:T(8,128)}, u32[]{:S(2)}) copy-start(s32[128,64]{0,1:T(8,128)} %param.7) | copy-start | bytes 98308
  26.7 46.0 %collective-permute-start.4 = (bf16[256,4096]{1,0:T(8,128)(2,1)}, bf16[256,4096]{1,0:T(8,128)(2,1)}, u32[]{:S(2)}, u32[]{:S(2)}) collective-permute-start(bf16[256,4096]{1,0:T(8,128)(2,1)} %bitcast.23), channel_id=1, source_target_pairs={{0,16},{16,0},{1,17},{17,1},{2,18},{18,2},{3,19},{19,3},{4,20},{20... | collective-permute-start | bytes 6291464 | tf_op jit(solution)/shard_map/ppermute | solution.py:142
  32.3 0.8 copy-start
  32.5 7.1 %collective-permute-start.3 = (bf16[128,8,512]{2,0,1:T(8,128)(2,1)S(1)}, bf16[128,8,512]{2,0,1:T(8,128)(2,1)}, u32[]{:S(2)}, u32[]{:S(2)}) collective-permute-start(bf16[128,8,512]{2,0,1:T(8,128)(2,1)S(1)} %bitcast.278), channel_id=1, source_target_pairs={{0,1},{1,0},{2,3},{3,2},{4,5},{5,4},{6,7},{7,6},{8,9},{9,8},{10,11... | collective-permute-start | bytes 3145736 | tf_op jit(solution)/shard_map/ppermute | solution.py:71
  75.7 1.2 collective-permute-start.5
  77.0 3.7 %collective-permute-start.6 = (f32[3,128]{1,0:T(4,128)S(1)}, f32[3,128]{1,0:T(4,128)S(1)}, u32[]{:S(2)}, u32[]{:S(2)}) collective-permute-start(f32[3,128]{1,0:T(4,128)S(1)} %pad_maximum_fusion.5), channel_id=1, source_target_pairs={{0,2},{1,3},{2,0},{3,1},{4,6},{5,7},{6,4},{7,5},{8,10},{9,11},{10,... | collective-permute-start | bytes 4616 | tf_op jit(solution)/shard_map/ppermute | solution.py:30
  80.7 4.1 %collective-permute-start.7 = (f32[3,128]{1,0:T(4,128)S(1)}, f32[3,128]{1,0:T(4,128)S(1)}, u32[]{:S(2)}, u32[]{:S(2)}) collective-permute-start(f32[3,128]{1,0:T(4,128)S(1)} %pad_maximum_fusion.6), channel_id=1, source_target_pairs={{0,4},{1,5},{2,6},{3,7},{4,0},{5,1},{6,2},{7,3},{8,12},{9,13},{10,... | collective-permute-start | bytes 4616 | tf_op jit(solution)/shard_map/ppermute | solution.py:30
  84.8 5.5 %collective-permute-start.8 = (f32[3,128]{1,0:T(4,128)S(1)}, f32[3,128]{1,0:T(4,128)S(1)}, u32[]{:S(2)}, u32[]{:S(2)}) collective-permute-start(f32[3,128]{1,0:T(4,128)S(1)} %pad_maximum_fusion.7), channel_id=1, source_target_pairs={{0,8},{1,9},{2,10},{3,11},{4,12},{5,13},{6,14},{7,15},{8,0},{9,1},... | collective-permute-start | bytes 4616 | tf_op jit(solution)/shard_map/ppermute | solution.py:30
  103.7 2.7 %collective-permute-start.9 = (bf16[128,8,512]{0,2,1:T(8,128)(2,1)S(1)}, bf16[128,8,512]{0,2,1:T(8,128)(2,1)S(1)}, u32[]{:S(2)}, u32[]{:S(2)}) collective-permute-start(bf16[128,8,512]{0,2,1:T(8,128)(2,1)S(1)} %fusion.5), channel_id=1, source_target_pairs={{0,1},{1,0},{2,3},{3,2},{4,5},{5,4},{6,7},{7,6},{8,9},{9,8},{10,11... | collective-permute-start | bytes 3145736 | tf_op jit(solution)/shard_map/ppermute | solution.py:54
  104.2 38.5 %collective-permute-start.14 = (bf16[128,4096]{0,1:T(8,128)(2,1)}, bf16[128,4096]{0,1:T(8,128)(2,1)}, u32[]{:S(2)}, u32[]{:S(2)}) collective-permute-start(bf16[128,4096]{0,1:T(8,128)(2,1)} %get-tuple-element.19), channel_id=1, source_target_pairs={{0,16},{16,0},{1,17},{17,1},{2,18},{18,2},{3,19},{19,3},{4,20},{20... | collective-permute-start | bytes 3145736 | tf_op jit(solution)/shard_map/ppermute | solution.py:130
  105.7 25.5 %collective-permute-start.13 = (bf16[1,128,256]{2,1,0:T(8,128)(2,1)S(1)}, bf16[1,128,256]{2,1,0:T(8,128)(2,1)S(1)}, u32[]{:S(2)}, u32[]{:S(2)}) collective-permute-start(bf16[1,128,256]{2,1,0:T(8,128)(2,1)S(1)} %bitcast.282), channel_id=1, source_target_pairs={{0,16},{16,0},{1,17},{17,1},{2,18},{18,2},{3,19},{19,3},{4,20},{20... | collective-permute-start | bytes 196616 | tf_op jit(solution)/shard_map/ppermute | solution.py:88
  112.3 19.0 %collective-permute-start.10 = (bf16[128,4,512]{2,0,1:T(8,128)(2,1)S(1)}, bf16[128,4,512]{2,0,1:T(8,128)(2,1)S(1)}, u32[]{:S(2)}, u32[]{:S(2)}) collective-permute-start(bf16[128,4,512]{2,0,1:T(8,128)(2,1)S(1)} %fusion.6), channel_id=1, source_target_pairs={{0,2},{1,3},{2,0},{3,1},{4,6},{5,7},{6,4},{7,5},{8,10},{9,11},{10,... | collective-permute-start | bytes 1572872 | tf_op jit(solution)/shard_map/ppermute | solution.py:54
  131.7 7.8 %collective-permute-start.11 = (bf16[128,2,512]{2,0,1:T(8,128)(2,1)S(1)}, bf16[128,2,512]{2,0,1:T(8,128)(2,1)S(1)}, u32[]{:S(2)}, u32[]{:S(2)}) collective-permute-start(bf16[128,2,512]{2,0,1:T(8,128)(2,1)S(1)} %fusion.13), channel_id=1, source_target_pairs={{0,4},{1,5},{2,6},{3,7},{4,0},{5,1},{6,2},{7,3},{8,12},{9,13},{10,... | collective-permute-start | bytes 786440 | tf_op jit(solution)/shard_map/ppermute | solution.py:54
  139.6 10.0 %collective-permute-start.12 = (bf16[128,1,512]{2,0,1:T(8,128)(2,1)S(1)}, bf16[128,1,512]{2,0,1:T(8,128)(2,1)S(1)}, u32[]{:S(2)}, u32[]{:S(2)}) collective-permute-start(bf16[128,1,512]{2,0,1:T(8,128)(2,1)S(1)} %fusion.15), channel_id=1, source_target_pairs={{0,8},{1,9},{2,10},{3,11},{4,12},{5,13},{6,14},{7,15},{8,0},{9,1},... | collective-permute-start | bytes 393224 | tf_op jit(solution)/shard_map/ppermute | solution.py:54
